TPU v7x, 32 devices: a whole 2x2x4 slice. The times are simulated.
32 devices in a mesh: tile: 8 (over z, core), deg: 4 (over y, x).
Axes of the slice: x: 2, y: 2, z: 4, core: 2. Of those that a mesh axis runs over, the one named last changes fastest.
Arguments:
- field: float32 [3, 8, 128, 512], P(None, None, 'tile', 'deg'), may hold values from -6 to 6
- flow: float32 [3, 8, 128, 512], P(None, None, 'tile', 'deg'), may hold values from -3 to 3
- match_ops: bfloat16 [32, 512, 512], P(('tile', 'deg')), may hold values from -0.5 to 20.5
- wave_of_slot: int32 [32], replicated, may hold values from 0 to 31, each once
Outputs:
- advanced: float32 [3, 8, 128, 512], P(None, None, 'tile', 'deg')
Inputs may be any that keep to these rules, and one draw needn't show every extreme that they name: `wave_of_slot`: every wavenumber from 0 to 31 is named by exactly one slot.
All inputs are finite; a program needn't handle non-finite values.
Results may differ from a plain program's by a relative error of at most 0.00065.
Values may be sent and summed in bfloat16 or wider, within the bound.
No kernel may reach another device: no remote copies, remote signals or barrier semaphores. Data moves between devices by JAX's collectives and lax.ppermute only.
A program may use at most 64 MiB of HBM per device.

v0:
```python
import math

import jax
import jax.numpy as jnp
from jax import lax
from jax.sharding import PartitionSpec as P

P_SIZE = 8


diffusivity = 0.05
time_step = 0.01
highest = lax.Precision.HIGHEST
gll_interior = [0.2092992179024789, 0.5917001814331423, 0.8717401485096066]


def padded_2(value, sides, width):
    for axis, dim in sides:
        size, length = (lax.axis_size(axis), value.shape[dim])
        up = [(i, (i + 1) % size) for i in range(size)]
        down = [(j, i) for i, j in up]
        last = lax.slice_in_dim(value, length - width, length, axis=dim)
        first = lax.slice_in_dim(value, 0, width, axis=dim)
        before = lax.ppermute(last, axis, up)
        after = lax.ppermute(first, axis, down)
        value = jnp.concatenate([before, value, after], axis=dim)
    return value


def legendre_value(point, degree):
    previous = 1.0
    current = point
    for order in range(1, degree):
        following = ((2 * order + 1) * point * current - order * previous) / (order + 1)
        previous = current
        current = following
    return current


def gll_tables(count):
    degree = count - 1
    points = [-1.0] + [-value for value in reversed(gll_interior)] + list(gll_interior) + [1.0]
    values = [legendre_value(point, degree) for point in points]
    weights = [2.0 / (degree * (degree + 1) * value * value) for value in values]
    matrix = [
        [
            values[row] / (values[col] * (points[row] - points[col])) if row != col else 0.0
            for col in range(count)
        ]
        for row in range(count)
    ]
    matrix[0][0] = -degree * (degree + 1) / 4.0
    matrix[count - 1][count - 1] = degree * (degree + 1) / 4.0
    return (points, weights, matrix)


def apply_along(values, axis_pos, matrix):
    shape = values.shape
    blocks = values.reshape(
        shape[:axis_pos] + (shape[axis_pos] // P_SIZE, P_SIZE) + shape[axis_pos + 1 :]
    )
    letters = list("abcdefg"[: blocks.ndim])
    source = list(letters)
    source[axis_pos + 1] = "p"
    target = list(letters)
    target[axis_pos + 1] = "q"
    formula = "".join(source) + ",qp->" + "".join(target)
    return jnp.einsum(formula, blocks, matrix, precision=highest).reshape(shape)


def assemble_dim(values, axis_pos, left, right):
    shape = values.shape
    count = shape[axis_pos] // P_SIZE
    blocks = values.reshape(shape[:axis_pos] + (count, P_SIZE) + shape[axis_pos + 1 :])
    edge_shape = shape[:axis_pos] + (1, 1) + shape[axis_pos + 1 :]
    first = lax.slice_in_dim(blocks, 0, 1, axis=axis_pos + 1)
    last = lax.slice_in_dim(blocks, P_SIZE - 1, P_SIZE, axis=axis_pos + 1)
    before = jnp.concatenate(
        [left.reshape(edge_shape), lax.slice_in_dim(last, 0, count - 1, axis=axis_pos)],
        axis=axis_pos,
    )
    after = jnp.concatenate(
        [lax.slice_in_dim(first, 1, count, axis=axis_pos), right.reshape(edge_shape)], axis=axis_pos
    )
    middle = lax.slice_in_dim(blocks, 1, P_SIZE - 1, axis=axis_pos + 1)
    joined = jnp.concatenate([first + before, middle, last + after], axis=axis_pos + 1)
    return joined.reshape(shape)


def assembled_weights(weights, count, lead, trail):
    position = jnp.arange(count * P_SIZE, dtype=jnp.int32)
    local_point = position % P_SIZE
    element = position // P_SIZE
    base = jnp.tile(weights, count)
    starts = (
        jnp.where(local_point == 0, jnp.where(element > 0, 1.0, lead), 0.0) * weights[P_SIZE - 1]
    )
    ends = (
        jnp.where(local_point == P_SIZE - 1, jnp.where(element < count - 1, 1.0, trail), 0.0)
        * weights[0]
    )
    return base + starts + ends


def phases(waves, elem_start, elem_count, span, points):
    element = elem_start + jnp.arange(elem_count * P_SIZE, dtype=jnp.int32) // P_SIZE
    whole = waves[:, None] * (2 * element + 1)[None, :] % span
    fraction = waves.astype(jnp.float32)[:, None] * jnp.tile(points, elem_count)[None, :]
    return 2.0 * math.pi / span * (whole.astype(jnp.float32) + fraction)


def local(field, flow, match_ops, wave_of_slot):
    tiles = lax.axis_size("tile")
    groups = lax.axis_size("deg")
    tile_index = lax.axis_index("tile")
    group_index = lax.axis_index("deg")
    radial_nodes = field.shape[1]
    na_dev = field.shape[2]
    nb_dev = field.shape[3]
    elems_a = na_dev // P_SIZE
    elems_b = nb_dev // P_SIZE
    span = 2 * elems_a * tiles
    per_tile = wave_of_slot.shape[0] // tiles
    scale = P_SIZE / (na_dev * tiles)
    points_list, weights_list, matrix_list = gll_tables(P_SIZE)
    points = jnp.asarray(points_list, jnp.float32)
    weights = jnp.asarray(weights_list, jnp.float32)
    dmat = jnp.asarray(matrix_list, jnp.float32)
    block = jnp.kron(jnp.eye(elems_b, dtype=jnp.float32), dmat)
    lead = (group_index > 0).astype(jnp.float32)
    trail = (group_index < groups - 1).astype(jnp.float32)
    w_r = jnp.tile(weights, radial_nodes // P_SIZE)
    w_a = jnp.tile(weights, elems_a)
    w_b = jnp.tile(weights, elems_b)
    mass3 = w_r[:, None, None] * w_a[None, :, None] * w_b[None, None, :]
    surface_weight = w_a[:, None] * w_b[None, :]
    assembled = (
        assembled_weights(weights, radial_nodes // P_SIZE, 0.0, 0.0)[:, None, None]
        * assembled_weights(weights, elems_a, 1.0, 1.0)[None, :, None]
        * assembled_weights(weights, elems_b, lead, trail)[None, None, :]
    )
    column_mask = jnp.concatenate([lead[None], jnp.ones((nb_dev,), jnp.float32), trail[None]])

    def derive(values, direction, transpose):
        if direction == 2:
            table = block if transpose else block.T
            return jnp.dot(values, table, precision=highest)
        return apply_along(values, direction, dmat.T if transpose else dmat)

    flow_parts = [flow[0], flow[1], flow[2]]
    grad_flow = [
        [derive(flow_parts[component], direction, False) for direction in range(3)]
        for component in range(3)
    ]

    def analyse(surface):
        angle = phases(wave_of_slot, tile_index * elems_a, elems_a, span, points)
        table = (
            jnp.stack([jnp.cos(angle), jnp.sin(angle)], axis=1) * (w_a * scale)[None, None, :]
        ).reshape(lax.axis_size("tile") * per_tile * 2, na_dev)
        return jnp.dot(table, surface, precision=highest).reshape(
            lax.axis_size("tile") * per_tile, 2, nb_dev
        )

    def surface_flux(surface):
        coeff = lax.psum_scatter(analyse(surface), "tile", scatter_dimension=0, tiled=True)
        owned = lax.all_to_all(
            coeff.astype(jnp.bfloat16), "deg", split_axis=0, concat_axis=2, tiled=True
        )
        mapped = jnp.einsum("kpq,kcq->kcp", match_ops, owned, preferred_element_type=jnp.float32)
        matched = lax.all_to_all(mapped, "deg", split_axis=2, concat_axis=0, tiled=True)
        my_waves = lax.dynamic_slice_in_dim(wave_of_slot, tile_index * per_tile, per_tile)
        flat_matched = matched.reshape(per_tile * 2, nb_dev)
        angle = phases(
            my_waves, jnp.int32(0) // P_SIZE, lax.axis_size("tile") * na_dev // P_SIZE, span, points
        )
        table = jnp.stack([jnp.cos(angle).T, jnp.sin(angle).T], axis=2).reshape(
            lax.axis_size("tile") * na_dev, per_tile * 2
        )
        total = lax.psum_scatter(
            jnp.dot(table, flat_matched, precision=highest), "tile", scatter_dimension=0, tiled=True
        )
        return -total

    def tendency(parts):
        rhs = []
        for component in range(3):
            slopes = [derive(parts[component], direction, False) for direction in range(3)]
            stretch = (
                parts[0] * grad_flow[component][0]
                + parts[1] * grad_flow[component][1]
                + parts[2] * grad_flow[component][2]
            )
            carried = (
                flow_parts[0] * slopes[0] + flow_parts[1] * slopes[1] + flow_parts[2] * slopes[2]
            )
            spread = (
                derive(mass3 * slopes[0], 0, True)
                + derive(mass3 * slopes[1], 1, True)
                + derive(mass3 * slopes[2], 2, True)
            )
            rhs.append(mass3 * (stretch - carried) - diffusivity * spread)
        flux = surface_flux(parts[0][radial_nodes - 1])
        rhs[0] = rhs[0].at[radial_nodes - 1].add(diffusivity * surface_weight * flux)
        stacked = jnp.stack(rhs)
        plane_r = jnp.zeros_like(lax.slice_in_dim(stacked, 0, 1, axis=1))
        stacked = assemble_dim(stacked, 1, plane_r, plane_r)
        padded = padded_2(stacked.astype(jnp.bfloat16), (("tile", 2), ("deg", 3)), 1).astype(
            stacked.dtype
        )
        padded = padded * column_mask
        along_a = assemble_dim(padded[:, :, 1:-1, :], 2, padded[:, :, 0:1, :], padded[:, :, -1:, :])
        along_b = assemble_dim(
            along_a[:, :, :, 1:-1], 3, along_a[:, :, :, 0:1], along_a[:, :, :, -1:]
        )
        return along_b / assembled[None]

    section = field + time_step * tendency([field[0], field[1], field[2]])
    return 0.5 * (field + section + time_step * tendency([section[0], section[1], section[2]]))


def solution(mesh):
    placed = (
        P(None, None, "tile", "deg"),
        P(None, None, "tile", "deg"),
        P(("tile", "deg"), None, None),
        P(),
    )
    return jax.shard_map(
        local, mesh=mesh, in_specs=placed, out_specs=P(None, None, "tile", "deg"), check_vma=False
    )
```

profile of v0, /device:TPU:0, one launch (start us, length us, event | category | flops | bytes accessed | tf_op | source)
XLA Modules:
  0.0 227.2 jit_solution(8538211180107501560)
XLA Ops:
  6.5 0.7 tile.8
  7.3 0.7 tile.11
  8.1 0.7 convert_element_type.71
  8.8 0.8 fusion.130
  9.6 0.6 copy-done.26
  10.2 1.0 fusion.116
  11.2 30.3 %all-reduce = bf16[32,2,128]{2,0,1:T(8,128)(2,1)S(1)} all-reduce(f32[32,2,128]{2,0,1:T(8,128)S(1)} %fusion.116), channel_id=2, replica_groups=mesh['tile'=8,'deg'=4] {'tile'}, use_global_device_ids=true, to_apply=%region_0.1.clone | all-reduce | flops 8192 | bytes 49152
  41.5 1.2 dynamic-slice.16
  43.4 0.6 copy.334
  43.9 3.7 %all-to-all-start = ((bf16[4,2,128]{2,1,0:T(2,128)(2,1)}), bf16[4,2,128]{2,1,0:T(2,128)(2,1)S(1)}, u32[]{:S(2)}, u32[]{:S(2)}) async-start(bf16[4,2,128]{2,1,0:T(2,128)(2,1)} %copy.334), calls=%async_computation | async-start | bytes 4096 | tf_op jit(solution)/shard_map/all_to_all | solution.py:167
  47.7 0.8 broadcast_multiply_fusion.3
  48.5 0.9 slice_bitcast_fusion.6
  49.4 1.1 fusion.51
  50.5 1.0 convolution_bitcast_fusion.6
  51.6 0.9 fusion.169
  52.6 0.7 broadcast_multiply_fusion.5
  53.3 1.0 fusion.54
  54.4 0.8 broadcast_multiply_fusion
  55.2 0.5 reshape.990
  62.1 0.5 broadcast.860
  62.6 1.2 reduce.4
  63.8 0.8 reshape.1012
  64.6 4.2 %all-to-all-start.1 = ((f32[4,1,256]{2,1,0:T(1,128)}), f32[4,1,256]{2,1,0:T(1,128)S(1)}, u32[]{:S(2)}, u32[]{:S(2)}) async-start(f32[4,1,256]{2,1,0:T(1,128)} %reshape.1012), calls=%async_computation.1 | async-start | bytes 8192 | tf_op jit(solution)/shard_map/all_to_all | solution.py:171
  68.8 4.7 %all-to-all-done.1 = f32[4,1,256]{2,1,0:T(1,128)S(1)} async-done(((f32[4,1,256]{2,1,0:T(1,128)}), f32[4,1,256]{2,1,0:T(1,128)S(1)}, u32[]{:S(2)}, u32[]{:S(2)}) %all-to-all-start.1) | async-done | bytes 4128 | tf_op jit(solution)/shard_map/all_to_all | solution.py:171
  73.5 0.6 reduce.5
  74.6 0.9 fusion.172
  76.1 25.9 %reduce-scatter.5.cloned.1.call-done = f32[16,128]{1,0:T(8,128)} async-done(((f32[128,128]{1,0:T(8,128)}), f32[16,128]{1,0:T(8,128)}) %reduce-scatter.5.cloned.1.call-update) | async-done | bytes 8208 | tf_op jit(solution)/shard_map/reduce_scatter | solution.py:180
  102.0 0.8 fusion.123
  103.0 0.4 collective-permute-start
  103.5 0.9 collective-permute-done.1
  104.4 3.5 %collective-permute-done = bf16[3,8,1,128]{3,1,2,0:T(8,128)(2,1)S(1)} collective-permute-done((bf16[3,8,1,128]{3,1,2,0:T(8,128)(2,1)S(1)}, bf16[3,8,1,128]{3,1,2,0:T(8,128)(2,1)S(1)}, u32[]{:S(2)}, u32[]{:S(2)}) %collective-permute-start) | collective-permute-done | bytes 6176 | tf_op jit(solution)/shard_map/ppermute | solution.py:24
  108.0 2.7 %collective-permute-start.3 = (bf16[3,8,18,1]{3,1,2,0:T(8,128)(2,1)S(1)}, bf16[3,8,18,1]{3,1,2,0:T(8,128)(2,1)S(1)}, u32[]{:S(2)}, u32[]{:S(2)}) collective-permute-start(bf16[3,8,18,1]{3,1,2,0:T(8,128)(2,1)S(1)} %get-tuple-element.73), channel_id=1, source_target_pairs={{1,0},{2,1},{3,2},{0,3},{5,4},{6,5},{7,6},{4,7},{9,8},{10,9},{11,1... | collective-permute-start | bytes 2600 | tf_op jit(solution)/shard_map/ppermute | solution.py:25
  110.8 2.2 collective-permute-done.3
  113.0 3.3 %collective-permute-done.2 = bf16[3,8,18,1]{3,1,2,0:T(8,128)(2,1)S(1)} collective-permute-done((bf16[3,8,18,1]{3,1,2,0:T(8,128)(2,1)S(1)}, bf16[3,8,18,1]{3,1,2,0:T(8,128)(2,1)S(1)}, u32[]{:S(2)}, u32[]{:S(2)}) %collective-permute-start.2) | collective-permute-done | bytes 896 | tf_op jit(solution)/shard_map/ppermute | solution.py:24
  117.0 0.5 copy.465
  117.7 1.3 slice.297
  119.4 0.5 slice_add_fusion.3
  120.0 2.0 maximum_bitcast_fusion
  122.1 0.4 copy.372
  126.1 26.0 %all-reduce.1 = bf16[32,2,128]{2,0,1:T(8,128)(2,1)S(1)} all-reduce(f32[32,2,128]{2,0,1:T(8,128)S(1)} %fusion.115), channel_id=4, replica_groups=mesh['tile'=8,'deg'=4] {'tile'}, use_global_device_ids=true, to_apply=%region_2.3.clone | all-reduce | flops 8192 | bytes 49152
  152.1 0.6 copy.387
  152.7 3.2 %all-to-all-start.2 = ((bf16[4,2,128]{2,1,0:T(2,128)(2,1)}), bf16[4,2,128]{2,1,0:T(2,128)(2,1)S(1)}, u32[]{:S(2)}, u32[]{:S(2)}) async-start(bf16[4,2,128]{2,1,0:T(2,128)(2,1)} %copy.387), calls=%async_computation.3 | async-start | bytes 4096 | tf_op jit(solution)/shard_map/all_to_all | solution.py:167
  156.9 3.5 %all-to-all-done.2 = bf16[4,2,128]{2,1,0:T(2,128)(2,1)S(1)} async-done(((bf16[4,2,128]{2,1,0:T(2,128)(2,1)}), bf16[4,2,128]{2,1,0:T(2,128)(2,1)S(1)}, u32[]{:S(2)}, u32[]{:S(2)}) %all-to-all-start.2) | async-done | bytes 2080 | tf_op jit(solution)/shard_map/all_to_all | solution.py:167
  160.7 1.2 reduce.6
  161.9 0.8 reshape.1014
  162.7 3.2 %all-to-all-start.3 = ((f32[4,1,256]{2,1,0:T(1,128)}), f32[4,1,256]{2,1,0:T(1,128)S(1)}, u32[]{:S(2)}, u32[]{:S(2)}) async-start(f32[4,1,256]{2,1,0:T(1,128)} %reshape.1014), calls=%async_computation.4 | async-start | bytes 8192 | tf_op jit(solution)/shard_map/all_to_all | solution.py:171
  166.3 4.3 %all-to-all-done.3 = f32[4,1,256]{2,1,0:T(1,128)S(1)} async-done(((f32[4,1,256]{2,1,0:T(1,128)}), f32[4,1,256]{2,1,0:T(1,128)S(1)}, u32[]{:S(2)}, u32[]{:S(2)}) %all-to-all-start.3) | async-done | bytes 4128 | tf_op jit(solution)/shard_map/all_to_all | solution.py:171
  170.6 0.6 reduce.7
  171.2 0.4 reshape.1015
  171.7 0.9 fusion.173
  172.9 26.3 %reduce-scatter.7.cloned.1.call-done = f32[16,128]{1,0:T(8,128)} async-done(((f32[128,128]{1,0:T(8,128)}), f32[16,128]{1,0:T(8,128)}) %reduce-scatter.7.cloned.1.call-update) | async-done | bytes 8208 | tf_op jit(solution)/shard_map/reduce_scatter | solution.py:180
  199.2 0.8 negate_multiply_fusion
  200.2 0.4 collective-permute-start.4
  200.6 0.9 collective-permute-done.5
  201.6 3.5 %collective-permute-done.4 = bf16[3,8,1,128]{3,1,2,0:T(8,128)(2,1)S(1)} collective-permute-done((bf16[3,8,1,128]{3,1,2,0:T(8,128)(2,1)S(1)}, bf16[3,8,1,128]{3,1,2,0:T(8,128)(2,1)S(1)}, u32[]{:S(2)}, u32[]{:S(2)}) %collective-permute-start.4) | collective-permute-done | bytes 6176 | tf_op jit(solution)/shard_map/ppermute | solution.py:24
  205.2 2.7 %collective-permute-start.7 = (bf16[3,8,18,1]{3,1,2,0:T(8,128)(2,1)S(1)}, bf16[3,8,18,1]{3,1,2,0:T(8,128)(2,1)S(1)}, u32[]{:S(2)}, u32[]{:S(2)}) collective-permute-start(bf16[3,8,18,1]{3,1,2,0:T(8,128)(2,1)S(1)} %get-tuple-element.71), channel_id=1, source_target_pairs={{1,0},{2,1},{3,2},{0,3},{5,4},{6,5},{7,6},{4,7},{9,8},{10,9},{11,1... | collective-permute-start | bytes 2600 | tf_op jit(solution)/shard_map/ppermute | solution.py:25
  207.9 2.3 %collective-permute-done.7 = bf16[3,8,18,1]{3,1,2,0:T(8,128)(2,1)S(1)} collective-permute-done((bf16[3,8,18,1]{3,1,2,0:T(8,128)(2,1)S(1)}, bf16[3,8,18,1]{3,1,2,0:T(8,128)(2,1)S(1)}, u32[]{:S(2)}, u32[]{:S(2)}) %collective-permute-start.7) | collective-permute-done | bytes 896 | tf_op jit(solution)/shard_map/ppermute | solution.py:25
  210.2 3.3 %collective-permute-done.6 = bf16[3,8,18,1]{3,1,2,0:T(8,128)(2,1)S(1)} collective-permute-done((bf16[3,8,18,1]{3,1,2,0:T(8,128)(2,1)S(1)}, bf16[3,8,18,1]{3,1,2,0:T(8,128)(2,1)S(1)}, u32[]{:S(2)}, u32[]{:S(2)}) %collective-permute-start.6) | collective-permute-done | bytes 896 | tf_op jit(solution)/shard_map/ppermute | solution.py:24
  214.1 0.5 copy.469
  214.8 1.3 slice.320
  216.6 0.5 slice_add_fusion.1
  217.1 2.0 maximum_bitcast_fusion.1
  219.2 0.4 copy.424
  219.6 0.8 add_multiply_fusion
  (192 shorter events, 15.8 us)
Async XLA Ops:
  6.5 55.3 %copy-start = (bf16[1,512,512]{2,1,0:T(8,128)(2,1)S(1)}, bf16[1,512,512]{2,1,0:T(8,128)(2,1)}, u32[]{:S(2)}) copy-start(bf16[1,512,512]{2,1,0:T(8,128)(2,1)} %param.13) | copy-start | bytes 1572868
  8.7 39.7 %copy-start.32 = (f32[16]{0:T(128)}, f32[16]{0:T(128)S(1)}, u32[]{:S(2)}) copy-start(f32[16]{0:T(128)S(1)} %get-tuple-element.95) | copy-start | bytes 196
  9.5 0.6 copy-start.26
  9.6 0.6 copy-start.28
  43.9 17.9 %all-to-all-start = ((bf16[4,2,128]{2,1,0:T(2,128)(2,1)}), bf16[4,2,128]{2,1,0:T(2,128)(2,1)S(1)}, u32[]{:S(2)}, u32[]{:S(2)}) async-start(bf16[4,2,128]{2,1,0:T(2,128)(2,1)} %copy.334), calls=%async_computation | async-start | bytes 4096 | tf_op jit(solution)/shard_map/all_to_all | solution.py:167
  48.5 12.3 %copy-start.24 = (f32[8,2,8]{2,1,0:T(2,128)}, f32[8,2,8]{2,1,0:T(2,128)S(1)}, u32[]{:S(2)}) copy-start(f32[8,2,8]{2,1,0:T(2,128)S(1)} %broadcast_multiply_fusion.3) | copy-start | bytes 1540
  49.4 6.3 %copy-start.2 = (f32[3,8,16,128]{3,2,1,0:T(8,128)S(1)}, f32[3,8,16,128]{3,2,1,0:T(8,128)}, u32[]{:S(2)}) copy-start(f32[3,8,16,128]{3,2,1,0:T(8,128)} %param.12) | copy-start | bytes 589828
  49.4 6.5 %copy-start.1 = (f32[3,8,16,128]{3,2,1,0:T(8,128)S(1)}, f32[3,8,16,128]{3,2,1,0:T(8,128)}, u32[]{:S(2)}) copy-start(f32[3,8,16,128]{3,2,1,0:T(8,128)} %param.11) | copy-start | bytes 589828
  51.6 7.2 %copy-start.10 = (f32[8,16,128]{2,1,0:T(8,128)}, f32[8,16,128]{2,1,0:T(8,128)S(1)}, u32[]{:S(2)}) copy-start(f32[8,16,128]{2,1,0:T(8,128)S(1)} %convolution_bitcast_fusion.6) | copy-start | bytes 196612
  51.6 4.9 %copy-start.22 = (f32[8,8,1,1]{1,0,3,2:T(8,128)S(1)}, f32[8,8,1,1]{1,0,3,2:T(8,128)}, u32[]{:S(2)}) copy-start(f32[8,8,1,1]{1,0,3,2:T(8,128)} %constant.239) | copy-start | bytes 772
  54.3 3.2 %copy-start.23 = (f32[8]{0:T(128)S(1)}, f32[8]{0:T(128)}, u32[]{:S(2)}) copy-start(f32[8]{0:T(128)} %constant.223.clone) | copy-start | bytes 100
  55.2 2.8 %copy-start.3 = (f32[8,8,1]{1,0,2:T(8,128)S(1)}, f32[8,8,1]{1,0,2:T(8,128)}, u32[]{:S(2)}) copy-start(f32[8,8,1]{1,0,2:T(8,128)} %constant.238) | copy-start | bytes 772
  56.0 3.1 %copy-start.4 = (f32[8,16,128]{2,1,0:T(8,128)}, f32[8,16,128]{2,1,0:T(8,128)S(1)}, u32[]{:S(2)}) copy-start(f32[8,16,128]{2,1,0:T(8,128)S(1)} %convolution_bitcast_fusion.5) | copy-start | bytes 196612
  56.5 19.0 %copy-start.6 = (f32[8,16,128]{2,1,0:T(8,128)}, f32[8,16,128]{2,1,0:T(8,128)S(1)}, u32[]{:S(2)}) copy-start(f32[8,16,128]{2,1,0:T(8,128)S(1)} %convolution_bitcast_fusion.9) | copy-start | bytes 196612
  57.0 3.0 %copy-start.31 = (f32[8]{0:T(128)S(1)}, f32[8]{0:T(128)}, u32[]{:S(2)}) copy-start(f32[8]{0:T(128)} %constant.222.clone) | copy-start | bytes 100
  57.0 3.1 %copy-start.30 = (s32[32]{0:T(128)S(1)}, s32[32]{0:T(128)}, u32[]{:S(2)}) copy-start(s32[32]{0:T(128)} %param.14) | copy-start | bytes 388
  57.3 4.0 %copy-start.8 = (f32[8,16,128]{2,1,0:T(8,128)}, f32[8,16,128]{2,1,0:T(8,128)S(1)}, u32[]{:S(2)}) copy-start(f32[8,16,128]{2,1,0:T(8,128)S(1)} %convolution_bitcast_fusion.13) | copy-start | bytes 196612
  57.5 3.8 %copy-start.12 = (f32[8,16,128]{2,1,0:T(8,128)}, f32[8,16,128]{2,1,0:T(8,128)S(1)}, u32[]{:S(2)}) copy-start(f32[8,16,128]{2,1,0:T(8,128)S(1)} %convolution_bitcast_fusion.14) | copy-start | bytes 196612
  58.4 2.7 %copy-start.14 = (f32[8,16,128]{2,0,1:T(8,128)}, f32[8,16,128]{2,0,1:T(8,128)S(1)}, u32[]{:S(2)}) copy-start(f32[8,16,128]{2,0,1:T(8,128)S(1)} %fusion.98) | copy-start | bytes 196612
  59.5 16.0 %copy-start.16 = (f32[8,16,128]{2,0,1:T(8,128)}, f32[8,16,128]{2,0,1:T(8,128)S(1)}, u32[]{:S(2)}) copy-start(f32[8,16,128]{2,0,1:T(8,128)S(1)} %fusion.84) | copy-start | bytes 196612
  60.0 1.8 copy-start.18
  61.8 14.1 %copy-start.20 = (f32[8,16,128]{2,1,0:T(8,128)}, f32[8,16,128]{2,1,0:T(8,128)S(1)}, u32[]{:S(2)}) copy-start(f32[8,16,128]{2,1,0:T(8,128)S(1)} %convolution_bitcast_fusion.10) | copy-start | bytes 196612
  64.6 8.9 %all-to-all-start.1 = ((f32[4,1,256]{2,1,0:T(1,128)}), f32[4,1,256]{2,1,0:T(1,128)S(1)}, u32[]{:S(2)}, u32[]{:S(2)}) async-start(f32[4,1,256]{2,1,0:T(1,128)} %reshape.1012), calls=%async_computation.1 | async-start | bytes 8192 | tf_op jit(solution)/shard_map/all_to_all | solution.py:171
  68.8 33.2 %reduce-scatter.5.cloned.1.call-start = ((), (), s32[]{:S(2)}) async-start(), calls=%async_computation.6 | async-start | bytes 73728 | tf_op jit(solution)/shard_map/reduce_scatter | solution.py:180
  102.8 1.5 collective-permute-start.1
  103.0 4.9 %collective-permute-start = (bf16[3,8,1,128]{3,1,2,0:T(8,128)(2,1)S(1)}, bf16[3,8,1,128]{3,1,2,0:T(8,128)(2,1)S(1)}, u32[]{:S(2)}, u32[]{:S(2)}) collective-permute-start(bf16[3,8,1,128]{3,1,2,0:T(8,128)(2,1)S(1)} %get-tuple-element.76), channel_id=1, source_target_pairs={{0,4},{4,8},{8,12},{12,16},{16,20},{20,24},{24,28},{28,0},{1,5},{5... | collective-permute-start | bytes 18440 | tf_op jit(solution)/shard_map/ppermute | solution.py:24
  108.0 5.0 %collective-permute-start.3 = (bf16[3,8,18,1]{3,1,2,0:T(8,128)(2,1)S(1)}, bf16[3,8,18,1]{3,1,2,0:T(8,128)(2,1)S(1)}, u32[]{:S(2)}, u32[]{:S(2)}) collective-permute-start(bf16[3,8,18,1]{3,1,2,0:T(8,128)(2,1)S(1)} %get-tuple-element.73), channel_id=1, source_target_pairs={{1,0},{2,1},{3,2},{0,3},{5,4},{6,5},{7,6},{4,7},{9,8},{10,9},{11,1... | collective-permute-start | bytes 2600 | tf_op jit(solution)/shard_map/ppermute | solution.py:25
  110.7 5.6 %collective-permute-start.2 = (bf16[3,8,18,1]{3,1,2,0:T(8,128)(2,1)S(1)}, bf16[3,8,18,1]{3,1,2,0:T(8,128)(2,1)S(1)}, u32[]{:S(2)}, u32[]{:S(2)}) collective-permute-start(bf16[3,8,18,1]{3,1,2,0:T(8,128)(2,1)S(1)} %get-tuple-element.72), channel_id=1, source_target_pairs={{0,1},{1,2},{2,3},{3,0},{4,5},{5,6},{6,7},{7,4},{8,9},{9,10},{10,1... | collective-permute-start | bytes 2600 | tf_op jit(solution)/shard_map/ppermute | solution.py:24
  122.0 1.8 copy-start.5
  122.0 1.8 copy-start.7
  122.0 1.8 copy-start.9
  122.0 1.8 copy-start.11
  122.0 1.8 copy-start.13
  122.1 1.8 copy-start.15
  122.1 1.8 copy-start.17
  122.1 1.8 copy-start.19
  122.5 1.4 copy-start.21
  122.5 1.5 copy-start.27
  122.5 1.5 copy-start.29
  122.5 1.5 copy-start.33
  122.5 1.8 copy-start.25
  152.7 7.8 %all-to-all-start.2 = ((bf16[4,2,128]{2,1,0:T(2,128)(2,1)}), bf16[4,2,128]{2,1,0:T(2,128)(2,1)S(1)}, u32[]{:S(2)}, u32[]{:S(2)}) async-start(bf16[4,2,128]{2,1,0:T(2,128)(2,1)} %copy.387), calls=%async_computation.3 | async-start | bytes 4096 | tf_op jit(solution)/shard_map/all_to_all | solution.py:167
  162.7 7.9 %all-to-all-start.3 = ((f32[4,1,256]{2,1,0:T(1,128)}), f32[4,1,256]{2,1,0:T(1,128)S(1)}, u32[]{:S(2)}, u32[]{:S(2)}) async-start(f32[4,1,256]{2,1,0:T(1,128)} %reshape.1014), calls=%async_computation.4 | async-start | bytes 8192 | tf_op jit(solution)/shard_map/all_to_all | solution.py:171
  166.0 33.2 %reduce-scatter.7.cloned.1.call-start = ((), (), s32[]{:S(2)}) async-start(), calls=%async_computation.7 | async-start | bytes 73728 | tf_op jit(solution)/shard_map/reduce_scatter | solution.py:180
  200.0 1.5 collective-permute-start.5
  200.2 4.9 %collective-permute-start.4 = (bf16[3,8,1,128]{3,1,2,0:T(8,128)(2,1)S(1)}, bf16[3,8,1,128]{3,1,2,0:T(8,128)(2,1)S(1)}, u32[]{:S(2)}, u32[]{:S(2)}) collective-permute-start(bf16[3,8,1,128]{3,1,2,0:T(8,128)(2,1)S(1)} %get-tuple-element.74), channel_id=1, source_target_pairs={{0,4},{4,8},{8,12},{12,16},{16,20},{20,24},{24,28},{28,0},{1,5},{5... | collective-permute-start | bytes 18440 | tf_op jit(solution)/shard_map/ppermute | solution.py:24
  205.2 5.0 %collective-permute-start.7 = (bf16[3,8,18,1]{3,1,2,0:T(8,128)(2,1)S(1)}, bf16[3,8,18,1]{3,1,2,0:T(8,128)(2,1)S(1)}, u32[]{:S(2)}, u32[]{:S(2)}) collective-permute-start(bf16[3,8,18,1]{3,1,2,0:T(8,128)(2,1)S(1)} %get-tuple-element.71), channel_id=1, source_target_pairs={{1,0},{2,1},{3,2},{0,3},{5,4},{6,5},{7,6},{4,7},{9,8},{10,9},{11,1... | collective-permute-start | bytes 2600 | tf_op jit(solution)/shard_map/ppermute | solution.py:25
  207.9 5.6 %collective-permute-start.6 = (bf16[3,8,18,1]{3,1,2,0:T(8,128)(2,1)S(1)}, bf16[3,8,18,1]{3,1,2,0:T(8,128)(2,1)S(1)}, u32[]{:S(2)}, u32[]{:S(2)}) collective-permute-start(bf16[3,8,18,1]{3,1,2,0:T(8,128)(2,1)S(1)} %get-tuple-element.70), channel_id=1, source_target_pairs={{0,1},{1,2},{2,3},{3,0},{4,5},{5,6},{6,7},{7,4},{8,9},{9,10},{10,1... | collective-permute-start | bytes 2600 | tf_op jit(solution)/shard_map/ppermute | solution.py:24
Sparse Core Ops, SparseCore 0:
  75.7 26.3 reduce-scatter.4
  172.8 26.3 reduce-scatter.6
where the time goes:
time: 228 us; the launch traced here: 227 us
  waiting for transfers between devices  84.8 us (37%)
  blocking collectives  56.3 us (25%)
  starting transfers between devices  21 us (9%)
  local copies, waits for them, and re-layouts  17.1 us (8%)
  matrix products  16.9 us (7%)
  other arithmetic  15.9 us (7%)
  between operations  15.3 us (7%)
    unnamed x2, blocking collectives  56.3 us
    reduce_scatter x2, waiting for transfers between devices, surface_flux(): lax.psum_scatter(jnp.dot(table, flat_matched, precision=highest), 'tile',...  52.2 us
    ppermute x4, waiting for transfers between devices, padded_2(): before = lax.ppermute(last, axis, up)  13.6 us
    dot_general x30, matrix products, apply_along(): return jnp.einsum(formula, blocks, matrix, precision=highest).reshape(shape)  9.26 us
    all_to_all x2, waiting for transfers between devices, surface_flux(): lax.all_to_all(mapped, 'deg', split_axis=2, concat_axis=0, tiled=True)  8.98 us
    all_to_all x2, starting transfers between devices, surface_flux(): lax.all_to_all(mapped, 'deg', split_axis=2, concat_axis=0, tiled=True)  7.44 us
    all_to_all x2, starting transfers between devices, surface_flux(): lax.all_to_all(coeff.astype(jnp.bfloat16), 'deg', split_axis=0, concat_ax...  6.94 us
    unnamed x81, local copies, waits for them, and re-layouts  6.64 us
  transfers between devices with their start and end apart: 14, of which 13 were waited for; matrix products, arithmetic and copies ran while one was open for 7% of the time, Pallas kernels for 0%

commit v1 on v0

--- a/solution.py
+++ b/solution.py
@@ -109,9 +109,27 @@
     return 2.0 * math.pi / span * (whole.astype(jnp.float32) + fraction)
 
 
+def phases_at(waves, position, span, points):
+    element = position // P_SIZE
+    whole = waves[:, None] * (2 * element + 1)[None, :] % span
+    fraction = waves.astype(jnp.float32)[:, None] * points[position % P_SIZE][None, :]
+    return 2.0 * math.pi / span * (whole.astype(jnp.float32) + fraction)
+
+
+def shift_pairs(sizes, steps):
+    count = sizes[0] * sizes[1]
+    pairs = []
+    for source in range(count):
+        t, g = divmod(source, sizes[1])
+        target = ((t + steps[0]) % sizes[0]) * sizes[1] + (g + steps[1]) % sizes[1]
+        pairs.append((source, target))
+    return pairs
+
+
 def local(field, flow, match_ops, wave_of_slot):
     tiles = lax.axis_size("tile")
     groups = lax.axis_size("deg")
+    both = ("tile", "deg")
     tile_index = lax.axis_index("tile")
     group_index = lax.axis_index("deg")
     radial_nodes = field.shape[1]
@@ -119,8 +137,8 @@
     nb_dev = field.shape[3]
     elems_a = na_dev // P_SIZE
     elems_b = nb_dev // P_SIZE
+    nb = nb_dev * groups
     span = 2 * elems_a * tiles
-    per_tile = wave_of_slot.shape[0] // tiles
     scale = P_SIZE / (na_dev * tiles)
     points_list, weights_list, matrix_list = gll_tables(P_SIZE)
     points = jnp.asarray(points_list, jnp.float32)
@@ -133,13 +151,15 @@
     w_a = jnp.tile(weights, elems_a)
     w_b = jnp.tile(weights, elems_b)
     mass3 = w_r[:, None, None] * w_a[None, :, None] * w_b[None, None, :]
-    surface_weight = w_a[:, None] * w_b[None, :]
     assembled = (
         assembled_weights(weights, radial_nodes // P_SIZE, 0.0, 0.0)[:, None, None]
         * assembled_weights(weights, elems_a, 1.0, 1.0)[None, :, None]
         * assembled_weights(weights, elems_b, lead, trail)[None, None, :]
     )
     column_mask = jnp.concatenate([lead[None], jnp.ones((nb_dev,), jnp.float32), trail[None]])
+    rows_ext = (tile_index * na_dev - 1 + jnp.arange(na_dev + 2, dtype=jnp.int32)) % (na_dev * tiles)
+    cols_ext = group_index * nb_dev - 1 + jnp.arange(nb_dev + 2, dtype=jnp.int32)
+    surface_ext = weights[rows_ext % P_SIZE][:, None] * weights[cols_ext % P_SIZE][None, :]
 
     def derive(values, direction, transpose):
         if direction == 2:
@@ -153,34 +173,50 @@
         for component in range(3)
     ]
 
-    def analyse(surface):
+    def surface_flux(surface):
         angle = phases(wave_of_slot, tile_index * elems_a, elems_a, span, points)
         table = (
             jnp.stack([jnp.cos(angle), jnp.sin(angle)], axis=1) * (w_a * scale)[None, None, :]
-        ).reshape(lax.axis_size("tile") * per_tile * 2, na_dev)
-        return jnp.dot(table, surface, precision=highest).reshape(
-            lax.axis_size("tile") * per_tile, 2, nb_dev
-        )
-
-    def surface_flux(surface):
-        coeff = lax.psum_scatter(analyse(surface), "tile", scatter_dimension=0, tiled=True)
-        owned = lax.all_to_all(
-            coeff.astype(jnp.bfloat16), "deg", split_axis=0, concat_axis=2, tiled=True
-        )
-        mapped = jnp.einsum("kpq,kcq->kcp", match_ops, owned, preferred_element_type=jnp.float32)
-        matched = lax.all_to_all(mapped, "deg", split_axis=2, concat_axis=0, tiled=True)
-        my_waves = lax.dynamic_slice_in_dim(wave_of_slot, tile_index * per_tile, per_tile)
-        flat_matched = matched.reshape(per_tile * 2, nb_dev)
-        angle = phases(
-            my_waves, jnp.int32(0) // P_SIZE, lax.axis_size("tile") * na_dev // P_SIZE, span, points
-        )
-        table = jnp.stack([jnp.cos(angle).T, jnp.sin(angle).T], axis=2).reshape(
-            lax.axis_size("tile") * na_dev, per_tile * 2
-        )
-        total = lax.psum_scatter(
-            jnp.dot(table, flat_matched, precision=highest), "tile", scatter_dimension=0, tiled=True
-        )
-        return -total
+        ).reshape(-1, na_dev)
+        partial = jnp.dot(table, surface, precision=highest).reshape(-1, 2, nb_dev)
+        gathered = lax.all_to_all(partial, both, 0, 0, tiled=True)
+        coeff = gathered.reshape(tiles, groups, 2, nb_dev).sum(axis=0)
+        coeff = coeff.transpose(1, 0, 2).reshape(2, nb)
+        owned = coeff.astype(jnp.bfloat16)
+        mapped = jnp.einsum(
+            "pq,cq->cp", match_ops[0], owned, preferred_element_type=jnp.float32
+        )
+        edged = jnp.concatenate([mapped[:, :1], mapped, mapped[:, -1:]], axis=1)
+        pieces = jnp.stack(
+            [edged[:, g * nb_dev : g * nb_dev + nb_dev + 2] for g in range(groups)], axis=0
+        )
+        sent = jnp.broadcast_to(pieces[None], (tiles,) + pieces.shape).reshape(
+            tiles * groups, 2, nb_dev + 2
+        )
+        returned = lax.all_to_all(sent, both, 0, 0, tiled=True)
+        angle = phases_at(wave_of_slot, rows_ext, span, points)
+        synth = jnp.stack([jnp.cos(angle).T, jnp.sin(angle).T], axis=2).reshape(na_dev + 2, -1)
+        flux = -jnp.dot(synth, returned.reshape(-1, nb_dev + 2), precision=highest)
+        return diffusivity * surface_ext * flux
+
+    def halo(stacked):
+        a_lo = lax.slice_in_dim(stacked, 0, 1, axis=2)
+        a_hi = lax.slice_in_dim(stacked, na_dev - 1, na_dev, axis=2)
+        b_lo = lax.slice_in_dim(stacked, 0, 1, axis=3)
+        b_hi = lax.slice_in_dim(stacked, nb_dev - 1, nb_dev, axis=3)
+        sizes = (tiles, groups)
+        from_up = lax.ppermute(a_hi, both, shift_pairs(sizes, (1, 0)))
+        from_down = lax.ppermute(a_lo, both, shift_pairs(sizes, (-1, 0)))
+        from_left = lax.ppermute(b_hi, both, shift_pairs(sizes, (0, 1)))
+        from_right = lax.ppermute(b_lo, both, shift_pairs(sizes, (0, -1)))
+        corner_ul = lax.ppermute(a_hi[:, :, :, -1:], both, shift_pairs(sizes, (1, 1)))
+        corner_ur = lax.ppermute(a_hi[:, :, :, :1], both, shift_pairs(sizes, (1, -1)))
+        corner_dl = lax.ppermute(a_lo[:, :, :, -1:], both, shift_pairs(sizes, (-1, 1)))
+        corner_dr = lax.ppermute(a_lo[:, :, :, :1], both, shift_pairs(sizes, (-1, -1)))
+        top = jnp.concatenate([corner_ul, from_up, corner_ur], axis=3)
+        middle = jnp.concatenate([from_left, stacked, from_right], axis=3)
+        bottom = jnp.concatenate([corner_dl, from_down, corner_dr], axis=3)
+        return jnp.concatenate([top, middle, bottom], axis=2)
 
     def tendency(parts):
         rhs = []
@@ -200,14 +236,12 @@
                 + derive(mass3 * slopes[2], 2, True)
             )
             rhs.append(mass3 * (stretch - carried) - diffusivity * spread)
-        flux = surface_flux(parts[0][radial_nodes - 1])
-        rhs[0] = rhs[0].at[radial_nodes - 1].add(diffusivity * surface_weight * flux)
+        flux_term = surface_flux(parts[0][radial_nodes - 1])
         stacked = jnp.stack(rhs)
-        plane_r = jnp.zeros_like(lax.slice_in_dim(stacked, 0, 1, axis=1))
-        stacked = assemble_dim(stacked, 1, plane_r, plane_r)
-        padded = padded_2(stacked.astype(jnp.bfloat16), (("tile", 2), ("deg", 3)), 1).astype(
-            stacked.dtype
-        )
+        padded = halo(stacked)
+        padded = padded.at[0, radial_nodes - 1].add(flux_term)
+        plane_r = jnp.zeros_like(lax.slice_in_dim(padded, 0, 1, axis=1))
+        padded = assemble_dim(padded, 1, plane_r, plane_r)
         padded = padded * column_mask
         along_a = assemble_dim(padded[:, :, 1:-1, :], 2, padded[:, :, 0:1, :], padded[:, :, -1:, :])
         along_b = assemble_dim(

time: 228 us -> 120 us (0.53)
  blocking collectives: 56.3 us -> 0 us
  waiting for transfers between devices: 84.8 us -> 33.5 us
  starting transfers between devices: 21 us -> 35.9 us
  between operations: 15.3 us -> 1.32 us
  other arithmetic: 15.9 us -> 10.6 us
  local copies, waits for them, and re-layouts: 17.1 us -> 20.8 us
    unnamed x2 -> x0, blocking collectives: 56.3 us -> none
    reduce_scatter x2 -> x0, waiting for transfers between devices: 52.2 us -> none  [surface_flux(): lax.psum_scatter(jnp.dot(table, flat_matched, precision=highest), 'tile',...]
    ppermute x8 -> x16, starting transfers between devices: 6.53 us -> 20.6 us  [the longest x2 6.99 us: halo(): lax.ppermute(a_lo[:, :, :, :1], both, shift_pairs(sizes, (-1, -1)))]
    all_to_all x4, waiting for transfers between devices: 12.5 us -> 22.3 us  [the longest x2 13 us: surface_flux(): returned = lax.all_to_all(sent, both, 0, 0, tiled=True)]
    ppermute x8 -> x16, waiting for transfers between devices: 20 us -> 11.2 us  [the longest x2 9.37 us: halo(): lax.ppermute(a_hi[:, :, :, :1], both, shift_pairs(sizes, (1, -1)))]
    scatter-add x1 -> x2, local copies, waits for them, and re-layouts: 0.05 us -> 3.12 us  [tendency(): padded = padded.at[0, radial_nodes - 1].add(flux_term)]
    unnamed x81 -> x67, local copies, waits for them, and re-layouts: 6.64 us -> 3.79 us
    unnamed x2 -> x0, other arithmetic: 2.44 us -> none
  transfers between devices with their start and end apart: 14 -> 20, of which waited for: 13 -> 9; matrix products, arithmetic and copies ran while one was open for 7% -> 8% of each run, Pallas kernels for 0% -> 0%
where the time goes in v1:
time: 120 us; the launch traced here: 119 us
  starting transfers between devices  35.9 us (30%)
  waiting for transfers between devices  33.5 us (28%)
  local copies, waits for them, and re-layouts  20.8 us (17%)
  matrix products  17 us (14%)
  other arithmetic  10.6 us (9%)
  between operations  1.32 us (1%)
    all_to_all x2, waiting for transfers between devices, surface_flux(): returned = lax.all_to_all(sent, both, 0, 0, tiled=True)  13 us
    ppermute x2, waiting for transfers between devices, halo(): lax.ppermute(a_hi[:, :, :, :1], both, shift_pairs(sizes, (1, -1)))  9.37 us
    all_to_all x2, waiting for transfers between devices, surface_flux(): gathered = lax.all_to_all(partial, both, 0, 0, tiled=True)  9.35 us
    dot_general x30, matrix products, apply_along(): return jnp.einsum(formula, blocks, matrix, precision=highest).reshape(shape)  9.03 us
    all_to_all x2, starting transfers between devices, surface_flux(): returned = lax.all_to_all(sent, both, 0, 0, tiled=True)  8.27 us
    all_to_all x2, starting transfers between devices, surface_flux(): gathered = lax.all_to_all(partial, both, 0, 0, tiled=True)  7.03 us
    ppermute x2, starting transfers between devices, halo(): lax.ppermute(a_lo[:, :, :, :1], both, shift_pairs(sizes, (-1, -1)))  6.99 us
    reshape x3, other arithmetic, assemble_dim(): return joined.reshape(shape)  6.03 us
  transfers between devices with their start and end apart: 20, of which 9 were waited for; matrix products, arithmetic and copies ran while one was open for 8% of the time, Pallas kernels for 0%

profile of v1, /device:TPU:0, one launch (start us, length us, event | category | flops | bytes accessed | tf_op | source)
XLA Modules:
  0.0 119.1 jit_solution(12244946012910490459)
XLA Ops:
  0.0 1.1 copy.266
  1.1 0.9 fusion.73
  2.0 0.9 fusion.78
  2.9 0.9 fusion.207
  3.8 1.0 convolution_bitcast_fusion.10
  6.5 0.5 reshape.1213
  7.9 0.3 convolution_bitcast_fusion.16
  10.0 0.9 fusion.61
  11.5 0.9 fusion.66
  13.0 0.9 fusion.71
  14.2 6.4 %collective-permute-start.7 = (f32[3,8,1,1]{3,1,2,0:T(8,128)S(1)}, f32[3,8,1,1]{3,1,2,0:T(8,128)S(1)}, u32[]{:S(2)}, u32[]{:S(2)}) collective-permute-start(f32[3,8,1,1]{3,1,2,0:T(8,128)S(1)} %get-tuple-element.65), channel_id=1, source_target_pairs={{0,31},{1,28},{2,29},{3,30},{4,3},{5,0},{6,1},{7,2},{8,7},{9,4},{1... | collective-permute-start | bytes 296 | tf_op jit(solution)/shard_map/ppermute | solution.py:215
  20.6 0.9 collective-permute-start.6
  21.6 2.4 %collective-permute-start.4 = (f32[3,8,16,1]{3,1,2,0:T(8,128)S(1)}, f32[3,8,16,1]{3,1,2,0:T(8,128)S(1)}, u32[]{:S(2)}, u32[]{:S(2)}) collective-permute-start(f32[3,8,16,1]{3,1,2,0:T(8,128)S(1)} %get-tuple-element.71), channel_id=1, source_target_pairs={{0,3},{1,0},{2,1},{3,2},{4,7},{5,4},{6,5},{7,6},{8,11},{9,8},{10,9... | collective-permute-start | bytes 4616 | tf_op jit(solution)/shard_map/ppermute | solution.py:211
  24.3 0.3 fusion.131
  24.6 0.6 copy.253
  25.2 4.0 %all-to-all-start = ((f32[32,2,128]{2,1,0:T(2,128)}), f32[32,2,128]{2,1,0:T(2,128)S(1)}, u32[]{:S(2)}, u32[]{:S(2)}) async-start(f32[32,2,128]{2,1,0:T(2,128)} %copy.253), calls=%async_computation | async-start | bytes 65536 | tf_op jit(solution)/shard_map/all_to_all | solution.py:182
  29.4 0.7 gather_fusion.1
  30.1 0.7 gather_fusion
  30.8 0.7 fusion.210
  31.5 0.7 and_reduce_fusion
  32.4 0.7 broadcast_multiply_fusion.3
  33.2 3.3 %all-to-all-done = f32[32,2,128]{2,1,0:T(2,128)S(1)} async-done(((f32[32,2,128]{2,1,0:T(2,128)}), f32[32,2,128]{2,1,0:T(2,128)S(1)}, u32[]{:S(2)}, u32[]{:S(2)}) %all-to-all-start) | async-done | bytes 32800 | tf_op jit(solution)/shard_map/all_to_all | solution.py:182
  37.0 0.3 collective-permute-start.2
  37.3 0.5 collective-permute-start.1
  37.8 5.1 %collective-permute-done.2 = f32[3,8,1,1]{3,1,2,0:T(8,128)S(1)} collective-permute-done((f32[3,8,1,1]{3,1,2,0:T(8,128)S(1)}, f32[3,8,1,1]{3,1,2,0:T(8,128)S(1)}, u32[]{:S(2)}, u32[]{:S(2)}) %collective-permute-start.2) | collective-permute-done | bytes 128 | tf_op jit(solution)/shard_map/ppermute | solution.py:213
  42.9 0.6 broadcast_in_dim.55
  43.5 5.7 %all-to-all-start.1 = ((f32[32,2,130]{2,1,0:T(2,128)}), f32[32,2,130]{2,1,0:T(2,128)S(1)}, u32[]{:S(2)}, u32[]{:S(2)}) async-start(f32[32,2,130]{2,1,0:T(2,128)} %bitcast.62), calls=%async_computation.1 | async-start | bytes 131072 | tf_op jit(solution)/shard_map/all_to_all | solution.py:196
  49.2 0.4 collective-permute-done
  49.9 6.9 %all-to-all-done.1 = f32[32,2,130]{2,1,0:T(2,128)S(1)} async-done(((f32[32,2,130]{2,1,0:T(2,128)}), f32[32,2,130]{2,1,0:T(2,128)S(1)}, u32[]{:S(2)}, u32[]{:S(2)}) %all-to-all-start.1) | async-done | bytes 33312 | tf_op jit(solution)/shard_map/all_to_all | solution.py:196
  57.0 2.0 %broadcast_select_fusion = f32[1,1,18,130]{3,1,2,0:T(1,128)S(1)} fusion(pred[]{:T(512)} %and_reduce_fusion, f32[18,130]{1,0:T(8,128)S(1)} %fusion.22, f32[3,8,18,130]{3,1,2,0:T(8,128)S(1)} %maximum_maximum_fusion, s32[]{:T(128)} %bitcast.49, s32[]{:T(128)} %bitcast.50), kind=kLoop, calls=%fused_computation.203 | loop fusion | flops 4680 | bytes 28089 | tf_op jit(solution)/shard_map/reshape | solution.py:87
  58.9 1.6 %scatter-add.6 = f32[3,8,18,130]{3,1,2,0:T(8,128)S(1)} dynamic-update-slice(f32[3,8,18,130]{3,1,2,0:T(8,128)S(1)} %maximum_maximum_fusion, f32[1,1,18,130]{3,1,2,0:T(1,128)S(1)} %broadcast_select_fusion, s32[]{:T(128)} %bitcast.49, s32[]{:T(128)} %bitcast.50, s32[]{:T(128)} %constant.232.clone.1, s32[]{:T(128)} %constant.232.clone.1) | dynamic-update-slice | bytes 18724 | tf_op jit(solution)/shard_map/scatter-add | solution.py:242
  61.1 0.5 copy.372
  61.8 1.3 %slice.422 = f32[3,8,16,16,6]{2,4,3,1,0:T(8,128)} slice(f32[3,8,16,16,8]{2,4,3,1,0:T(8,128)S(1)} %bitcast.480), slice={[0:3], [0:8], [0:16], [0:16], [1:7]} | slice | bytes 294912 | tf_op jit(solution)/shard_map/slice | solution.py:85
  63.6 0.5 slice_add_fusion.3
  64.1 2.0 %maximum_bitcast_fusion = f32[3,8,16,128]{2,3,1,0:T(8,128)S(1)} fusion(f32[3,8,16,16,1]{2,4,3,1,0:T(1,128)S(1)} %get-tuple-element.34, f32[3,8,16,16,6]{2,4,3,1,0:T(8,128)} %slice.422, f32[3,8,16,16,1]{2,4,3,1,0:T(1,128)S(1)} %get-tuple-element.33), kind=kLoop, calls=%fused_computation.2 | loop fusion | flops 98304 | bytes 393216 | tf_op jit(solution)/shard_map/reshape | solution.py:87
  66.1 0.4 copy.264
  66.6 0.4 copy-done.18
  68.3 0.3 convolution_bitcast_fusion.2
  72.1 0.6 collective-permute-start.15
  72.8 0.7 collective-permute-start.14
  73.4 1.1 collective-permute-start.13
  74.6 1.9 %collective-permute-start.12 = (f32[3,8,16,1]{3,1,2,0:T(8,128)S(1)}, f32[3,8,16,1]{3,1,2,0:T(8,128)S(1)}, u32[]{:S(2)}, u32[]{:S(2)}) collective-permute-start(f32[3,8,16,1]{3,1,2,0:T(8,128)S(1)} %get-tuple-element.60), channel_id=1, source_target_pairs={{0,3},{1,0},{2,1},{3,2},{4,7},{5,4},{6,5},{7,6},{8,11},{9,8},{10,9... | collective-permute-start | bytes 4616 | tf_op jit(solution)/shard_map/ppermute | solution.py:211
  76.7 0.3 fusion.130
  77.0 0.4 collective-permute-done.13
  77.4 3.0 %collective-permute-start.10 = (f32[3,8,1,1]{3,1,2,0:T(8,128)S(1)}, f32[3,8,1,1]{3,1,2,0:T(8,128)S(1)}, u32[]{:S(2)}, u32[]{:S(2)}) collective-permute-start(f32[3,8,1,1]{3,1,2,0:T(8,128)S(1)} %get-tuple-element.56), channel_id=1, source_target_pairs={{0,7},{1,4},{2,5},{3,6},{4,11},{5,8},{6,9},{7,10},{8,15},{9,12},{1... | collective-permute-start | bytes 296 | tf_op jit(solution)/shard_map/ppermute | solution.py:213
  80.5 0.6 copy.298
  81.1 4.3 %collective-permute-done.10 = f32[3,8,1,1]{3,1,2,0:T(8,128)S(1)} collective-permute-done((f32[3,8,1,1]{3,1,2,0:T(8,128)S(1)}, f32[3,8,1,1]{3,1,2,0:T(8,128)S(1)}, u32[]{:S(2)}, u32[]{:S(2)}) %collective-permute-start.10) | collective-permute-done | bytes 128 | tf_op jit(solution)/shard_map/ppermute | solution.py:213
  85.4 2.7 %collective-permute-start.8 = (f32[3,8,1,1]{3,1,2,0:T(8,128)S(1)}, f32[3,8,1,1]{3,1,2,0:T(8,128)S(1)}, u32[]{:S(2)}, u32[]{:S(2)}) collective-permute-start(f32[3,8,1,1]{3,1,2,0:T(8,128)S(1)} %get-tuple-element.53), channel_id=1, source_target_pairs={{0,5},{1,6},{2,7},{3,4},{4,9},{5,10},{6,11},{7,8},{8,13},{9,14},{1... | collective-permute-start | bytes 296 | tf_op jit(solution)/shard_map/ppermute | solution.py:212
  88.1 3.0 %all-to-all-start.2 = ((f32[32,2,128]{2,1,0:T(2,128)}), f32[32,2,128]{2,1,0:T(2,128)S(1)}, u32[]{:S(2)}, u32[]{:S(2)}) async-start(f32[32,2,128]{2,1,0:T(2,128)} %copy.298), calls=%async_computation.2 | async-start | bytes 65536 | tf_op jit(solution)/shard_map/all_to_all | solution.py:182
  91.1 1.0 collective-permute-done.8
  92.4 6.0 %all-to-all-done.2 = f32[32,2,128]{2,1,0:T(2,128)S(1)} async-done(((f32[32,2,128]{2,1,0:T(2,128)}), f32[32,2,128]{2,1,0:T(2,128)S(1)}, u32[]{:S(2)}, u32[]{:S(2)}) %all-to-all-start.2) | async-done | bytes 32800 | tf_op jit(solution)/shard_map/all_to_all | solution.py:182
  98.9 0.6 broadcast_in_dim.106
  99.5 2.6 %all-to-all-start.3 = ((f32[32,2,130]{2,1,0:T(2,128)}), f32[32,2,130]{2,1,0:T(2,128)S(1)}, u32[]{:S(2)}, u32[]{:S(2)}) async-start(f32[32,2,130]{2,1,0:T(2,128)} %bitcast.111), calls=%async_computation.3 | async-start | bytes 131072 | tf_op jit(solution)/shard_map/all_to_all | solution.py:196
  102.1 1.4 %constant_dynamic-slice_fusion = f32[1,1,18,130]{3,1,2,0:T(1,128)S(1)} fusion(f32[3,8,18,130]{3,1,2,0:T(8,128)S(1)} %maximum_maximum_fusion.1, s32[]{:T(128)} %bitcast.49, s32[]{:T(128)} %bitcast.50), kind=kLoop, calls=%fused_computation.390 | loop fusion | bytes 18728 | tf_op jit(solution)/shard_map/dynamic-slice.10
  103.5 6.1 %all-to-all-done.3 = f32[32,2,130]{2,1,0:T(2,128)S(1)} async-done(((f32[32,2,130]{2,1,0:T(2,128)}), f32[32,2,130]{2,1,0:T(2,128)S(1)}, u32[]{:S(2)}, u32[]{:S(2)}) %all-to-all-start.3) | async-done | bytes 33312 | tf_op jit(solution)/shard_map/all_to_all | solution.py:196
  109.6 0.8 fusion.24
  110.4 1.5 %scatter-add.9 = f32[3,8,18,130]{3,1,2,0:T(8,128)S(1)} dynamic-update-slice(f32[3,8,18,130]{3,1,2,0:T(8,128)S(1)} %maximum_maximum_fusion.1, f32[1,1,18,130]{3,1,2,0:T(1,128)S(1)} %copy.301, s32[]{:T(128)} %bitcast.49, s32[]{:T(128)} %bitcast.50, s32[]{:T(128)} %constant.232.clone.1, s32[]{:T(128)} %constant.232.clone.1) | dynamic-update-slice | bytes 18724 | tf_op jit(solution)/shard_map/scatter-add | solution.py:242
  112.4 0.5 copy.377
  113.1 1.3 %slice.448 = f32[3,8,16,16,6]{2,4,3,1,0:T(8,128)} slice(f32[3,8,16,16,8]{2,4,3,1,0:T(8,128)S(1)} %bitcast.483), slice={[0:3], [0:8], [0:16], [0:16], [1:7]} | slice | bytes 294912 | tf_op jit(solution)/shard_map/slice | solution.py:85
  114.9 0.5 slice_add_fusion.1
  115.4 2.0 %maximum_bitcast_fusion.1 = f32[3,8,16,128]{2,3,1,0:T(8,128)S(1)} fusion(f32[3,8,16,16,1]{2,4,3,1,0:T(1,128)S(1)} %get-tuple-element.30, f32[3,8,16,16,6]{2,4,3,1,0:T(8,128)} %slice.448, f32[3,8,16,16,1]{2,4,3,1,0:T(1,128)S(1)} %get-tuple-element.29), kind=kLoop, calls=%fused_computation.3 | loop fusion | flops 98304 | bytes 393216 | tf_op jit(solution)/shard_map/reshape | solution.py:87
  117.5 0.4 copy.309
  117.9 0.4 copy-done.19
  118.4 0.7 copy.310
  (206 shorter events, 15.0 us)
Async XLA Ops:
  0.0 36.6 %copy-start = (bf16[1,512,512]{2,1,0:T(8,128)(2,1)S(1)}, bf16[1,512,512]{2,1,0:T(8,128)(2,1)}, u32[]{:S(2)}) copy-start(bf16[1,512,512]{2,1,0:T(8,128)(2,1)} %param.13) | copy-start | bytes 1572868
  0.0 4.9 %copy-start.20 = (f32[8,8,1,1]{1,0,3,2:T(8,128)S(1)}, f32[8,8,1,1]{1,0,3,2:T(8,128)}, u32[]{:S(2)}) copy-start(f32[8,8,1,1]{1,0,3,2:T(8,128)} %constant.292) | copy-start | bytes 772
  0.0 5.1 %copy-start.1 = (f32[8]{0:T(128)S(1)}, f32[8]{0:T(128)}, u32[]{:S(2)}) copy-start(f32[8]{0:T(128)} %constant.258.clone) | copy-start | bytes 100
  0.0 6.1 %copy-start.5 = (f32[3,8,16,128]{3,2,1,0:T(8,128)S(1)}, f32[3,8,16,128]{3,2,1,0:T(8,128)}, u32[]{:S(2)}) copy-start(f32[3,8,16,128]{3,2,1,0:T(8,128)} %param.12) | copy-start | bytes 589828
  1.1 5.3 %copy-start.26 = (f32[8,8]{1,0:T(8,128)S(1)}, f32[8,8]{1,0:T(8,128)}, u32[]{:S(2)}) copy-start(f32[8,8]{1,0:T(8,128)} %constant.259.clone) | copy-start | bytes 772
  5.3 27.1 %copy-start.24 = (f32[128]{0:T(128)}, f32[128]{0:T(128)S(1)}, u32[]{:S(2)}) copy-start(f32[128]{0:T(128)S(1)} %mul.673) | copy-start | bytes 1540
  5.8 1.7 %copy-start.4 = (f32[8,8,1]{1,0,2:T(8,128)S(1)}, f32[8,8,1]{1,0,2:T(8,128)}, u32[]{:S(2)}) copy-start(f32[8,8,1]{1,0,2:T(8,128)} %constant.291) | copy-start | bytes 772
  8.9 2.0 %copy-start.14 = (f32[8,2,8,128]{3,0,2,1:T(8,128)}, f32[8,2,8,128]{3,0,2,1:T(8,128)S(1)}, u32[]{:S(2)}) copy-start(f32[8,2,8,128]{3,0,2,1:T(8,128)S(1)} %copy.241) | copy-start | bytes 196612
  9.2 3.2 %copy-start.16 = (f32[8,16,128]{2,0,1:T(8,128)}, f32[8,16,128]{2,0,1:T(8,128)S(1)}, u32[]{:S(2)}) copy-start(f32[8,16,128]{2,0,1:T(8,128)S(1)} %fusion.93) | copy-start | bytes 196612
  9.2 3.2 %copy-start.10 = (f32[8,2,8,128]{3,0,2,1:T(8,128)}, f32[8,2,8,128]{3,0,2,1:T(8,128)S(1)}, u32[]{:S(2)}) copy-start(f32[8,2,8,128]{3,0,2,1:T(8,128)S(1)} %copy.228) | copy-start | bytes 196612
  9.4 3.0 %copy-start.12 = (f32[8,16,128]{2,0,1:T(8,128)}, f32[8,16,128]{2,0,1:T(8,128)S(1)}, u32[]{:S(2)}) copy-start(f32[8,16,128]{2,0,1:T(8,128)S(1)} %fusion.92) | copy-start | bytes 196612
  9.5 4.4 %copy-start.6 = (f32[8,2,8,128]{3,0,2,1:T(8,128)}, f32[8,2,8,128]{3,0,2,1:T(8,128)S(1)}, u32[]{:S(2)}) copy-start(f32[8,2,8,128]{3,0,2,1:T(8,128)S(1)} %copy.212) | copy-start | bytes 196612
  9.7 4.2 %copy-start.8 = (f32[8,16,128]{2,0,1:T(8,128)}, f32[8,16,128]{2,0,1:T(8,128)S(1)}, u32[]{:S(2)}) copy-start(f32[8,16,128]{2,0,1:T(8,128)S(1)} %fusion.91) | copy-start | bytes 196612
  12.7 11.4 %copy-start.2 = (f32[8]{0:T(128)S(1)}, f32[8]{0:T(128)}, u32[]{:S(2)}) copy-start(f32[8]{0:T(128)} %constant.257.clone) | copy-start | bytes 100
  12.7 11.5 %copy-start.27 = (s32[32]{0:T(128)S(1)}, s32[32]{0:T(128)}, u32[]{:S(2)}) copy-start(s32[32]{0:T(128)} %param.14) | copy-start | bytes 388
  12.7 11.6 %copy-start.3 = (f32[3,8,16,128]{3,2,1,0:T(8,128)S(1)}, f32[3,8,16,128]{3,2,1,0:T(8,128)}, u32[]{:S(2)}) copy-start(f32[3,8,16,128]{3,2,1,0:T(8,128)} %param.11) | copy-start | bytes 589828
  14.1 17.3 %copy-start.28 = (s32[4]{0:T(128)S(1)}, s32[4]{0:T(128)}, u32[]{:S(2)}) copy-start(s32[4]{0:T(128)} %constant.235.clone.1) | copy-start | bytes 52
  14.2 22.8 %collective-permute-start.7 = (f32[3,8,1,1]{3,1,2,0:T(8,128)S(1)}, f32[3,8,1,1]{3,1,2,0:T(8,128)S(1)}, u32[]{:S(2)}, u32[]{:S(2)}) collective-permute-start(f32[3,8,1,1]{3,1,2,0:T(8,128)S(1)} %get-tuple-element.65), channel_id=1, source_target_pairs={{0,31},{1,28},{2,29},{3,30},{4,3},{5,0},{6,1},{7,2},{8,7},{9,4},{1... | collective-permute-start | bytes 296 | tf_op jit(solution)/shard_map/ppermute | solution.py:215
  20.6 29.0 %collective-permute-start.6 = (f32[3,8,1,128]{3,1,2,0:T(8,128)S(1)}, f32[3,8,1,128]{3,1,2,0:T(8,128)S(1)}, u32[]{:S(2)}, u32[]{:S(2)}) collective-permute-start(f32[3,8,1,128]{3,1,2,0:T(8,128)S(1)} %get-tuple-element.69), channel_id=1, source_target_pairs={{0,28},{1,29},{2,30},{3,31},{4,0},{5,1},{6,2},{7,3},{8,4},{9,5},{1... | collective-permute-start | bytes 36872 | tf_op jit(solution)/shard_map/ppermute | solution.py:209
  21.5 15.8 %collective-permute-start.5 = (f32[3,8,1,1]{3,1,2,0:T(8,128)S(1)}, f32[3,8,1,1]{3,1,2,0:T(8,128)S(1)}, u32[]{:S(2)}, u32[]{:S(2)}) collective-permute-start(f32[3,8,1,1]{3,1,2,0:T(8,128)S(1)} %get-tuple-element.66), channel_id=1, source_target_pairs={{0,29},{1,30},{2,31},{3,28},{4,1},{5,2},{6,3},{7,0},{8,5},{9,6},{1... | collective-permute-start | bytes 296 | tf_op jit(solution)/shard_map/ppermute | solution.py:214
  21.6 28.0 %collective-permute-start.4 = (f32[3,8,16,1]{3,1,2,0:T(8,128)S(1)}, f32[3,8,16,1]{3,1,2,0:T(8,128)S(1)}, u32[]{:S(2)}, u32[]{:S(2)}) collective-permute-start(f32[3,8,16,1]{3,1,2,0:T(8,128)S(1)} %get-tuple-element.71), channel_id=1, source_target_pairs={{0,3},{1,0},{2,1},{3,2},{4,7},{5,4},{6,5},{7,6},{8,11},{9,8},{10,9... | collective-permute-start | bytes 4616 | tf_op jit(solution)/shard_map/ppermute | solution.py:211
  24.0 25.6 %collective-permute-start.3 = (f32[3,8,16,1]{3,1,2,0:T(8,128)S(1)}, f32[3,8,16,1]{3,1,2,0:T(8,128)S(1)}, u32[]{:S(2)}, u32[]{:S(2)}) collective-permute-start(f32[3,8,16,1]{3,1,2,0:T(8,128)S(1)} %get-tuple-element.70), channel_id=1, source_target_pairs={{0,1},{1,2},{2,3},{3,0},{4,5},{5,6},{6,7},{7,4},{8,9},{9,10},{10,1... | collective-permute-start | bytes 4616 | tf_op jit(solution)/shard_map/ppermute | solution.py:210
  25.2 11.3 %all-to-all-start = ((f32[32,2,128]{2,1,0:T(2,128)}), f32[32,2,128]{2,1,0:T(2,128)S(1)}, u32[]{:S(2)}, u32[]{:S(2)}) async-start(f32[32,2,128]{2,1,0:T(2,128)} %copy.253), calls=%async_computation | async-start | bytes 65536 | tf_op jit(solution)/shard_map/all_to_all | solution.py:182
  37.0 5.9 %collective-permute-start.2 = (f32[3,8,1,1]{3,1,2,0:T(8,128)S(1)}, f32[3,8,1,1]{3,1,2,0:T(8,128)S(1)}, u32[]{:S(2)}, u32[]{:S(2)}) collective-permute-start(f32[3,8,1,1]{3,1,2,0:T(8,128)S(1)} %get-tuple-element.67), channel_id=1, source_target_pairs={{0,7},{1,4},{2,5},{3,6},{4,11},{5,8},{6,9},{7,10},{8,15},{9,12},{1... | collective-permute-start | bytes 296 | tf_op jit(solution)/shard_map/ppermute | solution.py:213
  37.3 12.3 %collective-permute-start.1 = (f32[3,8,1,128]{3,1,2,0:T(8,128)S(1)}, f32[3,8,1,128]{3,1,2,0:T(8,128)S(1)}, u32[]{:S(2)}, u32[]{:S(2)}) collective-permute-start(f32[3,8,1,128]{3,1,2,0:T(8,128)S(1)} %get-tuple-element.68), channel_id=1, source_target_pairs={{0,4},{1,5},{2,6},{3,7},{4,8},{5,9},{6,10},{7,11},{8,12},{9,13},{1... | collective-permute-start | bytes 36872 | tf_op jit(solution)/shard_map/ppermute | solution.py:208
  42.9 6.7 %collective-permute-start = (f32[3,8,1,1]{3,1,2,0:T(8,128)S(1)}, f32[3,8,1,1]{3,1,2,0:T(8,128)S(1)}, u32[]{:S(2)}, u32[]{:S(2)}) collective-permute-start(f32[3,8,1,1]{3,1,2,0:T(8,128)S(1)} %get-tuple-element.64), channel_id=1, source_target_pairs={{0,5},{1,6},{2,7},{3,4},{4,9},{5,10},{6,11},{7,8},{8,13},{9,14},{1... | collective-permute-start | bytes 296 | tf_op jit(solution)/shard_map/ppermute | solution.py:212
  43.5 13.2 %all-to-all-start.1 = ((f32[32,2,130]{2,1,0:T(2,128)}), f32[32,2,130]{2,1,0:T(2,128)S(1)}, u32[]{:S(2)}, u32[]{:S(2)}) async-start(f32[32,2,130]{2,1,0:T(2,128)} %bitcast.62), calls=%async_computation.1 | async-start | bytes 131072 | tf_op jit(solution)/shard_map/all_to_all | solution.py:196
  66.1 0.8 copy-start.18
  66.1 1.3 %copy-start.25 = (f32[128]{0:T(128)S(1)}, f32[128]{0:T(128)}, u32[]{:S(2)}) copy-start(f32[128]{0:T(128)} %copy-done.24) | copy-start | bytes 1540
  67.5 2.2 %copy-start.15 = (f32[8,2,8,128]{3,0,2,1:T(8,128)S(1)}, f32[8,2,8,128]{3,0,2,1:T(8,128)}, u32[]{:S(2)}) copy-start(f32[8,2,8,128]{3,0,2,1:T(8,128)} %copy-done.14) | copy-start | bytes 196612
  67.5 2.2 %copy-start.17 = (f32[8,16,128]{2,0,1:T(8,128)S(1)}, f32[8,16,128]{2,0,1:T(8,128)}, u32[]{:S(2)}) copy-start(f32[8,16,128]{2,0,1:T(8,128)} %copy-done.16) | copy-start | bytes 196612
  67.5 2.2 %copy-start.22 = (f32[8,16,128]{2,0,1:T(8,128)S(1)}, f32[8,16,128]{2,0,1:T(8,128)}, u32[]{:S(2)}) copy-start(f32[8,16,128]{2,0,1:T(8,128)} %get-tuple-element.99) | copy-start | bytes 196612
  68.2 2.1 %copy-start.11 = (f32[8,2,8,128]{3,0,2,1:T(8,128)S(1)}, f32[8,2,8,128]{3,0,2,1:T(8,128)}, u32[]{:S(2)}) copy-start(f32[8,2,8,128]{3,0,2,1:T(8,128)} %copy-done.10) | copy-start | bytes 196612
  68.2 2.1 %copy-start.13 = (f32[8,16,128]{2,0,1:T(8,128)S(1)}, f32[8,16,128]{2,0,1:T(8,128)}, u32[]{:S(2)}) copy-start(f32[8,16,128]{2,0,1:T(8,128)} %copy-done.12) | copy-start | bytes 196612
  68.2 2.1 %copy-start.23 = (f32[8,16,128]{2,0,1:T(8,128)S(1)}, f32[8,16,128]{2,0,1:T(8,128)}, u32[]{:S(2)}) copy-start(f32[8,16,128]{2,0,1:T(8,128)} %get-tuple-element.101) | copy-start | bytes 196612
  69.0 1.9 %copy-start.7 = (f32[8,2,8,128]{3,0,2,1:T(8,128)S(1)}, f32[8,2,8,128]{3,0,2,1:T(8,128)}, u32[]{:S(2)}) copy-start(f32[8,2,8,128]{3,0,2,1:T(8,128)} %copy-done.6) | copy-start | bytes 196612
  69.0 1.9 %copy-start.9 = (f32[8,16,128]{2,0,1:T(8,128)S(1)}, f32[8,16,128]{2,0,1:T(8,128)}, u32[]{:S(2)}) copy-start(f32[8,16,128]{2,0,1:T(8,128)} %copy-done.8) | copy-start | bytes 196612
  69.0 1.9 %copy-start.21 = (f32[8,16,128]{2,0,1:T(8,128)S(1)}, f32[8,16,128]{2,0,1:T(8,128)}, u32[]{:S(2)}) copy-start(f32[8,16,128]{2,0,1:T(8,128)} %get-tuple-element.103) | copy-start | bytes 196612
  72.1 4.6 %collective-permute-start.15 = (f32[3,8,1,1]{3,1,2,0:T(8,128)S(1)}, f32[3,8,1,1]{3,1,2,0:T(8,128)S(1)}, u32[]{:S(2)}, u32[]{:S(2)}) collective-permute-start(f32[3,8,1,1]{3,1,2,0:T(8,128)S(1)} %get-tuple-element.54), channel_id=1, source_target_pairs={{0,31},{1,28},{2,29},{3,30},{4,3},{5,0},{6,1},{7,2},{8,7},{9,4},{1... | collective-permute-start | bytes 296 | tf_op jit(solution)/shard_map/ppermute | solution.py:215
  72.8 19.4 %collective-permute-start.14 = (f32[3,8,1,128]{3,1,2,0:T(8,128)S(1)}, f32[3,8,1,128]{3,1,2,0:T(8,128)S(1)}, u32[]{:S(2)}, u32[]{:S(2)}) collective-permute-start(f32[3,8,1,128]{3,1,2,0:T(8,128)S(1)} %get-tuple-element.58), channel_id=1, source_target_pairs={{0,28},{1,29},{2,30},{3,31},{4,0},{5,1},{6,2},{7,3},{8,4},{9,5},{1... | collective-permute-start | bytes 36872 | tf_op jit(solution)/shard_map/ppermute | solution.py:209
  73.4 4.0 %collective-permute-start.13 = (f32[3,8,1,1]{3,1,2,0:T(8,128)S(1)}, f32[3,8,1,1]{3,1,2,0:T(8,128)S(1)}, u32[]{:S(2)}, u32[]{:S(2)}) collective-permute-start(f32[3,8,1,1]{3,1,2,0:T(8,128)S(1)} %get-tuple-element.55), channel_id=1, source_target_pairs={{0,29},{1,30},{2,31},{3,28},{4,1},{5,2},{6,3},{7,0},{8,5},{9,6},{1... | collective-permute-start | bytes 296 | tf_op jit(solution)/shard_map/ppermute | solution.py:214
  74.6 17.5 %collective-permute-start.12 = (f32[3,8,16,1]{3,1,2,0:T(8,128)S(1)}, f32[3,8,16,1]{3,1,2,0:T(8,128)S(1)}, u32[]{:S(2)}, u32[]{:S(2)}) collective-permute-start(f32[3,8,16,1]{3,1,2,0:T(8,128)S(1)} %get-tuple-element.60), channel_id=1, source_target_pairs={{0,3},{1,0},{2,1},{3,2},{4,7},{5,4},{6,5},{7,6},{8,11},{9,8},{10,9... | collective-permute-start | bytes 4616 | tf_op jit(solution)/shard_map/ppermute | solution.py:211
  76.5 15.6 %collective-permute-start.11 = (f32[3,8,16,1]{3,1,2,0:T(8,128)S(1)}, f32[3,8,16,1]{3,1,2,0:T(8,128)S(1)}, u32[]{:S(2)}, u32[]{:S(2)}) collective-permute-start(f32[3,8,16,1]{3,1,2,0:T(8,128)S(1)} %get-tuple-element.59), channel_id=1, source_target_pairs={{0,1},{1,2},{2,3},{3,0},{4,5},{5,6},{6,7},{7,4},{8,9},{9,10},{10,1... | collective-permute-start | bytes 4616 | tf_op jit(solution)/shard_map/ppermute | solution.py:210
  76.7 15.4 %collective-permute-start.9 = (f32[3,8,1,128]{3,1,2,0:T(8,128)S(1)}, f32[3,8,1,128]{3,1,2,0:T(8,128)S(1)}, u32[]{:S(2)}, u32[]{:S(2)}) collective-permute-start(f32[3,8,1,128]{3,1,2,0:T(8,128)S(1)} %get-tuple-element.57), channel_id=1, source_target_pairs={{0,4},{1,5},{2,6},{3,7},{4,8},{5,9},{6,10},{7,11},{8,12},{9,13},{1... | collective-permute-start | bytes 36872 | tf_op jit(solution)/shard_map/ppermute | solution.py:208
  77.4 8.0 %collective-permute-start.10 = (f32[3,8,1,1]{3,1,2,0:T(8,128)S(1)}, f32[3,8,1,1]{3,1,2,0:T(8,128)S(1)}, u32[]{:S(2)}, u32[]{:S(2)}) collective-permute-start(f32[3,8,1,1]{3,1,2,0:T(8,128)S(1)} %get-tuple-element.56), channel_id=1, source_target_pairs={{0,7},{1,4},{2,5},{3,6},{4,11},{5,8},{6,9},{7,10},{8,15},{9,12},{1... | collective-permute-start | bytes 296 | tf_op jit(solution)/shard_map/ppermute | solution.py:213
  85.4 6.7 %collective-permute-start.8 = (f32[3,8,1,1]{3,1,2,0:T(8,128)S(1)}, f32[3,8,1,1]{3,1,2,0:T(8,128)S(1)}, u32[]{:S(2)}, u32[]{:S(2)}) collective-permute-start(f32[3,8,1,1]{3,1,2,0:T(8,128)S(1)} %get-tuple-element.53), channel_id=1, source_target_pairs={{0,5},{1,6},{2,7},{3,4},{4,9},{5,10},{6,11},{7,8},{8,13},{9,14},{1... | collective-permute-start | bytes 296 | tf_op jit(solution)/shard_map/ppermute | solution.py:212
  88.1 10.3 %all-to-all-start.2 = ((f32[32,2,128]{2,1,0:T(2,128)}), f32[32,2,128]{2,1,0:T(2,128)S(1)}, u32[]{:S(2)}, u32[]{:S(2)}) async-start(f32[32,2,128]{2,1,0:T(2,128)} %copy.298), calls=%async_computation.2 | async-start | bytes 65536 | tf_op jit(solution)/shard_map/all_to_all | solution.py:182
  99.5 10.1 %all-to-all-start.3 = ((f32[32,2,130]{2,1,0:T(2,128)}), f32[32,2,130]{2,1,0:T(2,128)S(1)}, u32[]{:S(2)}, u32[]{:S(2)}) async-start(f32[32,2,130]{2,1,0:T(2,128)} %bitcast.111), calls=%async_computation.3 | async-start | bytes 131072 | tf_op jit(solution)/shard_map/all_to_all | solution.py:196
  117.4 0.8 copy-start.19

commit v2 on v1

--- a/solution.py
+++ b/solution.py
@@ -1,9 +1,11 @@
 import math
 
+import numpy as np
 import jax
 import jax.numpy as jnp
 from jax import lax
 from jax.sharding import PartitionSpec as P
+from jax.experimental import pallas as pl
 
 P_SIZE = 8
 
@@ -25,6 +27,46 @@
         after = lax.ppermute(first, axis, down)
         value = jnp.concatenate([before, value, after], axis=dim)
     return value
+
+
+def product(a, b):
+    return jnp.dot(a, b, precision=highest, preferred_element_type=jnp.float32)
+
+
+def gradient_kernel(flow_ref, mats_ref, out_ref):
+    for component in range(3):
+        x = flow_ref[component]
+        out_ref[3 * component] = product(mats_ref[0], x)
+        out_ref[3 * component + 1] = product(mats_ref[1], x)
+        out_ref[3 * component + 2] = product(x, mats_ref[2])
+
+
+def volume_kernel(parts_ref, flow_ref, grad_ref, mats_ref, mass_ref, out_ref):
+    mass = mass_ref[...]
+    p = [parts_ref[i] for i in range(3)]
+    f = [flow_ref[i] for i in range(3)]
+    for c in range(3):
+        x = p[c]
+        s0 = product(mats_ref[0], x)
+        s1 = product(mats_ref[1], x)
+        s2 = product(x, mats_ref[2])
+        stretch = p[0] * grad_ref[3 * c] + p[1] * grad_ref[3 * c + 1] + p[2] * grad_ref[3 * c + 2]
+        carried = f[0] * s0 + f[1] * s1 + f[2] * s2
+        spread = (
+            product(mats_ref[3], mass * s0)
+            + product(mats_ref[4], mass * s1)
+            + product(mass * s2, mats_ref[5])
+        )
+        out_ref[c] = mass * (stretch - carried) - diffusivity * spread
+
+
+def derivative_tables(radial_nodes, na_dev, nb_dev):
+    _, _, matrix_list = gll_tables(P_SIZE)
+    dmat = np.asarray(matrix_list, np.float32)
+    radial = np.kron(dmat, np.eye(na_dev, dtype=np.float32))
+    first = np.kron(np.eye(radial_nodes * na_dev // P_SIZE, dtype=np.float32), dmat)
+    second = np.kron(np.eye(nb_dev // P_SIZE, dtype=np.float32), dmat)
+    return jnp.asarray(np.stack([radial, first, second.T, radial.T, first.T, second]))
 
 
 def legendre_value(point, degree):
@@ -140,11 +182,9 @@
     nb = nb_dev * groups
     span = 2 * elems_a * tiles
     scale = P_SIZE / (na_dev * tiles)
-    points_list, weights_list, matrix_list = gll_tables(P_SIZE)
+    points_list, weights_list, _ = gll_tables(P_SIZE)
     points = jnp.asarray(points_list, jnp.float32)
     weights = jnp.asarray(weights_list, jnp.float32)
-    dmat = jnp.asarray(matrix_list, jnp.float32)
-    block = jnp.kron(jnp.eye(elems_b, dtype=jnp.float32), dmat)
     lead = (group_index > 0).astype(jnp.float32)
     trail = (group_index < groups - 1).astype(jnp.float32)
     w_r = jnp.tile(weights, radial_nodes // P_SIZE)
@@ -161,17 +201,13 @@
     cols_ext = group_index * nb_dev - 1 + jnp.arange(nb_dev + 2, dtype=jnp.int32)
     surface_ext = weights[rows_ext % P_SIZE][:, None] * weights[cols_ext % P_SIZE][None, :]
 
-    def derive(values, direction, transpose):
-        if direction == 2:
-            table = block if transpose else block.T
-            return jnp.dot(values, table, precision=highest)
-        return apply_along(values, direction, dmat.T if transpose else dmat)
-
-    flow_parts = [flow[0], flow[1], flow[2]]
-    grad_flow = [
-        [derive(flow_parts[component], direction, False) for direction in range(3)]
-        for component in range(3)
-    ]
+    rows = radial_nodes * na_dev
+    mats = derivative_tables(radial_nodes, na_dev, nb_dev)
+    flat_mass = mass3.reshape(rows, nb_dev)
+    flat_flow = flow.reshape(3, rows, nb_dev)
+    grads = pl.pallas_call(
+        gradient_kernel, out_shape=jax.ShapeDtypeStruct((9, rows, nb_dev), jnp.float32)
+    )(flat_flow, mats)
 
     def surface_flux(surface):
         angle = phases(wave_of_slot, tile_index * elems_a, elems_a, span, points)
@@ -219,25 +255,11 @@
         return jnp.concatenate([top, middle, bottom], axis=2)
 
     def tendency(parts):
-        rhs = []
-        for component in range(3):
-            slopes = [derive(parts[component], direction, False) for direction in range(3)]
-            stretch = (
-                parts[0] * grad_flow[component][0]
-                + parts[1] * grad_flow[component][1]
-                + parts[2] * grad_flow[component][2]
-            )
-            carried = (
-                flow_parts[0] * slopes[0] + flow_parts[1] * slopes[1] + flow_parts[2] * slopes[2]
-            )
-            spread = (
-                derive(mass3 * slopes[0], 0, True)
-                + derive(mass3 * slopes[1], 1, True)
-                + derive(mass3 * slopes[2], 2, True)
-            )
-            rhs.append(mass3 * (stretch - carried) - diffusivity * spread)
-        flux_term = surface_flux(parts[0][radial_nodes - 1])
-        stacked = jnp.stack(rhs)
+        stacked = pl.pallas_call(
+            volume_kernel, out_shape=jax.ShapeDtypeStruct((3, rows, nb_dev), jnp.float32)
+        )(parts.reshape(3, rows, nb_dev), flat_flow, grads, mats, flat_mass)
+        stacked = stacked.reshape(parts.shape)
+        flux_term = surface_flux(parts[0, radial_nodes - 1])
         padded = halo(stacked)
         padded = padded.at[0, radial_nodes - 1].add(flux_term)
         plane_r = jnp.zeros_like(lax.slice_in_dim(padded, 0, 1, axis=1))
@@ -249,8 +271,8 @@
         )
         return along_b / assembled[None]
 
-    section = field + time_step * tendency([field[0], field[1], field[2]])
-    return 0.5 * (field + section + time_step * tendency([section[0], section[1], section[2]]))
+    section = field + time_step * tendency(field)
+    return 0.5 * (field + section + time_step * tendency(section))
 
 
 def solution(mesh):

time: 120 us -> 111 us (0.925)
  matrix products: 17 us -> 5.99 us
  Pallas kernels: 0 us -> 9.46 us
  waiting for transfers between devices: 33.5 us -> 27.8 us
  starting transfers between devices: 35.9 us -> 41 us
  local copies, waits for them, and re-layouts: 20.8 us -> 17.7 us
  other arithmetic: 10.6 us -> 7.65 us
    dot_general x45 -> x0, matrix products: 14.9 us -> none  [the longest x30 9.03 us: apply_along(): return jnp.einsum(formula, blocks, matrix, precision=highest).reshape(shape)]
    pallas_call x0 -> x3, Pallas kernels: none -> 9.46 us  [the longest x2 6.92 us: tendency(): pl.pallas_call(volume_kernel, out_shape=jax.ShapeDtypeStruct((3, rows, nb...]
    all_to_all x2, waiting for transfers between devices: 9.35 us -> 4 us  [surface_flux(): gathered = lax.all_to_all(partial, both, 0, 0, tiled=True)]
    ppermute x2, starting transfers between devices: 6.99 us -> 11.7 us  [halo(): lax.ppermute(a_lo[:, :, :, :1], both, shift_pairs(sizes, (-1, -1)))]
    reshape x3 -> x4, other arithmetic: 6.03 us -> 1.53 us  [assemble_dim(): return joined.reshape(shape)]
    unnamed x67 -> x20, local copies, waits for them, and re-layouts: 3.79 us -> 0.12 us
    slice x8 -> x6, local copies, waits for them, and re-layouts: 1.07 us -> 4.38 us  [the longest x2 2.34 us: halo(): a_hi[:, :, :, -1:]]
    dot_general x2, matrix products: 1 us -> 4.21 us  [surface_flux(): flux = -jnp.dot(synth, returned.reshape(-1, nb_dev + 2), precision=highest)]
  transfers between devices with their start and end apart: 20 -> 20, of which waited for: 9 -> 7; matrix products, arithmetic and copies ran while one was open for 8% -> 10% of each run, Pallas kernels for 0% -> 0%
where the time goes in v2:
time: 111 us; the launch traced here: 110 us
  starting transfers between devices  41 us (37%)
  waiting for transfers between devices  27.8 us (25%)
  local copies, waits for them, and re-layouts  17.7 us (16%)
  Pallas kernels  9.46 us (9%)
  other arithmetic  7.65 us (7%)
  matrix products  5.99 us (5%)
    all_to_all x2, waiting for transfers between devices, surface_flux(): returned = lax.all_to_all(sent, both, 0, 0, tiled=True)  13.3 us
    ppermute x2, starting transfers between devices, halo(): lax.ppermute(a_lo[:, :, :, :1], both, shift_pairs(sizes, (-1, -1)))  11.7 us
    ppermute x2, waiting for transfers between devices, halo(): lax.ppermute(a_hi[:, :, :, :1], both, shift_pairs(sizes, (1, -1)))  9.94 us
    all_to_all x2, starting transfers between devices, surface_flux(): returned = lax.all_to_all(sent, both, 0, 0, tiled=True)  9.72 us
    pallas_call x2, Pallas kernels, tendency(): pl.pallas_call(volume_kernel, out_shape=jax.ShapeDtypeStruct((3, rows, nb...  6.92 us
    all_to_all x2, starting transfers between devices, surface_flux(): gathered = lax.all_to_all(partial, both, 0, 0, tiled=True)  6.52 us
    ppermute x2, starting transfers between devices, halo(): from_right = lax.ppermute(b_lo, both, shift_pairs(sizes, (0, -1)))  4.92 us
    dot_general x2, matrix products, surface_flux(): flux = -jnp.dot(synth, returned.reshape(-1, nb_dev + 2), precision=highest)  4.21 us
  transfers between devices with their start and end apart: 20, of which 7 were waited for; matrix products, arithmetic and copies ran while one was open for 10% of the time, Pallas kernels for 0%

profile of v2, /device:TPU:0, one launch (start us, length us, event | category | flops | bytes accessed | tf_op | source)
XLA Modules:
  0.0 110.2 jit_solution(16759449675423714364)
XLA Ops:
  0.0 0.7 tile.7
  0.8 0.7 mul.387
  1.6 0.7 tile.6
  2.4 2.5 %shard_map.73.grad_ref = f32[9,128,128]{2,1,0:T(8,128)} custom-call(f32[3,128,128]{2,1,0:T(8,128)} %bitcast.163, f32[6,128,128]{2,1,0:T(8,128)} %constant.258.clone.mats_ref), custom_call_target="tpu_custom_call" | custom-call | tf_op jit(solution)/shard_map/pallas_call | solution.py:208
  5.0 0.7 broadcast_multiply_fusion.3.mass_ref
  5.7 3.5 %shard_map.74 = f32[3,128,128]{2,1,0:T(8,128)} custom-call(f32[3,128,128]{2,1,0:T(8,128)} %bitcast.166, f32[3,128,128]{2,1,0:T(8,128)} %bitcast.164, f32[9,128,128]{2,1,0:T(8,128)} %shard_map.73.grad_ref, f32[6,128,128]{2,1,0:T(8,128)} %constant.258.clone.mats_ref, f32[128,128]{1,0:T(8,128)} %broadcast_multiply_fusion.3.mass_ref), custom_call_target="tpu_custom_call" | custom-call | tf_op jit(solution)/shard_map/pallas_call | solution.py:258
  9.2 1.2 %fusion.76 = (f32[3,8,1,1]{3,2,1,0:T(1,128)S(1)}, f32[3,8,1,1]{3,2,1,0:T(1,128)S(1)}, f32[3,8,1,1]{3,2,1,0:T(1,128)S(1)}, f32[3,8,1,1]{3,2,1,0:T(1,128)S(1)}) fusion(f32[3,8,16,128]{3,2,1,0:T(8,128)} %bitcast.155), kind=kLoop, calls=%fused_computation.198 | loop fusion | bytes 768 | tf_op jit(solution)/shard_map/slice | solution.py:248
  10.3 6.4 %collective-permute-start.7 = (f32[3,8,1,1]{3,2,1,0:T(1,128)S(1)}, f32[3,8,1,1]{3,2,1,0:T(1,128)S(1)}, u32[]{:S(2)}, u32[]{:S(2)}) collective-permute-start(f32[3,8,1,1]{3,2,1,0:T(1,128)S(1)} %get-tuple-element.62), channel_id=1, source_target_pairs={{0,31},{1,28},{2,29},{3,30},{4,3},{5,0},{6,1},{7,2},{8,7},{9,4},{1... | collective-permute-start | bytes 296 | tf_op jit(solution)/shard_map/ppermute | solution.py:251
  16.8 1.0 fusion.77
  17.7 0.9 collective-permute-start.6
  18.6 1.1 %fusion.78 = (f32[3,8,16,1]{3,2,1,0:T(8,128)S(1)}, f32[3,8,16,1]{3,2,1,0:T(8,128)S(1)}) fusion(f32[3,8,16,128]{3,2,1,0:T(8,128)} %bitcast.157), kind=kLoop, calls=%fused_computation.200 | loop fusion | bytes 6144 | tf_op jit(solution)/shard_map/slice | solution.py:242
  19.8 2.5 %collective-permute-start.4 = (f32[3,8,16,1]{3,2,1,0:T(8,128)S(1)}, f32[3,8,16,1]{3,2,1,0:T(8,128)S(1)}, u32[]{:S(2)}, u32[]{:S(2)}) collective-permute-start(f32[3,8,16,1]{3,2,1,0:T(8,128)S(1)} %get-tuple-element.68), channel_id=1, source_target_pairs={{0,3},{1,0},{2,1},{3,2},{4,7},{5,4},{6,5},{7,6},{8,11},{9,8},{10,9... | collective-permute-start | bytes 4616 | tf_op jit(solution)/shard_map/ppermute | solution.py:247
  22.5 0.3 fusion.19
  22.8 0.6 copy.74
  23.5 4.0 %all-to-all-start = ((f32[32,2,128]{2,1,0:T(2,128)}), f32[32,2,128]{2,1,0:T(2,128)S(1)}, u32[]{:S(2)}, u32[]{:S(2)}) async-start(f32[32,2,128]{2,1,0:T(2,128)} %copy.74), calls=%async_computation | async-start | bytes 65536 | tf_op jit(solution)/shard_map/all_to_all | solution.py:218
  27.6 0.7 gather_fusion.1
  28.3 0.7 gather_fusion
  29.0 0.6 fusion.81
  29.7 0.7 and_reduce_fusion
  30.7 4.0 %all-to-all-done = f32[32,2,128]{2,1,0:T(2,128)S(1)} async-done(((f32[32,2,128]{2,1,0:T(2,128)}), f32[32,2,128]{2,1,0:T(2,128)S(1)}, u32[]{:S(2)}, u32[]{:S(2)}) %all-to-all-start) | async-done | bytes 32800 | tf_op jit(solution)/shard_map/all_to_all | solution.py:218
  34.8 0.2 fusion.14
  35.2 0.3 collective-permute-start.2
  35.5 0.5 collective-permute-start.1
  36.0 5.1 %collective-permute-done.2 = f32[3,8,1,1]{3,2,1,0:T(1,128)S(1)} collective-permute-done((f32[3,8,1,1]{3,2,1,0:T(1,128)S(1)}, f32[3,8,1,1]{3,2,1,0:T(1,128)S(1)}, u32[]{:S(2)}, u32[]{:S(2)}) %collective-permute-start.2) | collective-permute-done | bytes 128 | tf_op jit(solution)/shard_map/ppermute | solution.py:249
  41.0 0.6 broadcast_in_dim.51
  41.7 5.7 %all-to-all-start.1 = ((f32[32,2,130]{2,1,0:T(2,128)}), f32[32,2,130]{2,1,0:T(2,128)S(1)}, u32[]{:S(2)}, u32[]{:S(2)}) async-start(f32[32,2,130]{2,1,0:T(2,128)} %bitcast.16), calls=%async_computation.1 | async-start | bytes 131072 | tf_op jit(solution)/shard_map/all_to_all | solution.py:232
  47.4 0.4 collective-permute-done
  47.8 0.5 maximum_maximum_fusion
  48.3 6.6 %all-to-all-done.1 = f32[32,2,130]{2,1,0:T(2,128)S(1)} async-done(((f32[32,2,130]{2,1,0:T(2,128)}), f32[32,2,130]{2,1,0:T(2,128)S(1)}, u32[]{:S(2)}, u32[]{:S(2)}) %all-to-all-start.1) | async-done | bytes 33312 | tf_op jit(solution)/shard_map/all_to_all | solution.py:232
  54.9 2.1 %fusion.8 = f32[3,8,18,130]{3,2,1,0:T(8,128)S(1)} fusion(f32[3,8,18,130]{3,2,1,0:T(8,128)S(1)} %maximum_maximum_fusion, s32[]{:T(128)} %bitcast.3, s32[]{:T(128)} %bitcast.4, f32[32,2,130]{2,1,0:T(2,128)S(1)} %all-to-all-done.1, f32[18,32,1]{1,0,2:T(8,128)S(1)} %get-tuple-element.82, f32[18,32,1]{1,0,2:T(8,128)S(1)} %get-tuple-element.81, ...), kind=kOutput, calls=%fused_computation.14 | convolution fusion | flops 1812312 | bytes 140809 | tf_op jit(solution)/shard_map/dot_general | solution.py:235
  57.9 0.2 slice_reduce_fusion.3
  58.1 0.5 copy.83
  58.6 0.2 fusion.70
  59.0 0.5 slice_add_fusion.3
  59.5 0.6 maximum_bitcast_fusion
  60.1 0.4 copy.86
  60.6 0.7 multiply_add_fusion
  61.3 3.4 %shard_map.75 = f32[3,128,128]{2,1,0:T(8,128)} custom-call(f32[3,128,128]{2,1,0:T(8,128)} %bitcast.167, f32[3,128,128]{2,1,0:T(8,128)} %bitcast.165, f32[9,128,128]{2,1,0:T(8,128)} %shard_map.73.grad_ref, f32[6,128,128]{2,1,0:T(8,128)} %constant.258.clone.mats_ref, f32[128,128]{1,0:T(8,128)} %broadcast_multiply_fusion.3.mass_ref), custom_call_target="tpu_custom_call" | custom-call | tf_op jit(solution)/shard_map/pallas_call | solution.py:258
  64.8 1.2 %fusion.73 = (f32[3,8,1,1]{3,2,1,0:T(1,128)S(1)}, f32[3,8,1,1]{3,2,1,0:T(1,128)S(1)}, f32[3,8,1,1]{3,2,1,0:T(1,128)S(1)}, f32[3,8,1,1]{3,2,1,0:T(1,128)S(1)}) fusion(f32[3,8,16,128]{3,2,1,0:T(8,128)} %bitcast.159), kind=kLoop, calls=%fused_computation.195 | loop fusion | bytes 768 | tf_op jit(solution)/shard_map/slice | solution.py:248
  65.9 1.1 %fusion.75 = (f32[3,8,16,1]{3,2,1,0:T(8,128)S(1)}, f32[3,8,16,1]{3,2,1,0:T(8,128)S(1)}) fusion(f32[3,8,16,128]{3,2,1,0:T(8,128)} %bitcast.160), kind=kLoop, calls=%fused_computation.197 | loop fusion | bytes 6144 | tf_op jit(solution)/shard_map/slice | solution.py:242
  67.1 1.0 fusion.18
  68.1 0.6 copy.87
  68.7 2.6 %all-to-all-start.2 = ((f32[32,2,128]{2,1,0:T(2,128)}), f32[32,2,128]{2,1,0:T(2,128)S(1)}, u32[]{:S(2)}, u32[]{:S(2)}) async-start(f32[32,2,128]{2,1,0:T(2,128)} %copy.87), calls=%async_computation.2 | async-start | bytes 65536 | tf_op jit(solution)/shard_map/all_to_all | solution.py:218
  71.3 1.0 fusion.74
  72.3 5.3 %collective-permute-start.15 = (f32[3,8,1,1]{3,2,1,0:T(1,128)S(1)}, f32[3,8,1,1]{3,2,1,0:T(1,128)S(1)}, u32[]{:S(2)}, u32[]{:S(2)}) collective-permute-start(f32[3,8,1,1]{3,2,1,0:T(1,128)S(1)} %get-tuple-element.54), channel_id=1, source_target_pairs={{0,31},{1,28},{2,29},{3,30},{4,3},{5,0},{6,1},{7,2},{8,7},{9,4},{1... | collective-permute-start | bytes 296 | tf_op jit(solution)/shard_map/ppermute | solution.py:251
  77.6 0.5 collective-permute-start.14
  78.1 2.4 %collective-permute-start.12 = (f32[3,8,16,1]{3,2,1,0:T(8,128)S(1)}, f32[3,8,16,1]{3,2,1,0:T(8,128)S(1)}, u32[]{:S(2)}, u32[]{:S(2)}) collective-permute-start(f32[3,8,16,1]{3,2,1,0:T(8,128)S(1)} %get-tuple-element.60), channel_id=1, source_target_pairs={{0,3},{1,0},{2,1},{3,2},{4,7},{5,4},{6,5},{7,6},{8,11},{9,8},{10,9... | collective-permute-start | bytes 4616 | tf_op jit(solution)/shard_map/ppermute | solution.py:247
  80.6 0.2 fusion.12
  81.0 2.6 %collective-permute-start.10 = (f32[3,8,1,1]{3,2,1,0:T(1,128)S(1)}, f32[3,8,1,1]{3,2,1,0:T(1,128)S(1)}, u32[]{:S(2)}, u32[]{:S(2)}) collective-permute-start(f32[3,8,1,1]{3,2,1,0:T(1,128)S(1)} %get-tuple-element.56), channel_id=1, source_target_pairs={{0,7},{1,4},{2,5},{3,6},{4,11},{5,8},{6,9},{7,10},{8,15},{9,12},{1... | collective-permute-start | bytes 296 | tf_op jit(solution)/shard_map/ppermute | solution.py:249
  83.6 1.4 %collective-permute-start.9 = (f32[3,8,1,128]{3,2,1,0:T(1,128)S(1)}, f32[3,8,1,128]{3,2,1,0:T(1,128)S(1)}, u32[]{:S(2)}, u32[]{:S(2)}) collective-permute-start(f32[3,8,1,128]{3,2,1,0:T(1,128)S(1)} %get-tuple-element.57), channel_id=1, source_target_pairs={{0,4},{1,5},{2,6},{3,7},{4,8},{5,9},{6,10},{7,11},{8,12},{9,13},{1... | collective-permute-start | bytes 36872 | tf_op jit(solution)/shard_map/ppermute | solution.py:244
  85.1 4.9 %collective-permute-done.10 = f32[3,8,1,1]{3,2,1,0:T(1,128)S(1)} collective-permute-done((f32[3,8,1,1]{3,2,1,0:T(1,128)S(1)}, f32[3,8,1,1]{3,2,1,0:T(1,128)S(1)}, u32[]{:S(2)}, u32[]{:S(2)}) %collective-permute-start.10) | collective-permute-done | bytes 128 | tf_op jit(solution)/shard_map/ppermute | solution.py:249
  89.9 1.9 %collective-permute-start.8 = (f32[3,8,1,1]{3,2,1,0:T(1,128)S(1)}, f32[3,8,1,1]{3,2,1,0:T(1,128)S(1)}, u32[]{:S(2)}, u32[]{:S(2)}) collective-permute-start(f32[3,8,1,1]{3,2,1,0:T(1,128)S(1)} %get-tuple-element.53), channel_id=1, source_target_pairs={{0,5},{1,6},{2,7},{3,4},{4,9},{5,10},{6,11},{7,8},{8,13},{9,14},{1... | collective-permute-start | bytes 296 | tf_op jit(solution)/shard_map/ppermute | solution.py:248
  91.8 0.6 broadcast_in_dim.102
  92.4 4.0 %all-to-all-start.3 = ((f32[32,2,130]{2,1,0:T(2,128)}), f32[32,2,130]{2,1,0:T(2,128)S(1)}, u32[]{:S(2)}, u32[]{:S(2)}) async-start(f32[32,2,130]{2,1,0:T(2,128)} %bitcast.39), calls=%async_computation.3 | async-start | bytes 131072 | tf_op jit(solution)/shard_map/all_to_all | solution.py:232
  96.7 0.5 maximum_maximum_fusion.1
  97.1 6.6 %all-to-all-done.3 = f32[32,2,130]{2,1,0:T(2,128)S(1)} async-done(((f32[32,2,130]{2,1,0:T(2,128)}), f32[32,2,130]{2,1,0:T(2,128)S(1)}, u32[]{:S(2)}, u32[]{:S(2)}) %all-to-all-start.3) | async-done | bytes 33312 | tf_op jit(solution)/shard_map/all_to_all | solution.py:232
  103.8 2.1 %fusion.11 = f32[3,8,18,130]{3,2,1,0:T(8,128)S(1)} fusion(f32[3,8,18,130]{3,2,1,0:T(8,128)S(1)} %maximum_maximum_fusion.1, s32[]{:T(128)} %bitcast.3, s32[]{:T(128)} %bitcast.4, f32[32,2,130]{2,1,0:T(2,128)S(1)} %all-to-all-done.3, f32[18,32,1]{1,0,2:T(8,128)S(1)} %get-tuple-element.82, f32[18,32,1]{1,0,2:T(8,128)S(1)} %get-tuple-element.81, ...), kind=kOutput, calls=%fused_computation.17 | convolution fusion | flops 1812312 | bytes 140809 | tf_op jit(solution)/shard_map/dot_general | solution.py:235
  106.8 0.2 slice_reduce_fusion.1
  107.0 0.5 copy.96
  107.5 0.2 fusion.69
  107.9 0.5 slice_add_fusion.1
  108.4 0.6 maximum_bitcast_fusion.1
  109.0 0.4 copy.99
  109.5 0.8 add_multiply_fusion
  (96 shorter events, 3.6 us)
Async XLA Ops:
  0.0 34.8 %copy-start = (bf16[1,512,512]{2,1,0:T(8,128)(2,1)S(1)}, bf16[1,512,512]{2,1,0:T(8,128)(2,1)}, u32[]{:S(2)}) copy-start(bf16[1,512,512]{2,1,0:T(8,128)(2,1)} %param.13) | copy-start | bytes 1572868
  5.0 17.3 %copy-start.2 = (f32[8]{0:T(128)S(1)}, f32[8]{0:T(128)}, u32[]{:S(2)}) copy-start(f32[8]{0:T(128)} %constant.256.clone) | copy-start | bytes 100
  5.0 17.4 %copy-start.6 = (s32[32]{0:T(128)S(1)}, s32[32]{0:T(128)}, u32[]{:S(2)}) copy-start(s32[32]{0:T(128)} %param.14) | copy-start | bytes 388
  5.0 17.5 %copy-start.5 = (f32[3,8,16,128]{3,2,1,0:T(8,128)S(1)}, f32[3,8,16,128]{3,2,1,0:T(8,128)}, u32[]{:S(2)}) copy-start(f32[3,8,16,128]{3,2,1,0:T(8,128)} %param.11) | copy-start | bytes 589828
  5.7 22.5 %copy-start.1 = (f32[8]{0:T(128)S(1)}, f32[8]{0:T(128)}, u32[]{:S(2)}) copy-start(f32[8]{0:T(128)} %constant.257.clone) | copy-start | bytes 100
  5.7 24.0 %copy-start.7 = (s32[4]{0:T(128)S(1)}, s32[4]{0:T(128)}, u32[]{:S(2)}) copy-start(s32[4]{0:T(128)} %constant.233.clone.1) | copy-start | bytes 52
  10.3 37.5 %copy-start.3 = (f32[3,128,128]{2,1,0:T(8,128)S(1)}, f32[3,128,128]{2,1,0:T(8,128)}, u32[]{:S(2)}) copy-start(f32[3,128,128]{2,1,0:T(8,128)} %shard_map.74) | copy-start | bytes 589828
  10.3 24.8 %collective-permute-start.7 = (f32[3,8,1,1]{3,2,1,0:T(1,128)S(1)}, f32[3,8,1,1]{3,2,1,0:T(1,128)S(1)}, u32[]{:S(2)}, u32[]{:S(2)}) collective-permute-start(f32[3,8,1,1]{3,2,1,0:T(1,128)S(1)} %get-tuple-element.62), channel_id=1, source_target_pairs={{0,31},{1,28},{2,29},{3,30},{4,3},{5,0},{6,1},{7,2},{8,7},{9,4},{1... | collective-permute-start | bytes 296 | tf_op jit(solution)/shard_map/ppermute | solution.py:251
  17.7 30.0 %collective-permute-start.6 = (f32[3,8,1,128]{3,2,1,0:T(1,128)S(1)}, f32[3,8,1,128]{3,2,1,0:T(1,128)S(1)}, u32[]{:S(2)}, u32[]{:S(2)}) collective-permute-start(f32[3,8,1,128]{3,2,1,0:T(1,128)S(1)} %get-tuple-element.66), channel_id=1, source_target_pairs={{0,28},{1,29},{2,30},{3,31},{4,0},{5,1},{6,2},{7,3},{8,4},{9,5},{1... | collective-permute-start | bytes 36872 | tf_op jit(solution)/shard_map/ppermute | solution.py:245
  18.6 16.8 %collective-permute-start.5 = (f32[3,8,1,1]{3,2,1,0:T(1,128)S(1)}, f32[3,8,1,1]{3,2,1,0:T(1,128)S(1)}, u32[]{:S(2)}, u32[]{:S(2)}) collective-permute-start(f32[3,8,1,1]{3,2,1,0:T(1,128)S(1)} %get-tuple-element.63), channel_id=1, source_target_pairs={{0,29},{1,30},{2,31},{3,28},{4,1},{5,2},{6,3},{7,0},{8,5},{9,6},{1... | collective-permute-start | bytes 296 | tf_op jit(solution)/shard_map/ppermute | solution.py:250
  19.8 28.0 %collective-permute-start.4 = (f32[3,8,16,1]{3,2,1,0:T(8,128)S(1)}, f32[3,8,16,1]{3,2,1,0:T(8,128)S(1)}, u32[]{:S(2)}, u32[]{:S(2)}) collective-permute-start(f32[3,8,16,1]{3,2,1,0:T(8,128)S(1)} %get-tuple-element.68), channel_id=1, source_target_pairs={{0,3},{1,0},{2,1},{3,2},{4,7},{5,4},{6,5},{7,6},{8,11},{9,8},{10,9... | collective-permute-start | bytes 4616 | tf_op jit(solution)/shard_map/ppermute | solution.py:247
  22.2 25.5 %collective-permute-start.3 = (f32[3,8,16,1]{3,2,1,0:T(8,128)S(1)}, f32[3,8,16,1]{3,2,1,0:T(8,128)S(1)}, u32[]{:S(2)}, u32[]{:S(2)}) collective-permute-start(f32[3,8,16,1]{3,2,1,0:T(8,128)S(1)} %get-tuple-element.67), channel_id=1, source_target_pairs={{0,1},{1,2},{2,3},{3,0},{4,5},{5,6},{6,7},{7,4},{8,9},{9,10},{10,1... | collective-permute-start | bytes 4616 | tf_op jit(solution)/shard_map/ppermute | solution.py:246
  23.5 11.3 %all-to-all-start = ((f32[32,2,128]{2,1,0:T(2,128)}), f32[32,2,128]{2,1,0:T(2,128)S(1)}, u32[]{:S(2)}, u32[]{:S(2)}) async-start(f32[32,2,128]{2,1,0:T(2,128)} %copy.74), calls=%async_computation | async-start | bytes 65536 | tf_op jit(solution)/shard_map/all_to_all | solution.py:218
  35.2 5.9 %collective-permute-start.2 = (f32[3,8,1,1]{3,2,1,0:T(1,128)S(1)}, f32[3,8,1,1]{3,2,1,0:T(1,128)S(1)}, u32[]{:S(2)}, u32[]{:S(2)}) collective-permute-start(f32[3,8,1,1]{3,2,1,0:T(1,128)S(1)} %get-tuple-element.64), channel_id=1, source_target_pairs={{0,7},{1,4},{2,5},{3,6},{4,11},{5,8},{6,9},{7,10},{8,15},{9,12},{1... | collective-permute-start | bytes 296 | tf_op jit(solution)/shard_map/ppermute | solution.py:249
  35.5 12.3 %collective-permute-start.1 = (f32[3,8,1,128]{3,2,1,0:T(1,128)S(1)}, f32[3,8,1,128]{3,2,1,0:T(1,128)S(1)}, u32[]{:S(2)}, u32[]{:S(2)}) collective-permute-start(f32[3,8,1,128]{3,2,1,0:T(1,128)S(1)} %get-tuple-element.65), channel_id=1, source_target_pairs={{0,4},{1,5},{2,6},{3,7},{4,8},{5,9},{6,10},{7,11},{8,12},{9,13},{1... | collective-permute-start | bytes 36872 | tf_op jit(solution)/shard_map/ppermute | solution.py:244
  41.0 6.7 %collective-permute-start = (f32[3,8,1,1]{3,2,1,0:T(1,128)S(1)}, f32[3,8,1,1]{3,2,1,0:T(1,128)S(1)}, u32[]{:S(2)}, u32[]{:S(2)}) collective-permute-start(f32[3,8,1,1]{3,2,1,0:T(1,128)S(1)} %get-tuple-element.61), channel_id=1, source_target_pairs={{0,5},{1,6},{2,7},{3,4},{4,9},{5,10},{6,11},{7,8},{8,13},{9,14},{1... | collective-permute-start | bytes 296 | tf_op jit(solution)/shard_map/ppermute | solution.py:248
  41.7 13.2 %all-to-all-start.1 = ((f32[32,2,130]{2,1,0:T(2,128)}), f32[32,2,130]{2,1,0:T(2,128)S(1)}, u32[]{:S(2)}, u32[]{:S(2)}) async-start(f32[32,2,130]{2,1,0:T(2,128)} %bitcast.16), calls=%async_computation.1 | async-start | bytes 131072 | tf_op jit(solution)/shard_map/all_to_all | solution.py:232
  64.7 31.9 %copy-start.4 = (f32[3,128,128]{2,1,0:T(8,128)S(1)}, f32[3,128,128]{2,1,0:T(8,128)}, u32[]{:S(2)}) copy-start(f32[3,128,128]{2,1,0:T(8,128)} %shard_map.75) | copy-start | bytes 589828
  68.7 11.8 %all-to-all-start.2 = ((f32[32,2,128]{2,1,0:T(2,128)}), f32[32,2,128]{2,1,0:T(2,128)S(1)}, u32[]{:S(2)}, u32[]{:S(2)}) async-start(f32[32,2,128]{2,1,0:T(2,128)} %copy.87), calls=%async_computation.2 | async-start | bytes 65536 | tf_op jit(solution)/shard_map/all_to_all | solution.py:218
  72.3 8.7 %collective-permute-start.15 = (f32[3,8,1,1]{3,2,1,0:T(1,128)S(1)}, f32[3,8,1,1]{3,2,1,0:T(1,128)S(1)}, u32[]{:S(2)}, u32[]{:S(2)}) collective-permute-start(f32[3,8,1,1]{3,2,1,0:T(1,128)S(1)} %get-tuple-element.54), channel_id=1, source_target_pairs={{0,31},{1,28},{2,29},{3,30},{4,3},{5,0},{6,1},{7,2},{8,7},{9,4},{1... | collective-permute-start | bytes 296 | tf_op jit(solution)/shard_map/ppermute | solution.py:251
  77.6 19.1 %collective-permute-start.14 = (f32[3,8,1,128]{3,2,1,0:T(1,128)S(1)}, f32[3,8,1,128]{3,2,1,0:T(1,128)S(1)}, u32[]{:S(2)}, u32[]{:S(2)}) collective-permute-start(f32[3,8,1,128]{3,2,1,0:T(1,128)S(1)} %get-tuple-element.58), channel_id=1, source_target_pairs={{0,28},{1,29},{2,30},{3,31},{4,0},{5,1},{6,2},{7,3},{8,4},{9,5},{1... | collective-permute-start | bytes 36872 | tf_op jit(solution)/shard_map/ppermute | solution.py:245
  78.1 5.5 %collective-permute-start.13 = (f32[3,8,1,1]{3,2,1,0:T(1,128)S(1)}, f32[3,8,1,1]{3,2,1,0:T(1,128)S(1)}, u32[]{:S(2)}, u32[]{:S(2)}) collective-permute-start(f32[3,8,1,1]{3,2,1,0:T(1,128)S(1)} %get-tuple-element.55), channel_id=1, source_target_pairs={{0,29},{1,30},{2,31},{3,28},{4,1},{5,2},{6,3},{7,0},{8,5},{9,6},{1... | collective-permute-start | bytes 296 | tf_op jit(solution)/shard_map/ppermute | solution.py:250
  78.1 18.6 %collective-permute-start.12 = (f32[3,8,16,1]{3,2,1,0:T(8,128)S(1)}, f32[3,8,16,1]{3,2,1,0:T(8,128)S(1)}, u32[]{:S(2)}, u32[]{:S(2)}) collective-permute-start(f32[3,8,16,1]{3,2,1,0:T(8,128)S(1)} %get-tuple-element.60), channel_id=1, source_target_pairs={{0,3},{1,0},{2,1},{3,2},{4,7},{5,4},{6,5},{7,6},{8,11},{9,8},{10,9... | collective-permute-start | bytes 4616 | tf_op jit(solution)/shard_map/ppermute | solution.py:247
  80.5 16.1 %collective-permute-start.11 = (f32[3,8,16,1]{3,2,1,0:T(8,128)S(1)}, f32[3,8,16,1]{3,2,1,0:T(8,128)S(1)}, u32[]{:S(2)}, u32[]{:S(2)}) collective-permute-start(f32[3,8,16,1]{3,2,1,0:T(8,128)S(1)} %get-tuple-element.59), channel_id=1, source_target_pairs={{0,1},{1,2},{2,3},{3,0},{4,5},{5,6},{6,7},{7,4},{8,9},{9,10},{10,1... | collective-permute-start | bytes 4616 | tf_op jit(solution)/shard_map/ppermute | solution.py:246
  81.0 8.9 %collective-permute-start.10 = (f32[3,8,1,1]{3,2,1,0:T(1,128)S(1)}, f32[3,8,1,1]{3,2,1,0:T(1,128)S(1)}, u32[]{:S(2)}, u32[]{:S(2)}) collective-permute-start(f32[3,8,1,1]{3,2,1,0:T(1,128)S(1)} %get-tuple-element.56), channel_id=1, source_target_pairs={{0,7},{1,4},{2,5},{3,6},{4,11},{5,8},{6,9},{7,10},{8,15},{9,12},{1... | collective-permute-start | bytes 296 | tf_op jit(solution)/shard_map/ppermute | solution.py:249
  83.6 13.1 %collective-permute-start.9 = (f32[3,8,1,128]{3,2,1,0:T(1,128)S(1)}, f32[3,8,1,128]{3,2,1,0:T(1,128)S(1)}, u32[]{:S(2)}, u32[]{:S(2)}) collective-permute-start(f32[3,8,1,128]{3,2,1,0:T(1,128)S(1)} %get-tuple-element.57), channel_id=1, source_target_pairs={{0,4},{1,5},{2,6},{3,7},{4,8},{5,9},{6,10},{7,11},{8,12},{9,13},{1... | collective-permute-start | bytes 36872 | tf_op jit(solution)/shard_map/ppermute | solution.py:244
  89.9 6.7 %collective-permute-start.8 = (f32[3,8,1,1]{3,2,1,0:T(1,128)S(1)}, f32[3,8,1,1]{3,2,1,0:T(1,128)S(1)}, u32[]{:S(2)}, u32[]{:S(2)}) collective-permute-start(f32[3,8,1,1]{3,2,1,0:T(1,128)S(1)} %get-tuple-element.53), channel_id=1, source_target_pairs={{0,5},{1,6},{2,7},{3,4},{4,9},{5,10},{6,11},{7,8},{8,13},{9,14},{1... | collective-permute-start | bytes 296 | tf_op jit(solution)/shard_map/ppermute | solution.py:248
  92.4 11.3 %all-to-all-start.3 = ((f32[32,2,130]{2,1,0:T(2,128)}), f32[32,2,130]{2,1,0:T(2,128)S(1)}, u32[]{:S(2)}, u32[]{:S(2)}) async-start(f32[32,2,130]{2,1,0:T(2,128)} %bitcast.39), calls=%async_computation.3 | async-start | bytes 131072 | tf_op jit(solution)/shard_map/all_to_all | solution.py:232

commit v3 on v2

--- a/solution.py
+++ b/solution.py
@@ -209,7 +209,7 @@
         gradient_kernel, out_shape=jax.ShapeDtypeStruct((9, rows, nb_dev), jnp.float32)
     )(flat_flow, mats)
 
-    def surface_flux(surface):
+    def owner_map(surface):
         angle = phases(wave_of_slot, tile_index * elems_a, elems_a, span, points)
         table = (
             jnp.stack([jnp.cos(angle), jnp.sin(angle)], axis=1) * (w_a * scale)[None, None, :]
@@ -226,14 +226,66 @@
         pieces = jnp.stack(
             [edged[:, g * nb_dev : g * nb_dev + nb_dev + 2] for g in range(groups)], axis=0
         )
-        sent = jnp.broadcast_to(pieces[None], (tiles,) + pieces.shape).reshape(
-            tiles * groups, 2, nb_dev + 2
-        )
-        returned = lax.all_to_all(sent, both, 0, 0, tiled=True)
+        return jnp.broadcast_to(pieces[None], (tiles,) + pieces.shape).reshape(
+            tiles, groups, 2 * (nb_dev + 2)
+        )
+
+    def flux_of(returned):
         angle = phases_at(wave_of_slot, rows_ext, span, points)
         synth = jnp.stack([jnp.cos(angle).T, jnp.sin(angle).T], axis=2).reshape(na_dev + 2, -1)
         flux = -jnp.dot(synth, returned.reshape(-1, nb_dev + 2), precision=highest)
         return diffusivity * surface_ext * flux
+
+    mapped_len = 2 * (nb_dev + 2)
+    slot_len = 3 * radial_nodes * max(nb_dev, na_dev)
+    carried_halo = tiles >= 3 and groups >= 3 and tiles * groups <= 64
+
+    def joint_exchange(sent, stacked):
+        a_lo = lax.slice_in_dim(stacked, 0, 1, axis=2)
+        a_hi = lax.slice_in_dim(stacked, na_dev - 1, na_dev, axis=2)
+        b_lo = lax.slice_in_dim(stacked, 0, 1, axis=3)
+        b_hi = lax.slice_in_dim(stacked, nb_dev - 1, nb_dev, axis=3)
+        out_pieces = [
+            ((1, 0), a_hi),
+            ((-1, 0), a_lo),
+            ((0, 1), b_hi),
+            ((0, -1), b_lo),
+            ((1, 1), a_hi[:, :, :, -1:]),
+            ((1, -1), a_hi[:, :, :, :1]),
+            ((-1, 1), a_lo[:, :, :, -1:]),
+            ((-1, -1), a_lo[:, :, :, :1]),
+        ]
+        slots = jnp.zeros((tiles, groups, slot_len), jnp.float32)
+        for (dt, dg), piece in out_pieces:
+            flat = piece.reshape(1, 1, -1)
+            flat = jnp.pad(flat, ((0, 0), (0, 0), (0, slot_len - flat.shape[2])))
+            slots = lax.dynamic_update_slice(
+                slots, flat, ((tile_index + dt) % tiles, (group_index + dg) % groups, 0)
+            )
+        message = jnp.concatenate([sent, slots], axis=2).reshape(tiles * groups, -1)
+        received = lax.all_to_all(message, both, 0, 0, tiled=True).reshape(tiles, groups, -1)
+        returned = received[:, :, :mapped_len].reshape(tiles * groups, 2, nb_dev + 2)
+
+        def take(dt, dg, like):
+            row = lax.dynamic_slice(
+                received,
+                ((tile_index - dt) % tiles, (group_index - dg) % groups, mapped_len),
+                (1, 1, like.size),
+            )
+            return row.reshape(like.shape)
+
+        from_up = take(1, 0, a_hi)
+        from_down = take(-1, 0, a_lo)
+        from_left = take(0, 1, b_hi)
+        from_right = take(0, -1, b_lo)
+        corner_ul = take(1, 1, a_hi[:, :, :, -1:])
+        corner_ur = take(1, -1, a_hi[:, :, :, :1])
+        corner_dl = take(-1, 1, a_lo[:, :, :, -1:])
+        corner_dr = take(-1, -1, a_lo[:, :, :, :1])
+        top = jnp.concatenate([corner_ul, from_up, corner_ur], axis=3)
+        middle = jnp.concatenate([from_left, stacked, from_right], axis=3)
+        bottom = jnp.concatenate([corner_dl, from_down, corner_dr], axis=3)
+        return returned, jnp.concatenate([top, middle, bottom], axis=2)
 
     def halo(stacked):
         a_lo = lax.slice_in_dim(stacked, 0, 1, axis=2)
@@ -259,8 +311,15 @@
             volume_kernel, out_shape=jax.ShapeDtypeStruct((3, rows, nb_dev), jnp.float32)
         )(parts.reshape(3, rows, nb_dev), flat_flow, grads, mats, flat_mass)
         stacked = stacked.reshape(parts.shape)
-        flux_term = surface_flux(parts[0, radial_nodes - 1])
-        padded = halo(stacked)
+        sent = owner_map(parts[0, radial_nodes - 1])
+        if carried_halo:
+            returned, padded = joint_exchange(sent, stacked)
+        else:
+            returned = lax.all_to_all(
+                sent.reshape(tiles * groups, -1), both, 0, 0, tiled=True
+            ).reshape(tiles * groups, 2, nb_dev + 2)
+            padded = halo(stacked)
+        flux_term = flux_of(returned)
         padded = padded.at[0, radial_nodes - 1].add(flux_term)
         plane_r = jnp.zeros_like(lax.slice_in_dim(padded, 0, 1, axis=1))
         padded = assemble_dim(padded, 1, plane_r, plane_r)

time: 111 us -> 106 us (0.955)
  starting transfers between devices: 41 us -> 15.9 us
  blocking collectives: 0 us -> 16.6 us
  waiting for transfers between devices: 27.8 us -> 17 us
  local copies, waits for them, and re-layouts: 17.7 us -> 28 us
  other arithmetic: 7.65 us -> 11.3 us
    ppermute x16 -> x0, starting transfers between devices: 24.8 us -> none  [the longest x2 11.7 us: halo(): lax.ppermute(a_lo[:, :, :, :1], both, shift_pairs(sizes, (-1, -1)))]
    all_to_all x0 -> x1, blocking collectives: none -> 16.6 us  [joint_exchange(): lax.all_to_all(message, both, 0, 0, tiled=True).reshape(tiles, groups, -1)]
    ppermute x16 -> x0, waiting for transfers between devices: 10.5 us -> none  [the longest x2 9.94 us: halo(): lax.ppermute(a_hi[:, :, :, :1], both, shift_pairs(sizes, (1, -1)))]
    dynamic_update_slice x0 -> x16, local copies, waits for them, and re-layouts: none -> 3.02 us  [joint_exchange(): lax.dynamic_update_slice(slots, flat, ((tile_index + dt) % tiles, (group_...]
    reshape x0 -> x26, local copies, waits for them, and re-layouts: none -> 2.9 us  [the longest x12 1.68 us: take(): return row.reshape(like.shape)]
    all_to_all x0 -> x2, other arithmetic: none -> 2.09 us  [joint_exchange(): lax.all_to_all(message, both, 0, 0, tiled=True).reshape(tiles, groups, -1)]
    all_to_all x0 -> x2, local copies, waits for them, and re-layouts: none -> 1.39 us  [joint_exchange(): lax.all_to_all(message, both, 0, 0, tiled=True).reshape(tiles, groups, -1)]
    broadcast_in_dim x2, local copies, waits for them, and re-layouts: 1.28 us -> 0.02 us  [owner_map(): jnp.broadcast_to(pieces[None], (tiles,) + pieces.shape)]
  transfers between devices with their start and end apart: 20 -> 3, of which waited for: 7 -> 2; matrix products, arithmetic and copies ran while one was open for 10% -> 15% of each run, Pallas kernels for 0% -> 6%
where the time goes in v3:
time: 106 us; the launch traced here: 105 us
  local copies, waits for them, and re-layouts  28 us (26%)
  waiting for transfers between devices  17 us (16%)
  blocking collectives  16.6 us (16%)
  starting transfers between devices  15.9 us (15%)
  other arithmetic  11.3 us (11%)
  Pallas kernels  9.46 us (9%)
  matrix products  5.98 us (6%)
  between operations  1.1 us (1%)
    all_to_all x1, blocking collectives, joint_exchange(): lax.all_to_all(message, both, 0, 0, tiled=True).reshape(tiles, groups, -1)  16.6 us
    all_to_all x1, waiting for transfers between devices, joint_exchange(): lax.all_to_all(message, both, 0, 0, tiled=True).reshape(tiles, groups, -1)  13.4 us
    all_to_all x2, starting transfers between devices, owner_map(): gathered = lax.all_to_all(partial, both, 0, 0, tiled=True)  9.86 us
    pallas_call x2, Pallas kernels, tendency(): pl.pallas_call(volume_kernel, out_shape=jax.ShapeDtypeStruct((3, rows, nb...  6.9 us
    all_to_all x1, starting transfers between devices, joint_exchange(): lax.all_to_all(message, both, 0, 0, tiled=True).reshape(tiles, groups, -1)  6.01 us
    dot_general x2, matrix products, flux_of(): flux = -jnp.dot(synth, returned.reshape(-1, nb_dev + 2), precision=highest)  4.2 us
    all_to_all x2, waiting for transfers between devices, owner_map(): gathered = lax.all_to_all(partial, both, 0, 0, tiled=True)  3.65 us
    dynamic_update_slice x16, local copies, waits for them, and re-layouts, joint_exchange(): lax.dynamic_update_slice(slots, flat, ((tile_index + dt) % tiles, (group_...  3.02 us
  transfers between devices with their start and end apart: 3, of which 2 were waited for; matrix products, arithmetic and copies ran while one was open for 15% of the time, Pallas kernels for 6%

profile of v3, /device:TPU:0, one launch (start us, length us, event | category | flops | bytes accessed | tf_op | source)
XLA Modules:
  0.0 105.4 jit_solution(9780505297369334860)
XLA Ops:
  0.0 0.7 tile.9
  0.8 0.7 convert_element_type.77
  1.5 0.7 tile.8
  2.2 0.8 fusion.29
  3.0 1.0 fusion.19
  4.0 0.6 copy.100
  4.6 7.3 %all-to-all-start = ((f32[32,2,128]{2,1,0:T(2,128)}), f32[32,2,128]{2,1,0:T(2,128)S(1)}, u32[]{:S(2)}, u32[]{:S(2)}) async-start(f32[32,2,128]{2,1,0:T(2,128)} %copy.100), calls=%async_computation | async-start | bytes 65536 | tf_op jit(solution)/shard_map/all_to_all | solution.py:218
  12.1 0.7 mul.398
  12.9 0.7 tile.11
  13.7 2.6 %shard_map.73.grad_ref = f32[9,128,128]{2,1,0:T(8,128)} custom-call(f32[3,128,128]{2,1,0:T(8,128)} %bitcast.130, f32[6,128,128]{2,1,0:T(8,128)} %constant.414.clone.mats_ref), custom_call_target="tpu_custom_call" | custom-call | tf_op jit(solution)/shard_map/pallas_call | solution.py:208
  16.2 0.7 broadcast_multiply_fusion.3.mass_ref
  17.0 3.5 %shard_map.74 = f32[3,128,128]{2,1,0:T(8,128)} custom-call(f32[3,128,128]{2,1,0:T(8,128)} %bitcast.133, f32[3,128,128]{2,1,0:T(8,128)} %bitcast.131, f32[9,128,128]{2,1,0:T(8,128)} %shard_map.73.grad_ref, f32[6,128,128]{2,1,0:T(8,128)} %constant.414.clone.mats_ref, f32[128,128]{1,0:T(8,128)} %broadcast_multiply_fusion.3.mass_ref), custom_call_target="tpu_custom_call" | custom-call | tf_op jit(solution)/shard_map/pallas_call | solution.py:310
  20.4 1.0 fusion.76
  21.4 1.3 %slice_reduce_fusion.6 = (f32[3,8,16]{2,1,0:T(8,128)S(1)}, f32[3,8,16]{2,1,0:T(8,128)S(1)}) fusion(f32[3,8,16,128]{3,2,1,0:T(8,128)} %bitcast.123), kind=kLoop, calls=%fused_computation.40 | loop fusion | bytes 6144 | tf_op jit(solution)/shard_map/slice | solution.py:246
  22.7 1.3 %slice_reduce_fusion.12 = (f32[3,8]{1,0:T(4,128)S(1)}, f32[3,8]{1,0:T(4,128)S(1)}, f32[3,8]{1,0:T(4,128)S(1)}, f32[3,8]{1,0:T(4,128)S(1)}) fusion(f32[3,8,16,128]{3,2,1,0:T(8,128)} %bitcast.124), kind=kLoop, calls=%fused_computation.77 | loop fusion | bytes 768 | tf_op jit(solution)/shard_map/slice | solution.py:256
  24.7 0.2 dynamic_update_slice.48
  25.9 0.2 dynamic_update_slice.54
  26.5 0.7 gather_fusion.1
  27.2 0.7 fusion.79
  27.9 0.6 fusion.70
  28.5 0.8 and_reduce_fusion
  29.4 0.2 fusion.12
  30.4 1.1 %all_to_all.19 = f32[32,1,3332]{2,1,0:T(1,128)} reshape(f32[32,3332]{1,0:T(8,128)S(1)} %pad_maximum_fusion) | data formatting | bytes 852992 | tf_op jit(solution)/shard_map/all_to_all | solution.py:266
  31.4 6.0 %all-to-all-start.1 = ((f32[32,1,3332]{2,1,0:T(1,128)}), f32[32,1,3332]{2,1,0:T(1,128)S(1)}, u32[]{:S(2)}, u32[]{:S(2)}) async-start(f32[32,1,3332]{2,1,0:T(1,128)} %all_to_all.19), calls=%async_computation.1 | async-start | bytes 884736 | tf_op jit(solution)/shard_map/all_to_all | solution.py:266
  37.5 0.7 gather_fusion
  38.5 13.4 %all-to-all-done.1 = f32[32,1,3332]{2,1,0:T(1,128)S(1)} async-done(((f32[32,1,3332]{2,1,0:T(1,128)}), f32[32,1,3332]{2,1,0:T(1,128)S(1)}, u32[]{:S(2)}, u32[]{:S(2)}) %all-to-all-start.1) | async-done | bytes 426528 | tf_op jit(solution)/shard_map/all_to_all | solution.py:266
  51.9 1.0 reduce.15
  53.4 0.2 reshape.1195
  53.6 0.2 reshape.1196
  54.4 0.5 maximum_maximum_fusion
  54.9 2.1 %fusion.6 = f32[3,8,18,130]{3,2,1,0:T(8,128)S(1)} fusion(f32[3,8,18,130]{3,2,1,0:T(8,128)S(1)} %maximum_maximum_fusion, s32[]{:T(128)} %bitcast.12, s32[]{:T(128)} %bitcast.13, f32[18,64]{0,1:T(8,128)S(1)} %bitcast.135, f32[64,130]{1,0:T(8,128)S(1)} %reshape_reshape.6, f32[130]{0:T(256)S(1)} %broadcast_select_fusion, f32[18]{0:T(128)S(1)} %gather_fusion, ...), kind=kOutput, calls=%fused_computation.12 | convolution fusion | flops 1811160 | bytes 149001 | tf_op jit(solution)/shard_map/dot_general | solution.py:236
  57.8 0.5 copy.114
  58.5 0.2 fusion.72
  58.7 0.2 slice_reduce_fusion.5
  59.0 0.5 slice_add_fusion.3
  59.5 0.6 maximum_bitcast_fusion
  60.1 0.4 copy.117
  60.6 0.5 copy-done.5
  61.1 0.3 fusion.18
  61.4 0.3 copy-done.6
  61.8 3.4 %shard_map.75 = f32[3,128,128]{2,1,0:T(8,128)} custom-call(f32[3,128,128]{2,1,0:T(8,128)} %bitcast.134, f32[3,128,128]{2,1,0:T(8,128)} %bitcast.132, f32[9,128,128]{2,1,0:T(8,128)} %shard_map.73.grad_ref, f32[6,128,128]{2,1,0:T(8,128)} %constant.414.clone.mats_ref, f32[128,128]{1,0:T(8,128)} %broadcast_multiply_fusion.3.mass_ref), custom_call_target="tpu_custom_call" | custom-call | tf_op jit(solution)/shard_map/pallas_call | solution.py:310
  65.2 1.0 fusion.75
  66.2 1.3 %slice_reduce_fusion.8 = (f32[3,8]{1,0:T(4,128)S(1)}, f32[3,8]{1,0:T(4,128)S(1)}, f32[3,8]{1,0:T(4,128)S(1)}, f32[3,8]{1,0:T(4,128)S(1)}) fusion(f32[3,8,16,128]{3,2,1,0:T(8,128)} %bitcast.127), kind=kLoop, calls=%fused_computation.73 | loop fusion | bytes 768 | tf_op jit(solution)/shard_map/slice | solution.py:256
  67.5 0.6 copy.118
  68.1 2.6 %all-to-all-start.2 = ((f32[32,2,128]{2,1,0:T(2,128)}), f32[32,2,128]{2,1,0:T(2,128)S(1)}, u32[]{:S(2)}, u32[]{:S(2)}) async-start(f32[32,2,128]{2,1,0:T(2,128)} %copy.118), calls=%async_computation.2 | async-start | bytes 65536 | tf_op jit(solution)/shard_map/all_to_all | solution.py:218
  70.7 1.3 %slice_reduce_fusion.2 = (f32[3,8,16]{2,1,0:T(8,128)S(1)}, f32[3,8,16]{2,1,0:T(8,128)S(1)}) fusion(f32[3,8,16,128]{3,2,1,0:T(8,128)} %bitcast.128), kind=kLoop, calls=%fused_computation.34 | loop fusion | bytes 6144 | tf_op jit(solution)/shard_map/slice | solution.py:246
  73.0 0.2 dynamic_update_slice.58
  73.2 0.2 dynamic_update_slice.59
  74.4 3.6 %all-to-all-done.2 = f32[32,2,128]{2,1,0:T(2,128)S(1)} async-done(((f32[32,2,128]{2,1,0:T(2,128)}), f32[32,2,128]{2,1,0:T(2,128)S(1)}, u32[]{:S(2)}, u32[]{:S(2)}) %all-to-all-start.2) | async-done | bytes 32800 | tf_op jit(solution)/shard_map/all_to_all | solution.py:218
  78.0 0.2 fusion.10
  79.0 0.3 all_to_all.22
  79.3 16.6 %all_to_all.28 = f32[32,1,3332]{2,1,0:T(1,128)S(1)} all-to-all(f32[32,1,3332]{2,1,0:T(1,128)S(1)} %all_to_all.22), channel_id=1, replica_groups=mesh['tile'=8,'deg'=4] {'tile','deg'}, dimensions={0} | all-to-all | bytes 852992 | tf_op jit(solution)/shard_map/all_to_all | solution.py:266
  96.0 1.0 reduce.31
  97.5 0.2 reshape.1201
  97.7 0.2 reshape.1202
  98.5 0.5 maximum_maximum_fusion.1
  98.9 2.1 %fusion.9 = f32[3,8,18,130]{3,2,1,0:T(8,128)S(1)} fusion(f32[3,8,18,130]{3,2,1,0:T(8,128)S(1)} %maximum_maximum_fusion.1, s32[]{:T(128)} %bitcast.12, s32[]{:T(128)} %bitcast.13, f32[18,64]{0,1:T(8,128)S(1)} %bitcast.136, f32[64,130]{1,0:T(8,128)S(1)} %reshape_reshape.7, f32[130]{0:T(256)S(1)} %broadcast_select_fusion, f32[18]{0:T(128)S(1)} %gather_fusion, ...), kind=kOutput, calls=%fused_computation.15 | convolution fusion | flops 1811160 | bytes 149001 | tf_op jit(solution)/shard_map/dot_general | solution.py:236
  101.9 0.5 copy.132
  102.6 0.2 fusion.71
  102.8 0.2 slice_reduce_fusion.1
  103.0 0.5 slice_add_fusion.1
  103.6 0.6 maximum_bitcast_fusion.1
  104.2 0.4 copy.135
  104.6 0.8 add_multiply_fusion
  (150 shorter events, 10.0 us)
Async XLA Ops:
  0.0 29.4 %copy-start = (bf16[1,512,512]{2,1,0:T(8,128)(2,1)S(1)}, bf16[1,512,512]{2,1,0:T(8,128)(2,1)}, u32[]{:S(2)}) copy-start(bf16[1,512,512]{2,1,0:T(8,128)(2,1)} %param.13) | copy-start | bytes 1572868
  4.6 24.7 %all-to-all-start = ((f32[32,2,128]{2,1,0:T(2,128)}), f32[32,2,128]{2,1,0:T(2,128)S(1)}, u32[]{:S(2)}, u32[]{:S(2)}) async-start(f32[32,2,128]{2,1,0:T(2,128)} %copy.100), calls=%async_computation | async-start | bytes 65536 | tf_op jit(solution)/shard_map/all_to_all | solution.py:218
  13.7 10.4 %copy-start.1 = (f32[8]{0:T(128)S(1)}, f32[8]{0:T(128)}, u32[]{:S(2)}) copy-start(f32[8]{0:T(128)} %constant.413.clone) | copy-start | bytes 100
  16.9 9.6 %copy-start.2 = (f32[8]{0:T(128)S(1)}, f32[8]{0:T(128)}, u32[]{:S(2)}) copy-start(f32[8]{0:T(128)} %constant.412.clone) | copy-start | bytes 100
  20.4 7.5 %copy-start.7 = (s32[32]{0:T(128)S(1)}, s32[32]{0:T(128)}, u32[]{:S(2)}) copy-start(s32[32]{0:T(128)} %param.14) | copy-start | bytes 388
  20.4 8.1 %copy-start.8 = (s32[4]{0:T(128)S(1)}, s32[4]{0:T(128)}, u32[]{:S(2)}) copy-start(s32[4]{0:T(128)} %constant.402.clone.1) | copy-start | bytes 52
  31.4 20.5 %all-to-all-start.1 = ((f32[32,1,3332]{2,1,0:T(1,128)}), f32[32,1,3332]{2,1,0:T(1,128)S(1)}, u32[]{:S(2)}, u32[]{:S(2)}) async-start(f32[32,1,3332]{2,1,0:T(1,128)} %all_to_all.19), calls=%async_computation.1 | async-start | bytes 884736 | tf_op jit(solution)/shard_map/all_to_all | solution.py:266
  37.5 16.8 %copy-start.3 = (f32[3,128,128]{2,1,0:T(8,128)S(1)}, f32[3,128,128]{2,1,0:T(8,128)}, u32[]{:S(2)}) copy-start(f32[3,128,128]{2,1,0:T(8,128)} %shard_map.74) | copy-start | bytes 589828
  60.1 0.9 copy-start.5
  61.1 0.7 copy-start.6
  68.1 9.9 %all-to-all-start.2 = ((f32[32,2,128]{2,1,0:T(2,128)}), f32[32,2,128]{2,1,0:T(2,128)S(1)}, u32[]{:S(2)}, u32[]{:S(2)}) async-start(f32[32,2,128]{2,1,0:T(2,128)} %copy.118), calls=%async_computation.2 | async-start | bytes 65536 | tf_op jit(solution)/shard_map/all_to_all | solution.py:218
  79.3 19.1 %copy-start.4 = (f32[3,128,128]{2,1,0:T(8,128)S(1)}, f32[3,128,128]{2,1,0:T(8,128)}, u32[]{:S(2)}) copy-start(f32[3,128,128]{2,1,0:T(8,128)} %shard_map.75) | copy-start | bytes 589828

commit v4 on v3

--- a/solution.py
+++ b/solution.py
@@ -306,12 +306,20 @@
         bottom = jnp.concatenate([corner_dl, from_down, corner_dr], axis=3)
         return jnp.concatenate([top, middle, bottom], axis=2)
 
-    def tendency(parts):
+    def assemble_ext(padded):
+        last = padded.ndim - 1
+        padded = padded * column_mask
+        along_a = assemble_dim(
+            padded[..., 1:-1, :], last - 1, padded[..., 0:1, :], padded[..., -1:, :]
+        )
+        return assemble_dim(along_a[..., 1:-1], last, along_a[..., 0:1], along_a[..., -1:])
+
+    def tendency(parts, surface):
         stacked = pl.pallas_call(
             volume_kernel, out_shape=jax.ShapeDtypeStruct((3, rows, nb_dev), jnp.float32)
         )(parts.reshape(3, rows, nb_dev), flat_flow, grads, mats, flat_mass)
         stacked = stacked.reshape(parts.shape)
-        sent = owner_map(parts[0, radial_nodes - 1])
+        sent = owner_map(surface)
         if carried_halo:
             returned, padded = joint_exchange(sent, stacked)
         else:
@@ -320,18 +328,18 @@
             ).reshape(tiles * groups, 2, nb_dev + 2)
             padded = halo(stacked)
         flux_term = flux_of(returned)
+        outer = padded[0, radial_nodes - 1] + flux_term
+        outer_rate = assemble_ext(outer) / assembled[radial_nodes - 1]
         padded = padded.at[0, radial_nodes - 1].add(flux_term)
         plane_r = jnp.zeros_like(lax.slice_in_dim(padded, 0, 1, axis=1))
         padded = assemble_dim(padded, 1, plane_r, plane_r)
-        padded = padded * column_mask
-        along_a = assemble_dim(padded[:, :, 1:-1, :], 2, padded[:, :, 0:1, :], padded[:, :, -1:, :])
-        along_b = assemble_dim(
-            along_a[:, :, :, 1:-1], 3, along_a[:, :, :, 0:1], along_a[:, :, :, -1:]
-        )
-        return along_b / assembled[None]
-
-    section = field + time_step * tendency(field)
-    return 0.5 * (field + section + time_step * tendency(section))
+        return assemble_ext(padded) / assembled[None], outer_rate
+
+    first_rate, first_outer = tendency(field, field[0, radial_nodes - 1])
+    section = field + time_step * first_rate
+    section_outer = field[0, radial_nodes - 1] + time_step * first_outer
+    second_rate, _ = tendency(section, section_outer)
+    return 0.5 * (field + section + time_step * second_rate)
 
 
 def solution(mesh):

time: 106 us -> 107 us (level)
  no operation moved by 1% of the time
where the time goes in v4:
time: 107 us; the launch traced here: 106 us
  local copies, waits for them, and re-layouts  28.1 us (26%)
  waiting for transfers between devices  17 us (16%)
  blocking collectives  16.6 us (16%)
  starting transfers between devices  15.9 us (15%)
  other arithmetic  12.1 us (11%)
  Pallas kernels  9.46 us (9%)
  matrix products  6.01 us (6%)
  between operations  1.19 us (1%)
    all_to_all x1, blocking collectives, joint_exchange(): lax.all_to_all(message, both, 0, 0, tiled=True).reshape(tiles, groups, -1)  16.6 us
    all_to_all x1, waiting for transfers between devices, joint_exchange(): lax.all_to_all(message, both, 0, 0, tiled=True).reshape(tiles, groups, -1)  13.4 us
    all_to_all x2, starting transfers between devices, owner_map(): gathered = lax.all_to_all(partial, both, 0, 0, tiled=True)  9.86 us
    pallas_call x2, Pallas kernels, tendency(): pl.pallas_call(volume_kernel, out_shape=jax.ShapeDtypeStruct((3, rows, nb...  6.91 us
    all_to_all x1, starting transfers between devices, joint_exchange(): lax.all_to_all(message, both, 0, 0, tiled=True).reshape(tiles, groups, -1)  6.01 us
    dot_general x2, matrix products, flux_of(): flux = -jnp.dot(synth, returned.reshape(-1, nb_dev + 2), precision=highest)  4.21 us
    all_to_all x2, waiting for transfers between devices, owner_map(): gathered = lax.all_to_all(partial, both, 0, 0, tiled=True)  3.65 us
    dynamic_update_slice x16, local copies, waits for them, and re-layouts, joint_exchange(): lax.dynamic_update_slice(slots, flat, ((tile_index + dt) % tiles, (group_...  3.02 us
  transfers between devices with their start and end apart: 3, of which 2 were waited for; matrix products, arithmetic and copies ran while one was open for 15% of the time, Pallas kernels for 6%

profile of v4, /device:TPU:0, one launch (start us, length us, event | category | flops | bytes accessed | tf_op | source)
XLA Modules:
  0.0 106.4 jit_solution(762025766559894963)
XLA Ops:
  0.0 0.7 tile.9
  0.8 0.7 convert_element_type.77
  1.5 0.7 tile.8
  2.2 0.8 fusion.36
  3.0 1.0 fusion.18
  4.0 0.6 copy.163
  4.6 7.3 %all-to-all-start = ((f32[32,2,128]{2,1,0:T(2,128)}), f32[32,2,128]{2,1,0:T(2,128)S(1)}, u32[]{:S(2)}, u32[]{:S(2)}) async-start(f32[32,2,128]{2,1,0:T(2,128)} %copy.163), calls=%async_computation | async-start | bytes 65536 | tf_op jit(solution)/shard_map/all_to_all | solution.py:218
  12.1 0.7 mul.412
  12.9 0.7 tile.11
  13.7 2.6 %shard_map.73.grad_ref = f32[9,128,128]{2,1,0:T(8,128)} custom-call(f32[3,128,128]{2,1,0:T(8,128)} %bitcast.157, f32[6,128,128]{2,1,0:T(8,128)} %constant.415.clone.mats_ref), custom_call_target="tpu_custom_call" | custom-call | tf_op jit(solution)/shard_map/pallas_call | solution.py:208
  16.2 0.7 broadcast_multiply_fusion.3.mass_ref
  17.0 3.5 %shard_map.74 = f32[3,128,128]{2,1,0:T(8,128)} custom-call(f32[3,128,128]{2,1,0:T(8,128)} %bitcast.156, f32[3,128,128]{2,1,0:T(8,128)} %bitcast.158, f32[9,128,128]{2,1,0:T(8,128)} %shard_map.73.grad_ref, f32[6,128,128]{2,1,0:T(8,128)} %constant.415.clone.mats_ref, f32[128,128]{1,0:T(8,128)} %broadcast_multiply_fusion.3.mass_ref), custom_call_target="tpu_custom_call" | custom-call | tf_op jit(solution)/shard_map/pallas_call | solution.py:318
  20.4 1.0 fusion.84
  21.4 1.3 %slice_reduce_fusion.6 = (f32[3,8,16]{2,1,0:T(8,128)S(1)}, f32[3,8,16]{2,1,0:T(8,128)S(1)}) fusion(f32[3,8,16,128]{3,2,1,0:T(8,128)} %bitcast.149), kind=kLoop, calls=%fused_computation.36 | loop fusion | bytes 6144 | tf_op jit(solution)/shard_map/slice | solution.py:246
  22.7 1.3 %slice_reduce_fusion.12 = (f32[3,8]{1,0:T(4,128)S(1)}, f32[3,8]{1,0:T(4,128)S(1)}, f32[3,8]{1,0:T(4,128)S(1)}, f32[3,8]{1,0:T(4,128)S(1)}) fusion(f32[3,8,16,128]{3,2,1,0:T(8,128)} %bitcast.150), kind=kLoop, calls=%fused_computation.81 | loop fusion | bytes 768 | tf_op jit(solution)/shard_map/slice | solution.py:256
  24.7 0.2 dynamic_update_slice.48
  25.9 0.2 dynamic_update_slice.54
  26.5 0.7 gather_fusion.1
  27.2 0.7 fusion.89
  27.9 0.6 fusion.78
  28.5 0.8 and_reduce_fusion
  29.4 0.2 fusion.8
  30.4 1.1 %all_to_all.19 = f32[32,1,3332]{2,1,0:T(1,128)} reshape(f32[32,3332]{1,0:T(8,128)S(1)} %pad_maximum_fusion) | data formatting | bytes 852992 | tf_op jit(solution)/shard_map/all_to_all | solution.py:266
  31.4 6.0 %all-to-all-start.1 = ((f32[32,1,3332]{2,1,0:T(1,128)}), f32[32,1,3332]{2,1,0:T(1,128)S(1)}, u32[]{:S(2)}, u32[]{:S(2)}) async-start(f32[32,1,3332]{2,1,0:T(1,128)} %all_to_all.19), calls=%async_computation.1 | async-start | bytes 884736 | tf_op jit(solution)/shard_map/all_to_all | solution.py:266
  37.6 0.7 gather_fusion
  38.5 13.4 %all-to-all-done.1 = f32[32,1,3332]{2,1,0:T(1,128)S(1)} async-done(((f32[32,1,3332]{2,1,0:T(1,128)}), f32[32,1,3332]{2,1,0:T(1,128)S(1)}, u32[]{:S(2)}, u32[]{:S(2)}) %all-to-all-start.1) | async-done | bytes 426528 | tf_op jit(solution)/shard_map/all_to_all | solution.py:266
  51.9 1.0 reduce.15
  53.4 0.2 reshape.1228
  53.6 0.2 reshape.1229
  54.3 0.5 maximum_maximum_fusion
  54.9 2.1 %fusion.10 = (f32[3,8,18,130]{3,2,1,0:T(8,128)S(1)}, f32[18,130]{1,0:T(8,128)S(1)}) fusion(f32[3,8,18,130]{3,2,1,0:T(8,128)S(1)} %copy.243, s32[]{:T(128)} %bitcast.12, s32[]{:T(128)} %bitcast.13, pred[]{:T(512)} %and_reduce_fusion, f32[18,64]{0,1:T(8,128)S(1)} %bitcast.164, f32[64,130]{1,0:T(8,128)S(1)} %reshape_reshape.6, ...), kind=kOutput, calls=%fused_computation.52 | convolution fusion | flops 1811160 | bytes 173577 | tf_op jit(solution)/shard_map/dot_general | solution.py:236
  58.4 0.5 copy.177
  59.0 0.2 fusion.80
  59.2 0.2 slice_reduce_fusion.5
  59.5 0.5 slice_add_fusion.3
  60.0 0.6 maximum_bitcast_fusion
  60.7 0.4 copy.180
  61.1 0.5 copy-done.5
  61.6 0.7 multiply_add_fusion
  62.3 3.4 %shard_map.75 = f32[3,128,128]{2,1,0:T(8,128)} custom-call(f32[3,128,128]{2,1,0:T(8,128)} %bitcast.160, f32[3,128,128]{2,1,0:T(8,128)} %bitcast.159, f32[9,128,128]{2,1,0:T(8,128)} %shard_map.73.grad_ref, f32[6,128,128]{2,1,0:T(8,128)} %constant.415.clone.mats_ref, f32[128,128]{1,0:T(8,128)} %broadcast_multiply_fusion.3.mass_ref), custom_call_target="tpu_custom_call" | custom-call | tf_op jit(solution)/shard_map/pallas_call | solution.py:318
  65.7 1.0 fusion.83
  66.7 1.3 %slice_reduce_fusion.8 = (f32[3,8]{1,0:T(4,128)S(1)}, f32[3,8]{1,0:T(4,128)S(1)}, f32[3,8]{1,0:T(4,128)S(1)}, f32[3,8]{1,0:T(4,128)S(1)}) fusion(f32[3,8,16,128]{3,2,1,0:T(8,128)} %bitcast.153), kind=kLoop, calls=%fused_computation.77 | loop fusion | bytes 768 | tf_op jit(solution)/shard_map/slice | solution.py:256
  68.2 0.3 fusion.17
  68.5 0.6 copy.183
  69.1 2.6 %all-to-all-start.2 = ((f32[32,2,128]{2,1,0:T(2,128)}), f32[32,2,128]{2,1,0:T(2,128)S(1)}, u32[]{:S(2)}, u32[]{:S(2)}) async-start(f32[32,2,128]{2,1,0:T(2,128)} %copy.183), calls=%async_computation.2 | async-start | bytes 65536 | tf_op jit(solution)/shard_map/all_to_all | solution.py:218
  71.7 1.3 %slice_reduce_fusion.2 = (f32[3,8,16]{2,1,0:T(8,128)S(1)}, f32[3,8,16]{2,1,0:T(8,128)S(1)}) fusion(f32[3,8,16,128]{3,2,1,0:T(8,128)} %bitcast.154), kind=kLoop, calls=%fused_computation.30 | loop fusion | bytes 6144 | tf_op jit(solution)/shard_map/slice | solution.py:246
  74.2 0.2 dynamic_update_slice.59
  75.0 0.2 dynamic_update_slice.63
  75.4 3.6 %all-to-all-done.2 = f32[32,2,128]{2,1,0:T(2,128)S(1)} async-done(((f32[32,2,128]{2,1,0:T(2,128)}), f32[32,2,128]{2,1,0:T(2,128)S(1)}, u32[]{:S(2)}, u32[]{:S(2)}) %all-to-all-start.2) | async-done | bytes 32800 | tf_op jit(solution)/shard_map/all_to_all | solution.py:218
  79.0 0.2 fusion.6
  80.0 0.3 all_to_all.22
  80.3 16.6 %all_to_all.28 = f32[32,1,3332]{2,1,0:T(1,128)S(1)} all-to-all(f32[32,1,3332]{2,1,0:T(1,128)S(1)} %all_to_all.22), channel_id=1, replica_groups=mesh['tile'=8,'deg'=4] {'tile','deg'}, dimensions={0} | all-to-all | bytes 852992 | tf_op jit(solution)/shard_map/all_to_all | solution.py:266
  97.0 1.0 reduce.33
  98.5 0.2 reshape.1234
  98.7 0.2 reshape.1235
  99.5 0.5 maximum_maximum_fusion.1
  99.9 2.1 %fusion.5 = f32[3,8,18,130]{3,2,1,0:T(8,128)S(1)} fusion(f32[3,8,18,130]{3,2,1,0:T(8,128)S(1)} %maximum_maximum_fusion.1, s32[]{:T(128)} %bitcast.12, s32[]{:T(128)} %bitcast.13, f32[18,64]{0,1:T(8,128)S(1)} %bitcast.165, f32[64,130]{1,0:T(8,128)S(1)} %reshape_reshape.7, f32[130]{0:T(256)S(1)} %broadcast_select_fusion, f32[18]{0:T(128)S(1)} %gather_fusion, ...), kind=kOutput, calls=%fused_computation.11 | convolution fusion | flops 1811160 | bytes 149001 | tf_op jit(solution)/shard_map/dot_general | solution.py:236
  102.9 0.5 copy.197
  103.5 0.2 fusion.79
  103.8 0.2 slice_reduce_fusion.1
  104.0 0.5 slice_add_fusion.1
  104.6 0.6 maximum_bitcast_fusion.1
  105.2 0.4 copy.200
  105.6 0.8 add_multiply_fusion
  (164 shorter events, 10.5 us)
Async XLA Ops:
  0.0 29.4 %copy-start = (bf16[1,512,512]{2,1,0:T(8,128)(2,1)S(1)}, bf16[1,512,512]{2,1,0:T(8,128)(2,1)}, u32[]{:S(2)}) copy-start(bf16[1,512,512]{2,1,0:T(8,128)(2,1)} %param.13) | copy-start | bytes 1572868
  4.6 24.7 %all-to-all-start = ((f32[32,2,128]{2,1,0:T(2,128)}), f32[32,2,128]{2,1,0:T(2,128)S(1)}, u32[]{:S(2)}, u32[]{:S(2)}) async-start(f32[32,2,128]{2,1,0:T(2,128)} %copy.163), calls=%async_computation | async-start | bytes 65536 | tf_op jit(solution)/shard_map/all_to_all | solution.py:218
  13.7 10.4 %copy-start.1 = (f32[8]{0:T(128)S(1)}, f32[8]{0:T(128)}, u32[]{:S(2)}) copy-start(f32[8]{0:T(128)} %constant.414.clone) | copy-start | bytes 100
  16.9 9.6 %copy-start.2 = (f32[8]{0:T(128)S(1)}, f32[8]{0:T(128)}, u32[]{:S(2)}) copy-start(f32[8]{0:T(128)} %constant.413.clone) | copy-start | bytes 100
  20.4 7.5 %copy-start.6 = (s32[32]{0:T(128)S(1)}, s32[32]{0:T(128)}, u32[]{:S(2)}) copy-start(s32[32]{0:T(128)} %param.14) | copy-start | bytes 388
  20.4 8.1 %copy-start.7 = (s32[4]{0:T(128)S(1)}, s32[4]{0:T(128)}, u32[]{:S(2)}) copy-start(s32[4]{0:T(128)} %constant.403.clone.1) | copy-start | bytes 52
  31.4 20.5 %all-to-all-start.1 = ((f32[32,1,3332]{2,1,0:T(1,128)}), f32[32,1,3332]{2,1,0:T(1,128)S(1)}, u32[]{:S(2)}, u32[]{:S(2)}) async-start(f32[32,1,3332]{2,1,0:T(1,128)} %all_to_all.19), calls=%async_computation.1 | async-start | bytes 884736 | tf_op jit(solution)/shard_map/all_to_all | solution.py:266
  37.5 16.9 %copy-start.3 = (f32[3,128,128]{2,1,0:T(8,128)S(1)}, f32[3,128,128]{2,1,0:T(8,128)}, u32[]{:S(2)}) copy-start(f32[3,128,128]{2,1,0:T(8,128)} %shard_map.74) | copy-start | bytes 589828
  60.7 0.9 copy-start.5
  69.1 9.9 %all-to-all-start.2 = ((f32[32,2,128]{2,1,0:T(2,128)}), f32[32,2,128]{2,1,0:T(2,128)S(1)}, u32[]{:S(2)}, u32[]{:S(2)}) async-start(f32[32,2,128]{2,1,0:T(2,128)} %copy.183), calls=%async_computation.2 | async-start | bytes 65536 | tf_op jit(solution)/shard_map/all_to_all | solution.py:218
  80.3 19.1 %copy-start.4 = (f32[3,128,128]{2,1,0:T(8,128)S(1)}, f32[3,128,128]{2,1,0:T(8,128)}, u32[]{:S(2)}) copy-start(f32[3,128,128]{2,1,0:T(8,128)} %shard_map.75) | copy-start | bytes 589828

commit v5 on v4

--- a/solution.py
+++ b/solution.py
@@ -237,7 +237,7 @@
         return diffusivity * surface_ext * flux
 
     mapped_len = 2 * (nb_dev + 2)
-    slot_len = 3 * radial_nodes * max(nb_dev, na_dev)
+    slot_len = 3 * radial_nodes * na_dev
     carried_halo = tiles >= 3 and groups >= 3 and tiles * groups <= 64
 
     def joint_exchange(sent, stacked):
@@ -245,9 +245,11 @@
         a_hi = lax.slice_in_dim(stacked, na_dev - 1, na_dev, axis=2)
         b_lo = lax.slice_in_dim(stacked, 0, 1, axis=3)
         b_hi = lax.slice_in_dim(stacked, nb_dev - 1, nb_dev, axis=3)
+        up = [(i, (i + 1) % tiles) for i in range(tiles)]
+        down = [(j, i) for i, j in up]
+        from_up = lax.ppermute(a_hi, "tile", up)
+        from_down = lax.ppermute(a_lo, "tile", down)
         out_pieces = [
-            ((1, 0), a_hi),
-            ((-1, 0), a_lo),
             ((0, 1), b_hi),
             ((0, -1), b_lo),
             ((1, 1), a_hi[:, :, :, -1:]),
@@ -274,8 +276,6 @@
             )
             return row.reshape(like.shape)
 
-        from_up = take(1, 0, a_hi)
-        from_down = take(-1, 0, a_lo)
         from_left = take(0, 1, b_hi)
         from_right = take(0, -1, b_lo)
         corner_ul = take(1, 1, a_hi[:, :, :, -1:])

time: 107 us -> 91.3 us (0.85)
  blocking collectives: 16.6 us -> 0 us
  starting transfers between devices: 15.9 us -> 26.9 us
  waiting for transfers between devices: 17 us -> 11 us
  local copies, waits for them, and re-layouts: 28.1 us -> 24.4 us
    all_to_all x1 -> x0, blocking collectives: 16.6 us -> none  [joint_exchange(): lax.all_to_all(message, both, 0, 0, tiled=True).reshape(tiles, groups, -1)]
    ppermute x0 -> x4, starting transfers between devices: none -> 7.19 us  [the longest x2 6.58 us: joint_exchange(): from_down = lax.ppermute(a_lo, 'tile', down)]
    all_to_all x1 -> x2, starting transfers between devices: 6.01 us -> 9.69 us  [joint_exchange(): lax.all_to_all(message, both, 0, 0, tiled=True).reshape(tiles, groups, -1)]
    all_to_all x2, waiting for transfers between devices: 3.65 us -> 0.01 us  [owner_map(): gathered = lax.all_to_all(partial, both, 0, 0, tiled=True)]
    dynamic_update_slice x16 -> x12, local copies, waits for them, and re-layouts: 3.02 us -> 0.52 us  [joint_exchange(): lax.dynamic_update_slice(slots, flat, ((tile_index + dt) % tiles, (group_...]
    all_to_all x1 -> x2, waiting for transfers between devices: 13.4 us -> 11 us  [joint_exchange(): lax.all_to_all(message, both, 0, 0, tiled=True).reshape(tiles, groups, -1)]
    all_to_all x2, other arithmetic: 2.09 us -> 0.46 us  [joint_exchange(): lax.all_to_all(message, both, 0, 0, tiled=True).reshape(tiles, groups, -1)]
    reshape x6, other arithmetic: 1.58 us -> 3 us  [assemble_dim(): return joined.reshape(shape)]
  transfers between devices with their start and end apart: 3 -> 8, of which waited for: 2 -> 2; matrix products, arithmetic and copies ran while one was open for 15% -> 24% of each run, Pallas kernels for 6% -> 10%
where the time goes in v5:
time: 91.3 us; the launch traced here: 90.6 us
  starting transfers between devices  26.9 us (29%)
  local copies, waits for them, and re-layouts  24.4 us (27%)
  other arithmetic  11.7 us (13%)
  waiting for transfers between devices  11 us (12%)
  Pallas kernels  9.46 us (10%)
  matrix products  6.18 us (7%)
    all_to_all x2, waiting for transfers between devices, joint_exchange(): lax.all_to_all(message, both, 0, 0, tiled=True).reshape(tiles, groups, -1)  11 us
    all_to_all x2, starting transfers between devices, owner_map(): gathered = lax.all_to_all(partial, both, 0, 0, tiled=True)  10 us
    all_to_all x2, starting transfers between devices, joint_exchange(): lax.all_to_all(message, both, 0, 0, tiled=True).reshape(tiles, groups, -1)  9.69 us
    pallas_call x2, Pallas kernels, tendency(): pl.pallas_call(volume_kernel, out_shape=jax.ShapeDtypeStruct((3, rows, nb...  6.91 us
    ppermute x2, starting transfers between devices, joint_exchange(): from_down = lax.ppermute(a_lo, 'tile', down)  6.58 us
    dot_general x2, matrix products, flux_of(): flux = -jnp.dot(synth, returned.reshape(-1, nb_dev + 2), precision=highest)  4.37 us
    reshape x6, other arithmetic, assemble_dim(): return joined.reshape(shape)  3 us
    slice x2, local copies, waits for them, and re-layouts, joint_exchange(): a_lo[:, :, :, :1]  2.67 us
  transfers between devices with their start and end apart: 8, of which 2 were waited for; matrix products, arithmetic and copies ran while one was open for 24% of the time, Pallas kernels for 10%

profile of v5, /device:TPU:0, one launch (start us, length us, event | category | flops | bytes accessed | tf_op | source)
XLA Modules:
  0.0 90.6 jit_solution(18044098382342390940)
XLA Ops:
  0.0 0.7 convert_element_type.72
  0.7 0.7 tile.8
  1.5 0.7 tile.9
  2.2 0.8 fusion.36
  3.0 1.0 %fusion.18 = f32[32,2,128]{2,0,1:T(8,128)S(1)} fusion(f32[32,1,16]{0,2,1:T(8,128)S(1)} %get-tuple-element.108, f32[32,1,16]{0,2,1:T(8,128)S(1)} %get-tuple-element.107, f32[16]{0:T(128)S(1)} %get-tuple-element.110, f32[3,8,16,128]{3,2,1,0:T(8,128)} %param.11), kind=kOutput, calls=%fused_computation.76 | convolution fusion | flops 1574912 | bytes 45120 | tf_op jit(solution)/shard_map/dot_general | solution.py:217
  4.0 0.6 copy.163
  4.6 7.3 %all-to-all-start = ((f32[32,2,128]{2,1,0:T(2,128)}), f32[32,2,128]{2,1,0:T(2,128)S(1)}, u32[]{:S(2)}, u32[]{:S(2)}) async-start(f32[32,2,128]{2,1,0:T(2,128)} %copy.163), calls=%async_computation | async-start | bytes 65536 | tf_op jit(solution)/shard_map/all_to_all | solution.py:218
  12.1 0.7 mul.412
  12.9 0.7 tile.11
  13.6 0.7 broadcast_multiply_fusion.3.mass_ref
  14.3 2.5 %shard_map.73.grad_ref = f32[9,128,128]{2,1,0:T(8,128)} custom-call(f32[3,128,128]{2,1,0:T(8,128)} %bitcast.149, f32[6,128,128]{2,1,0:T(8,128)} %constant.381.clone.mats_ref), custom_call_target="tpu_custom_call" | custom-call | tf_op jit(solution)/shard_map/pallas_call | solution.py:208
  16.9 3.5 %shard_map.74 = f32[3,128,128]{2,1,0:T(8,128)} custom-call(f32[3,128,128]{2,1,0:T(8,128)} %bitcast.148, f32[3,128,128]{2,1,0:T(8,128)} %bitcast.150, f32[9,128,128]{2,1,0:T(8,128)} %shard_map.73.grad_ref, f32[6,128,128]{2,1,0:T(8,128)} %constant.381.clone.mats_ref, f32[128,128]{1,0:T(8,128)} %broadcast_multiply_fusion.3.mass_ref), custom_call_target="tpu_custom_call" | custom-call | tf_op jit(solution)/shard_map/pallas_call | solution.py:318
  20.3 1.0 %fusion.84 = (f32[3,8,1,128]{3,2,1,0:T(1,128)S(1)}, f32[3,8,1,128]{3,2,1,0:T(1,128)S(1)}) fusion(f32[3,8,16,128]{3,2,1,0:T(8,128)} %bitcast.140), kind=kLoop, calls=%fused_computation.238 | loop fusion | bytes 49152 | tf_op jit(solution)/shard_map/slice | solution.py:245
  21.3 0.3 collective-permute-start
  21.6 3.3 %collective-permute-start.1 = (f32[3,8,1,128]{3,2,1,0:T(1,128)S(1)}, f32[3,8,1,128]{3,2,1,0:T(1,128)S(1)}, u32[]{:S(2)}, u32[]{:S(2)}) collective-permute-start(f32[3,8,1,128]{3,2,1,0:T(1,128)S(1)} %get-tuple-element.82), channel_id=1, source_target_pairs={{4,0},{8,4},{12,8},{16,12},{20,16},{24,20},{28,24},{0,28},{5,1},{9... | collective-permute-start | bytes 36872 | tf_op jit(solution)/shard_map/ppermute | solution.py:251
  25.0 1.3 %slice_reduce_fusion.12 = (f32[3,8]{1,0:T(4,128)S(1)}, f32[3,8]{1,0:T(4,128)S(1)}, f32[3,8]{1,0:T(4,128)S(1)}, f32[3,8]{1,0:T(4,128)S(1)}) fusion(f32[3,8,16,128]{3,2,1,0:T(8,128)} %bitcast.141), kind=kLoop, calls=%fused_computation.81 | loop fusion | bytes 768 | tf_op jit(solution)/shard_map/slice | solution.py:258
  26.4 1.3 %slice_reduce_fusion.6 = (f32[3,8,16]{2,1,0:T(8,128)S(1)}, f32[3,8,16]{2,1,0:T(8,128)S(1)}) fusion(f32[3,8,16,128]{3,2,1,0:T(8,128)} %bitcast.142), kind=kLoop, calls=%fused_computation.34 | loop fusion | bytes 6144 | tf_op jit(solution)/shard_map/slice | solution.py:246
  27.7 0.7 gather_fusion.1
  29.3 0.6 fusion.78
  30.1 0.8 and_reduce_fusion
  30.9 0.2 fusion.8
  31.8 0.7 all_to_all.19
  32.5 4.0 %all-to-all-start.1 = ((f32[32,1,644]{2,1,0:T(1,128)}), f32[32,1,644]{2,1,0:T(1,128)S(1)}, u32[]{:S(2)}, u32[]{:S(2)}) async-start(f32[32,1,644]{2,1,0:T(1,128)} %all_to_all.19), calls=%async_computation.1 | async-start | bytes 196608 | tf_op jit(solution)/shard_map/all_to_all | solution.py:268
  36.5 0.6 fusion.89
  37.3 0.7 gather_fusion
  38.0 6.5 %all-to-all-done.1 = f32[32,1,644]{2,1,0:T(1,128)S(1)} async-done(((f32[32,1,644]{2,1,0:T(1,128)}), f32[32,1,644]{2,1,0:T(1,128)S(1)}, u32[]{:S(2)}, u32[]{:S(2)}) %all-to-all-start.1) | async-done | bytes 82464 | tf_op jit(solution)/shard_map/all_to_all | solution.py:268
  44.5 0.2 reduce.15
  45.5 0.2 reshape.1196
  45.7 0.2 reshape.1197
  46.0 0.5 maximum_maximum_fusion
  46.5 2.2 %fusion.10 = (f32[3,8,18,130]{3,2,1,0:T(8,128)S(1)}, f32[18,130]{1,0:T(8,128)S(1)}) fusion(f32[3,8,18,130]{3,2,1,0:T(8,128)S(1)} %copy.241, s32[]{:T(128)} %bitcast.8, s32[]{:T(128)} %bitcast.9, pred[]{:T(512)} %and_reduce_fusion, f32[18,64]{0,1:T(8,128)S(1)} %bitcast.156, f32[64,130]{1,0:T(8,128)S(1)} %reshape_reshape.6, f32[130]{0:T(256)S(1)} %broadcast_select_fusion, ...), kind=kOutput, calls=%fused_computation.52 | convolution fusion | flops 1811160 | bytes 173577 | tf_op jit(solution)/shard_map/dot_general | solution.py:236
  48.8 0.2 slice_reduce_fusion.17
  49.9 0.2 slice_reduce_fusion.5
  50.2 0.5 copy.177
  50.7 0.2 fusion.80
  51.0 1.3 %slice.467 = f32[3,8,16,16,6]{2,4,3,1,0:T(8,128)} slice(f32[3,8,16,16,8]{2,4,3,1,0:T(8,128)S(1)} %bitcast.135), slice={[0:3], [0:8], [0:16], [0:16], [1:7]} | slice | bytes 294912 | tf_op jit(solution)/shard_map/slice | solution.py:127
  52.4 0.3 fusion.17
  52.7 0.6 copy.183
  53.4 2.7 %all-to-all-start.2 = ((f32[32,2,128]{2,1,0:T(2,128)}), f32[32,2,128]{2,1,0:T(2,128)S(1)}, u32[]{:S(2)}, u32[]{:S(2)}) async-start(f32[32,2,128]{2,1,0:T(2,128)} %copy.183), calls=%async_computation.2 | async-start | bytes 65536 | tf_op jit(solution)/shard_map/all_to_all | solution.py:218
  56.1 0.5 slice_add_fusion.3
  56.6 2.0 %maximum_bitcast_fusion = f32[3,8,16,128]{2,3,1,0:T(8,128)S(1)} fusion(f32[3,8,16,16,1]{2,4,3,1,0:T(1,128)S(1)} %get-tuple-element.64, f32[3,8,16,16,6]{2,4,3,1,0:T(8,128)} %slice.467, f32[3,8,16,16,1]{2,4,3,1,0:T(1,128)S(1)} %get-tuple-element.63), kind=kLoop, calls=%fused_computation.2 | loop fusion | flops 98304 | bytes 393216 | tf_op jit(solution)/shard_map/reshape | solution.py:129
  58.7 0.4 copy.180
  59.1 0.7 multiply_add_fusion
  59.8 3.4 %shard_map.75 = f32[3,128,128]{2,1,0:T(8,128)} custom-call(f32[3,128,128]{2,1,0:T(8,128)} %bitcast.152, f32[3,128,128]{2,1,0:T(8,128)} %bitcast.151, f32[9,128,128]{2,1,0:T(8,128)} %shard_map.73.grad_ref, f32[6,128,128]{2,1,0:T(8,128)} %constant.381.clone.mats_ref, f32[128,128]{1,0:T(8,128)} %broadcast_multiply_fusion.3.mass_ref), custom_call_target="tpu_custom_call" | custom-call | tf_op jit(solution)/shard_map/pallas_call | solution.py:318
  63.3 1.4 %slice_reduce_fusion.8 = (f32[3,8]{1,0:T(4,128)S(1)}, f32[3,8]{1,0:T(4,128)S(1)}, f32[3,8]{1,0:T(4,128)S(1)}, f32[3,8]{1,0:T(4,128)S(1)}) fusion(f32[3,8,16,128]{3,2,1,0:T(8,128)} %bitcast.144), kind=kLoop, calls=%fused_computation.77 | loop fusion | bytes 768 | tf_op jit(solution)/shard_map/slice | solution.py:258
  65.0 1.3 %slice_reduce_fusion.2 = (f32[3,8,16]{2,1,0:T(8,128)S(1)}, f32[3,8,16]{2,1,0:T(8,128)S(1)}) fusion(f32[3,8,16,128]{3,2,1,0:T(8,128)} %bitcast.145), kind=kLoop, calls=%fused_computation.28 | loop fusion | bytes 6144 | tf_op jit(solution)/shard_map/slice | solution.py:246
  66.8 0.2 fusion.6
  67.7 0.7 all_to_all.22
  68.4 5.7 %all-to-all-start.3 = ((f32[32,1,644]{2,1,0:T(1,128)}), f32[32,1,644]{2,1,0:T(1,128)S(1)}, u32[]{:S(2)}, u32[]{:S(2)}) async-start(f32[32,1,644]{2,1,0:T(1,128)} %all_to_all.22), calls=%async_computation.3 | async-start | bytes 196608 | tf_op jit(solution)/shard_map/all_to_all | solution.py:268
  74.1 0.3 collective-permute-start.2
  74.4 3.3 %collective-permute-start.3 = (f32[3,8,1,128]{3,2,1,0:T(1,128)S(1)}, f32[3,8,1,128]{3,2,1,0:T(1,128)S(1)}, u32[]{:S(2)}, u32[]{:S(2)}) collective-permute-start(f32[3,8,1,128]{3,2,1,0:T(1,128)S(1)} %get-tuple-element.80), channel_id=1, source_target_pairs={{4,0},{8,4},{12,8},{16,12},{20,16},{24,20},{28,24},{0,28},{5,1},{9... | collective-permute-start | bytes 36872 | tf_op jit(solution)/shard_map/ppermute | solution.py:251
  77.7 4.4 %all-to-all-done.3 = f32[32,1,644]{2,1,0:T(1,128)S(1)} async-done(((f32[32,1,644]{2,1,0:T(1,128)}), f32[32,1,644]{2,1,0:T(1,128)S(1)}, u32[]{:S(2)}, u32[]{:S(2)}) %all-to-all-start.3) | async-done | bytes 82464 | tf_op jit(solution)/shard_map/all_to_all | solution.py:268
  82.2 0.2 reduce.33
  83.2 0.2 reshape.1202
  83.4 0.2 reshape.1203
  83.6 0.5 maximum_maximum_fusion.1
  84.1 2.2 %fusion.5 = f32[3,8,18,130]{3,2,1,0:T(8,128)S(1)} fusion(f32[3,8,18,130]{3,2,1,0:T(8,128)S(1)} %maximum_maximum_fusion.1, s32[]{:T(128)} %bitcast.8, s32[]{:T(128)} %bitcast.9, f32[18,64]{0,1:T(8,128)S(1)} %bitcast.157, f32[64,130]{1,0:T(8,128)S(1)} %reshape_reshape.7, f32[130]{0:T(256)S(1)} %broadcast_select_fusion, f32[18]{0:T(128)S(1)} %gather_fusion, ...), kind=kOutput, calls=%fused_computation.11 | convolution fusion | flops 1811160 | bytes 149001 | tf_op jit(solution)/shard_map/dot_general | solution.py:236
  87.0 0.2 slice_reduce_fusion.1
  87.4 0.5 copy.197
  87.9 0.2 fusion.79
  88.3 0.5 slice_add_fusion.1
  88.8 0.6 maximum_bitcast_fusion.1
  89.4 0.4 copy.200
  89.9 0.8 add_multiply_fusion
  (163 shorter events, 7.4 us)
Async XLA Ops:
  0.0 30.9 %copy-start = (bf16[1,512,512]{2,1,0:T(8,128)(2,1)S(1)}, bf16[1,512,512]{2,1,0:T(8,128)(2,1)}, u32[]{:S(2)}) copy-start(bf16[1,512,512]{2,1,0:T(8,128)(2,1)} %param.13) | copy-start | bytes 1572868
  4.6 26.2 %all-to-all-start = ((f32[32,2,128]{2,1,0:T(2,128)}), f32[32,2,128]{2,1,0:T(2,128)S(1)}, u32[]{:S(2)}, u32[]{:S(2)}) async-start(f32[32,2,128]{2,1,0:T(2,128)} %copy.163), calls=%async_computation | async-start | bytes 65536 | tf_op jit(solution)/shard_map/all_to_all | solution.py:218
  12.0 13.0 %copy-start.1 = (f32[8]{0:T(128)S(1)}, f32[8]{0:T(128)}, u32[]{:S(2)}) copy-start(f32[8]{0:T(128)} %constant.380.clone) | copy-start | bytes 100
  14.3 13.3 %copy-start.2 = (f32[8]{0:T(128)S(1)}, f32[8]{0:T(128)}, u32[]{:S(2)}) copy-start(f32[8]{0:T(128)} %constant.379.clone) | copy-start | bytes 100
  16.9 12.4 %copy-start.6 = (s32[32]{0:T(128)S(1)}, s32[32]{0:T(128)}, u32[]{:S(2)}) copy-start(s32[32]{0:T(128)} %param.14) | copy-start | bytes 388
  16.9 13.2 %copy-start.7 = (s32[4]{0:T(128)S(1)}, s32[4]{0:T(128)}, u32[]{:S(2)}) copy-start(s32[4]{0:T(128)} %constant.369.clone.1) | copy-start | bytes 52
  21.3 24.6 %collective-permute-start = (f32[3,8,1,128]{3,2,1,0:T(1,128)S(1)}, f32[3,8,1,128]{3,2,1,0:T(1,128)S(1)}, u32[]{:S(2)}, u32[]{:S(2)}) collective-permute-start(f32[3,8,1,128]{3,2,1,0:T(1,128)S(1)} %get-tuple-element.81), channel_id=1, source_target_pairs={{0,4},{4,8},{8,12},{12,16},{16,20},{20,24},{24,28},{28,0},{1,5},{5... | collective-permute-start | bytes 36872 | tf_op jit(solution)/shard_map/ppermute | solution.py:250
  21.6 24.3 %collective-permute-start.1 = (f32[3,8,1,128]{3,2,1,0:T(1,128)S(1)}, f32[3,8,1,128]{3,2,1,0:T(1,128)S(1)}, u32[]{:S(2)}, u32[]{:S(2)}) collective-permute-start(f32[3,8,1,128]{3,2,1,0:T(1,128)S(1)} %get-tuple-element.82), channel_id=1, source_target_pairs={{4,0},{8,4},{12,8},{16,12},{20,16},{24,20},{28,24},{0,28},{5,1},{9... | collective-permute-start | bytes 36872 | tf_op jit(solution)/shard_map/ppermute | solution.py:251
  29.9 16.0 %copy-start.3 = (f32[3,128,128]{2,1,0:T(8,128)S(1)}, f32[3,128,128]{2,1,0:T(8,128)}, u32[]{:S(2)}) copy-start(f32[3,128,128]{2,1,0:T(8,128)} %shard_map.74) | copy-start | bytes 589828
  32.5 12.0 %all-to-all-start.1 = ((f32[32,1,644]{2,1,0:T(1,128)}), f32[32,1,644]{2,1,0:T(1,128)S(1)}, u32[]{:S(2)}, u32[]{:S(2)}) async-start(f32[32,1,644]{2,1,0:T(1,128)} %all_to_all.19), calls=%async_computation.1 | async-start | bytes 196608 | tf_op jit(solution)/shard_map/all_to_all | solution.py:268
  51.0 1.4 %copy-start.5 = (f32[3,8,16,128]{3,2,1,0:T(8,128)S(1)}, f32[3,8,16,128]{3,2,1,0:T(8,128)}, u32[]{:S(2)}) copy-start(f32[3,8,16,128]{3,2,1,0:T(8,128)} %param.11) | copy-start | bytes 589828
  53.4 13.4 %all-to-all-start.2 = ((f32[32,2,128]{2,1,0:T(2,128)}), f32[32,2,128]{2,1,0:T(2,128)S(1)}, u32[]{:S(2)}, u32[]{:S(2)}) async-start(f32[32,2,128]{2,1,0:T(2,128)} %copy.183), calls=%async_computation.2 | async-start | bytes 65536 | tf_op jit(solution)/shard_map/all_to_all | solution.py:218
  63.3 10.8 %copy-start.4 = (f32[3,128,128]{2,1,0:T(8,128)S(1)}, f32[3,128,128]{2,1,0:T(8,128)}, u32[]{:S(2)}) copy-start(f32[3,128,128]{2,1,0:T(8,128)} %shard_map.75) | copy-start | bytes 589828
  68.4 13.7 %all-to-all-start.3 = ((f32[32,1,644]{2,1,0:T(1,128)}), f32[32,1,644]{2,1,0:T(1,128)S(1)}, u32[]{:S(2)}, u32[]{:S(2)}) async-start(f32[32,1,644]{2,1,0:T(1,128)} %all_to_all.22), calls=%async_computation.3 | async-start | bytes 196608 | tf_op jit(solution)/shard_map/all_to_all | solution.py:268
  74.1 9.5 %collective-permute-start.2 = (f32[3,8,1,128]{3,2,1,0:T(1,128)S(1)}, f32[3,8,1,128]{3,2,1,0:T(1,128)S(1)}, u32[]{:S(2)}, u32[]{:S(2)}) collective-permute-start(f32[3,8,1,128]{3,2,1,0:T(1,128)S(1)} %get-tuple-element.79), channel_id=1, source_target_pairs={{0,4},{4,8},{8,12},{12,16},{16,20},{20,24},{24,28},{28,0},{1,5},{5... | collective-permute-start | bytes 36872 | tf_op jit(solution)/shard_map/ppermute | solution.py:250
  74.4 9.2 %collective-permute-start.3 = (f32[3,8,1,128]{3,2,1,0:T(1,128)S(1)}, f32[3,8,1,128]{3,2,1,0:T(1,128)S(1)}, u32[]{:S(2)}, u32[]{:S(2)}) collective-permute-start(f32[3,8,1,128]{3,2,1,0:T(1,128)S(1)} %get-tuple-element.80), channel_id=1, source_target_pairs={{4,0},{8,4},{12,8},{16,12},{20,16},{24,20},{28,24},{0,28},{5,1},{9... | collective-permute-start | bytes 36872 | tf_op jit(solution)/shard_map/ppermute | solution.py:251

commit v6 on v5

--- a/solution.py
+++ b/solution.py
@@ -41,10 +41,12 @@
         out_ref[3 * component + 2] = product(x, mats_ref[2])
 
 
-def volume_kernel(parts_ref, flow_ref, grad_ref, mats_ref, mass_ref, out_ref):
+def volume_kernel(parts_ref, flow_ref, grad_ref, mats_ref, mass_ref, out_ref, rows_ref, cols_ref):
     mass = mass_ref[...]
     p = [parts_ref[i] for i in range(3)]
     f = [flow_ref[i] for i in range(3)]
+    planes = out_ref.shape[1] // rows_ref.shape[2]
+    width = out_ref.shape[2]
     for c in range(3):
         x = p[c]
         s0 = product(mats_ref[0], x)
@@ -57,7 +59,14 @@
             + product(mats_ref[4], mass * s1)
             + product(mass * s2, mats_ref[5])
         )
-        out_ref[c] = mass * (stretch - carried) - diffusivity * spread
+        result = mass * (stretch - carried) - diffusivity * spread
+        out_ref[c] = result
+        turned = result.T
+        cols_ref[0, c : c + 1, :] = turned[0:1, :]
+        cols_ref[1, c : c + 1, :] = turned[width - 1 : width, :]
+    for c in range(3):
+        rows_ref[0, c] = out_ref[c, pl.ds(0, rows_ref.shape[2], stride=planes), :]
+        rows_ref[1, c] = out_ref[c, pl.ds(planes - 1, rows_ref.shape[2], stride=planes), :]
 
 
 def derivative_tables(radial_nodes, na_dev, nb_dev):
@@ -240,27 +249,25 @@
     slot_len = 3 * radial_nodes * na_dev
     carried_halo = tiles >= 3 and groups >= 3 and tiles * groups <= 64
 
-    def joint_exchange(sent, stacked):
-        a_lo = lax.slice_in_dim(stacked, 0, 1, axis=2)
-        a_hi = lax.slice_in_dim(stacked, na_dev - 1, na_dev, axis=2)
-        b_lo = lax.slice_in_dim(stacked, 0, 1, axis=3)
-        b_hi = lax.slice_in_dim(stacked, nb_dev - 1, nb_dev, axis=3)
+    def joint_exchange(sent, stacked, edge_rows, edge_cols):
+        a_lo = edge_rows[0].reshape(3, radial_nodes, 1, nb_dev)
+        a_hi = edge_rows[1].reshape(3, radial_nodes, 1, nb_dev)
         up = [(i, (i + 1) % tiles) for i in range(tiles)]
         down = [(j, i) for i, j in up]
         from_up = lax.ppermute(a_hi, "tile", up)
         from_down = lax.ppermute(a_lo, "tile", down)
+        b_lo = edge_cols[0].reshape(1, 1, -1)
+        b_hi = edge_cols[1].reshape(1, 1, -1)
         out_pieces = [
             ((0, 1), b_hi),
             ((0, -1), b_lo),
-            ((1, 1), a_hi[:, :, :, -1:]),
-            ((1, -1), a_hi[:, :, :, :1]),
-            ((-1, 1), a_lo[:, :, :, -1:]),
-            ((-1, -1), a_lo[:, :, :, :1]),
+            ((1, 1), b_hi),
+            ((1, -1), b_lo),
+            ((-1, 1), b_hi),
+            ((-1, -1), b_lo),
         ]
         slots = jnp.zeros((tiles, groups, slot_len), jnp.float32)
-        for (dt, dg), piece in out_pieces:
-            flat = piece.reshape(1, 1, -1)
-            flat = jnp.pad(flat, ((0, 0), (0, 0), (0, slot_len - flat.shape[2])))
+        for (dt, dg), flat in out_pieces:
             slots = lax.dynamic_update_slice(
                 slots, flat, ((tile_index + dt) % tiles, (group_index + dg) % groups, 0)
             )
@@ -268,20 +275,20 @@
         received = lax.all_to_all(message, both, 0, 0, tiled=True).reshape(tiles, groups, -1)
         returned = received[:, :, :mapped_len].reshape(tiles * groups, 2, nb_dev + 2)
 
-        def take(dt, dg, like):
+        def take(dt, dg):
             row = lax.dynamic_slice(
                 received,
                 ((tile_index - dt) % tiles, (group_index - dg) % groups, mapped_len),
-                (1, 1, like.size),
+                (1, 1, slot_len),
             )
-            return row.reshape(like.shape)
-
-        from_left = take(0, 1, b_hi)
-        from_right = take(0, -1, b_lo)
-        corner_ul = take(1, 1, a_hi[:, :, :, -1:])
-        corner_ur = take(1, -1, a_hi[:, :, :, :1])
-        corner_dl = take(-1, 1, a_lo[:, :, :, -1:])
-        corner_dr = take(-1, -1, a_lo[:, :, :, :1])
+            return row.reshape(3, radial_nodes, na_dev, 1)
+
+        from_left = take(0, 1)
+        from_right = take(0, -1)
+        corner_ul = take(1, 1)[:, :, na_dev - 1 :, :]
+        corner_ur = take(1, -1)[:, :, na_dev - 1 :, :]
+        corner_dl = take(-1, 1)[:, :, :1, :]
+        corner_dr = take(-1, -1)[:, :, :1, :]
         top = jnp.concatenate([corner_ul, from_up, corner_ur], axis=3)
         middle = jnp.concatenate([from_left, stacked, from_right], axis=3)
         bottom = jnp.concatenate([corner_dl, from_down, corner_dr], axis=3)
@@ -315,13 +322,18 @@
         return assemble_dim(along_a[..., 1:-1], last, along_a[..., 0:1], along_a[..., -1:])
 
     def tendency(parts, surface):
-        stacked = pl.pallas_call(
-            volume_kernel, out_shape=jax.ShapeDtypeStruct((3, rows, nb_dev), jnp.float32)
+        stacked, edge_rows, edge_cols = pl.pallas_call(
+            volume_kernel,
+            out_shape=(
+                jax.ShapeDtypeStruct((3, rows, nb_dev), jnp.float32),
+                jax.ShapeDtypeStruct((2, 3, radial_nodes, nb_dev), jnp.float32),
+                jax.ShapeDtypeStruct((2, 3, rows), jnp.float32),
+            ),
         )(parts.reshape(3, rows, nb_dev), flat_flow, grads, mats, flat_mass)
         stacked = stacked.reshape(parts.shape)
         sent = owner_map(surface)
         if carried_halo:
-            returned, padded = joint_exchange(sent, stacked)
+            returned, padded = joint_exchange(sent, stacked, edge_rows, edge_cols)
         else:
             returned = lax.all_to_all(
                 sent.reshape(tiles * groups, -1), both, 0, 0, tiled=True

time: 91.3 us -> 86.7 us (0.950)
  local copies, waits for them, and re-layouts: 24.4 us -> 19.4 us
    slice x6 -> x2, local copies, waits for them, and re-layouts: 6.19 us -> 1.41 us  [joint_exchange(): b_lo = edge_cols[0].reshape(1, 1, -1)]
    reshape x24 -> x12, local copies, waits for them, and re-layouts: 2.67 us -> 1.44 us  [take(): return row.reshape(3, radial_nodes, na_dev, 1)]
  transfers between devices with their start and end apart: 8 -> 8, of which waited for: 2 -> 2; matrix products, arithmetic and copies ran while one was open for 24% -> 18% of each run, Pallas kernels for 10% -> 11%
where the time goes in v6:
time: 86.7 us; the launch traced here: 86.1 us
  starting transfers between devices  26.9 us (31%)
  local copies, waits for them, and re-layouts  19.4 us (22%)
  other arithmetic  11.8 us (14%)
  waiting for transfers between devices  11.6 us (13%)
  Pallas kernels  9.49 us (11%)
  matrix products  6.18 us (7%)
    all_to_all x2, waiting for transfers between devices, joint_exchange(): lax.all_to_all(message, both, 0, 0, tiled=True).reshape(tiles, groups, -1)  11.6 us
    all_to_all x2, starting transfers between devices, owner_map(): gathered = lax.all_to_all(partial, both, 0, 0, tiled=True)  9.87 us
    all_to_all x2, starting transfers between devices, joint_exchange(): lax.all_to_all(message, both, 0, 0, tiled=True).reshape(tiles, groups, -1)  9.86 us
    pallas_call x2, Pallas kernels, tendency(): pl.pallas_call(volume_kernel, out_shape=(jax.ShapeDtypeStruct((3, rows, n...  6.92 us
    ppermute x2, starting transfers between devices, joint_exchange(): from_down = lax.ppermute(a_lo, 'tile', down)  6.6 us
    dot_general x2, matrix products, flux_of(): flux = -jnp.dot(synth, returned.reshape(-1, nb_dev + 2), precision=highest)  4.37 us
    reshape x6, other arithmetic, assemble_dim(): return joined.reshape(shape)  3 us
    pallas_call x1, Pallas kernels, local(): pl.pallas_call(gradient_kernel, out_shape=jax.ShapeDtypeStruct((9, rows,...  2.57 us
  transfers between devices with their start and end apart: 8, of which 2 were waited for; matrix products, arithmetic and copies ran while one was open for 18% of the time, Pallas kernels for 11%

profile of v6, /device:TPU:0, one launch (start us, length us, event | category | flops | bytes accessed | tf_op | source)
XLA Modules:
  0.0 86.1 jit_solution(13042156706198480373)
XLA Ops:
  0.0 0.7 convert_element_type.63
  0.7 0.7 tile.8
  1.5 0.7 tile.9
  2.2 0.8 fusion.36
  3.0 1.0 %fusion.18 = f32[32,2,128]{2,0,1:T(8,128)S(1)} fusion(f32[32,1,16]{0,2,1:T(8,128)S(1)} %get-tuple-element.112, f32[32,1,16]{0,2,1:T(8,128)S(1)} %get-tuple-element.111, f32[16]{0:T(128)S(1)} %get-tuple-element.114, f32[3,8,16,128]{3,2,1,0:T(8,128)} %param.11), kind=kOutput, calls=%fused_computation.76 | convolution fusion | flops 1574912 | bytes 45120 | tf_op jit(solution)/shard_map/dot_general | solution.py:226
  4.0 0.6 copy.171
  4.7 7.3 %all-to-all-start = ((f32[32,2,128]{2,1,0:T(2,128)}), f32[32,2,128]{2,1,0:T(2,128)S(1)}, u32[]{:S(2)}, u32[]{:S(2)}) async-start(f32[32,2,128]{2,1,0:T(2,128)} %copy.171), calls=%async_computation | async-start | bytes 65536 | tf_op jit(solution)/shard_map/all_to_all | solution.py:227
  12.1 0.7 mul.412
  12.9 0.7 tile.11
  13.6 0.7 broadcast_multiply_fusion.3.mass_ref
  14.3 2.6 %shard_map.73.grad_ref = f32[9,128,128]{2,1,0:T(8,128)} custom-call(f32[3,128,128]{2,1,0:T(8,128)} %bitcast.165, f32[6,128,128]{2,1,0:T(8,128)} %constant.380.clone.mats_ref), custom_call_target="tpu_custom_call" | custom-call | tf_op jit(solution)/shard_map/pallas_call | solution.py:217
  16.9 3.5 %shard_map.74 = (f32[3,128,128]{2,1,0:T(8,128)}, f32[2,3,8,128]{3,2,1,0:T(8,128)}, f32[2,3,128]{2,1,0:T(4,128)}) custom-call(f32[3,128,128]{2,1,0:T(8,128)} %bitcast.164, f32[3,128,128]{2,1,0:T(8,128)} %bitcast.166, f32[9,128,128]{2,1,0:T(8,128)} %shard_map.73.grad_ref, f32[6,128,128]{2,1,0:T(8,128)} %constant.380.clone.mats_ref, ...), custom_call_target="tpu_custom_call" | custom-call | tf_op jit(solution)/shard_map/pallas_call | solution.py:325
  20.4 0.7 slice_bitcast_fusion.23
  21.1 0.2 collective-permute-start
  21.3 3.3 %collective-permute-start.1 = (f32[3,8,1,128]{3,1,0,2:T(8,128)S(1)}, f32[3,8,1,128]{3,1,0,2:T(8,128)S(1)}, u32[]{:S(2)}, u32[]{:S(2)}) collective-permute-start(f32[3,8,1,128]{3,1,0,2:T(8,128)S(1)} %get-tuple-element.88), channel_id=1, source_target_pairs={{4,0},{8,4},{12,8},{16,12},{20,16},{24,20},{28,24},{0,28},{5,1},{9... | collective-permute-start | bytes 36872 | tf_op jit(solution)/shard_map/ppermute | solution.py:258
  24.8 0.7 gather_fusion.1
  25.5 0.7 fusion.88
  26.6 0.6 fusion.78
  27.4 0.8 and_reduce_fusion
  28.1 0.6 fusion.89
  28.8 0.2 fusion.8
  29.7 0.7 all_to_all.19
  30.4 4.0 %all-to-all-start.1 = ((f32[32,1,644]{2,1,0:T(1,128)}), f32[32,1,644]{2,1,0:T(1,128)S(1)}, u32[]{:S(2)}, u32[]{:S(2)}) async-start(f32[32,1,644]{2,1,0:T(1,128)} %all_to_all.19), calls=%async_computation.1 | async-start | bytes 196608 | tf_op jit(solution)/shard_map/all_to_all | solution.py:275
  34.5 0.7 gather_fusion
  35.3 7.1 %all-to-all-done.1 = f32[32,1,644]{2,1,0:T(1,128)S(1)} async-done(((f32[32,1,644]{2,1,0:T(1,128)}), f32[32,1,644]{2,1,0:T(1,128)S(1)}, u32[]{:S(2)}, u32[]{:S(2)}) %all-to-all-start.1) | async-done | bytes 82464 | tf_op jit(solution)/shard_map/all_to_all | solution.py:275
  42.4 0.2 reduce.9
  43.5 0.2 reshape.1147
  43.7 0.2 reshape.1146
  44.0 0.3 pad_maximum_fusion
  44.3 2.2 %fusion.10 = (f32[3,8,18,130]{3,2,1,0:T(8,128)S(1)}, f32[18,130]{1,0:T(8,128)S(1)}) fusion(f32[3,8,18,130]{3,2,1,0:T(8,128)S(1)} %copy.261, s32[]{:T(128)} %bitcast.10, s32[]{:T(128)} %bitcast.11, pred[]{:T(512)} %and_reduce_fusion, f32[18,64]{0,1:T(8,128)S(1)} %bitcast.172, f32[64,130]{1,0:T(8,128)S(1)} %reshape_reshape.6, ...), kind=kOutput, calls=%fused_computation.48 | convolution fusion | flops 1811160 | bytes 173577 | tf_op jit(solution)/shard_map/dot_general | solution.py:245
  46.6 0.2 slice_reduce_fusion.5
  47.7 0.2 slice_reduce_fusion.3
  48.1 0.5 copy.187
  48.6 0.2 fusion.80
  48.8 1.3 %slice.455 = f32[3,8,16,16,6]{2,4,3,1,0:T(8,128)} slice(f32[3,8,16,16,8]{2,4,3,1,0:T(8,128)S(1)} %bitcast.159), slice={[0:3], [0:8], [0:16], [0:16], [1:7]} | slice | bytes 294912 | tf_op jit(solution)/shard_map/slice | solution.py:136
  50.3 0.3 fusion.17
  50.6 0.6 copy.193
  51.2 2.6 %all-to-all-start.2 = ((f32[32,2,128]{2,1,0:T(2,128)}), f32[32,2,128]{2,1,0:T(2,128)S(1)}, u32[]{:S(2)}, u32[]{:S(2)}) async-start(f32[32,2,128]{2,1,0:T(2,128)} %copy.193), calls=%async_computation.2 | async-start | bytes 65536 | tf_op jit(solution)/shard_map/all_to_all | solution.py:227
  53.8 0.5 slice_add_fusion.3
  54.3 2.0 %maximum_bitcast_fusion = f32[3,8,16,128]{2,3,1,0:T(8,128)S(1)} fusion(f32[3,8,16,16,1]{2,4,3,1,0:T(1,128)S(1)} %get-tuple-element.64, f32[3,8,16,16,6]{2,4,3,1,0:T(8,128)} %slice.455, f32[3,8,16,16,1]{2,4,3,1,0:T(1,128)S(1)} %get-tuple-element.63), kind=kLoop, calls=%fused_computation.2 | loop fusion | flops 98304 | bytes 393216 | tf_op jit(solution)/shard_map/reshape | solution.py:138
  56.4 0.4 copy.190
  56.8 0.7 multiply_add_fusion
  57.5 3.5 %shard_map.75 = (f32[3,128,128]{2,1,0:T(8,128)}, f32[2,3,8,128]{3,2,1,0:T(8,128)}, f32[2,3,128]{2,1,0:T(4,128)}) custom-call(f32[3,128,128]{2,1,0:T(8,128)} %bitcast.168, f32[3,128,128]{2,1,0:T(8,128)} %bitcast.167, f32[9,128,128]{2,1,0:T(8,128)} %shard_map.73.grad_ref, f32[6,128,128]{2,1,0:T(8,128)} %constant.380.clone.mats_ref, ...), custom_call_target="tpu_custom_call" | custom-call | tf_op jit(solution)/shard_map/pallas_call | solution.py:325
  61.0 0.7 fusion.86
  62.1 0.2 fusion.6
  63.0 0.7 all_to_all.22
  63.7 5.8 %all-to-all-start.3 = ((f32[32,1,644]{2,1,0:T(1,128)}), f32[32,1,644]{2,1,0:T(1,128)S(1)}, u32[]{:S(2)}, u32[]{:S(2)}) async-start(f32[32,1,644]{2,1,0:T(1,128)} %all_to_all.22), calls=%async_computation.3 | async-start | bytes 196608 | tf_op jit(solution)/shard_map/all_to_all | solution.py:275
  69.6 0.3 collective-permute-start.2
  69.9 3.3 %collective-permute-start.3 = (f32[3,8,1,128]{3,1,0,2:T(8,128)S(1)}, f32[3,8,1,128]{3,1,0,2:T(8,128)S(1)}, u32[]{:S(2)}, u32[]{:S(2)}) collective-permute-start(f32[3,8,1,128]{3,1,0,2:T(8,128)S(1)} %get-tuple-element.84), channel_id=1, source_target_pairs={{4,0},{8,4},{12,8},{16,12},{20,16},{24,20},{28,24},{0,28},{5,1},{9... | collective-permute-start | bytes 36872 | tf_op jit(solution)/shard_map/ppermute | solution.py:258
  73.2 4.5 %all-to-all-done.3 = f32[32,1,644]{2,1,0:T(1,128)S(1)} async-done(((f32[32,1,644]{2,1,0:T(1,128)}), f32[32,1,644]{2,1,0:T(1,128)S(1)}, u32[]{:S(2)}, u32[]{:S(2)}) %all-to-all-start.3) | async-done | bytes 82464 | tf_op jit(solution)/shard_map/all_to_all | solution.py:275
  77.6 0.2 reduce.21
  78.8 0.2 reshape.1149
  79.0 0.2 reshape.1148
  79.3 0.3 pad_maximum_fusion.1
  79.6 2.2 %fusion.5 = f32[3,8,18,130]{3,2,1,0:T(8,128)S(1)} fusion(f32[3,8,18,130]{3,2,1,0:T(8,128)S(1)} %pad_maximum_fusion.1, s32[]{:T(128)} %bitcast.10, s32[]{:T(128)} %bitcast.11, f32[18,64]{0,1:T(8,128)S(1)} %bitcast.173, f32[64,130]{1,0:T(8,128)S(1)} %reshape_reshape.7, f32[130]{0:T(256)S(1)} %broadcast_select_fusion, f32[18]{0:T(128)S(1)} %gather_fusion, ...), kind=kOutput, calls=%fused_computation.11 | convolution fusion | flops 1811160 | bytes 149001 | tf_op jit(solution)/shard_map/dot_general | solution.py:245
  82.4 0.2 maximum_bitcast_fusion.3
  82.5 0.2 slice_reduce_fusion.1
  82.9 0.5 copy.209
  83.4 0.2 fusion.79
  83.6 0.2 slice.498
  83.8 0.5 slice_add_fusion.1
  84.3 0.6 maximum_bitcast_fusion.1
  84.9 0.4 copy.212
  85.3 0.8 add_multiply_fusion
  (160 shorter events, 6.4 us)
Async XLA Ops:
  0.0 28.8 %copy-start = (bf16[1,512,512]{2,1,0:T(8,128)(2,1)S(1)}, bf16[1,512,512]{2,1,0:T(8,128)(2,1)}, u32[]{:S(2)}) copy-start(bf16[1,512,512]{2,1,0:T(8,128)(2,1)} %param.13) | copy-start | bytes 1572868
  2.2 22.4 %copy-start.1 = (f32[8]{0:T(128)S(1)}, f32[8]{0:T(128)}, u32[]{:S(2)}) copy-start(f32[8]{0:T(128)} %constant.379.clone) | copy-start | bytes 100
  3.0 21.8 %copy-start.2 = (f32[8]{0:T(128)S(1)}, f32[8]{0:T(128)}, u32[]{:S(2)}) copy-start(f32[8]{0:T(128)} %constant.378.clone) | copy-start | bytes 100
  4.7 24.1 %all-to-all-start = ((f32[32,2,128]{2,1,0:T(2,128)}), f32[32,2,128]{2,1,0:T(2,128)S(1)}, u32[]{:S(2)}, u32[]{:S(2)}) async-start(f32[32,2,128]{2,1,0:T(2,128)} %copy.171), calls=%async_computation | async-start | bytes 65536 | tf_op jit(solution)/shard_map/all_to_all | solution.py:227
  14.3 12.3 %copy-start.7 = (s32[32]{0:T(128)S(1)}, s32[32]{0:T(128)}, u32[]{:S(2)}) copy-start(s32[32]{0:T(128)} %param.14) | copy-start | bytes 388
  14.3 13.0 %copy-start.8 = (s32[4]{0:T(128)S(1)}, s32[4]{0:T(128)}, u32[]{:S(2)}) copy-start(s32[4]{0:T(128)} %constant.368.clone.1) | copy-start | bytes 52
  21.1 22.1 %collective-permute-start = (f32[3,8,1,128]{3,1,0,2:T(8,128)S(1)}, f32[3,8,1,128]{3,1,0,2:T(8,128)S(1)}, u32[]{:S(2)}, u32[]{:S(2)}) collective-permute-start(f32[3,8,1,128]{3,1,0,2:T(8,128)S(1)} %get-tuple-element.87), channel_id=1, source_target_pairs={{0,4},{4,8},{8,12},{12,16},{16,20},{20,24},{24,28},{28,0},{1,5},{5... | collective-permute-start | bytes 36872 | tf_op jit(solution)/shard_map/ppermute | solution.py:257
  21.3 22.1 %collective-permute-start.1 = (f32[3,8,1,128]{3,1,0,2:T(8,128)S(1)}, f32[3,8,1,128]{3,1,0,2:T(8,128)S(1)}, u32[]{:S(2)}, u32[]{:S(2)}) collective-permute-start(f32[3,8,1,128]{3,1,0,2:T(8,128)S(1)} %get-tuple-element.88), channel_id=1, source_target_pairs={{4,0},{8,4},{12,8},{16,12},{20,16},{24,20},{28,24},{0,28},{5,1},{9... | collective-permute-start | bytes 36872 | tf_op jit(solution)/shard_map/ppermute | solution.py:258
  28.8 15.1 %copy-start.4 = (f32[3,128,128]{2,1,0:T(8,128)S(1)}, f32[3,128,128]{2,1,0:T(8,128)}, u32[]{:S(2)}) copy-start(f32[3,128,128]{2,1,0:T(8,128)} %get-tuple-element.37) | copy-start | bytes 589828
  30.4 12.0 %all-to-all-start.1 = ((f32[32,1,644]{2,1,0:T(1,128)}), f32[32,1,644]{2,1,0:T(1,128)S(1)}, u32[]{:S(2)}, u32[]{:S(2)}) async-start(f32[32,1,644]{2,1,0:T(1,128)} %all_to_all.19), calls=%async_computation.1 | async-start | bytes 196608 | tf_op jit(solution)/shard_map/all_to_all | solution.py:275
  48.8 1.4 %copy-start.3 = (f32[3,8,16,128]{3,2,1,0:T(8,128)S(1)}, f32[3,8,16,128]{3,2,1,0:T(8,128)}, u32[]{:S(2)}) copy-start(f32[3,8,16,128]{3,2,1,0:T(8,128)} %param.11) | copy-start | bytes 589828
  51.2 10.8 %all-to-all-start.2 = ((f32[32,2,128]{2,1,0:T(2,128)}), f32[32,2,128]{2,1,0:T(2,128)S(1)}, u32[]{:S(2)}, u32[]{:S(2)}) async-start(f32[32,2,128]{2,1,0:T(2,128)} %copy.193), calls=%async_computation.2 | async-start | bytes 65536 | tf_op jit(solution)/shard_map/all_to_all | solution.py:227
  61.0 8.6 %copy-start.6 = (f32[2,3,8,128]{3,2,1,0:T(8,128)S(1)}, f32[2,3,8,128]{3,2,1,0:T(8,128)}, u32[]{:S(2)}) copy-start(f32[2,3,8,128]{3,2,1,0:T(8,128)} %get-tuple-element.39) | copy-start | bytes 73732
  61.0 18.3 %copy-start.5 = (f32[3,128,128]{2,1,0:T(8,128)S(1)}, f32[3,128,128]{2,1,0:T(8,128)}, u32[]{:S(2)}) copy-start(f32[3,128,128]{2,1,0:T(8,128)} %get-tuple-element.40) | copy-start | bytes 589828
  63.7 13.9 %all-to-all-start.3 = ((f32[32,1,644]{2,1,0:T(1,128)}), f32[32,1,644]{2,1,0:T(1,128)S(1)}, u32[]{:S(2)}, u32[]{:S(2)}) async-start(f32[32,1,644]{2,1,0:T(1,128)} %all_to_all.22), calls=%async_computation.3 | async-start | bytes 196608 | tf_op jit(solution)/shard_map/all_to_all | solution.py:275
  69.6 8.9 %collective-permute-start.2 = (f32[3,8,1,128]{3,1,0,2:T(8,128)S(1)}, f32[3,8,1,128]{3,1,0,2:T(8,128)S(1)}, u32[]{:S(2)}, u32[]{:S(2)}) collective-permute-start(f32[3,8,1,128]{3,1,0,2:T(8,128)S(1)} %get-tuple-element.83), channel_id=1, source_target_pairs={{0,4},{4,8},{8,12},{12,16},{16,20},{20,24},{24,28},{28,0},{1,5},{5... | collective-permute-start | bytes 36872 | tf_op jit(solution)/shard_map/ppermute | solution.py:257
  69.9 8.8 %collective-permute-start.3 = (f32[3,8,1,128]{3,1,0,2:T(8,128)S(1)}, f32[3,8,1,128]{3,1,0,2:T(8,128)S(1)}, u32[]{:S(2)}, u32[]{:S(2)}) collective-permute-start(f32[3,8,1,128]{3,1,0,2:T(8,128)S(1)} %get-tuple-element.84), channel_id=1, source_target_pairs={{4,0},{8,4},{12,8},{16,12},{20,16},{24,20},{28,24},{0,28},{5,1},{9... | collective-permute-start | bytes 36872 | tf_op jit(solution)/shard_map/ppermute | solution.py:258

commit v7 on v6

--- a/solution.py
+++ b/solution.py
@@ -41,7 +41,18 @@
         out_ref[3 * component + 2] = product(x, mats_ref[2])
 
 
-def volume_kernel(parts_ref, flow_ref, grad_ref, mats_ref, mass_ref, out_ref, rows_ref, cols_ref):
+def volume_kernel(parts_ref, flow_ref, grad_ref, mats_ref, mass_ref, *outs):
+    volume_body(parts_ref, flow_ref, grad_ref, mats_ref, mass_ref, *outs)
+
+
+def first_volume_kernel(parts_ref, flow_ref, grad_ref, mats_ref, mass_ref, table_ref, *outs):
+    volume_body(parts_ref, flow_ref, grad_ref, mats_ref, mass_ref, *outs[:3])
+    depth = outs[0].shape[1] // outs[1].shape[2]
+    surface = parts_ref[0, pl.ds(outs[0].shape[1] - depth, depth), :]
+    outs[3][...] = product(table_ref[...], surface)
+
+
+def volume_body(parts_ref, flow_ref, grad_ref, mats_ref, mass_ref, out_ref, rows_ref, cols_ref):
     mass = mass_ref[...]
     p = [parts_ref[i] for i in range(3)]
     f = [flow_ref[i] for i in range(3)]
@@ -218,12 +229,13 @@
         gradient_kernel, out_shape=jax.ShapeDtypeStruct((9, rows, nb_dev), jnp.float32)
     )(flat_flow, mats)
 
-    def owner_map(surface):
-        angle = phases(wave_of_slot, tile_index * elems_a, elems_a, span, points)
-        table = (
-            jnp.stack([jnp.cos(angle), jnp.sin(angle)], axis=1) * (w_a * scale)[None, None, :]
-        ).reshape(-1, na_dev)
-        partial = jnp.dot(table, surface, precision=highest).reshape(-1, 2, nb_dev)
+    angle = phases(wave_of_slot, tile_index * elems_a, elems_a, span, points)
+    analysis = (
+        jnp.stack([jnp.cos(angle), jnp.sin(angle)], axis=1) * (w_a * scale)[None, None, :]
+    ).reshape(-1, na_dev)
+
+    def owner_map(partial):
+        partial = partial.reshape(-1, 2, nb_dev)
         gathered = lax.all_to_all(partial, both, 0, 0, tiled=True)
         coeff = gathered.reshape(tiles, groups, 2, nb_dev).sum(axis=0)
         coeff = coeff.transpose(1, 0, 2).reshape(2, nb)
@@ -322,16 +334,24 @@
         return assemble_dim(along_a[..., 1:-1], last, along_a[..., 0:1], along_a[..., -1:])
 
     def tendency(parts, surface):
-        stacked, edge_rows, edge_cols = pl.pallas_call(
-            volume_kernel,
-            out_shape=(
-                jax.ShapeDtypeStruct((3, rows, nb_dev), jnp.float32),
-                jax.ShapeDtypeStruct((2, 3, radial_nodes, nb_dev), jnp.float32),
-                jax.ShapeDtypeStruct((2, 3, rows), jnp.float32),
-            ),
-        )(parts.reshape(3, rows, nb_dev), flat_flow, grads, mats, flat_mass)
+        shapes = (
+            jax.ShapeDtypeStruct((3, rows, nb_dev), jnp.float32),
+            jax.ShapeDtypeStruct((2, 3, radial_nodes, nb_dev), jnp.float32),
+            jax.ShapeDtypeStruct((2, 3, rows), jnp.float32),
+        )
+        operands = (parts.reshape(3, rows, nb_dev), flat_flow, grads, mats, flat_mass)
+        if surface is None:
+            shapes = shapes + (jax.ShapeDtypeStruct(analysis.shape[:1] + (nb_dev,), jnp.float32),)
+            stacked, edge_rows, edge_cols, partial = pl.pallas_call(
+                first_volume_kernel, out_shape=shapes
+            )(*operands, analysis)
+        else:
+            stacked, edge_rows, edge_cols = pl.pallas_call(volume_kernel, out_shape=shapes)(
+                *operands
+            )
+            partial = jnp.dot(analysis, surface, precision=highest)
         stacked = stacked.reshape(parts.shape)
-        sent = owner_map(surface)
+        sent = owner_map(partial)
         if carried_halo:
             returned, padded = joint_exchange(sent, stacked, edge_rows, edge_cols)
         else:
@@ -347,7 +367,7 @@
         padded = assemble_dim(padded, 1, plane_r, plane_r)
         return assemble_ext(padded) / assembled[None], outer_rate
 
-    first_rate, first_outer = tendency(field, field[0, radial_nodes - 1])
+    first_rate, first_outer = tendency(field, None)
     section = field + time_step * first_rate
     section_outer = field[0, radial_nodes - 1] + time_step * first_outer
     second_rate, _ = tendency(section, section_outer)

time: 86.7 us -> 86.3 us (level)
  matrix products: 6.18 us -> 5.17 us
    dot_general x2 -> x1, matrix products: 1.34 us -> 0.33 us  [tendency(): partial = jnp.dot(analysis, surface, precision=highest)]
    reshape x6 -> x5, other arithmetic: 3 us -> 2.96 us  [assemble_dim(): return joined.reshape(shape)]
  transfers between devices with their start and end apart: 8 -> 8, of which waited for: 2 -> 2; matrix products, arithmetic and copies ran while one was open for 18% -> 16% of each run, Pallas kernels for 11% -> 4%
where the time goes in v7:
time: 86.3 us; the launch traced here: 85.8 us
  starting transfers between devices  26.9 us (31%)
  local copies, waits for them, and re-layouts  19.7 us (23%)
  other arithmetic  12.4 us (14%)
  waiting for transfers between devices  11.3 us (13%)
  Pallas kernels  9.44 us (11%)
  matrix products  5.17 us (6%)
  between operations  0.87 us (1%)
    all_to_all x2, waiting for transfers between devices, joint_exchange(): lax.all_to_all(message, both, 0, 0, tiled=True).reshape(tiles, groups, -1)  11.3 us
    all_to_all x2, starting transfers between devices, owner_map(): gathered = lax.all_to_all(partial, both, 0, 0, tiled=True)  9.88 us
    all_to_all x2, starting transfers between devices, joint_exchange(): lax.all_to_all(message, both, 0, 0, tiled=True).reshape(tiles, groups, -1)  9.87 us
    ppermute x2, starting transfers between devices, joint_exchange(): from_down = lax.ppermute(a_lo, 'tile', down)  6.59 us
    dot_general x2, matrix products, flux_of(): flux = -jnp.dot(synth, returned.reshape(-1, nb_dev + 2), precision=highest)  4.37 us
    pallas_call x1, Pallas kernels, tendency(): pl.pallas_call(volume_kernel, out_shape=shapes)(*operands)  3.46 us
    pallas_call x1, Pallas kernels, tendency(): pl.pallas_call(first_volume_kernel, out_shape=shapes)(*operands, analysis)  3.43 us
    reshape x5, other arithmetic, assemble_dim(): return joined.reshape(shape)  2.96 us
  transfers between devices with their start and end apart: 8, of which 2 were waited for; matrix products, arithmetic and copies ran while one was open for 16% of the time, Pallas kernels for 4%

profile of v7, /device:TPU:0, one launch (start us, length us, event | category | flops | bytes accessed | tf_op | source)
XLA Modules:
  0.0 85.8 jit_solution(16750896511081259796)
XLA Ops:
  0.0 0.7 convert_element_type.61
  0.7 0.7 tile.8
  1.5 0.7 tile.6
  2.3 0.7 mul.385
  3.1 0.7 tile.7
  3.9 0.8 fusion.31
  4.8 0.6 broadcast_multiply_fusion.4.table_ref
  5.4 0.7 broadcast_multiply_fusion.3.mass_ref
  6.1 2.5 %shard_map.73.grad_ref = f32[9,128,128]{2,1,0:T(8,128)} custom-call(f32[3,128,128]{2,1,0:T(8,128)} %bitcast.162, f32[6,128,128]{2,1,0:T(8,128)} %constant.375.clone.mats_ref), custom_call_target="tpu_custom_call" | custom-call | tf_op jit(solution)/shard_map/pallas_call | solution.py:228
  8.6 3.4 %shard_map.74 = (f32[3,128,128]{2,1,0:T(8,128)}, f32[2,3,8,128]{3,2,1,0:T(8,128)}, f32[2,3,128]{2,1,0:T(4,128)}, f32[64,128]{1,0:T(8,128)}) custom-call(f32[3,128,128]{2,1,0:T(8,128)} %bitcast.161, f32[3,128,128]{2,1,0:T(8,128)} %bitcast.163, f32[9,128,128]{2,1,0:T(8,128)} %shard_map.73.grad_ref, f32[6,128,128]{2,1,0:T(8,128)} %constant.375.clone.mats_ref, ...), custom_call_target="tpu_custom_call" | custom-call | tf_op jit(solution)/shard_map/pallas_call | solution.py:345
  12.1 7.3 %all-to-all-start = ((f32[32,2,128]{2,1,0:T(2,128)}), f32[32,2,128]{2,1,0:T(2,128)S(1)}, u32[]{:S(2)}, u32[]{:S(2)}) async-start(f32[32,2,128]{2,1,0:T(2,128)} %bitcast.180), calls=%async_computation | async-start | bytes 65536 | tf_op jit(solution)/shard_map/all_to_all | solution.py:239
  19.4 0.7 slice_bitcast_fusion.24
  20.1 0.3 collective-permute-start
  20.4 3.3 %collective-permute-start.1 = (f32[3,8,1,128]{3,1,0,2:T(8,128)S(1)}, f32[3,8,1,128]{3,1,0,2:T(8,128)S(1)}, u32[]{:S(2)}, u32[]{:S(2)}) collective-permute-start(f32[3,8,1,128]{3,1,0,2:T(8,128)S(1)} %get-tuple-element.90), channel_id=1, source_target_pairs={{4,0},{8,4},{12,8},{16,12},{20,16},{24,20},{28,24},{0,28},{5,1},{9... | collective-permute-start | bytes 36872 | tf_op jit(solution)/shard_map/ppermute | solution.py:270
  23.8 0.7 gather_fusion.1
  24.5 0.7 fusion.81
  25.7 0.6 fusion.71
  26.4 0.8 and_reduce_fusion
  27.2 0.6 fusion.82
  27.9 0.2 fusion.8
  28.8 0.7 all_to_all.19
  29.5 4.0 %all-to-all-start.1 = ((f32[32,1,644]{2,1,0:T(1,128)}), f32[32,1,644]{2,1,0:T(1,128)S(1)}, u32[]{:S(2)}, u32[]{:S(2)}) async-start(f32[32,1,644]{2,1,0:T(1,128)} %all_to_all.19), calls=%async_computation.1 | async-start | bytes 196608 | tf_op jit(solution)/shard_map/all_to_all | solution.py:287
  33.6 0.7 gather_fusion
  34.4 0.2 copy.191
  34.6 6.8 %all-to-all-done.1 = f32[32,1,644]{2,1,0:T(1,128)S(1)} async-done(((f32[32,1,644]{2,1,0:T(1,128)}), f32[32,1,644]{2,1,0:T(1,128)S(1)}, u32[]{:S(2)}, u32[]{:S(2)}) %all-to-all-start.1) | async-done | bytes 82464 | tf_op jit(solution)/shard_map/all_to_all | solution.py:287
  41.4 0.2 reduce.9
  42.6 0.2 reshape.1142
  42.8 0.2 reshape.1141
  43.0 0.3 pad_maximum_fusion
  43.4 2.2 %fusion.17 = (f32[3,8,18,130]{3,2,1,0:T(8,128)S(1)}, f32[18,130]{1,0:T(8,128)S(1)}) fusion(f32[3,8,18,130]{3,2,1,0:T(8,128)S(1)} %copy.257, s32[]{:T(128)} %bitcast.11, s32[]{:T(128)} %bitcast.12, pred[]{:T(512)} %and_reduce_fusion, f32[18,64]{0,1:T(8,128)S(1)} %bitcast.169, f32[64,130]{1,0:T(8,128)S(1)} %reshape_reshape.6, ...), kind=kOutput, calls=%fused_computation.55 | convolution fusion | flops 1811160 | bytes 173577 | tf_op jit(solution)/shard_map/dot_general | solution.py:257
  45.7 0.7 slice_reduce_fusion.5
  47.3 0.2 slice_reduce_fusion.3
  47.7 0.5 copy.188
  48.1 0.2 fusion.73
  48.4 1.3 %slice.454 = f32[3,8,16,16,6]{2,4,3,1,0:T(8,128)} slice(f32[3,8,16,16,8]{2,4,3,1,0:T(8,128)S(1)} %bitcast.156), slice={[0:3], [0:8], [0:16], [0:16], [1:7]} | slice | bytes 294912 | tf_op jit(solution)/shard_map/slice | solution.py:147
  49.7 0.3 fusion.14
  50.1 0.6 copy.196
  50.7 2.6 %all-to-all-start.2 = ((f32[32,2,128]{2,1,0:T(2,128)}), f32[32,2,128]{2,1,0:T(2,128)S(1)}, u32[]{:S(2)}, u32[]{:S(2)}) async-start(f32[32,2,128]{2,1,0:T(2,128)} %copy.196), calls=%async_computation.2 | async-start | bytes 65536 | tf_op jit(solution)/shard_map/all_to_all | solution.py:239
  53.3 0.5 slice_add_fusion.3
  53.8 2.0 %maximum_bitcast_fusion = f32[3,8,16,128]{2,3,1,0:T(8,128)S(1)} fusion(f32[3,8,16,16,1]{2,4,3,1,0:T(1,128)S(1)} %get-tuple-element.66, f32[3,8,16,16,6]{2,4,3,1,0:T(8,128)} %slice.454, f32[3,8,16,16,1]{2,4,3,1,0:T(1,128)S(1)} %get-tuple-element.65), kind=kLoop, calls=%fused_computation.2 | loop fusion | flops 98304 | bytes 393216 | tf_op jit(solution)/shard_map/reshape | solution.py:149
  55.8 0.4 copy.192
  56.3 0.7 multiply_add_fusion
  57.0 3.5 %shard_map.75 = (f32[3,128,128]{2,1,0:T(8,128)}, f32[2,3,8,128]{3,2,1,0:T(8,128)}, f32[2,3,128]{2,1,0:T(4,128)}) custom-call(f32[3,128,128]{2,1,0:T(8,128)} %bitcast.165, f32[3,128,128]{2,1,0:T(8,128)} %bitcast.164, f32[9,128,128]{2,1,0:T(8,128)} %shard_map.73.grad_ref, f32[6,128,128]{2,1,0:T(8,128)} %constant.375.clone.mats_ref, ...), custom_call_target="tpu_custom_call" | custom-call | tf_op jit(solution)/shard_map/pallas_call | solution.py:349
  60.5 0.7 fusion.79
  61.4 0.2 dynamic_update_slice.47
  61.7 0.2 fusion.6
  62.6 0.7 all_to_all.22
  63.3 5.8 %all-to-all-start.3 = ((f32[32,1,644]{2,1,0:T(1,128)}), f32[32,1,644]{2,1,0:T(1,128)S(1)}, u32[]{:S(2)}, u32[]{:S(2)}) async-start(f32[32,1,644]{2,1,0:T(1,128)} %all_to_all.22), calls=%async_computation.3 | async-start | bytes 196608 | tf_op jit(solution)/shard_map/all_to_all | solution.py:287
  69.2 0.3 collective-permute-start.2
  69.5 3.3 %collective-permute-start.3 = (f32[3,8,1,128]{3,1,0,2:T(8,128)S(1)}, f32[3,8,1,128]{3,1,0,2:T(8,128)S(1)}, u32[]{:S(2)}, u32[]{:S(2)}) collective-permute-start(f32[3,8,1,128]{3,1,0,2:T(8,128)S(1)} %get-tuple-element.86), channel_id=1, source_target_pairs={{4,0},{8,4},{12,8},{16,12},{20,16},{24,20},{28,24},{0,28},{5,1},{9... | collective-permute-start | bytes 36872 | tf_op jit(solution)/shard_map/ppermute | solution.py:270
  72.8 4.5 %all-to-all-done.3 = f32[32,1,644]{2,1,0:T(1,128)S(1)} async-done(((f32[32,1,644]{2,1,0:T(1,128)}), f32[32,1,644]{2,1,0:T(1,128)S(1)}, u32[]{:S(2)}, u32[]{:S(2)}) %all-to-all-start.3) | async-done | bytes 82464 | tf_op jit(solution)/shard_map/all_to_all | solution.py:287
  77.3 0.2 reduce.21
  78.5 0.2 reshape.1144
  78.7 0.2 reshape.1143
  78.9 0.3 pad_maximum_fusion.1
  79.2 2.2 %fusion.5 = f32[3,8,18,130]{3,2,1,0:T(8,128)S(1)} fusion(f32[3,8,18,130]{3,2,1,0:T(8,128)S(1)} %pad_maximum_fusion.1, s32[]{:T(128)} %bitcast.11, s32[]{:T(128)} %bitcast.12, f32[18,64]{0,1:T(8,128)S(1)} %bitcast.170, f32[64,130]{1,0:T(8,128)S(1)} %reshape_reshape.7, f32[130]{0:T(256)S(1)} %broadcast_select_fusion, f32[18]{0:T(128)S(1)} %gather_fusion, ...), kind=kOutput, calls=%fused_computation.11 | convolution fusion | flops 1811160 | bytes 149001 | tf_op jit(solution)/shard_map/dot_general | solution.py:257
  82.2 0.2 slice_reduce_fusion.1
  82.5 0.5 copy.212
  83.0 0.2 fusion.72
  83.2 0.2 slice.497
  83.4 0.5 slice_add_fusion.1
  83.9 0.6 maximum_bitcast_fusion.1
  84.6 0.4 copy.215
  85.0 0.8 add_multiply_fusion
  (167 shorter events, 6.7 us)
Async XLA Ops:
  0.0 27.9 %copy-start = (bf16[1,512,512]{2,1,0:T(8,128)(2,1)S(1)}, bf16[1,512,512]{2,1,0:T(8,128)(2,1)}, u32[]{:S(2)}) copy-start(bf16[1,512,512]{2,1,0:T(8,128)(2,1)} %param.13) | copy-start | bytes 1572868
  2.2 21.4 %copy-start.9 = (f32[16]{0:T(128)}, f32[16]{0:T(128)S(1)}, u32[]{:S(2)}) copy-start(f32[16]{0:T(128)S(1)} %get-tuple-element.116) | copy-start | bytes 196
  4.6 19.0 %copy-start.1 = (f32[8]{0:T(128)S(1)}, f32[8]{0:T(128)}, u32[]{:S(2)}) copy-start(f32[8]{0:T(128)} %constant.374.clone) | copy-start | bytes 100
  4.7 19.1 %copy-start.2 = (f32[8]{0:T(128)S(1)}, f32[8]{0:T(128)}, u32[]{:S(2)}) copy-start(f32[8]{0:T(128)} %constant.373.clone) | copy-start | bytes 100
  6.1 19.6 %copy-start.7 = (s32[32]{0:T(128)S(1)}, s32[32]{0:T(128)}, u32[]{:S(2)}) copy-start(s32[32]{0:T(128)} %param.14) | copy-start | bytes 388
  8.6 17.8 %copy-start.11 = (s32[4]{0:T(128)S(1)}, s32[4]{0:T(128)}, u32[]{:S(2)}) copy-start(s32[4]{0:T(128)} %constant.363.clone.1) | copy-start | bytes 52
  12.1 15.8 %all-to-all-start = ((f32[32,2,128]{2,1,0:T(2,128)}), f32[32,2,128]{2,1,0:T(2,128)S(1)}, u32[]{:S(2)}, u32[]{:S(2)}) async-start(f32[32,2,128]{2,1,0:T(2,128)} %bitcast.180), calls=%async_computation | async-start | bytes 65536 | tf_op jit(solution)/shard_map/all_to_all | solution.py:239
  20.1 22.3 %collective-permute-start = (f32[3,8,1,128]{3,1,0,2:T(8,128)S(1)}, f32[3,8,1,128]{3,1,0,2:T(8,128)S(1)}, u32[]{:S(2)}, u32[]{:S(2)}) collective-permute-start(f32[3,8,1,128]{3,1,0,2:T(8,128)S(1)} %get-tuple-element.89), channel_id=1, source_target_pairs={{0,4},{4,8},{8,12},{12,16},{16,20},{20,24},{24,28},{28,0},{1,5},{5... | collective-permute-start | bytes 36872 | tf_op jit(solution)/shard_map/ppermute | solution.py:269
  20.4 21.9 %collective-permute-start.1 = (f32[3,8,1,128]{3,1,0,2:T(8,128)S(1)}, f32[3,8,1,128]{3,1,0,2:T(8,128)S(1)}, u32[]{:S(2)}, u32[]{:S(2)}) collective-permute-start(f32[3,8,1,128]{3,1,0,2:T(8,128)S(1)} %get-tuple-element.90), channel_id=1, source_target_pairs={{4,0},{8,4},{12,8},{16,12},{20,16},{24,20},{28,24},{0,28},{5,1},{9... | collective-permute-start | bytes 36872 | tf_op jit(solution)/shard_map/ppermute | solution.py:270
  23.8 10.5 %copy-start.3 = (f32[3,8,16,128]{3,2,1,0:T(8,128)S(1)}, f32[3,8,16,128]{3,2,1,0:T(8,128)}, u32[]{:S(2)}) copy-start(f32[3,8,16,128]{3,2,1,0:T(8,128)} %param.11) | copy-start | bytes 589828
  28.7 14.3 %copy-start.4 = (f32[3,128,128]{2,1,0:T(8,128)S(1)}, f32[3,128,128]{2,1,0:T(8,128)}, u32[]{:S(2)}) copy-start(f32[3,128,128]{2,1,0:T(8,128)} %get-tuple-element.39) | copy-start | bytes 589828
  29.5 12.0 %all-to-all-start.1 = ((f32[32,1,644]{2,1,0:T(1,128)}), f32[32,1,644]{2,1,0:T(1,128)S(1)}, u32[]{:S(2)}, u32[]{:S(2)}) async-start(f32[32,1,644]{2,1,0:T(1,128)} %all_to_all.19), calls=%async_computation.1 | async-start | bytes 196608 | tf_op jit(solution)/shard_map/all_to_all | solution.py:287
  48.4 1.3 %copy-start.8 = (f32[16]{0:T(128)S(1)}, f32[16]{0:T(128)}, u32[]{:S(2)}) copy-start(f32[16]{0:T(128)} %get-tuple-element.60) | copy-start | bytes 196
  48.4 1.4 %copy-start.10 = (f32[16]{0:T(128)S(1)}, f32[16]{0:T(128)}, u32[]{:S(2)}) copy-start(f32[16]{0:T(128)} %copy-done.9) | copy-start | bytes 196
  50.7 11.0 %all-to-all-start.2 = ((f32[32,2,128]{2,1,0:T(2,128)}), f32[32,2,128]{2,1,0:T(2,128)S(1)}, u32[]{:S(2)}, u32[]{:S(2)}) async-start(f32[32,2,128]{2,1,0:T(2,128)} %copy.196), calls=%async_computation.2 | async-start | bytes 65536 | tf_op jit(solution)/shard_map/all_to_all | solution.py:239
  60.5 8.7 %copy-start.6 = (f32[2,3,8,128]{3,2,1,0:T(8,128)S(1)}, f32[2,3,8,128]{3,2,1,0:T(8,128)}, u32[]{:S(2)}) copy-start(f32[2,3,8,128]{3,2,1,0:T(8,128)} %get-tuple-element.41) | copy-start | bytes 73732
  60.5 18.4 %copy-start.5 = (f32[3,128,128]{2,1,0:T(8,128)S(1)}, f32[3,128,128]{2,1,0:T(8,128)}, u32[]{:S(2)}) copy-start(f32[3,128,128]{2,1,0:T(8,128)} %get-tuple-element.42) | copy-start | bytes 589828
  63.3 13.9 %all-to-all-start.3 = ((f32[32,1,644]{2,1,0:T(1,128)}), f32[32,1,644]{2,1,0:T(1,128)S(1)}, u32[]{:S(2)}, u32[]{:S(2)}) async-start(f32[32,1,644]{2,1,0:T(1,128)} %all_to_all.22), calls=%async_computation.3 | async-start | bytes 196608 | tf_op jit(solution)/shard_map/all_to_all | solution.py:287
  69.2 8.9 %collective-permute-start.2 = (f32[3,8,1,128]{3,1,0,2:T(8,128)S(1)}, f32[3,8,1,128]{3,1,0,2:T(8,128)S(1)}, u32[]{:S(2)}, u32[]{:S(2)}) collective-permute-start(f32[3,8,1,128]{3,1,0,2:T(8,128)S(1)} %get-tuple-element.85), channel_id=1, source_target_pairs={{0,4},{4,8},{8,12},{12,16},{16,20},{20,24},{24,28},{28,0},{1,5},{5... | collective-permute-start | bytes 36872 | tf_op jit(solution)/shard_map/ppermute | solution.py:269
  69.5 8.8 %collective-permute-start.3 = (f32[3,8,1,128]{3,1,0,2:T(8,128)S(1)}, f32[3,8,1,128]{3,1,0,2:T(8,128)S(1)}, u32[]{:S(2)}, u32[]{:S(2)}) collective-permute-start(f32[3,8,1,128]{3,1,0,2:T(8,128)S(1)} %get-tuple-element.86), channel_id=1, source_target_pairs={{4,0},{8,4},{12,8},{16,12},{20,16},{24,20},{28,24},{0,28},{5,1},{9... | collective-permute-start | bytes 36872 | tf_op jit(solution)/shard_map/ppermute | solution.py:270

commit v8 on v7

--- a/solution.py
+++ b/solution.py
@@ -164,17 +164,25 @@
     return base + starts + ends
 
 
+def static_assembled(weights, count, lead, trail):
+    position = np.arange(count * P_SIZE)
+    local_point = position % P_SIZE
+    element = position // P_SIZE
+    starts = np.where(local_point == 0, np.where(element > 0, 1.0, lead), 0.0) * weights[P_SIZE - 1]
+    ends = np.where(local_point == P_SIZE - 1, np.where(element < count - 1, 1.0, trail), 0.0)
+    return (np.tile(weights, count) + starts + ends * weights[0]).astype(np.float32)
+
+
 def phases(waves, elem_start, elem_count, span, points):
     element = elem_start + jnp.arange(elem_count * P_SIZE, dtype=jnp.int32) // P_SIZE
     whole = waves[:, None] * (2 * element + 1)[None, :] % span
-    fraction = waves.astype(jnp.float32)[:, None] * jnp.tile(points, elem_count)[None, :]
+    fraction = waves.astype(jnp.float32)[:, None] * np.tile(points, elem_count)[None, :]
     return 2.0 * math.pi / span * (whole.astype(jnp.float32) + fraction)
 
 
-def phases_at(waves, position, span, points):
-    element = position // P_SIZE
+def phases_at(waves, element, point_values, span):
     whole = waves[:, None] * (2 * element + 1)[None, :] % span
-    fraction = waves.astype(jnp.float32)[:, None] * points[position % P_SIZE][None, :]
+    fraction = waves.astype(jnp.float32)[:, None] * point_values[None, :]
     return 2.0 * math.pi / span * (whole.astype(jnp.float32) + fraction)
 
 
@@ -203,23 +211,31 @@
     span = 2 * elems_a * tiles
     scale = P_SIZE / (na_dev * tiles)
     points_list, weights_list, _ = gll_tables(P_SIZE)
-    points = jnp.asarray(points_list, jnp.float32)
-    weights = jnp.asarray(weights_list, jnp.float32)
+    points = np.asarray(points_list, np.float32)
+    weights = np.asarray(weights_list, np.float32)
     lead = (group_index > 0).astype(jnp.float32)
     trail = (group_index < groups - 1).astype(jnp.float32)
-    w_r = jnp.tile(weights, radial_nodes // P_SIZE)
-    w_a = jnp.tile(weights, elems_a)
-    w_b = jnp.tile(weights, elems_b)
+    w_r = np.tile(weights, radial_nodes // P_SIZE)
+    w_a = np.tile(weights, elems_a)
+    w_b = np.tile(weights, elems_b)
     mass3 = w_r[:, None, None] * w_a[None, :, None] * w_b[None, None, :]
+    b_first = np.zeros((nb_dev,), np.float32)
+    b_first[0] = weights[P_SIZE - 1]
+    b_last = np.zeros((nb_dev,), np.float32)
+    b_last[nb_dev - 1] = weights[0]
+    assembled_b = static_assembled(weights, elems_b, 0.0, 0.0) + lead * b_first + trail * b_last
     assembled = (
-        assembled_weights(weights, radial_nodes // P_SIZE, 0.0, 0.0)[:, None, None]
-        * assembled_weights(weights, elems_a, 1.0, 1.0)[None, :, None]
-        * assembled_weights(weights, elems_b, lead, trail)[None, None, :]
+        (
+            static_assembled(weights, radial_nodes // P_SIZE, 0.0, 0.0)[:, None]
+            * static_assembled(weights, elems_a, 1.0, 1.0)[None, :]
+        )[:, :, None]
+        * assembled_b[None, None, :]
     )
     column_mask = jnp.concatenate([lead[None], jnp.ones((nb_dev,), jnp.float32), trail[None]])
     rows_ext = (tile_index * na_dev - 1 + jnp.arange(na_dev + 2, dtype=jnp.int32)) % (na_dev * tiles)
-    cols_ext = group_index * nb_dev - 1 + jnp.arange(nb_dev + 2, dtype=jnp.int32)
-    surface_ext = weights[rows_ext % P_SIZE][:, None] * weights[cols_ext % P_SIZE][None, :]
+    row_points = (np.arange(na_dev + 2) - 1) % P_SIZE
+    col_points = (np.arange(nb_dev + 2) - 1) % P_SIZE
+    surface_ext = diffusivity * weights[row_points][:, None] * weights[col_points][None, :]
 
     rows = radial_nodes * na_dev
     mats = derivative_tables(radial_nodes, na_dev, nb_dev)
@@ -252,10 +268,10 @@
         )
 
     def flux_of(returned):
-        angle = phases_at(wave_of_slot, rows_ext, span, points)
+        angle = phases_at(wave_of_slot, rows_ext // P_SIZE, points[row_points], span)
         synth = jnp.stack([jnp.cos(angle).T, jnp.sin(angle).T], axis=2).reshape(na_dev + 2, -1)
         flux = -jnp.dot(synth, returned.reshape(-1, nb_dev + 2), precision=highest)
-        return diffusivity * surface_ext * flux
+        return surface_ext * flux
 
     mapped_len = 2 * (nb_dev + 2)
     slot_len = 3 * radial_nodes * na_dev

time: 86.3 us -> 83.1 us (0.963)
  local copies, waits for them, and re-layouts: 19.7 us -> 15.8 us
    another operation x6 -> x3, local copies, waits for them, and re-layouts: 2.62 us -> 0.66 us  [the longest x1 0.66 us: local(): w_b = jnp.tile(weights, elems_b)]
    gather x2 -> x0, local copies, waits for them, and re-layouts: 1.4 us -> none  [the longest x1 0.7 us: phases_at(): points[position % P_SIZE][None, :]]
    mul x8 -> x1, local copies, waits for them, and re-layouts: 1.31 us -> 0.16 us  [local(): (static_assembled(weights, radial_nodes // P_SIZE, 0.0, 0.0)[:, None] * s...]
  transfers between devices with their start and end apart: 8 -> 8, of which waited for: 2 -> 2; matrix products, arithmetic and copies ran while one was open for 16% -> 14% of each run, Pallas kernels for 4% -> 4%
where the time goes in v8:
time: 83.1 us; the launch traced here: 82.5 us
  starting transfers between devices  26.9 us (32%)
  local copies, waits for them, and re-layouts  15.8 us (19%)
  other arithmetic  12.2 us (15%)
  waiting for transfers between devices  11.9 us (14%)
  Pallas kernels  9.48 us (11%)
  matrix products  5.22 us (6%)
  between operations  0.87 us (1%)
    all_to_all x2, waiting for transfers between devices, joint_exchange(): lax.all_to_all(message, both, 0, 0, tiled=True).reshape(tiles, groups, -1)  11.9 us
    all_to_all x2, starting transfers between devices, joint_exchange(): lax.all_to_all(message, both, 0, 0, tiled=True).reshape(tiles, groups, -1)  9.86 us
    all_to_all x2, starting transfers between devices, owner_map(): gathered = lax.all_to_all(partial, both, 0, 0, tiled=True)  9.85 us
    ppermute x2, starting transfers between devices, joint_exchange(): from_down = lax.ppermute(a_lo, 'tile', down)  6.66 us
    dot_general x2, matrix products, flux_of(): flux = -jnp.dot(synth, returned.reshape(-1, nb_dev + 2), precision=highest)  4.43 us
    pallas_call x1, Pallas kernels, tendency(): pl.pallas_call(volume_kernel, out_shape=shapes)(*operands)  3.46 us
    pallas_call x1, Pallas kernels, tendency(): pl.pallas_call(first_volume_kernel, out_shape=shapes)(*operands, analysis)  3.42 us
    reshape x5, other arithmetic, assemble_dim(): return joined.reshape(shape)  2.98 us
  transfers between devices with their start and end apart: 8, of which 2 were waited for; matrix products, arithmetic and copies ran while one was open for 14% of the time, Pallas kernels for 4%

profile of v8, /device:TPU:0, one launch (start us, length us, event | category | flops | bytes accessed | tf_op | source)
XLA Modules:
  0.0 82.5 jit_solution(11185719582735945645)
XLA Ops:
  0.0 0.7 convert_element_type.71
  0.7 0.8 fusion.31
  1.6 1.3 %broadcast_multiply_fusion.3.table_ref = f32[64,16]{1,0:T(8,128)} fusion(f32[64,16]{1,0:T(8,128)S(1)} %bitcast.170, f32[16]{0:T(128)} %constant.309), kind=kLoop, calls=%fused_computation.76 | loop fusion | flops 1024 | bytes 8256 | tf_op jit(solution)/shard_map/mul | solution.py:250
  2.9 2.6 %shard_map.148.grad_ref = f32[9,128,128]{2,1,0:T(8,128)} custom-call(f32[3,128,128]{2,1,0:T(8,128)} %bitcast.157, f32[6,128,128]{2,1,0:T(8,128)} %constant.301.clone.mats_ref), custom_call_target="tpu_custom_call" | custom-call | tf_op jit(solution)/shard_map/pallas_call | solution.py:244
  5.5 3.4 %shard_map.149 = (f32[3,128,128]{2,1,0:T(8,128)}, f32[2,3,8,128]{3,2,1,0:T(8,128)}, f32[2,3,128]{2,1,0:T(4,128)}, f32[64,128]{1,0:T(8,128)}) custom-call(f32[3,128,128]{2,1,0:T(8,128)} %bitcast.156, f32[3,128,128]{2,1,0:T(8,128)} %bitcast.158, f32[9,128,128]{2,1,0:T(8,128)} %shard_map.148.grad_ref, f32[6,128,128]{2,1,0:T(8,128)} %constant.301.clone.mats_ref, ...), custom_call_target="tpu_custom_call" | custom-call | tf_op jit(solution)/shard_map/pallas_call | solution.py:361
  8.9 7.3 %all-to-all-start = ((f32[32,2,128]{2,1,0:T(2,128)}), f32[32,2,128]{2,1,0:T(2,128)S(1)}, u32[]{:S(2)}, u32[]{:S(2)}) async-start(f32[32,2,128]{2,1,0:T(2,128)} %bitcast.175), calls=%async_computation | async-start | bytes 65536 | tf_op jit(solution)/shard_map/all_to_all | solution.py:255
  16.3 0.7 slice_bitcast_fusion.24
  17.0 0.3 collective-permute-start
  17.2 3.3 %collective-permute-start.1 = (f32[3,8,1,128]{3,1,0,2:T(8,128)S(1)}, f32[3,8,1,128]{3,1,0,2:T(8,128)S(1)}, u32[]{:S(2)}, u32[]{:S(2)}) collective-permute-start(f32[3,8,1,128]{3,1,0,2:T(8,128)S(1)} %get-tuple-element.90), channel_id=1, source_target_pairs={{4,0},{8,4},{12,8},{16,12},{20,16},{24,20},{28,24},{0,28},{5,1},{9... | collective-permute-start | bytes 36872 | tf_op jit(solution)/shard_map/ppermute | solution.py:286
  20.6 0.7 fusion.66
  21.6 0.6 fusion.56
  22.3 0.1 broadcast_multiply_fusion.2
  22.4 0.8 and_reduce_fusion
  23.2 0.6 fusion.67
  23.9 0.2 fusion.8
  24.8 0.7 all_to_all.19
  25.5 4.0 %all-to-all-start.1 = ((f32[32,1,644]{2,1,0:T(1,128)}), f32[32,1,644]{2,1,0:T(1,128)S(1)}, u32[]{:S(2)}, u32[]{:S(2)}) async-start(f32[32,1,644]{2,1,0:T(1,128)} %all_to_all.19), calls=%async_computation.1 | async-start | bytes 196608 | tf_op jit(solution)/shard_map/all_to_all | solution.py:303
  29.7 0.2 copy.199
  29.9 7.5 %all-to-all-done.1 = f32[32,1,644]{2,1,0:T(1,128)S(1)} async-done(((f32[32,1,644]{2,1,0:T(1,128)}), f32[32,1,644]{2,1,0:T(1,128)S(1)}, u32[]{:S(2)}, u32[]{:S(2)}) %all-to-all-start.1) | async-done | bytes 82464 | tf_op jit(solution)/shard_map/all_to_all | solution.py:303
  37.5 0.2 reduce.9
  37.7 0.1 fusion.37
  38.6 0.2 reshape.985
  38.8 0.2 reshape.984
  39.0 0.3 pad_maximum_fusion
  39.4 2.2 %fusion.17 = (f32[3,8,18,130]{3,2,1,0:T(8,128)S(1)}, f32[18,130]{1,0:T(8,128)S(1)}) fusion(f32[3,8,18,130]{3,2,1,0:T(8,128)S(1)} %copy.265, s32[]{:T(128)} %bitcast.11, s32[]{:T(128)} %bitcast.12, pred[]{:T(512)} %and_reduce_fusion, f32[18,130]{1,0:T(8,128)S(1)} %copy-done.4, f32[18,64]{0,1:T(8,128)S(1)} %bitcast.164, f32[64,130]{1,0:T(8,128)S(1)} %reshape_reshape.6), kind=kOutput, calls=%fused_computation.52 | convolution fusion | flops 1806480 | bytes 196617 | tf_op jit(solution)/shard_map/dot_general | solution.py:273
  41.7 0.7 slice_reduce_fusion.5
  42.8 0.6 fusion.61
  43.8 0.2 maximum_bitcast_fusion.2
  44.0 0.2 slice_reduce_fusion.3
  44.2 0.1 slice.425
  44.3 0.5 copy.196
  44.8 0.2 fusion.58
  45.1 1.4 %slice.429 = f32[3,8,16,16,6]{2,4,3,1,0:T(8,128)} slice(f32[3,8,16,16,8]{2,4,3,1,0:T(8,128)S(1)} %bitcast.151), slice={[0:3], [0:8], [0:16], [0:16], [1:7]} | slice | bytes 294912 | tf_op jit(solution)/shard_map/slice | solution.py:147
  46.5 0.3 fusion.14
  46.8 0.6 copy.204
  47.5 2.5 %all-to-all-start.2 = ((f32[32,2,128]{2,1,0:T(2,128)}), f32[32,2,128]{2,1,0:T(2,128)S(1)}, u32[]{:S(2)}, u32[]{:S(2)}) async-start(f32[32,2,128]{2,1,0:T(2,128)} %copy.204), calls=%async_computation.2 | async-start | bytes 65536 | tf_op jit(solution)/shard_map/all_to_all | solution.py:255
  50.0 0.5 slice_add_fusion.3
  50.5 2.0 %maximum_bitcast_fusion = f32[3,8,16,128]{2,3,1,0:T(8,128)S(1)} fusion(f32[3,8,16,16,1]{2,4,3,1,0:T(1,128)S(1)} %get-tuple-element.66, f32[3,8,16,16,6]{2,4,3,1,0:T(8,128)} %slice.429, f32[3,8,16,16,1]{2,4,3,1,0:T(1,128)S(1)} %get-tuple-element.65), kind=kLoop, calls=%fused_computation | loop fusion | flops 98304 | bytes 393216 | tf_op jit(solution)/shard_map/reshape | solution.py:149
  52.6 0.4 copy.200
  53.0 0.7 multiply_add_fusion
  53.7 3.5 %shard_map.150 = (f32[3,128,128]{2,1,0:T(8,128)}, f32[2,3,8,128]{3,2,1,0:T(8,128)}, f32[2,3,128]{2,1,0:T(4,128)}) custom-call(f32[3,128,128]{2,1,0:T(8,128)} %bitcast.160, f32[3,128,128]{2,1,0:T(8,128)} %bitcast.159, f32[9,128,128]{2,1,0:T(8,128)} %shard_map.148.grad_ref, f32[6,128,128]{2,1,0:T(8,128)} %constant.301.clone.mats_ref, ...), custom_call_target="tpu_custom_call" | custom-call | tf_op jit(solution)/shard_map/pallas_call | solution.py:365
  57.2 0.7 fusion.64
  58.3 0.2 fusion.6
  59.2 0.7 all_to_all.22
  59.9 5.8 %all-to-all-start.3 = ((f32[32,1,644]{2,1,0:T(1,128)}), f32[32,1,644]{2,1,0:T(1,128)S(1)}, u32[]{:S(2)}, u32[]{:S(2)}) async-start(f32[32,1,644]{2,1,0:T(1,128)} %all_to_all.22), calls=%async_computation.3 | async-start | bytes 196608 | tf_op jit(solution)/shard_map/all_to_all | solution.py:303
  65.8 0.3 collective-permute-start.2
  66.1 3.4 %collective-permute-start.3 = (f32[3,8,1,128]{3,1,0,2:T(8,128)S(1)}, f32[3,8,1,128]{3,1,0,2:T(8,128)S(1)}, u32[]{:S(2)}, u32[]{:S(2)}) collective-permute-start(f32[3,8,1,128]{3,1,0,2:T(8,128)S(1)} %get-tuple-element.86), channel_id=1, source_target_pairs={{4,0},{8,4},{12,8},{16,12},{20,16},{24,20},{28,24},{0,28},{5,1},{9... | collective-permute-start | bytes 36872 | tf_op jit(solution)/shard_map/ppermute | solution.py:286
  69.4 4.4 %all-to-all-done.3 = f32[32,1,644]{2,1,0:T(1,128)S(1)} async-done(((f32[32,1,644]{2,1,0:T(1,128)}), f32[32,1,644]{2,1,0:T(1,128)S(1)}, u32[]{:S(2)}, u32[]{:S(2)}) %all-to-all-start.3) | async-done | bytes 82464 | tf_op jit(solution)/shard_map/all_to_all | solution.py:303
  73.8 0.2 reduce.20
  74.1 0.1 fusion.43
  75.1 0.2 reshape.987
  75.3 0.2 reshape.986
  75.5 0.3 pad_maximum_fusion.1
  75.8 2.2 %fusion.5 = f32[3,8,18,130]{3,2,1,0:T(8,128)S(1)} fusion(f32[3,8,18,130]{3,2,1,0:T(8,128)S(1)} %pad_maximum_fusion.1, s32[]{:T(128)} %bitcast.11, s32[]{:T(128)} %bitcast.12, f32[18,130]{1,0:T(8,128)S(1)} %copy-done.4, f32[18,64]{0,1:T(8,128)S(1)} %bitcast.165, f32[64,130]{1,0:T(8,128)S(1)} %reshape_reshape.7, pred[]{:T(512)} %and_reduce_fusion), kind=kOutput, calls=%fused_computation.9 | convolution fusion | flops 1806480 | bytes 172041 | tf_op jit(solution)/shard_map/dot_general | solution.py:273
  78.6 0.2 maximum_bitcast_fusion.3
  78.8 0.2 slice_reduce_fusion.1
  79.0 0.1 slice.468
  79.1 0.5 copy.220
  79.6 0.2 fusion.57
  79.8 0.2 slice.472
  80.1 0.5 slice_add_fusion.1
  80.6 0.6 maximum_bitcast_fusion.1
  81.3 0.4 copy.223
  81.7 0.8 add_multiply_fusion
  (159 shorter events, 5.3 us)
Async XLA Ops:
  0.0 23.9 %copy-start = (bf16[1,512,512]{2,1,0:T(8,128)(2,1)S(1)}, bf16[1,512,512]{2,1,0:T(8,128)(2,1)}, u32[]{:S(2)}) copy-start(bf16[1,512,512]{2,1,0:T(8,128)(2,1)} %param.21) | copy-start | bytes 1572868
  2.9 18.7 %copy-start.10 = (s32[32]{0:T(128)S(1)}, s32[32]{0:T(128)}, u32[]{:S(2)}) copy-start(s32[32]{0:T(128)} %param.22) | copy-start | bytes 388
  2.9 18.7 %copy-start.14 = (f32[18]{0:T(128)S(1)}, f32[18]{0:T(128)}, u32[]{:S(2)}) copy-start(f32[18]{0:T(128)} %constant.310) | copy-start | bytes 220
  2.9 19.4 %copy-start.16 = (f32[128]{0:T(128)S(1)}, f32[128]{0:T(128)}, u32[]{:S(2)}) copy-start(f32[128]{0:T(128)} %constant.299.clone) | copy-start | bytes 1540
  2.9 19.4 %copy-start.17 = (f32[128]{0:T(128)S(1)}, f32[128]{0:T(128)}, u32[]{:S(2)}) copy-start(f32[128]{0:T(128)} %constant.298.clone) | copy-start | bytes 1540
  2.9 19.4 %copy-start.18 = (f32[128]{0:T(128)S(1)}, f32[128]{0:T(128)}, u32[]{:S(2)}) copy-start(f32[128]{0:T(128)} %constant.297.clone) | copy-start | bytes 1540
  2.9 19.4 %copy-start.9 = (f32[8,16]{1,0:T(8,128)S(1)}, f32[8,16]{1,0:T(8,128)}, u32[]{:S(2)}) copy-start(f32[8,16]{1,0:T(8,128)} %constant.311) | copy-start | bytes 1540
  2.9 19.5 %copy-start.15 = (s32[4]{0:T(128)S(1)}, s32[4]{0:T(128)}, u32[]{:S(2)}) copy-start(s32[4]{0:T(128)} %constant.289.clone.1) | copy-start | bytes 52
  8.9 20.7 %copy-start.1 = (f32[3,8,16,128]{3,2,1,0:T(8,128)S(1)}, f32[3,8,16,128]{3,2,1,0:T(8,128)}, u32[]{:S(2)}) copy-start(f32[3,8,16,128]{3,2,1,0:T(8,128)} %param.19) | copy-start | bytes 589828
  8.9 14.9 %all-to-all-start = ((f32[32,2,128]{2,1,0:T(2,128)}), f32[32,2,128]{2,1,0:T(2,128)S(1)}, u32[]{:S(2)}, u32[]{:S(2)}) async-start(f32[32,2,128]{2,1,0:T(2,128)} %bitcast.175), calls=%async_computation | async-start | bytes 65536 | tf_op jit(solution)/shard_map/all_to_all | solution.py:255
  17.0 21.4 %collective-permute-start = (f32[3,8,1,128]{3,1,0,2:T(8,128)S(1)}, f32[3,8,1,128]{3,1,0,2:T(8,128)S(1)}, u32[]{:S(2)}, u32[]{:S(2)}) collective-permute-start(f32[3,8,1,128]{3,1,0,2:T(8,128)S(1)} %get-tuple-element.89), channel_id=1, source_target_pairs={{0,4},{4,8},{8,12},{12,16},{16,20},{20,24},{24,28},{28,0},{1,5},{5... | collective-permute-start | bytes 36872 | tf_op jit(solution)/shard_map/ppermute | solution.py:285
  17.2 21.0 %collective-permute-start.1 = (f32[3,8,1,128]{3,1,0,2:T(8,128)S(1)}, f32[3,8,1,128]{3,1,0,2:T(8,128)S(1)}, u32[]{:S(2)}, u32[]{:S(2)}) collective-permute-start(f32[3,8,1,128]{3,1,0,2:T(8,128)S(1)} %get-tuple-element.90), channel_id=1, source_target_pairs={{4,0},{8,4},{12,8},{16,12},{20,16},{24,20},{28,24},{0,28},{5,1},{9... | collective-permute-start | bytes 36872 | tf_op jit(solution)/shard_map/ppermute | solution.py:286
  24.1 14.9 %copy-start.2 = (f32[3,128,128]{2,1,0:T(8,128)S(1)}, f32[3,128,128]{2,1,0:T(8,128)}, u32[]{:S(2)}) copy-start(f32[3,128,128]{2,1,0:T(8,128)} %get-tuple-element.39) | copy-start | bytes 589828
  25.5 12.0 %all-to-all-start.1 = ((f32[32,1,644]{2,1,0:T(1,128)}), f32[32,1,644]{2,1,0:T(1,128)S(1)}, u32[]{:S(2)}, u32[]{:S(2)}) async-start(f32[32,1,644]{2,1,0:T(1,128)} %all_to_all.19), calls=%async_computation.1 | async-start | bytes 196608 | tf_op jit(solution)/shard_map/all_to_all | solution.py:303
  29.6 12.9 %copy-start.7 = (f32[130]{0:T(256)}, f32[130]{0:T(256)S(1)}, u32[]{:S(2)}) copy-start(f32[130]{0:T(256)S(1)} %pad_maximum_fusion.16) | copy-start | bytes 1564
  38.4 1.0 %copy-start.4 = (f32[18,130]{1,0:T(8,128)S(1)}, f32[18,130]{1,0:T(8,128)}, u32[]{:S(2)}) copy-start(f32[18,130]{1,0:T(8,128)} %constant.306.clone) | copy-start | bytes 28084
  45.0 1.4 %copy-start.5 = (f32[16,15,1]{0,2,1:T(1,128)S(1)}, f32[16,15,1]{0,2,1:T(1,128)}, u32[]{:S(2)}) copy-start(f32[16,15,1]{0,2,1:T(1,128)} %get-tuple-element.84) | copy-start | bytes 2884
  45.0 1.4 %copy-start.11 = (f32[16]{0:T(128)S(1)}, f32[16]{0:T(128)}, u32[]{:S(2)}) copy-start(f32[16]{0:T(128)} %get-tuple-element.59) | copy-start | bytes 196
  45.1 1.4 %copy-start.12 = (f32[16]{0:T(128)S(1)}, f32[16]{0:T(128)}, u32[]{:S(2)}) copy-start(f32[16]{0:T(128)} %get-tuple-element.60) | copy-start | bytes 196
  45.1 1.4 %copy-start.13 = (f32[16]{0:T(128)S(1)}, f32[16]{0:T(128)}, u32[]{:S(2)}) copy-start(f32[16]{0:T(128)} %constant.309) | copy-start | bytes 196
  47.5 10.8 %all-to-all-start.2 = ((f32[32,2,128]{2,1,0:T(2,128)}), f32[32,2,128]{2,1,0:T(2,128)S(1)}, u32[]{:S(2)}, u32[]{:S(2)}) async-start(f32[32,2,128]{2,1,0:T(2,128)} %copy.204), calls=%async_computation.2 | async-start | bytes 65536 | tf_op jit(solution)/shard_map/all_to_all | solution.py:255
  57.2 8.6 %copy-start.6 = (f32[2,3,8,128]{3,2,1,0:T(8,128)S(1)}, f32[2,3,8,128]{3,2,1,0:T(8,128)}, u32[]{:S(2)}) copy-start(f32[2,3,8,128]{3,2,1,0:T(8,128)} %get-tuple-element.41) | copy-start | bytes 73732
  57.2 18.3 %copy-start.3 = (f32[3,128,128]{2,1,0:T(8,128)S(1)}, f32[3,128,128]{2,1,0:T(8,128)}, u32[]{:S(2)}) copy-start(f32[3,128,128]{2,1,0:T(8,128)} %get-tuple-element.42) | copy-start | bytes 589828
  59.9 18.1 %copy-start.8 = (f32[130]{0:T(256)S(1)}, f32[130]{0:T(256)}, u32[]{:S(2)}) copy-start(f32[130]{0:T(256)} %copy-done.7) | copy-start | bytes 1564
  59.9 13.9 %all-to-all-start.3 = ((f32[32,1,644]{2,1,0:T(1,128)}), f32[32,1,644]{2,1,0:T(1,128)S(1)}, u32[]{:S(2)}, u32[]{:S(2)}) async-start(f32[32,1,644]{2,1,0:T(1,128)} %all_to_all.22), calls=%async_computation.3 | async-start | bytes 196608 | tf_op jit(solution)/shard_map/all_to_all | solution.py:303
  65.8 8.9 %collective-permute-start.2 = (f32[3,8,1,128]{3,1,0,2:T(8,128)S(1)}, f32[3,8,1,128]{3,1,0,2:T(8,128)S(1)}, u32[]{:S(2)}, u32[]{:S(2)}) collective-permute-start(f32[3,8,1,128]{3,1,0,2:T(8,128)S(1)} %get-tuple-element.85), channel_id=1, source_target_pairs={{0,4},{4,8},{8,12},{12,16},{16,20},{20,24},{24,28},{28,0},{1,5},{5... | collective-permute-start | bytes 36872 | tf_op jit(solution)/shard_map/ppermute | solution.py:285
  66.1 8.9 %collective-permute-start.3 = (f32[3,8,1,128]{3,1,0,2:T(8,128)S(1)}, f32[3,8,1,128]{3,1,0,2:T(8,128)S(1)}, u32[]{:S(2)}, u32[]{:S(2)}) collective-permute-start(f32[3,8,1,128]{3,1,0,2:T(8,128)S(1)} %get-tuple-element.86), channel_id=1, source_target_pairs={{4,0},{8,4},{12,8},{16,12},{20,16},{24,20},{28,24},{0,28},{5,1},{9... | collective-permute-start | bytes 36872 | tf_op jit(solution)/shard_map/ppermute | solution.py:286

commit v9 on v8

--- a/solution.py
+++ b/solution.py
@@ -231,7 +231,6 @@
         )[:, :, None]
         * assembled_b[None, None, :]
     )
-    column_mask = jnp.concatenate([lead[None], jnp.ones((nb_dev,), jnp.float32), trail[None]])
     rows_ext = (tile_index * na_dev - 1 + jnp.arange(na_dev + 2, dtype=jnp.int32)) % (na_dev * tiles)
     row_points = (np.arange(na_dev + 2) - 1) % P_SIZE
     col_points = (np.arange(nb_dev + 2) - 1) % P_SIZE
@@ -341,13 +340,24 @@
         bottom = jnp.concatenate([corner_dl, from_down, corner_dr], axis=3)
         return jnp.concatenate([top, middle, bottom], axis=2)
 
+    join_b = np.zeros((nb_dev + 2, nb_dev), np.float32)
+    join_b[np.arange(nb_dev) + 1, np.arange(nb_dev)] = 1.0
+    inner_first = np.arange(P_SIZE, nb_dev, P_SIZE)
+    join_b[inner_first, inner_first] = 1.0
+    inner_last = np.arange(P_SIZE - 1, nb_dev - 1, P_SIZE)
+    join_b[inner_last + 2, inner_last] = 1.0
+    edge_lead = np.zeros((nb_dev + 2, nb_dev), np.float32)
+    edge_lead[0, 0] = 1.0
+    edge_trail = np.zeros((nb_dev + 2, nb_dev), np.float32)
+    edge_trail[nb_dev + 1, nb_dev - 1] = 1.0
+    join_b = join_b + lead * edge_lead + trail * edge_trail
+
     def assemble_ext(padded):
         last = padded.ndim - 1
-        padded = padded * column_mask
         along_a = assemble_dim(
             padded[..., 1:-1, :], last - 1, padded[..., 0:1, :], padded[..., -1:, :]
         )
-        return assemble_dim(along_a[..., 1:-1], last, along_a[..., 0:1], along_a[..., -1:])
+        return jnp.dot(along_a, join_b, precision=highest)
 
     def tendency(parts, surface):
         shapes = (

time: 83.1 us -> 78.2 us (0.941)
  other arithmetic: 12.2 us -> 4.39 us
  matrix products: 5.22 us -> 7.76 us
  starting transfers between devices: 26.9 us -> 25.7 us
  waiting for transfers between devices: 11.9 us -> 13 us
    unnamed x49 -> x56, local copies, waits for them, and re-layouts: 0.56 us -> 7.33 us
    reshape x5 -> x0, other arithmetic: 2.98 us -> none  [assemble_dim(): return joined.reshape(shape)]
    dot_general x0 -> x3, matrix products: none -> 2.66 us  [assemble_ext(): return jnp.dot(along_a, join_b, precision=highest)]
    slice x10 -> x0, local copies, waits for them, and re-layouts: 2.52 us -> none  [the longest x6 1.32 us: assemble_ext(): along_a[..., 1:-1]]
    slice x6 -> x3, local copies, waits for them, and re-layouts: 1.7 us -> 0.08 us  [assemble_dim(): middle = lax.slice_in_dim(blocks, 1, P_SIZE - 1, axis=axis_pos + 1)]
    slice x2 -> x4, local copies, waits for them, and re-layouts: 0.02 us -> 1.44 us  [joint_exchange(): received[:, :, :mapped_len].reshape(tiles * groups, 2, nb_dev + 2)]
    all_to_all x2, waiting for transfers between devices: 0.01 us -> 1.31 us  [owner_map(): gathered = lax.all_to_all(partial, both, 0, 0, tiled=True)]
    all_to_all x2, starting transfers between devices: 9.86 us -> 8.57 us  [joint_exchange(): lax.all_to_all(message, both, 0, 0, tiled=True).reshape(tiles, groups, -1)]
  transfers between devices with their start and end apart: 8 -> 8, of which waited for: 2 -> 3; matrix products, arithmetic and copies ran while one was open for 14% -> 11% of each run, Pallas kernels for 4% -> 4%
where the time goes in v9:
time: 78.2 us; the launch traced here: 77.3 us
  starting transfers between devices  25.7 us (33%)
  local copies, waits for them, and re-layouts  16.3 us (21%)
  waiting for transfers between devices  13 us (17%)
  Pallas kernels  9.44 us (12%)
  matrix products  7.76 us (10%)
  other arithmetic  4.39 us (6%)
    all_to_all x2, waiting for transfers between devices, joint_exchange(): lax.all_to_all(message, both, 0, 0, tiled=True).reshape(tiles, groups, -1)  11.6 us
    all_to_all x2, starting transfers between devices, owner_map(): gathered = lax.all_to_all(partial, both, 0, 0, tiled=True)  9.86 us
    all_to_all x2, starting transfers between devices, joint_exchange(): lax.all_to_all(message, both, 0, 0, tiled=True).reshape(tiles, groups, -1)  8.57 us
    unnamed x56, local copies, waits for them, and re-layouts  7.33 us
    ppermute x2, starting transfers between devices, joint_exchange(): from_down = lax.ppermute(a_lo, 'tile', down)  6.66 us
    dot_general x2, matrix products, flux_of(): flux = -jnp.dot(synth, returned.reshape(-1, nb_dev + 2), precision=highest)  4.31 us
    pallas_call x1, Pallas kernels, tendency(): pl.pallas_call(volume_kernel, out_shape=shapes)(*operands)  3.47 us
    pallas_call x1, Pallas kernels, tendency(): pl.pallas_call(first_volume_kernel, out_shape=shapes)(*operands, analysis)  3.42 us
  transfers between devices with their start and end apart: 8, of which 3 were waited for; matrix products, arithmetic and copies ran while one was open for 11% of the time, Pallas kernels for 4%

profile of v9, /device:TPU:0, one launch (start us, length us, event | category | flops | bytes accessed | tf_op | source)
XLA Modules:
  0.0 77.3 jit_solution(1146409161784114597)
XLA Ops:
  0.0 0.7 copy-done.15
  0.7 0.7 copy-done.18
  1.4 0.1 fusion.52
  1.6 0.7 copy-done.16
  2.3 0.6 broadcast_multiply_fusion.1.table_ref
  2.9 2.6 %shard_map.175.grad_ref = f32[9,128,128]{2,1,0:T(8,128)} custom-call(f32[3,128,128]{2,1,0:T(8,128)} %bitcast.122, f32[6,128,128]{2,1,0:T(8,128)} %constant.305.clone.mats_ref), custom_call_target="tpu_custom_call" | custom-call | tf_op jit(solution)/shard_map/pallas_call | solution.py:243
  5.4 3.4 %shard_map.176 = (f32[3,128,128]{2,1,0:T(8,128)}, f32[2,3,8,128]{3,2,1,0:T(8,128)}, f32[2,3,128]{2,1,0:T(4,128)}, f32[64,128]{1,0:T(8,128)}) custom-call(f32[3,128,128]{2,1,0:T(8,128)} %bitcast.127, f32[3,128,128]{2,1,0:T(8,128)} %bitcast.123, f32[9,128,128]{2,1,0:T(8,128)} %shard_map.175.grad_ref, f32[6,128,128]{2,1,0:T(8,128)} %constant.305.clone.mats_ref, ...), custom_call_target="tpu_custom_call" | custom-call | tf_op jit(solution)/shard_map/pallas_call | solution.py:371
  8.8 7.3 %all-to-all-start = ((f32[32,2,128]{2,1,0:T(2,128)}), f32[32,2,128]{2,1,0:T(2,128)S(1)}, u32[]{:S(2)}, u32[]{:S(2)}) async-start(f32[32,2,128]{2,1,0:T(2,128)} %bitcast.134), calls=%async_computation | async-start | bytes 65536 | tf_op jit(solution)/shard_map/all_to_all | solution.py:254
  16.2 0.3 collective-permute-start
  16.5 3.3 %collective-permute-start.1 = (f32[3,8,1,128]{3,1,0,2:T(8,128)S(1)}, f32[3,8,1,128]{3,1,0,2:T(8,128)S(1)}, u32[]{:S(2)}, u32[]{:S(2)}) collective-permute-start(f32[3,8,1,128]{3,1,0,2:T(8,128)S(1)} %get-tuple-element.72), channel_id=1, source_target_pairs={{4,0},{8,4},{12,8},{16,12},{20,16},{24,20},{28,24},{0,28},{5,1},{9... | collective-permute-start | bytes 36872 | tf_op jit(solution)/shard_map/ppermute | solution.py:285
  19.8 0.7 copy-done.14
  20.8 0.6 copy-done.17
  21.5 0.6 fusion.78
  22.3 0.6 copy-done.19
  22.9 0.8 %and_reduce_fusion = pred[]{:T(512)} fusion(s32[4]{0:T(128)S(1)} %copy-done.19, s32[1]{0:T(128)} %constant.293.clone.1, s32[2]{0:T(128)S(1)} %iota_multiply_fusion), kind=kLoop, calls=%fused_computation.142 | loop fusion | flops 23 | bytes 29 | tf_op jit(solution)/shard_map/reduce.2
  23.7 0.2 fusion.16
  24.0 0.1 pad_maximum_fusion.15
  24.1 0.1 stack.49
  24.2 0.1 stack.50
  24.3 0.1 stack.51
  24.3 0.1 stack.52
  24.6 0.7 all_to_all.19
  25.3 4.0 %all-to-all-start.1 = ((f32[32,1,644]{2,1,0:T(1,128)}), f32[32,1,644]{2,1,0:T(1,128)S(1)}, u32[]{:S(2)}, u32[]{:S(2)}) async-start(f32[32,1,644]{2,1,0:T(1,128)} %all_to_all.19), calls=%async_computation.1 | async-start | bytes 196608 | tf_op jit(solution)/shard_map/all_to_all | solution.py:302
  29.3 0.6 fusion.86
  30.0 7.3 %all-to-all-done.1 = f32[32,1,644]{2,1,0:T(1,128)S(1)} async-done(((f32[32,1,644]{2,1,0:T(1,128)}), f32[32,1,644]{2,1,0:T(1,128)S(1)}, u32[]{:S(2)}, u32[]{:S(2)}) %all-to-all-start.1) | async-done | bytes 82464 | tf_op jit(solution)/shard_map/all_to_all | solution.py:302
  37.3 0.2 reduce.9
  37.5 0.1 fusion.58
  38.2 0.2 reshape.935
  38.4 0.2 reshape.936
  38.8 0.6 copy-done.4
  39.3 0.3 pad_maximum_fusion
  39.7 0.7 slice-done.1
  40.5 0.7 copy-done.7
  41.2 2.2 %fusion.34 = (f32[3,8,18,130]{3,2,1,0:T(8,128)S(1)}, f32[18,130]{1,0:T(8,128)S(1)}) fusion(f32[3,8,18,130]{3,2,1,0:T(8,128)S(1)} %copy.123, s32[]{:T(128)} %bitcast.11, s32[]{:T(128)} %bitcast.12, pred[]{:T(512)} %and_reduce_fusion, f32[18,130]{1,0:T(8,128)S(1)} %copy-done.7, f32[18,64]{0,1:T(8,128)S(1)} %bitcast.125, f32[64,130]{1,0:T(8,128)S(1)} %reshape_reshape.6), kind=kOutput, calls=%fused_computation.58 | convolution fusion | flops 1806480 | bytes 196617 | tf_op jit(solution)/shard_map/dot_general | solution.py:272
  43.7 0.8 %copy-done.3 = f32[3,8,16,128]{3,2,1,0:T(8,128)S(1)} copy-done((f32[3,8,16,128]{3,2,1,0:T(8,128)S(1)}, f32[3,8,16,128]{3,2,1,0:T(8,128)}, u32[]{:S(2)}) %copy-start.3) | copy-done | bytes 196632
  44.7 0.2 fusion.13
  44.9 0.3 fusion.44
  45.2 0.6 copy.68
  45.8 2.6 %all-to-all-start.2 = ((f32[32,2,128]{2,1,0:T(2,128)}), f32[32,2,128]{2,1,0:T(2,128)S(1)}, u32[]{:S(2)}, u32[]{:S(2)}) async-start(f32[32,2,128]{2,1,0:T(2,128)} %copy.68), calls=%async_computation.2 | async-start | bytes 65536 | tf_op jit(solution)/shard_map/all_to_all | solution.py:254
  48.7 1.2 %fusion.3 = f32[3,8,16,128]{3,2,1,0:T(8,128)} fusion(f32[3,8,16,128]{3,2,1,0:T(8,128)S(1)} %copy-done.3, f32[3,8,2,1,130]{4,3,2,1,0:T(1,128)S(1)} %copy.67, f32[3,8,2,6,130]{4,3,2,1,0:T(8,128)S(1)} %slice.319, f32[3,8,2,1,130]{4,3,2,1,0:T(1,128)S(1)} %copy.66, f32[8,16,128]{2,1,0:T(8,128)S(1)} %broadcast_multiply_fusion, f32[130,128]{1,0:T(8,128)S(1)} %copy-done.9, ...), kind=kOutput, calls=%fused_computation.5 | convolution fusion | flops 76990976 | bytes 858120 | tf_op jit(solution)/shard_map/dot_general | solution.py:360
  49.9 3.5 %shard_map.177 = (f32[3,128,128]{2,1,0:T(8,128)}, f32[2,3,8,128]{3,2,1,0:T(8,128)}, f32[2,3,128]{2,1,0:T(4,128)}) custom-call(f32[3,128,128]{2,1,0:T(8,128)} %bitcast.130, f32[3,128,128]{2,1,0:T(8,128)} %bitcast.124, f32[9,128,128]{2,1,0:T(8,128)} %shard_map.175.grad_ref, f32[6,128,128]{2,1,0:T(8,128)} %constant.305.clone.mats_ref, ...), custom_call_target="tpu_custom_call" | custom-call | tf_op jit(solution)/shard_map/pallas_call | solution.py:375
  53.4 0.7 fusion.83
  54.4 1.3 %all-to-all-done.2 = f32[32,2,128]{2,1,0:T(2,128)S(1)} async-done(((f32[32,2,128]{2,1,0:T(2,128)}), f32[32,2,128]{2,1,0:T(2,128)S(1)}, u32[]{:S(2)}, u32[]{:S(2)}) %all-to-all-start.2) | async-done | bytes 32800 | tf_op jit(solution)/shard_map/all_to_all | solution.py:254
  55.7 0.2 fusion.14
  56.0 0.1 pad_maximum_fusion.13
  56.1 0.1 stack.55
  56.2 0.1 stack.56
  56.3 0.1 stack.57
  56.4 0.1 stack.58
  56.6 0.7 all_to_all.22
  57.3 4.5 %all-to-all-start.3 = ((f32[32,1,644]{2,1,0:T(1,128)}), f32[32,1,644]{2,1,0:T(1,128)S(1)}, u32[]{:S(2)}, u32[]{:S(2)}) async-start(f32[32,1,644]{2,1,0:T(1,128)} %all_to_all.22), calls=%async_computation.3 | async-start | bytes 196608 | tf_op jit(solution)/shard_map/all_to_all | solution.py:302
  61.9 0.3 collective-permute-start.2
  62.2 3.4 %collective-permute-start.3 = (f32[3,8,1,128]{3,1,0,2:T(8,128)S(1)}, f32[3,8,1,128]{3,1,0,2:T(8,128)S(1)}, u32[]{:S(2)}, u32[]{:S(2)}) collective-permute-start(f32[3,8,1,128]{3,1,0,2:T(8,128)S(1)} %get-tuple-element.68), channel_id=1, source_target_pairs={{4,0},{8,4},{12,8},{16,12},{20,16},{24,20},{28,24},{0,28},{5,1},{9... | collective-permute-start | bytes 36872 | tf_op jit(solution)/shard_map/ppermute | solution.py:285
  65.6 4.4 %all-to-all-done.3 = f32[32,1,644]{2,1,0:T(1,128)S(1)} async-done(((f32[32,1,644]{2,1,0:T(1,128)}), f32[32,1,644]{2,1,0:T(1,128)S(1)}, u32[]{:S(2)}, u32[]{:S(2)}) %all-to-all-start.3) | async-done | bytes 82464 | tf_op jit(solution)/shard_map/all_to_all | solution.py:302
  69.9 0.2 reduce.16
  70.2 0.1 fusion.64
  70.7 0.1 reshape.924
  71.0 0.2 reshape.937
  71.2 0.2 reshape.938
  71.5 0.7 slice-done
  72.3 0.3 pad_maximum_fusion.1
  72.6 2.2 %fusion.10 = f32[3,8,18,130]{3,2,1,0:T(8,128)S(1)} fusion(f32[3,8,18,130]{3,2,1,0:T(8,128)S(1)} %pad_maximum_fusion.1, s32[]{:T(128)} %bitcast.11, s32[]{:T(128)} %bitcast.12, f32[18,130]{1,0:T(8,128)S(1)} %copy-done.7, f32[18,64]{0,1:T(8,128)S(1)} %bitcast.126, f32[64,130]{1,0:T(8,128)S(1)} %reshape_reshape.7, pred[]{:T(512)} %and_reduce_fusion), kind=kOutput, calls=%fused_computation.14 | convolution fusion | flops 1806480 | bytes 172041 | tf_op jit(solution)/shard_map/dot_general | solution.py:272
  75.3 0.7 copy-done.6
  76.1 1.2 %fusion.4 = f32[3,8,16,128]{3,2,1,0:T(8,128)} fusion(f32[3,8,2,1,130]{4,3,2,1,0:T(1,128)S(1)} %copy.83, f32[3,8,2,6,130]{4,3,2,1,0:T(8,128)S(1)} %slice.346, f32[3,8,2,1,130]{4,3,2,1,0:T(1,128)S(1)} %copy.82, f32[3,8,16,128]{3,2,1,0:T(8,128)S(1)} %copy-done.3, f32[3,8,16,128]{3,2,1,0:T(8,128)S(1)} %copy-done.6, ...), kind=kOutput, calls=%fused_computation.6 | convolution fusion | flops 77089280 | bytes 1054728 | tf_op jit(solution)/shard_map/dot_general | solution.py:360
  (138 shorter events, 4.1 us)
Async XLA Ops:
  0.0 23.7 %copy-start = (bf16[1,512,512]{2,1,0:T(8,128)(2,1)S(1)}, bf16[1,512,512]{2,1,0:T(8,128)(2,1)}, u32[]{:S(2)}) copy-start(bf16[1,512,512]{2,1,0:T(8,128)(2,1)} %param.24) | copy-start | bytes 1572868
  0.0 0.7 copy-start.15
  0.7 0.7 copy-start.18
  1.6 0.7 copy-start.16
  8.8 7.3 %copy-start.12 = (f32[2,3,8,128]{3,2,1,0:T(8,128)S(1)}, f32[2,3,8,128]{3,2,1,0:T(8,128)}, u32[]{:S(2)}) copy-start(f32[2,3,8,128]{3,2,1,0:T(8,128)} %get-tuple-element.38) | copy-start | bytes 73732
  8.8 14.8 %all-to-all-start = ((f32[32,2,128]{2,1,0:T(2,128)}), f32[32,2,128]{2,1,0:T(2,128)S(1)}, u32[]{:S(2)}, u32[]{:S(2)}) async-start(f32[32,2,128]{2,1,0:T(2,128)} %bitcast.134), calls=%async_computation | async-start | bytes 65536 | tf_op jit(solution)/shard_map/all_to_all | solution.py:254
  16.2 21.9 %collective-permute-start = (f32[3,8,1,128]{3,1,0,2:T(8,128)S(1)}, f32[3,8,1,128]{3,1,0,2:T(8,128)S(1)}, u32[]{:S(2)}, u32[]{:S(2)}) collective-permute-start(f32[3,8,1,128]{3,1,0,2:T(8,128)S(1)} %get-tuple-element.71), channel_id=1, source_target_pairs={{0,4},{4,8},{8,12},{12,16},{16,20},{20,24},{24,28},{28,0},{1,5},{5... | collective-permute-start | bytes 36872 | tf_op jit(solution)/shard_map/ppermute | solution.py:284
  16.5 22.2 %collective-permute-start.1 = (f32[3,8,1,128]{3,1,0,2:T(8,128)S(1)}, f32[3,8,1,128]{3,1,0,2:T(8,128)S(1)}, u32[]{:S(2)}, u32[]{:S(2)}) collective-permute-start(f32[3,8,1,128]{3,1,0,2:T(8,128)S(1)} %get-tuple-element.72), channel_id=1, source_target_pairs={{4,0},{8,4},{12,8},{16,12},{20,16},{24,20},{28,24},{0,28},{5,1},{9... | collective-permute-start | bytes 36872 | tf_op jit(solution)/shard_map/ppermute | solution.py:285
  19.8 0.7 copy-start.14
  20.8 0.7 copy-start.17
  21.5 0.7 copy-start.20
  21.5 0.7 copy-start.21
  21.5 0.7 copy-start.22
  21.5 0.7 copy-start.13
  22.2 0.7 copy-start.19
  25.3 12.0 %all-to-all-start.1 = ((f32[32,1,644]{2,1,0:T(1,128)}), f32[32,1,644]{2,1,0:T(1,128)S(1)}, u32[]{:S(2)}, u32[]{:S(2)}) async-start(f32[32,1,644]{2,1,0:T(1,128)} %all_to_all.19), calls=%async_computation.1 | async-start | bytes 196608 | tf_op jit(solution)/shard_map/all_to_all | solution.py:302
  37.5 0.6 copy-start.2
  38.4 0.9 %copy-start.4 = (f32[3,128,128]{2,1,0:T(8,128)S(1)}, f32[3,128,128]{2,1,0:T(8,128)}, u32[]{:S(2)}) copy-start(f32[3,128,128]{2,1,0:T(8,128)} %get-tuple-element.39) | copy-start | bytes 589828
  39.6 0.8 %slice-start.1 = ((f32[8,4,644]{2,1,0:T(4,128)}), f32[8,4,260]{2,1,0:T(4,128)S(1)}, s32[]{:S(2)}) async-start(f32[8,4,644]{2,1,0:T(4,128)} %copy-done.2), calls=%async_computation.5 | async-start | bytes 98304 | tf_op jit(solution)/shard_map/slice | solution.py:303
  40.4 0.7 copy-start.7
  43.6 0.9 %copy-start.3 = (f32[3,8,16,128]{3,2,1,0:T(8,128)S(1)}, f32[3,8,16,128]{3,2,1,0:T(8,128)}, u32[]{:S(2)}) copy-start(f32[3,8,16,128]{3,2,1,0:T(8,128)} %param.22) | copy-start | bytes 589828
  43.6 1.0 %copy-start.8 = (f32[130,128]{1,0:T(8,128)S(1)}, f32[130,128]{1,0:T(8,128)}, u32[]{:S(2)}) copy-start(f32[130,128]{1,0:T(8,128)} %constant.308.clone) | copy-start | bytes 199684
  43.6 1.0 %copy-start.9 = (f32[130,128]{1,0:T(8,128)S(1)}, f32[130,128]{1,0:T(8,128)}, u32[]{:S(2)}) copy-start(f32[130,128]{1,0:T(8,128)} %constant.309.clone) | copy-start | bytes 199684
  43.7 1.0 %copy-start.10 = (f32[130,128]{1,0:T(8,128)S(1)}, f32[130,128]{1,0:T(8,128)}, u32[]{:S(2)}) copy-start(f32[130,128]{1,0:T(8,128)} %constant.310.clone) | copy-start | bytes 199684
  45.8 9.9 %all-to-all-start.2 = ((f32[32,2,128]{2,1,0:T(2,128)}), f32[32,2,128]{2,1,0:T(2,128)S(1)}, u32[]{:S(2)}, u32[]{:S(2)}) async-start(f32[32,2,128]{2,1,0:T(2,128)} %copy.68), calls=%async_computation.2 | async-start | bytes 65536 | tf_op jit(solution)/shard_map/all_to_all | solution.py:254
  57.3 4.5 %copy-start.11 = (f32[2,3,8,128]{3,2,1,0:T(8,128)S(1)}, f32[2,3,8,128]{3,2,1,0:T(8,128)}, u32[]{:S(2)}) copy-start(f32[2,3,8,128]{3,2,1,0:T(8,128)} %get-tuple-element.41) | copy-start | bytes 73732
  57.3 12.6 %all-to-all-start.3 = ((f32[32,1,644]{2,1,0:T(1,128)}), f32[32,1,644]{2,1,0:T(1,128)S(1)}, u32[]{:S(2)}, u32[]{:S(2)}) async-start(f32[32,1,644]{2,1,0:T(1,128)} %all_to_all.22), calls=%async_computation.3 | async-start | bytes 196608 | tf_op jit(solution)/shard_map/all_to_all | solution.py:302
  61.9 8.9 %collective-permute-start.2 = (f32[3,8,1,128]{3,1,0,2:T(8,128)S(1)}, f32[3,8,1,128]{3,1,0,2:T(8,128)S(1)}, u32[]{:S(2)}, u32[]{:S(2)}) collective-permute-start(f32[3,8,1,128]{3,1,0,2:T(8,128)S(1)} %get-tuple-element.67), channel_id=1, source_target_pairs={{0,4},{4,8},{8,12},{12,16},{16,20},{20,24},{24,28},{28,0},{1,5},{5... | collective-permute-start | bytes 36872 | tf_op jit(solution)/shard_map/ppermute | solution.py:284
  62.2 9.2 %collective-permute-start.3 = (f32[3,8,1,128]{3,1,0,2:T(8,128)S(1)}, f32[3,8,1,128]{3,1,0,2:T(8,128)S(1)}, u32[]{:S(2)}, u32[]{:S(2)}) collective-permute-start(f32[3,8,1,128]{3,1,0,2:T(8,128)S(1)} %get-tuple-element.68), channel_id=1, source_target_pairs={{4,0},{8,4},{12,8},{16,12},{20,16},{24,20},{28,24},{0,28},{5,1},{9... | collective-permute-start | bytes 36872 | tf_op jit(solution)/shard_map/ppermute | solution.py:285
  70.2 0.7 copy-start.1
  71.2 1.1 %copy-start.5 = (f32[3,128,128]{2,1,0:T(8,128)S(1)}, f32[3,128,128]{2,1,0:T(8,128)}, u32[]{:S(2)}) copy-start(f32[3,128,128]{2,1,0:T(8,128)} %get-tuple-element.42) | copy-start | bytes 589828
  71.4 0.8 %slice-start = ((f32[8,4,644]{2,1,0:T(4,128)}), f32[8,4,260]{2,1,0:T(4,128)S(1)}, s32[]{:S(2)}) async-start(f32[8,4,644]{2,1,0:T(4,128)} %copy-done.1), calls=%async_computation.4 | async-start | bytes 98304 | tf_op jit(solution)/shard_map/slice | solution.py:303
  75.1 0.9 %copy-start.6 = (f32[3,8,16,128]{3,2,1,0:T(8,128)S(1)}, f32[3,8,16,128]{3,2,1,0:T(8,128)}, u32[]{:S(2)}) copy-start(f32[3,8,16,128]{3,2,1,0:T(8,128)} %fusion.3) | copy-start | bytes 589828

commit v10 on v9

--- a/solution.py
+++ b/solution.py
@@ -258,19 +258,49 @@
         mapped = jnp.einsum(
             "pq,cq->cp", match_ops[0], owned, preferred_element_type=jnp.float32
         )
-        edged = jnp.concatenate([mapped[:, :1], mapped, mapped[:, -1:]], axis=1)
-        pieces = jnp.stack(
-            [edged[:, g * nb_dev : g * nb_dev + nb_dev + 2] for g in range(groups)], axis=0
-        )
+        chunks = []
+        for g in range(groups):
+            low = max(g * nb_dev - 1, 0)
+            high = min((g + 1) * nb_dev, nb - 1)
+            chunks.append(
+                jnp.concatenate(
+                    [
+                        mapped[:, g * nb_dev : (g + 1) * nb_dev],
+                        mapped[:, low : low + 1],
+                        mapped[:, high : high + 1],
+                    ],
+                    axis=1,
+                )
+            )
+        pieces = jnp.stack(chunks, axis=0)
         return jnp.broadcast_to(pieces[None], (tiles,) + pieces.shape).reshape(
             tiles, groups, 2 * (nb_dev + 2)
         )
 
+    row_order = np.concatenate([np.arange(1, na_dev + 1), [0, na_dev + 1]])
+    col_order = np.concatenate([np.arange(1, nb_dev + 1), [0, nb_dev + 1]])
+    surface_ordered = surface_ext[row_order][:, col_order]
+
     def flux_of(returned):
-        angle = phases_at(wave_of_slot, rows_ext // P_SIZE, points[row_points], span)
+        angle = phases_at(
+            wave_of_slot, rows_ext[row_order] // P_SIZE, points[row_points[row_order]], span
+        )
         synth = jnp.stack([jnp.cos(angle).T, jnp.sin(angle).T], axis=2).reshape(na_dev + 2, -1)
-        flux = -jnp.dot(synth, returned.reshape(-1, nb_dev + 2), precision=highest)
-        return surface_ext * flux
+        flux = surface_ordered * -jnp.dot(
+            synth, returned.reshape(-1, nb_dev + 2), precision=highest
+        )
+        a, b = na_dev, nb_dev
+        return (
+            flux[:a, :b],
+            flux[a : a + 1, :b],
+            flux[a + 1 :, :b],
+            flux[:a, b : b + 1],
+            flux[:a, b + 1 :],
+            flux[a : a + 1, b : b + 1],
+            flux[a : a + 1, b + 1 :],
+            flux[a + 1 :, b : b + 1],
+            flux[a + 1 :, b + 1 :],
+        )
 
     mapped_len = 2 * (nb_dev + 2)
     slot_len = 3 * radial_nodes * na_dev
@@ -316,10 +346,10 @@
         corner_ur = take(1, -1)[:, :, na_dev - 1 :, :]
         corner_dl = take(-1, 1)[:, :, :1, :]
         corner_dr = take(-1, -1)[:, :, :1, :]
-        top = jnp.concatenate([corner_ul, from_up, corner_ur], axis=3)
-        middle = jnp.concatenate([from_left, stacked, from_right], axis=3)
-        bottom = jnp.concatenate([corner_dl, from_down, corner_dr], axis=3)
-        return returned, jnp.concatenate([top, middle, bottom], axis=2)
+        return returned, (
+            stacked, from_up, from_down, from_left, from_right,
+            corner_ul, corner_ur, corner_dl, corner_dr,
+        )
 
     def halo(stacked):
         a_lo = lax.slice_in_dim(stacked, 0, 1, axis=2)
@@ -335,10 +365,10 @@
         corner_ur = lax.ppermute(a_hi[:, :, :, :1], both, shift_pairs(sizes, (1, -1)))
         corner_dl = lax.ppermute(a_lo[:, :, :, -1:], both, shift_pairs(sizes, (-1, 1)))
         corner_dr = lax.ppermute(a_lo[:, :, :, :1], both, shift_pairs(sizes, (-1, -1)))
-        top = jnp.concatenate([corner_ul, from_up, corner_ur], axis=3)
-        middle = jnp.concatenate([from_left, stacked, from_right], axis=3)
-        bottom = jnp.concatenate([corner_dl, from_down, corner_dr], axis=3)
-        return jnp.concatenate([top, middle, bottom], axis=2)
+        return (
+            stacked, from_up, from_down, from_left, from_right,
+            corner_ul, corner_ur, corner_dl, corner_dr,
+        )
 
     join_b = np.zeros((nb_dev + 2, nb_dev), np.float32)
     join_b[np.arange(nb_dev) + 1, np.arange(nb_dev)] = 1.0
@@ -346,18 +376,26 @@
     join_b[inner_first, inner_first] = 1.0
     inner_last = np.arange(P_SIZE - 1, nb_dev - 1, P_SIZE)
     join_b[inner_last + 2, inner_last] = 1.0
-    edge_lead = np.zeros((nb_dev + 2, nb_dev), np.float32)
-    edge_lead[0, 0] = 1.0
-    edge_trail = np.zeros((nb_dev + 2, nb_dev), np.float32)
-    edge_trail[nb_dev + 1, nb_dev - 1] = 1.0
-    join_b = join_b + lead * edge_lead + trail * edge_trail
-
-    def assemble_ext(padded):
-        last = padded.ndim - 1
-        along_a = assemble_dim(
-            padded[..., 1:-1, :], last - 1, padded[..., 0:1, :], padded[..., -1:, :]
-        )
-        return jnp.dot(along_a, join_b, precision=highest)
+    join_core = join_b[1:-1]
+    lane_first = np.zeros((nb_dev,), np.float32)
+    lane_first[0] = 1.0
+    lane_last = np.zeros((nb_dev,), np.float32)
+    lane_last[nb_dev - 1] = 1.0
+    edge_left = lead * lane_first
+    edge_right = trail * lane_last
+    plane_mask = np.zeros((3, radial_nodes, 1, 1), np.float32)
+    plane_mask[0, radial_nodes - 1] = 1.0
+
+    def assemble_pieces(core, up, down, left, right, ul, ur, dl, dr):
+        axis = core.ndim - 2
+        along_a = assemble_dim(core, axis, up, down)
+        side_left = assemble_dim(left, axis, ul, dl)
+        side_right = assemble_dim(right, axis, ur, dr)
+        return (
+            jnp.dot(along_a, join_core, precision=highest)
+            + side_left * edge_left
+            + side_right * edge_right
+        )
 
     def tendency(parts, surface):
         shapes = (
@@ -379,19 +417,21 @@
         stacked = stacked.reshape(parts.shape)
         sent = owner_map(partial)
         if carried_halo:
-            returned, padded = joint_exchange(sent, stacked, edge_rows, edge_cols)
+            returned, pieces = joint_exchange(sent, stacked, edge_rows, edge_cols)
         else:
             returned = lax.all_to_all(
                 sent.reshape(tiles * groups, -1), both, 0, 0, tiled=True
             ).reshape(tiles * groups, 2, nb_dev + 2)
-            padded = halo(stacked)
-        flux_term = flux_of(returned)
-        outer = padded[0, radial_nodes - 1] + flux_term
-        outer_rate = assemble_ext(outer) / assembled[radial_nodes - 1]
-        padded = padded.at[0, radial_nodes - 1].add(flux_term)
-        plane_r = jnp.zeros_like(lax.slice_in_dim(padded, 0, 1, axis=1))
-        padded = assemble_dim(padded, 1, plane_r, plane_r)
-        return assemble_ext(padded) / assembled[None], outer_rate
+            pieces = halo(stacked)
+        flux_pieces = flux_of(returned)
+        outer = [p[0, radial_nodes - 1] + f for p, f in zip(pieces, flux_pieces)]
+        outer_rate = assemble_pieces(*outer) / assembled[radial_nodes - 1]
+        whole = [p + plane_mask * f for p, f in zip(pieces, flux_pieces)]
+        joined = assemble_pieces(*whole)
+        if radial_nodes // P_SIZE > 1:
+            plane_r = jnp.zeros_like(lax.slice_in_dim(joined, 0, 1, axis=1))
+            joined = assemble_dim(joined, 1, plane_r, plane_r)
+        return joined / assembled[None], outer_rate
 
     first_rate, first_outer = tendency(field, None)
     section = field + time_step * first_rate

time: 78.2 us -> 93.1 us (1.19)
  other arithmetic: 4.39 us -> 12.1 us
  local copies, waits for them, and re-layouts: 16.3 us -> 22 us
  between operations: 0.7 us -> 5.73 us
  matrix products: 7.76 us -> 3.43 us
  starting transfers between devices: 25.7 us -> 27 us
    add x3 -> x7, other arithmetic: 0.15 us -> 5.71 us  [the longest x6 5.49 us: tendency(): whole = [p + plane_mask * f for p, f in zip(pieces, flux_pieces)]]
    dot_general x5, matrix products: 6.97 us -> 2.65 us  [the longest x3 2.2 us: assemble_pieces(): jnp.dot(along_a, join_core, precision=highest) + side_left * edge_left]
    slice x4 -> x11, local copies, waits for them, and re-layouts: 0.27 us -> 4.04 us  [the longest x4 2.4 us: tendency(): outer = [p[0, radial_nodes - 1] + f for p, f in zip(pieces, flux_pieces)]]
    add x3 -> x9, other arithmetic: 0.15 us -> 2.87 us  [assemble_dim(): first + before]
    slice x1 -> x9, local copies, waits for them, and re-layouts: 0.01 us -> 1.51 us  [assemble_dim(): lax.slice_in_dim(last, 0, count - 1, axis=axis_pos)]
    slice x4 -> x3, local copies, waits for them, and re-layouts: 1.44 us -> 0.01 us  [joint_exchange(): received[:, :, :mapped_len].reshape(tiles * groups, 2, nb_dev + 2)]
    all_to_all x2, waiting for transfers between devices: 1.31 us -> 0.01 us  [owner_map(): gathered = lax.all_to_all(partial, both, 0, 0, tiled=True)]
    all_to_all x2, starting transfers between devices: 8.57 us -> 9.86 us  [joint_exchange(): lax.all_to_all(message, both, 0, 0, tiled=True).reshape(tiles, groups, -1)]
  transfers between devices with their start and end apart: 8 -> 8, of which waited for: 3 -> 2; matrix products, arithmetic and copies ran while one was open for 11% -> 26% of each run, Pallas kernels for 4% -> 4%
where the time goes in v10:
time: 93.1 us; the launch traced here: 92.1 us
  starting transfers between devices  27 us (29%)
  local copies, waits for them, and re-layouts  22 us (24%)
  waiting for transfers between devices  12.3 us (13%)
  other arithmetic  12.1 us (13%)
  Pallas kernels  9.46 us (10%)
  between operations  5.73 us (6%)
  matrix products  3.43 us (4%)
    all_to_all x2, waiting for transfers between devices, joint_exchange(): lax.all_to_all(message, both, 0, 0, tiled=True).reshape(tiles, groups, -1)  12.3 us
    all_to_all x2, starting transfers between devices, owner_map(): gathered = lax.all_to_all(partial, both, 0, 0, tiled=True)  9.97 us
    all_to_all x2, starting transfers between devices, joint_exchange(): lax.all_to_all(message, both, 0, 0, tiled=True).reshape(tiles, groups, -1)  9.86 us
    unnamed x51, local copies, waits for them, and re-layouts  8.2 us
    ppermute x2, starting transfers between devices, joint_exchange(): from_down = lax.ppermute(a_lo, 'tile', down)  6.59 us
    add x6, other arithmetic, tendency(): whole = [p + plane_mask * f for p, f in zip(pieces, flux_pieces)]  5.49 us
    pallas_call x1, Pallas kernels, tendency(): pl.pallas_call(volume_kernel, out_shape=shapes)(*operands)  3.47 us
    pallas_call x1, Pallas kernels, tendency(): pl.pallas_call(first_volume_kernel, out_shape=shapes)(*operands, analysis)  3.42 us
  transfers between devices with their start and end apart: 8, of which 2 were waited for; matrix products, arithmetic and copies ran while one was open for 26% of the time, Pallas kernels for 4%

profile of v10, /device:TPU:0, one launch (start us, length us, event | category | flops | bytes accessed | tf_op | source)
XLA Modules:
  0.0 92.1 jit_solution(8240685054920960210)
XLA Ops:
  0.0 0.7 copy-done.13
  0.7 0.7 copy-done.17
  1.4 0.1 fusion.40
  1.6 0.7 copy-done.14
  2.3 0.6 broadcast_multiply_fusion.1.table_ref
  2.9 2.6 %shard_map.211.grad_ref = f32[9,128,128]{2,1,0:T(8,128)} custom-call(f32[3,128,128]{2,1,0:T(8,128)} %bitcast.166, f32[6,128,128]{2,1,0:T(8,128)} %constant.269.clone.mats_ref), custom_call_target="tpu_custom_call" | custom-call | tf_op jit(solution)/shard_map/pallas_call | solution.py:243
  5.4 3.4 %shard_map.212 = (f32[3,128,128]{2,1,0:T(8,128)}, f32[2,3,8,128]{3,2,1,0:T(8,128)}, f32[2,3,128]{2,1,0:T(4,128)}, f32[64,128]{1,0:T(8,128)}) custom-call(f32[3,128,128]{2,1,0:T(8,128)} %bitcast.176, f32[3,128,128]{2,1,0:T(8,128)} %bitcast.167, f32[9,128,128]{2,1,0:T(8,128)} %shard_map.211.grad_ref, f32[6,128,128]{2,1,0:T(8,128)} %constant.269.clone.mats_ref, ...), custom_call_target="tpu_custom_call" | custom-call | tf_op jit(solution)/shard_map/pallas_call | solution.py:409
  8.8 7.3 %all-to-all-start = ((f32[32,2,128]{2,1,0:T(2,128)}), f32[32,2,128]{2,1,0:T(2,128)S(1)}, u32[]{:S(2)}, u32[]{:S(2)}) async-start(f32[32,2,128]{2,1,0:T(2,128)} %bitcast.189), calls=%async_computation | async-start | bytes 65536 | tf_op jit(solution)/shard_map/all_to_all | solution.py:254
  16.2 0.3 collective-permute-start
  16.5 3.3 %collective-permute-start.1 = (f32[3,8,1,128]{3,1,0,2:T(8,128)S(1)}, f32[3,8,1,128]{3,1,0,2:T(8,128)S(1)}, u32[]{:S(2)}, u32[]{:S(2)}) collective-permute-start(f32[3,8,1,128]{3,1,0,2:T(8,128)S(1)} %get-tuple-element.82), channel_id=1, source_target_pairs={{4,0},{8,4},{12,8},{16,12},{20,16},{24,20},{28,24},{0,28},{5,1},{9... | collective-permute-start | bytes 36872 | tf_op jit(solution)/shard_map/ppermute | solution.py:315
  19.8 0.6 copy-done.16
  20.4 0.7 gather_fusion
  21.2 0.6 copy-done.15
  21.8 0.6 fusion.72
  22.5 0.7 copy-done.11
  23.3 0.6 copy-done.12
  24.3 0.2 fusion.18
  25.2 0.7 all_to_all.19
  26.0 4.0 %all-to-all-start.1 = ((f32[32,1,644]{2,1,0:T(1,128)}), f32[32,1,644]{2,1,0:T(1,128)S(1)}, u32[]{:S(2)}, u32[]{:S(2)}) async-start(f32[32,1,644]{2,1,0:T(1,128)} %all_to_all.19), calls=%async_computation.1 | async-start | bytes 196608 | tf_op jit(solution)/shard_map/all_to_all | solution.py:332
  30.1 7.9 %all-to-all-done.1 = f32[32,1,644]{2,1,0:T(1,128)S(1)} async-done(((f32[32,1,644]{2,1,0:T(1,128)}), f32[32,1,644]{2,1,0:T(1,128)S(1)}, u32[]{:S(2)}, u32[]{:S(2)}) %all-to-all-start.1) | async-done | bytes 82464 | tf_op jit(solution)/shard_map/all_to_all | solution.py:332
  37.9 0.2 reduce
  38.2 0.1 fusion.51
  38.3 0.5 copy-done.1
  39.4 0.6 slice.543
  40.1 0.2 fusion.10
  40.3 0.7 fusion.78
  41.0 0.7 slice.539
  41.9 0.2 fusion.42
  42.1 0.5 fusion.81
  42.9 0.6 slice.550
  43.5 0.6 slice.546
  44.1 0.6 fusion.82
  45.0 0.6 copy-done.7
  51.0 1.2 %slice_add_fusion.25 = (f32[2,1,1]{2,1,0:T(1,128)S(1)}, f32[2,1,1]{2,1,0:T(1,128)S(1)}) fusion(f32[2,8,1]{2,1,0:T(8,128)S(1)} %get-tuple-element.45, f32[1,1,1]{2,1,0:T(1,128)} %get-tuple-element.93, f32[1,1,1]{2,1,0:T(1,128)} %bitcast.42, f32[1,1,1]{2,1,0:T(1,128)} %bitcast.48, f32[1,1,1]{2,1,0:T(1,128)} %get-tuple-element.94), kind=kLoop, calls=%fused_computation.168 | loop fusion | flops 8 | bytes 48 | tf_op jit(solution)/shard_map/add | solution.py:148
  52.3 1.3 %slice_add_fusion.23 = (f32[2,1,1]{2,1,0:T(1,128)S(1)}, f32[2,1,1]{2,1,0:T(1,128)S(1)}) fusion(f32[2,8,1]{2,1,0:T(8,128)S(1)} %get-tuple-element.46, f32[1,1,1]{2,1,0:T(1,128)} %get-tuple-element.97, f32[1,1,1]{2,1,0:T(1,128)} %bitcast.53, f32[1,1,1]{2,1,0:T(1,128)} %bitcast.59, f32[1,1,1]{2,1,0:T(1,128)} %get-tuple-element.98), kind=kLoop, calls=%fused_computation.166 | loop fusion | flops 8 | bytes 48 | tf_op jit(solution)/shard_map/add | solution.py:148
  54.1 0.6 copy-done.4
  54.7 0.2 fusion.15
  54.9 0.3 fusion.26
  55.2 0.6 copy.145
  55.9 2.7 %all-to-all-start.2 = ((f32[32,2,128]{2,1,0:T(2,128)}), f32[32,2,128]{2,1,0:T(2,128)S(1)}, u32[]{:S(2)}, u32[]{:S(2)}) async-start(f32[32,2,128]{2,1,0:T(2,128)} %copy.145), calls=%async_computation.2 | async-start | bytes 65536 | tf_op jit(solution)/shard_map/all_to_all | solution.py:254
  58.6 2.6 %slice_add_fusion.19 = (f32[3,8,1,1]{2,1,0,3:T(8,128)S(1)}, f32[3,8,1,1]{2,1,0,3:T(8,128)S(1)}, f32[3,8,1,1]{2,1,0,3:T(8,128)S(1)}, f32[3,8,1,1]{2,1,0,3:T(8,128)S(1)}) fusion(f32[3,8,16,1]{2,1,0,3:T(8,128)S(1)} %reshape.1062, f32[3,8,1,1]{2,1,0,3:T(8,128)S(1)} %copy-done.8, f32[]{:T(128)} %bitcast.20, f32[]{:T(128)} %bitcast.26, ...), kind=kLoop, calls=%fused_computation.77 | loop fusion | flops 192 | bytes 880 | tf_op jit(solution)/shard_map/add | solution.py:429
  61.2 0.1 pad_maximum_fusion.5
  61.5 0.1 pad_maximum_fusion.6
  61.8 0.8 copy-done.22
  62.7 1.0 %fusion.6 = f32[3,8,16,128]{3,2,1,0:T(8,128)} fusion(f32[3,8,16,128]{3,2,1,0:T(8,128)S(1)} %copy-done.4, f32[128,128,1,1]{1,0,3,2:T(8,128)S(1)} %copy-done.22, f32[3,8,16,128]{3,1,0,2:T(8,128)S(1)} %bitcast.175, f32[8,16,128]{2,1,0:T(8,128)S(1)} %broadcast_multiply_fusion, f32[128]{0:T(128)S(1)} %get-tuple-element.148, f32[3,8,16]{2,1,0:T(8,128)S(1)} %mul.742, ...), kind=kOutput, calls=%fused_computation.9 | convolution fusion | flops 75841536 | bytes 724992 | tf_op jit(solution)/shard_map/dot_general | solution.py:395
  63.7 3.5 %shard_map.213 = (f32[3,128,128]{2,1,0:T(8,128)}, f32[2,3,8,128]{3,2,1,0:T(8,128)}, f32[2,3,128]{2,1,0:T(4,128)}) custom-call(f32[3,128,128]{2,1,0:T(8,128)} %bitcast.177, f32[3,128,128]{2,1,0:T(8,128)} %bitcast.168, f32[9,128,128]{2,1,0:T(8,128)} %shard_map.211.grad_ref, f32[6,128,128]{2,1,0:T(8,128)} %constant.269.clone.mats_ref, ...), custom_call_target="tpu_custom_call" | custom-call | tf_op jit(solution)/shard_map/pallas_call | solution.py:413
  67.1 0.7 fusion.86
  68.2 0.2 fusion.16
  69.3 0.7 all_to_all.22
  70.0 5.8 %all-to-all-start.3 = ((f32[32,1,644]{2,1,0:T(1,128)}), f32[32,1,644]{2,1,0:T(1,128)S(1)}, u32[]{:S(2)}, u32[]{:S(2)}) async-start(f32[32,1,644]{2,1,0:T(1,128)} %all_to_all.22), calls=%async_computation.3 | async-start | bytes 196608 | tf_op jit(solution)/shard_map/all_to_all | solution.py:332
  75.9 0.3 collective-permute-start.2
  76.2 3.3 %collective-permute-start.3 = (f32[3,8,1,128]{3,1,0,2:T(8,128)S(1)}, f32[3,8,1,128]{3,1,0,2:T(8,128)S(1)}, u32[]{:S(2)}, u32[]{:S(2)}) collective-permute-start(f32[3,8,1,128]{3,1,0,2:T(8,128)S(1)} %get-tuple-element.62), channel_id=1, source_target_pairs={{4,0},{8,4},{12,8},{16,12},{20,16},{24,20},{28,24},{0,28},{5,1},{9... | collective-permute-start | bytes 36872 | tf_op jit(solution)/shard_map/ppermute | solution.py:315
  79.5 4.5 %all-to-all-done.3 = f32[32,1,644]{2,1,0:T(1,128)S(1)} async-done(((f32[32,1,644]{2,1,0:T(1,128)}), f32[32,1,644]{2,1,0:T(1,128)S(1)}, u32[]{:S(2)}, u32[]{:S(2)}) %all-to-all-start.3) | async-done | bytes 82464 | tf_op jit(solution)/shard_map/all_to_all | solution.py:332
  83.9 0.2 reduce.13
  84.2 0.1 fusion.57
  84.4 0.2 fusion.9
  84.7 0.7 fusion.75
  85.3 0.2 slice_reduce_fusion.1
  85.5 0.1 reshape.1092
  86.8 2.6 %slice_add_fusion.15 = (f32[3,8,1,1]{2,1,0,3:T(8,128)S(1)}, f32[3,8,1,1]{2,1,0,3:T(8,128)S(1)}, f32[3,8,1,1]{2,1,0,3:T(8,128)S(1)}, f32[3,8,1,1]{2,1,0,3:T(8,128)S(1)}) fusion(f32[3,8,16,1]{2,1,0,3:T(8,128)S(1)} %reshape.1093, f32[3,8,1,1]{2,1,0,3:T(8,128)S(1)} %copy-done.8, f32[]{:T(128)} %bitcast.74, f32[]{:T(128)} %bitcast.76, ...), kind=kLoop, calls=%fused_computation.73 | loop fusion | flops 192 | bytes 880 | tf_op jit(solution)/shard_map/add | solution.py:429
  89.5 0.1 pad_maximum_fusion.7
  89.7 0.1 pad_maximum_fusion.8
  90.2 0.9 copy-done.5
  91.1 1.0 %fusion.8 = f32[3,8,16,128]{3,2,1,0:T(8,128)} fusion(f32[128,128,1,1]{1,0,3,2:T(8,128)S(1)} %copy-done.22, f32[3,8,16,128]{3,1,0,2:T(8,128)S(1)} %bitcast.174, f32[3,8,16,128]{3,2,1,0:T(8,128)S(1)} %copy-done.4, f32[3,8,16,128]{3,2,1,0:T(8,128)S(1)} %copy-done.5, f32[3,8,16]{2,1,0:T(8,128)S(1)} %mul.805, f32[3,8,16]{2,1,0:T(8,128)S(1)} %mul.793, ...), kind=kOutput, calls=%fused_computation.11 | convolution fusion | flops 75939840 | bytes 921600 | tf_op jit(solution)/shard_map/dot_general | solution.py:395
  (180 shorter events, 7.3 us)
Async XLA Ops:
  0.0 24.3 %copy-start = (bf16[1,512,512]{2,1,0:T(8,128)(2,1)S(1)}, bf16[1,512,512]{2,1,0:T(8,128)(2,1)}, u32[]{:S(2)}) copy-start(bf16[1,512,512]{2,1,0:T(8,128)(2,1)} %param.24) | copy-start | bytes 1572868
  0.0 0.7 copy-start.13
  0.7 0.7 copy-start.17
  1.6 0.7 copy-start.14
  8.8 7.3 %copy-start.10 = (f32[2,3,8,128]{3,2,1,0:T(8,128)S(1)}, f32[2,3,8,128]{3,2,1,0:T(8,128)}, u32[]{:S(2)}) copy-start(f32[2,3,8,128]{3,2,1,0:T(8,128)} %get-tuple-element.15) | copy-start | bytes 73732
  8.8 15.4 %all-to-all-start = ((f32[32,2,128]{2,1,0:T(2,128)}), f32[32,2,128]{2,1,0:T(2,128)S(1)}, u32[]{:S(2)}, u32[]{:S(2)}) async-start(f32[32,2,128]{2,1,0:T(2,128)} %bitcast.189), calls=%async_computation | async-start | bytes 65536 | tf_op jit(solution)/shard_map/all_to_all | solution.py:254
  16.2 37.9 %collective-permute-start = (f32[3,8,1,128]{3,1,0,2:T(8,128)S(1)}, f32[3,8,1,128]{3,1,0,2:T(8,128)S(1)}, u32[]{:S(2)}, u32[]{:S(2)}) collective-permute-start(f32[3,8,1,128]{3,1,0,2:T(8,128)S(1)} %get-tuple-element.81), channel_id=1, source_target_pairs={{0,4},{4,8},{8,12},{12,16},{16,20},{20,24},{24,28},{28,0},{1,5},{5... | collective-permute-start | bytes 36872 | tf_op jit(solution)/shard_map/ppermute | solution.py:314
  16.5 37.6 %collective-permute-start.1 = (f32[3,8,1,128]{3,1,0,2:T(8,128)S(1)}, f32[3,8,1,128]{3,1,0,2:T(8,128)S(1)}, u32[]{:S(2)}, u32[]{:S(2)}) collective-permute-start(f32[3,8,1,128]{3,1,0,2:T(8,128)S(1)} %get-tuple-element.82), channel_id=1, source_target_pairs={{4,0},{8,4},{12,8},{16,12},{20,16},{24,20},{28,24},{0,28},{5,1},{9... | collective-permute-start | bytes 36872 | tf_op jit(solution)/shard_map/ppermute | solution.py:315
  19.8 0.7 copy-start.16
  21.1 0.7 copy-start.15
  21.8 0.7 copy-start.18
  21.8 0.7 copy-start.19
  21.8 0.7 copy-start.20
  21.8 0.7 copy-start.21
  22.5 0.7 copy-start.11
  23.2 0.7 copy-start.12
  26.0 4.0 %copy-start.24 = (f32[128]{0:T(128)S(1)}, f32[128]{0:T(128)}, u32[]{:S(2)}) copy-start(f32[128]{0:T(128)} %constant.272.clone) | copy-start | bytes 1540
  26.0 12.0 %all-to-all-start.1 = ((f32[32,1,644]{2,1,0:T(1,128)}), f32[32,1,644]{2,1,0:T(1,128)S(1)}, u32[]{:S(2)}, u32[]{:S(2)}) async-start(f32[32,1,644]{2,1,0:T(1,128)} %all_to_all.19), calls=%async_computation.1 | async-start | bytes 196608 | tf_op jit(solution)/shard_map/all_to_all | solution.py:332
  38.2 0.7 copy-start.1
  38.9 1.1 %slice-start = ((f32[8,4,644]{2,1,0:T(4,128)}), f32[8,4,260]{2,1,0:T(4,128)S(1)}, s32[]{:S(2)}) async-start(f32[8,4,644]{2,1,0:T(4,128)} %copy-done.1), calls=%async_computation.4 | async-start | bytes 98304 | tf_op jit(solution)/shard_map/slice | solution.py:333
  39.0 1.1 %copy-start.6 = (f32[18,130]{1,0:T(8,128)S(1)}, f32[18,130]{1,0:T(8,128)}, u32[]{:S(2)}) copy-start(f32[18,130]{1,0:T(8,128)} %constant.278.clone) | copy-start | bytes 28084
  40.0 4.9 %copy-start.2 = (f32[3,128,128]{2,1,0:T(8,128)S(1)}, f32[3,128,128]{2,1,0:T(8,128)}, u32[]{:S(2)}) copy-start(f32[3,128,128]{2,1,0:T(8,128)} %get-tuple-element.12) | copy-start | bytes 589828
  44.9 0.7 copy-start.7
  53.8 0.9 %copy-start.4 = (f32[3,8,16,128]{3,2,1,0:T(8,128)S(1)}, f32[3,8,16,128]{3,2,1,0:T(8,128)}, u32[]{:S(2)}) copy-start(f32[3,8,16,128]{3,2,1,0:T(8,128)} %param.22) | copy-start | bytes 589828
  53.9 0.9 copy-start.23
  55.9 2.7 %copy-start.8 = (f32[3,8,1,1]{2,1,0,3:T(8,128)S(1)}, f32[3,8,1,1]{2,1,0,3:T(8,128)}, u32[]{:S(2)}) copy-start(f32[3,8,1,1]{2,1,0,3:T(8,128)} %constant.280.clone) | copy-start | bytes 292
  55.9 12.3 %all-to-all-start.2 = ((f32[32,2,128]{2,1,0:T(2,128)}), f32[32,2,128]{2,1,0:T(2,128)S(1)}, u32[]{:S(2)}, u32[]{:S(2)}) async-start(f32[32,2,128]{2,1,0:T(2,128)} %copy.145), calls=%async_computation.2 | async-start | bytes 65536 | tf_op jit(solution)/shard_map/all_to_all | solution.py:254
  61.8 0.8 copy-start.22
  70.0 5.8 %copy-start.9 = (f32[2,3,8,128]{3,2,1,0:T(8,128)S(1)}, f32[2,3,8,128]{3,2,1,0:T(8,128)}, u32[]{:S(2)}) copy-start(f32[2,3,8,128]{3,2,1,0:T(8,128)} %get-tuple-element.18) | copy-start | bytes 73732
  70.0 13.9 %all-to-all-start.3 = ((f32[32,1,644]{2,1,0:T(1,128)}), f32[32,1,644]{2,1,0:T(1,128)S(1)}, u32[]{:S(2)}, u32[]{:S(2)}) async-start(f32[32,1,644]{2,1,0:T(1,128)} %all_to_all.22), calls=%async_computation.3 | async-start | bytes 196608 | tf_op jit(solution)/shard_map/all_to_all | solution.py:332
  75.9 14.2 %collective-permute-start.2 = (f32[3,8,1,128]{3,1,0,2:T(8,128)S(1)}, f32[3,8,1,128]{3,1,0,2:T(8,128)S(1)}, u32[]{:S(2)}, u32[]{:S(2)}) collective-permute-start(f32[3,8,1,128]{3,1,0,2:T(8,128)S(1)} %get-tuple-element.61), channel_id=1, source_target_pairs={{0,4},{4,8},{8,12},{12,16},{16,20},{20,24},{24,28},{28,0},{1,5},{5... | collective-permute-start | bytes 36872 | tf_op jit(solution)/shard_map/ppermute | solution.py:314
  76.2 13.9 %collective-permute-start.3 = (f32[3,8,1,128]{3,1,0,2:T(8,128)S(1)}, f32[3,8,1,128]{3,1,0,2:T(8,128)S(1)}, u32[]{:S(2)}, u32[]{:S(2)}) collective-permute-start(f32[3,8,1,128]{3,1,0,2:T(8,128)S(1)} %get-tuple-element.62), channel_id=1, source_target_pairs={{4,0},{8,4},{12,8},{16,12},{20,16},{24,20},{28,24},{0,28},{5,1},{9... | collective-permute-start | bytes 36872 | tf_op jit(solution)/shard_map/ppermute | solution.py:315
  85.8 0.9 %copy-start.3 = (f32[3,128,128]{2,1,0:T(8,128)S(1)}, f32[3,128,128]{2,1,0:T(8,128)}, u32[]{:S(2)}) copy-start(f32[3,128,128]{2,1,0:T(8,128)} %get-tuple-element.16) | copy-start | bytes 589828
  90.1 0.9 %copy-start.5 = (f32[3,8,16,128]{3,2,1,0:T(8,128)S(1)}, f32[3,8,16,128]{3,2,1,0:T(8,128)}, u32[]{:S(2)}) copy-start(f32[3,8,16,128]{3,2,1,0:T(8,128)} %fusion.6) | copy-start | bytes 589828

commit v11 on v9

--- a/solution.py
+++ b/solution.py
@@ -352,6 +352,9 @@
     edge_trail[nb_dev + 1, nb_dev - 1] = 1.0
     join_b = join_b + lead * edge_lead + trail * edge_trail
 
+    plane_mask = np.zeros((3, radial_nodes, 1, 1), np.float32)
+    plane_mask[0, radial_nodes - 1] = 1.0
+
     def assemble_ext(padded):
         last = padded.ndim - 1
         along_a = assemble_dim(
@@ -388,7 +391,7 @@
         flux_term = flux_of(returned)
         outer = padded[0, radial_nodes - 1] + flux_term
         outer_rate = assemble_ext(outer) / assembled[radial_nodes - 1]
-        padded = padded.at[0, radial_nodes - 1].add(flux_term)
+        padded = padded + plane_mask * flux_term
         plane_r = jnp.zeros_like(lax.slice_in_dim(padded, 0, 1, axis=1))
         padded = assemble_dim(padded, 1, plane_r, plane_r)
         return assemble_ext(padded) / assembled[None], outer_rate

time: 78.2 us -> 73.7 us (0.942)
  matrix products: 7.76 us -> 3.89 us
  waiting for transfers between devices: 13 us -> 14.8 us
  starting transfers between devices: 25.7 us -> 24.3 us
    dot_general x2, matrix products: 4.31 us -> 0.45 us  [flux_of(): flux = -jnp.dot(synth, returned.reshape(-1, nb_dev + 2), precision=highest)]
    all_to_all x2, waiting for transfers between devices: 1.31 us -> 3.13 us  [owner_map(): gathered = lax.all_to_all(partial, both, 0, 0, tiled=True)]
    all_to_all x2, starting transfers between devices: 8.57 us -> 7.24 us  [joint_exchange(): lax.all_to_all(message, both, 0, 0, tiled=True).reshape(tiles, groups, -1)]
    unnamed x56 -> x55, local copies, waits for them, and re-layouts: 7.33 us -> 7.83 us
  transfers between devices with their start and end apart: 8 -> 8, of which waited for: 3 -> 4; matrix products, arithmetic and copies ran while one was open for 11% -> 10% of each run, Pallas kernels for 4% -> 5%
where the time goes in v11:
time: 73.7 us; the launch traced here: 72.9 us
  starting transfers between devices  24.3 us (33%)
  local copies, waits for them, and re-layouts  16 us (22%)
  waiting for transfers between devices  14.8 us (20%)
  Pallas kernels  9.44 us (13%)
  matrix products  3.89 us (5%)
  other arithmetic  3.74 us (5%)
    all_to_all x2, waiting for transfers between devices, joint_exchange(): lax.all_to_all(message, both, 0, 0, tiled=True).reshape(tiles, groups, -1)  11.6 us
    all_to_all x2, starting transfers between devices, owner_map(): gathered = lax.all_to_all(partial, both, 0, 0, tiled=True)  9.84 us
    unnamed x55, local copies, waits for them, and re-layouts  7.83 us
    all_to_all x2, starting transfers between devices, joint_exchange(): lax.all_to_all(message, both, 0, 0, tiled=True).reshape(tiles, groups, -1)  7.24 us
    ppermute x2, starting transfers between devices, joint_exchange(): from_down = lax.ppermute(a_lo, 'tile', down)  6.66 us
    pallas_call x1, Pallas kernels, tendency(): pl.pallas_call(volume_kernel, out_shape=shapes)(*operands)  3.47 us
    pallas_call x1, Pallas kernels, tendency(): pl.pallas_call(first_volume_kernel, out_shape=shapes)(*operands, analysis)  3.42 us
    all_to_all x2, waiting for transfers between devices, owner_map(): gathered = lax.all_to_all(partial, both, 0, 0, tiled=True)  3.13 us
  transfers between devices with their start and end apart: 8, of which 4 were waited for; matrix products, arithmetic and copies ran while one was open for 10% of the time, Pallas kernels for 5%

profile of v11, /device:TPU:0, one launch (start us, length us, event | category | flops | bytes accessed | tf_op | source)
XLA Modules:
  0.0 72.9 jit_solution(11439603610822330738)
XLA Ops:
  0.0 0.7 copy-done.16
  0.7 0.7 copy-done.19
  1.4 0.1 fusion.47
  1.5 0.1 copy.54
  1.6 0.7 copy-done.17
  2.3 0.6 broadcast_multiply_fusion.1.table_ref
  2.9 2.6 %shard_map.184.grad_ref = f32[9,128,128]{2,1,0:T(8,128)} custom-call(f32[3,128,128]{2,1,0:T(8,128)} %bitcast.110, f32[6,128,128]{2,1,0:T(8,128)} %constant.256.clone.mats_ref), custom_call_target="tpu_custom_call" | custom-call | tf_op jit(solution)/shard_map/pallas_call | solution.py:243
  5.4 3.4 %shard_map.185 = (f32[3,128,128]{2,1,0:T(8,128)}, f32[2,3,8,128]{3,2,1,0:T(8,128)}, f32[2,3,128]{2,1,0:T(4,128)}, f32[64,128]{1,0:T(8,128)}) custom-call(f32[3,128,128]{2,1,0:T(8,128)} %bitcast.115, f32[3,128,128]{2,1,0:T(8,128)} %bitcast.111, f32[9,128,128]{2,1,0:T(8,128)} %shard_map.184.grad_ref, f32[6,128,128]{2,1,0:T(8,128)} %constant.256.clone.mats_ref, ...), custom_call_target="tpu_custom_call" | custom-call | tf_op jit(solution)/shard_map/pallas_call | solution.py:374
  8.8 7.3 %all-to-all-start = ((f32[32,2,128]{2,1,0:T(2,128)}), f32[32,2,128]{2,1,0:T(2,128)S(1)}, u32[]{:S(2)}, u32[]{:S(2)}) async-start(f32[32,2,128]{2,1,0:T(2,128)} %bitcast.122), calls=%async_computation | async-start | bytes 65536 | tf_op jit(solution)/shard_map/all_to_all | solution.py:254
  16.2 0.3 collective-permute-start
  16.5 3.3 %collective-permute-start.1 = (f32[3,8,1,128]{3,1,0,2:T(8,128)S(1)}, f32[3,8,1,128]{3,1,0,2:T(8,128)S(1)}, u32[]{:S(2)}, u32[]{:S(2)}) collective-permute-start(f32[3,8,1,128]{3,1,0,2:T(8,128)S(1)} %get-tuple-element.50), channel_id=1, source_target_pairs={{4,0},{8,4},{12,8},{16,12},{20,16},{24,20},{28,24},{0,28},{5,1},{9... | collective-permute-start | bytes 36872 | tf_op jit(solution)/shard_map/ppermute | solution.py:285
  19.8 0.7 copy-done.15
  20.9 0.6 copy-done.20
  21.6 1.8 %all-to-all-done = f32[32,2,128]{2,1,0:T(2,128)S(1)} async-done(((f32[32,2,128]{2,1,0:T(2,128)}), f32[32,2,128]{2,1,0:T(2,128)S(1)}, u32[]{:S(2)}, u32[]{:S(2)}) %all-to-all-start) | async-done | bytes 32800 | tf_op jit(solution)/shard_map/all_to_all | solution.py:254
  23.5 0.2 fusion.12
  23.8 0.1 pad_maximum_fusion.14
  23.9 0.1 stack.49
  24.0 0.1 stack.50
  24.0 0.1 stack.51
  24.1 0.1 stack.52
  24.4 0.7 all_to_all.19
  25.1 2.7 %all-to-all-start.1 = ((f32[32,1,644]{2,1,0:T(1,128)}), f32[32,1,644]{2,1,0:T(1,128)S(1)}, u32[]{:S(2)}, u32[]{:S(2)}) async-start(f32[32,1,644]{2,1,0:T(1,128)} %all_to_all.19), calls=%async_computation.1 | async-start | bytes 196608 | tf_op jit(solution)/shard_map/all_to_all | solution.py:302
  27.8 0.6 fusion.73
  28.5 7.3 %all-to-all-done.1 = f32[32,1,644]{2,1,0:T(1,128)S(1)} async-done(((f32[32,1,644]{2,1,0:T(1,128)}), f32[32,1,644]{2,1,0:T(1,128)S(1)}, u32[]{:S(2)}, u32[]{:S(2)}) %all-to-all-start.1) | async-done | bytes 82464 | tf_op jit(solution)/shard_map/all_to_all | solution.py:302
  35.7 0.2 reduce
  36.0 0.1 fusion.53
  36.7 0.2 reshape.880
  36.9 0.2 reshape.881
  37.2 0.7 slice-done
  38.0 0.7 copy-done.7
  38.7 0.2 fusion.6
  38.9 0.7 copy-done.13
  39.6 0.4 multiply_add_fusion
  40.4 0.8 %copy-done.3 = f32[3,8,16,128]{3,2,1,0:T(8,128)S(1)} copy-done((f32[3,8,16,128]{3,2,1,0:T(8,128)S(1)}, f32[3,8,16,128]{3,2,1,0:T(8,128)}, u32[]{:S(2)}) %copy-start.3) | copy-done | bytes 196632
  41.3 0.2 fusion.9
  41.5 0.3 fusion.39
  41.8 0.6 copy.69
  42.4 2.5 %all-to-all-start.2 = ((f32[32,2,128]{2,1,0:T(2,128)}), f32[32,2,128]{2,1,0:T(2,128)S(1)}, u32[]{:S(2)}, u32[]{:S(2)}) async-start(f32[32,2,128]{2,1,0:T(2,128)} %copy.69), calls=%async_computation.2 | async-start | bytes 65536 | tf_op jit(solution)/shard_map/all_to_all | solution.py:254
  45.3 1.2 %fusion.3 = f32[3,8,16,128]{3,2,1,0:T(8,128)} fusion(f32[3,8,16,128]{3,2,1,0:T(8,128)S(1)} %copy-done.3, f32[3,8,2,1,130]{4,3,2,1,0:T(1,128)S(1)} %copy.68, f32[3,8,2,6,130]{4,3,2,1,0:T(8,128)S(1)} %slice.259, f32[3,8,2,1,130]{4,3,2,1,0:T(1,128)S(1)} %copy.67, f32[8,16,128]{2,1,0:T(8,128)S(1)} %broadcast_multiply_fusion, f32[130,128]{1,0:T(8,128)S(1)} %copy-done.9, ...), kind=kOutput, calls=%fused_computation.5 | convolution fusion | flops 76990976 | bytes 858120 | tf_op jit(solution)/shard_map/dot_general | solution.py:363
  46.5 3.5 %shard_map.186 = (f32[3,128,128]{2,1,0:T(8,128)}, f32[2,3,8,128]{3,2,1,0:T(8,128)}, f32[2,3,128]{2,1,0:T(4,128)}) custom-call(f32[3,128,128]{2,1,0:T(8,128)} %bitcast.118, f32[3,128,128]{2,1,0:T(8,128)} %bitcast.112, f32[9,128,128]{2,1,0:T(8,128)} %shard_map.184.grad_ref, f32[6,128,128]{2,1,0:T(8,128)} %constant.256.clone.mats_ref, ...), custom_call_target="tpu_custom_call" | custom-call | tf_op jit(solution)/shard_map/pallas_call | solution.py:378
  50.0 0.7 fusion.78
  51.0 1.3 %all-to-all-done.2 = f32[32,2,128]{2,1,0:T(2,128)S(1)} async-done(((f32[32,2,128]{2,1,0:T(2,128)}), f32[32,2,128]{2,1,0:T(2,128)S(1)}, u32[]{:S(2)}, u32[]{:S(2)}) %all-to-all-start.2) | async-done | bytes 32800 | tf_op jit(solution)/shard_map/all_to_all | solution.py:254
  52.3 0.2 fusion.10
  52.6 0.1 pad_maximum_fusion.12
  52.7 0.1 stack.55
  52.8 0.1 stack.56
  52.9 0.1 stack.57
  53.0 0.1 stack.58
  53.2 0.7 all_to_all.22
  53.9 4.5 %all-to-all-start.3 = ((f32[32,1,644]{2,1,0:T(1,128)}), f32[32,1,644]{2,1,0:T(1,128)S(1)}, u32[]{:S(2)}, u32[]{:S(2)}) async-start(f32[32,1,644]{2,1,0:T(1,128)} %all_to_all.22), calls=%async_computation.3 | async-start | bytes 196608 | tf_op jit(solution)/shard_map/all_to_all | solution.py:302
  58.5 0.3 collective-permute-start.2
  58.8 3.4 %collective-permute-start.3 = (f32[3,8,1,128]{3,1,0,2:T(8,128)S(1)}, f32[3,8,1,128]{3,1,0,2:T(8,128)S(1)}, u32[]{:S(2)}, u32[]{:S(2)}) collective-permute-start(f32[3,8,1,128]{3,1,0,2:T(8,128)S(1)} %get-tuple-element.46), channel_id=1, source_target_pairs={{4,0},{8,4},{12,8},{16,12},{20,16},{24,20},{28,24},{0,28},{5,1},{9... | collective-permute-start | bytes 36872 | tf_op jit(solution)/shard_map/ppermute | solution.py:285
  62.2 4.4 %all-to-all-done.3 = f32[32,1,644]{2,1,0:T(1,128)S(1)} async-done(((f32[32,1,644]{2,1,0:T(1,128)}), f32[32,1,644]{2,1,0:T(1,128)S(1)}, u32[]{:S(2)}, u32[]{:S(2)}) %all-to-all-start.3) | async-done | bytes 82464 | tf_op jit(solution)/shard_map/all_to_all | solution.py:302
  66.6 0.2 reduce.7
  66.8 0.1 fusion.59
  67.0 0.5 copy-done.2
  67.8 0.5 slice-done.1
  68.4 0.2 fusion.5
  68.9 0.2 reshape.882
  69.1 0.2 reshape.883
  69.5 0.6 copy-done.4
  70.0 0.4 maximum_add_fusion
  70.9 0.7 copy-done.6
  71.7 1.2 %fusion.4 = f32[3,8,16,128]{3,2,1,0:T(8,128)} fusion(f32[3,8,2,1,130]{4,3,2,1,0:T(1,128)S(1)} %copy.84, f32[3,8,2,6,130]{4,3,2,1,0:T(8,128)S(1)} %slice.286, f32[3,8,2,1,130]{4,3,2,1,0:T(1,128)S(1)} %copy.83, f32[3,8,16,128]{3,2,1,0:T(8,128)S(1)} %copy-done.3, f32[3,8,16,128]{3,2,1,0:T(8,128)S(1)} %copy-done.6, ...), kind=kOutput, calls=%fused_computation.6 | convolution fusion | flops 77089280 | bytes 1054728 | tf_op jit(solution)/shard_map/dot_general | solution.py:363
  (134 shorter events, 4.0 us)
Async XLA Ops:
  0.0 23.5 %copy-start = (bf16[1,512,512]{2,1,0:T(8,128)(2,1)S(1)}, bf16[1,512,512]{2,1,0:T(8,128)(2,1)}, u32[]{:S(2)}) copy-start(bf16[1,512,512]{2,1,0:T(8,128)(2,1)} %param.21) | copy-start | bytes 1572868
  0.0 0.7 copy-start.16
  0.7 0.7 copy-start.19
  1.6 0.7 copy-start.17
  8.8 7.3 %copy-start.12 = (f32[2,3,8,128]{3,2,1,0:T(8,128)S(1)}, f32[2,3,8,128]{3,2,1,0:T(8,128)}, u32[]{:S(2)}) copy-start(f32[2,3,8,128]{3,2,1,0:T(8,128)} %get-tuple-element.14) | copy-start | bytes 73732
  8.8 14.6 %all-to-all-start = ((f32[32,2,128]{2,1,0:T(2,128)}), f32[32,2,128]{2,1,0:T(2,128)S(1)}, u32[]{:S(2)}, u32[]{:S(2)}) async-start(f32[32,2,128]{2,1,0:T(2,128)} %bitcast.122), calls=%async_computation | async-start | bytes 65536 | tf_op jit(solution)/shard_map/all_to_all | solution.py:254
  16.2 20.3 %collective-permute-start = (f32[3,8,1,128]{3,1,0,2:T(8,128)S(1)}, f32[3,8,1,128]{3,1,0,2:T(8,128)S(1)}, u32[]{:S(2)}, u32[]{:S(2)}) collective-permute-start(f32[3,8,1,128]{3,1,0,2:T(8,128)S(1)} %get-tuple-element.49), channel_id=1, source_target_pairs={{0,4},{4,8},{8,12},{12,16},{16,20},{20,24},{24,28},{28,0},{1,5},{5... | collective-permute-start | bytes 36872 | tf_op jit(solution)/shard_map/ppermute | solution.py:284
  16.5 20.6 %collective-permute-start.1 = (f32[3,8,1,128]{3,1,0,2:T(8,128)S(1)}, f32[3,8,1,128]{3,1,0,2:T(8,128)S(1)}, u32[]{:S(2)}, u32[]{:S(2)}) collective-permute-start(f32[3,8,1,128]{3,1,0,2:T(8,128)S(1)} %get-tuple-element.50), channel_id=1, source_target_pairs={{4,0},{8,4},{12,8},{16,12},{20,16},{24,20},{28,24},{0,28},{5,1},{9... | collective-permute-start | bytes 36872 | tf_op jit(solution)/shard_map/ppermute | solution.py:285
  19.8 0.7 copy-start.15
  20.8 0.7 copy-start.14
  20.8 0.7 copy-start.20
  20.8 0.7 copy-start.21
  20.8 0.7 copy-start.22
  25.1 2.7 %copy-start.18 = (f32[18]{0:T(128)S(1)}, f32[18]{0:T(128)}, u32[]{:S(2)}) copy-start(f32[18]{0:T(128)} %constant.270) | copy-start | bytes 220
  25.1 10.7 %all-to-all-start.1 = ((f32[32,1,644]{2,1,0:T(1,128)}), f32[32,1,644]{2,1,0:T(1,128)S(1)}, u32[]{:S(2)}, u32[]{:S(2)}) async-start(f32[32,1,644]{2,1,0:T(1,128)} %all_to_all.19), calls=%async_computation.1 | async-start | bytes 196608 | tf_op jit(solution)/shard_map/all_to_all | solution.py:302
  36.0 0.6 copy-start.1
  36.9 2.0 %copy-start.5 = (f32[3,128,128]{2,1,0:T(8,128)S(1)}, f32[3,128,128]{2,1,0:T(8,128)}, u32[]{:S(2)}) copy-start(f32[3,128,128]{2,1,0:T(8,128)} %get-tuple-element.15) | copy-start | bytes 589828
  37.1 0.8 %slice-start = ((f32[8,4,644]{2,1,0:T(4,128)}), f32[8,4,260]{2,1,0:T(4,128)S(1)}, s32[]{:S(2)}) async-start(f32[8,4,644]{2,1,0:T(4,128)} %copy-done.1), calls=%async_computation.4 | async-start | bytes 98304 | tf_op jit(solution)/shard_map/slice | solution.py:303
  37.9 0.7 %copy-start.7 = (f32[18,130]{1,0:T(8,128)S(1)}, f32[18,130]{1,0:T(8,128)}, u32[]{:S(2)}) copy-start(f32[18,130]{1,0:T(8,128)} %constant.264.clone) | copy-start | bytes 28084
  38.9 0.7 copy-start.13
  40.2 0.9 %copy-start.3 = (f32[3,8,16,128]{3,2,1,0:T(8,128)S(1)}, f32[3,8,16,128]{3,2,1,0:T(8,128)}, u32[]{:S(2)}) copy-start(f32[3,8,16,128]{3,2,1,0:T(8,128)} %param.19) | copy-start | bytes 589828
  40.3 1.0 %copy-start.8 = (f32[130,128]{1,0:T(8,128)S(1)}, f32[130,128]{1,0:T(8,128)}, u32[]{:S(2)}) copy-start(f32[130,128]{1,0:T(8,128)} %constant.259.clone) | copy-start | bytes 199684
  40.3 1.0 %copy-start.9 = (f32[130,128]{1,0:T(8,128)S(1)}, f32[130,128]{1,0:T(8,128)}, u32[]{:S(2)}) copy-start(f32[130,128]{1,0:T(8,128)} %constant.260.clone) | copy-start | bytes 199684
  40.3 1.0 %copy-start.10 = (f32[130,128]{1,0:T(8,128)S(1)}, f32[130,128]{1,0:T(8,128)}, u32[]{:S(2)}) copy-start(f32[130,128]{1,0:T(8,128)} %constant.261.clone) | copy-start | bytes 199684
  42.4 9.8 %all-to-all-start.2 = ((f32[32,2,128]{2,1,0:T(2,128)}), f32[32,2,128]{2,1,0:T(2,128)S(1)}, u32[]{:S(2)}, u32[]{:S(2)}) async-start(f32[32,2,128]{2,1,0:T(2,128)} %copy.69), calls=%async_computation.2 | async-start | bytes 65536 | tf_op jit(solution)/shard_map/all_to_all | solution.py:254
  53.9 4.6 %copy-start.11 = (f32[2,3,8,128]{3,2,1,0:T(8,128)S(1)}, f32[2,3,8,128]{3,2,1,0:T(8,128)}, u32[]{:S(2)}) copy-start(f32[2,3,8,128]{3,2,1,0:T(8,128)} %get-tuple-element.17) | copy-start | bytes 73732
  53.9 12.6 %all-to-all-start.3 = ((f32[32,1,644]{2,1,0:T(1,128)}), f32[32,1,644]{2,1,0:T(1,128)S(1)}, u32[]{:S(2)}, u32[]{:S(2)}) async-start(f32[32,1,644]{2,1,0:T(1,128)} %all_to_all.22), calls=%async_computation.3 | async-start | bytes 196608 | tf_op jit(solution)/shard_map/all_to_all | solution.py:302
  58.5 10.3 %collective-permute-start.2 = (f32[3,8,1,128]{3,1,0,2:T(8,128)S(1)}, f32[3,8,1,128]{3,1,0,2:T(8,128)S(1)}, u32[]{:S(2)}, u32[]{:S(2)}) collective-permute-start(f32[3,8,1,128]{3,1,0,2:T(8,128)S(1)} %get-tuple-element.45), channel_id=1, source_target_pairs={{0,4},{4,8},{8,12},{12,16},{16,20},{20,24},{24,28},{28,0},{1,5},{5... | collective-permute-start | bytes 36872 | tf_op jit(solution)/shard_map/ppermute | solution.py:284
  58.8 10.5 %collective-permute-start.3 = (f32[3,8,1,128]{3,1,0,2:T(8,128)S(1)}, f32[3,8,1,128]{3,1,0,2:T(8,128)S(1)}, u32[]{:S(2)}, u32[]{:S(2)}) collective-permute-start(f32[3,8,1,128]{3,1,0,2:T(8,128)S(1)} %get-tuple-element.46), channel_id=1, source_target_pairs={{4,0},{8,4},{12,8},{16,12},{20,16},{24,20},{28,24},{0,28},{5,1},{9... | collective-permute-start | bytes 36872 | tf_op jit(solution)/shard_map/ppermute | solution.py:285
  66.8 0.6 copy-start.2
  67.5 0.8 %slice-start.1 = ((f32[8,4,644]{2,1,0:T(4,128)}), f32[8,4,260]{2,1,0:T(4,128)S(1)}, s32[]{:S(2)}) async-start(f32[8,4,644]{2,1,0:T(4,128)} %copy-done.2), calls=%async_computation.5 | async-start | bytes 98304 | tf_op jit(solution)/shard_map/slice | solution.py:303
  69.1 0.9 %copy-start.4 = (f32[3,128,128]{2,1,0:T(8,128)S(1)}, f32[3,128,128]{2,1,0:T(8,128)}, u32[]{:S(2)}) copy-start(f32[3,128,128]{2,1,0:T(8,128)} %get-tuple-element.18) | copy-start | bytes 589828
  70.7 0.9 %copy-start.6 = (f32[3,8,16,128]{3,2,1,0:T(8,128)S(1)}, f32[3,8,16,128]{3,2,1,0:T(8,128)}, u32[]{:S(2)}) copy-start(f32[3,8,16,128]{3,2,1,0:T(8,128)} %fusion.3) | copy-start | bytes 589828

commit v12 on v11

--- a/solution.py
+++ b/solution.py
@@ -50,6 +50,12 @@
     depth = outs[0].shape[1] // outs[1].shape[2]
     surface = parts_ref[0, pl.ds(outs[0].shape[1] - depth, depth), :]
     outs[3][...] = product(table_ref[...], surface)
+
+
+def second_volume_kernel(field_ref, rate_ref, flow_ref, grad_ref, mats_ref, mass_ref, *outs):
+    section_ref = outs[3]
+    section_ref[...] = field_ref[...] + time_step * rate_ref[...]
+    volume_body(section_ref, flow_ref, grad_ref, mats_ref, mass_ref, *outs[:3])
 
 
 def volume_body(parts_ref, flow_ref, grad_ref, mats_ref, mass_ref, out_ref, rows_ref, cols_ref):
@@ -362,14 +368,22 @@
         )
         return jnp.dot(along_a, join_b, precision=highest)
 
-    def tendency(parts, surface):
+    def tendency(parts, surface, rate=None):
         shapes = (
             jax.ShapeDtypeStruct((3, rows, nb_dev), jnp.float32),
             jax.ShapeDtypeStruct((2, 3, radial_nodes, nb_dev), jnp.float32),
             jax.ShapeDtypeStruct((2, 3, rows), jnp.float32),
         )
         operands = (parts.reshape(3, rows, nb_dev), flat_flow, grads, mats, flat_mass)
-        if surface is None:
+        section = None
+        if rate is not None:
+            shapes = shapes + (jax.ShapeDtypeStruct((3, rows, nb_dev), jnp.float32),)
+            stacked, edge_rows, edge_cols, section = pl.pallas_call(
+                second_volume_kernel, out_shape=shapes
+            )(parts.reshape(3, rows, nb_dev), rate.reshape(3, rows, nb_dev), *operands[1:])
+            section = section.reshape(parts.shape)
+            partial = jnp.dot(analysis, surface, precision=highest)
+        elif surface is None:
             shapes = shapes + (jax.ShapeDtypeStruct(analysis.shape[:1] + (nb_dev,), jnp.float32),)
             stacked, edge_rows, edge_cols, partial = pl.pallas_call(
                 first_volume_kernel, out_shape=shapes
@@ -394,12 +408,11 @@
         padded = padded + plane_mask * flux_term
         plane_r = jnp.zeros_like(lax.slice_in_dim(padded, 0, 1, axis=1))
         padded = assemble_dim(padded, 1, plane_r, plane_r)
-        return assemble_ext(padded) / assembled[None], outer_rate
-
-    first_rate, first_outer = tendency(field, None)
-    section = field + time_step * first_rate
+        return assemble_ext(padded) / assembled[None], outer_rate, section
+
+    first_rate, first_outer, _ = tendency(field, None)
     section_outer = field[0, radial_nodes - 1] + time_step * first_outer
-    second_rate, _ = tendency(section, section_outer)
+    second_rate, _, section = tendency(field, section_outer, first_rate)
     return 0.5 * (field + section + time_step * second_rate)
 
 

time: 73.7 us -> 74.5 us (1.011)
  no operation moved by 1% of the time
where the time goes in v12:
time: 74.5 us; the launch traced here: 73.6 us
  starting transfers between devices  24.4 us (33%)
  local copies, waits for them, and re-layouts  15.9 us (21%)
  waiting for transfers between devices  14.7 us (20%)
  Pallas kernels  9.5 us (13%)
  matrix products  4.58 us (6%)
  other arithmetic  3.74 us (5%)
    all_to_all x2, waiting for transfers between devices, joint_exchange(): lax.all_to_all(message, both, 0, 0, tiled=True).reshape(tiles, groups, -1)  11.6 us
    all_to_all x2, starting transfers between devices, owner_map(): gathered = lax.all_to_all(partial, both, 0, 0, tiled=True)  9.86 us
    unnamed x55, local copies, waits for them, and re-layouts  7.76 us
    all_to_all x2, starting transfers between devices, joint_exchange(): lax.all_to_all(message, both, 0, 0, tiled=True).reshape(tiles, groups, -1)  7.29 us
    ppermute x2, starting transfers between devices, joint_exchange(): from_down = lax.ppermute(a_lo, 'tile', down)  6.66 us
    pallas_call x1, Pallas kernels, tendency(): pl.pallas_call(second_volume_kernel, out_shape=shapes)  3.52 us
    pallas_call x1, Pallas kernels, tendency(): pl.pallas_call(first_volume_kernel, out_shape=shapes)(*operands, analysis)  3.42 us
    dot_general x3, matrix products, assemble_ext(): return jnp.dot(along_a, join_b, precision=highest)  3.34 us
  transfers between devices with their start and end apart: 8, of which 4 were waited for; matrix products, arithmetic and copies ran while one was open for 10% of the time, Pallas kernels for 5%

profile of v12, /device:TPU:0, one launch (start us, length us, event | category | flops | bytes accessed | tf_op | source)
XLA Modules:
  0.0 73.6 jit_solution(13776434045310722499)
XLA Ops:
  0.0 0.7 copy-done.15
  0.7 0.7 copy-done.18
  1.4 0.1 fusion.45
  1.6 0.7 copy-done.16
  2.3 0.6 broadcast_multiply_fusion.1.table_ref
  2.9 2.6 %shard_map.184.grad_ref = f32[9,128,128]{2,1,0:T(8,128)} custom-call(f32[3,128,128]{2,1,0:T(8,128)} %bitcast.111, f32[6,128,128]{2,1,0:T(8,128)} %constant.256.clone.mats_ref), custom_call_target="tpu_custom_call" | custom-call | tf_op jit(solution)/shard_map/pallas_call | solution.py:249
  5.4 3.4 %shard_map.185 = (f32[3,128,128]{2,1,0:T(8,128)}, f32[2,3,8,128]{3,2,1,0:T(8,128)}, f32[2,3,128]{2,1,0:T(4,128)}, f32[64,128]{1,0:T(8,128)}) custom-call(f32[3,128,128]{2,1,0:T(8,128)} %bitcast.114, f32[3,128,128]{2,1,0:T(8,128)} %bitcast.112, f32[9,128,128]{2,1,0:T(8,128)} %shard_map.184.grad_ref, f32[6,128,128]{2,1,0:T(8,128)} %constant.256.clone.mats_ref, ...), custom_call_target="tpu_custom_call" | custom-call | tf_op jit(solution)/shard_map/pallas_call | solution.py:388
  8.8 7.3 %all-to-all-start = ((f32[32,2,128]{2,1,0:T(2,128)}), f32[32,2,128]{2,1,0:T(2,128)S(1)}, u32[]{:S(2)}, u32[]{:S(2)}) async-start(f32[32,2,128]{2,1,0:T(2,128)} %bitcast.124), calls=%async_computation | async-start | bytes 65536 | tf_op jit(solution)/shard_map/all_to_all | solution.py:260
  16.2 0.3 collective-permute-start
  16.5 3.3 %collective-permute-start.1 = (f32[3,8,1,128]{3,1,0,2:T(8,128)S(1)}, f32[3,8,1,128]{3,1,0,2:T(8,128)S(1)}, u32[]{:S(2)}, u32[]{:S(2)}) collective-permute-start(f32[3,8,1,128]{3,1,0,2:T(8,128)S(1)} %get-tuple-element.52), channel_id=1, source_target_pairs={{4,0},{8,4},{12,8},{16,12},{20,16},{24,20},{28,24},{0,28},{5,1},{9... | collective-permute-start | bytes 36872 | tf_op jit(solution)/shard_map/ppermute | solution.py:291
  19.8 0.7 copy-done.14
  20.9 0.6 copy-done.19
  21.6 1.8 %all-to-all-done = f32[32,2,128]{2,1,0:T(2,128)S(1)} async-done(((f32[32,2,128]{2,1,0:T(2,128)}), f32[32,2,128]{2,1,0:T(2,128)S(1)}, u32[]{:S(2)}, u32[]{:S(2)}) %all-to-all-start) | async-done | bytes 32800 | tf_op jit(solution)/shard_map/all_to_all | solution.py:260
  23.5 0.2 fusion.10
  23.8 0.1 pad_maximum_fusion.14
  23.9 0.1 stack.49
  24.0 0.1 stack.50
  24.0 0.1 stack.51
  24.1 0.1 stack.52
  24.4 0.7 all_to_all.19
  25.1 2.7 %all-to-all-start.1 = ((f32[32,1,644]{2,1,0:T(1,128)}), f32[32,1,644]{2,1,0:T(1,128)S(1)}, u32[]{:S(2)}, u32[]{:S(2)}) async-start(f32[32,1,644]{2,1,0:T(1,128)} %all_to_all.19), calls=%async_computation.1 | async-start | bytes 196608 | tf_op jit(solution)/shard_map/all_to_all | solution.py:308
  27.8 0.6 fusion.71
  28.5 7.3 %all-to-all-done.1 = f32[32,1,644]{2,1,0:T(1,128)S(1)} async-done(((f32[32,1,644]{2,1,0:T(1,128)}), f32[32,1,644]{2,1,0:T(1,128)S(1)}, u32[]{:S(2)}, u32[]{:S(2)}) %all-to-all-start.1) | async-done | bytes 82464 | tf_op jit(solution)/shard_map/all_to_all | solution.py:308
  35.7 0.2 reduce
  36.0 0.1 fusion.51
  36.7 0.2 reshape.885
  36.9 0.2 reshape.886
  37.2 0.7 slice-done
  38.0 0.7 copy-done.6
  38.7 0.2 fusion.4
  38.9 0.7 copy-done.12
  39.6 0.4 multiply_add_fusion
  40.3 0.8 %copy-done.7 = f32[130,128]{1,0:T(8,128)S(1)} copy-done((f32[130,128]{1,0:T(8,128)S(1)}, f32[130,128]{1,0:T(8,128)}, u32[]{:S(2)}) %copy-start.7) | copy-done | bytes 66584
  41.2 0.9 %fusion.7 = f32[16,128,1]{1,0,2:T(8,128)S(1)} fusion(f32[130,128]{1,0:T(8,128)S(1)} %copy-done.8, f32[130,128]{1,0:T(8,128)S(1)} %copy-done.9, f32[130,128]{1,0:T(8,128)S(1)} %copy-done.7, f32[]{:T(128)S(6)} %convert_element_type.77, f32[]{:T(128)S(6)} %convert_element_type.76, f32[2,1,130]{2,1,0:T(1,128)S(1)} %get-tuple-element.54, ...), kind=kOutput, calls=%fused_computation.12 | convolution fusion | flops 3271744 | bytes 232584 | tf_op jit(solution)/shard_map/dot_general | solution.py:369
  42.1 0.3 fusion.37
  42.4 0.6 copy.69
  43.0 2.6 %all-to-all-start.2 = ((f32[32,2,128]{2,1,0:T(2,128)}), f32[32,2,128]{2,1,0:T(2,128)S(1)}, u32[]{:S(2)}, u32[]{:S(2)}) async-start(f32[32,2,128]{2,1,0:T(2,128)} %copy.69), calls=%async_computation.2 | async-start | bytes 65536 | tf_op jit(solution)/shard_map/all_to_all | solution.py:260
  45.9 1.2 %convolution_divide_fusion.1 = f32[3,8,16,128]{3,2,1,0:T(8,128)} fusion(f32[3,8,2,1,130]{4,3,2,1,0:T(1,128)S(1)} %copy.68, f32[3,8,2,6,130]{4,3,2,1,0:T(8,128)S(1)} %slice.259, f32[3,8,2,1,130]{4,3,2,1,0:T(1,128)S(1)} %copy.67, f32[8,16,128]{2,1,0:T(8,128)S(1)} %broadcast_multiply_fusion, f32[130,128]{1,0:T(8,128)S(1)} %copy-done.8, ...), kind=kOutput, calls=%fused_computation.3 | convolution fusion | flops 76892672 | bytes 661512 | tf_op jit(solution)/shard_map/dot_general | solution.py:369
  47.1 3.5 %shard_map.186 = (f32[3,128,128]{2,1,0:T(8,128)}, f32[2,3,8,128]{3,2,1,0:T(8,128)}, f32[2,3,128]{2,1,0:T(4,128)}, f32[3,128,128]{2,1,0:T(8,128)}) custom-call(f32[3,128,128]{2,1,0:T(8,128)} %bitcast.115, f32[3,128,128]{2,1,0:T(8,128)} %bitcast.119, f32[3,128,128]{2,1,0:T(8,128)} %bitcast.113, f32[9,128,128]{2,1,0:T(8,128)} %shard_map.184.grad_ref, ...), custom_call_target="tpu_custom_call" | custom-call | tf_op jit(solution)/shard_map/pallas_call | solution.py:381
  50.6 0.7 fusion.76
  51.6 1.3 %all-to-all-done.2 = f32[32,2,128]{2,1,0:T(2,128)S(1)} async-done(((f32[32,2,128]{2,1,0:T(2,128)}), f32[32,2,128]{2,1,0:T(2,128)S(1)}, u32[]{:S(2)}, u32[]{:S(2)}) %all-to-all-start.2) | async-done | bytes 32800 | tf_op jit(solution)/shard_map/all_to_all | solution.py:260
  52.9 0.2 fusion.8
  53.2 0.1 pad_maximum_fusion.12
  53.3 0.1 stack.55
  53.4 0.1 stack.56
  53.5 0.1 stack.57
  53.6 0.1 stack.58
  53.8 0.7 all_to_all.22
  54.5 4.6 %all-to-all-start.3 = ((f32[32,1,644]{2,1,0:T(1,128)}), f32[32,1,644]{2,1,0:T(1,128)S(1)}, u32[]{:S(2)}, u32[]{:S(2)}) async-start(f32[32,1,644]{2,1,0:T(1,128)} %all_to_all.22), calls=%async_computation.3 | async-start | bytes 196608 | tf_op jit(solution)/shard_map/all_to_all | solution.py:308
  59.2 0.3 collective-permute-start.2
  59.5 3.4 %collective-permute-start.3 = (f32[3,8,1,128]{3,1,0,2:T(8,128)S(1)}, f32[3,8,1,128]{3,1,0,2:T(8,128)S(1)}, u32[]{:S(2)}, u32[]{:S(2)}) collective-permute-start(f32[3,8,1,128]{3,1,0,2:T(8,128)S(1)} %get-tuple-element.48), channel_id=1, source_target_pairs={{4,0},{8,4},{12,8},{16,12},{20,16},{24,20},{28,24},{0,28},{5,1},{9... | collective-permute-start | bytes 36872 | tf_op jit(solution)/shard_map/ppermute | solution.py:291
  62.8 4.4 %all-to-all-done.3 = f32[32,1,644]{2,1,0:T(1,128)S(1)} async-done(((f32[32,1,644]{2,1,0:T(1,128)}), f32[32,1,644]{2,1,0:T(1,128)S(1)}, u32[]{:S(2)}, u32[]{:S(2)}) %all-to-all-start.3) | async-done | bytes 82464 | tf_op jit(solution)/shard_map/all_to_all | solution.py:308
  67.2 0.2 reduce.7
  67.5 0.1 fusion.57
  67.6 0.5 copy-done.3
  68.4 0.5 slice-done.1
  69.0 0.2 fusion.3
  69.5 0.2 reshape.887
  69.8 0.2 reshape.888
  70.1 0.6 copy-done.4
  70.7 0.4 maximum_add_fusion
  71.6 0.6 copy-done.22
  72.2 0.1 copy-done.1
  72.3 1.2 %fusion.2 = f32[3,8,16,128]{3,2,1,0:T(8,128)} fusion(f32[3,8,2,1,130]{4,3,2,1,0:T(1,128)S(1)} %copy.84, f32[3,8,2,6,130]{4,3,2,1,0:T(8,128)S(1)} %slice.286, f32[3,8,2,1,130]{4,3,2,1,0:T(1,128)S(1)} %copy.83, f32[3,8,16,128]{3,2,1,0:T(8,128)S(1)} %copy-done.1, f32[3,8,16,128]{3,2,1,0:T(8,128)S(1)} %bitcast.126, ...), kind=kOutput, calls=%fused_computation.4 | convolution fusion | flops 77089280 | bytes 1054728 | tf_op jit(solution)/shard_map/dot_general | solution.py:369
  (134 shorter events, 4.0 us)
Async XLA Ops:
  0.0 23.5 %copy-start = (bf16[1,512,512]{2,1,0:T(8,128)(2,1)S(1)}, bf16[1,512,512]{2,1,0:T(8,128)(2,1)}, u32[]{:S(2)}) copy-start(bf16[1,512,512]{2,1,0:T(8,128)(2,1)} %param.21) | copy-start | bytes 1572868
  0.0 0.7 copy-start.15
  0.7 0.7 copy-start.18
  1.6 0.7 copy-start.16
  8.8 7.3 %copy-start.11 = (f32[2,3,8,128]{3,2,1,0:T(8,128)S(1)}, f32[2,3,8,128]{3,2,1,0:T(8,128)}, u32[]{:S(2)}) copy-start(f32[2,3,8,128]{3,2,1,0:T(8,128)} %get-tuple-element.15) | copy-start | bytes 73732
  8.8 14.6 %all-to-all-start = ((f32[32,2,128]{2,1,0:T(2,128)}), f32[32,2,128]{2,1,0:T(2,128)S(1)}, u32[]{:S(2)}, u32[]{:S(2)}) async-start(f32[32,2,128]{2,1,0:T(2,128)} %bitcast.124), calls=%async_computation | async-start | bytes 65536 | tf_op jit(solution)/shard_map/all_to_all | solution.py:260
  16.2 20.3 %collective-permute-start = (f32[3,8,1,128]{3,1,0,2:T(8,128)S(1)}, f32[3,8,1,128]{3,1,0,2:T(8,128)S(1)}, u32[]{:S(2)}, u32[]{:S(2)}) collective-permute-start(f32[3,8,1,128]{3,1,0,2:T(8,128)S(1)} %get-tuple-element.51), channel_id=1, source_target_pairs={{0,4},{4,8},{8,12},{12,16},{16,20},{20,24},{24,28},{28,0},{1,5},{5... | collective-permute-start | bytes 36872 | tf_op jit(solution)/shard_map/ppermute | solution.py:290
  16.5 20.6 %collective-permute-start.1 = (f32[3,8,1,128]{3,1,0,2:T(8,128)S(1)}, f32[3,8,1,128]{3,1,0,2:T(8,128)S(1)}, u32[]{:S(2)}, u32[]{:S(2)}) collective-permute-start(f32[3,8,1,128]{3,1,0,2:T(8,128)S(1)} %get-tuple-element.52), channel_id=1, source_target_pairs={{4,0},{8,4},{12,8},{16,12},{20,16},{24,20},{28,24},{0,28},{5,1},{9... | collective-permute-start | bytes 36872 | tf_op jit(solution)/shard_map/ppermute | solution.py:291
  19.8 0.7 copy-start.14
  20.8 0.7 copy-start.13
  20.8 0.7 copy-start.19
  20.8 0.7 copy-start.20
  20.8 0.7 copy-start.21
  25.1 2.7 %copy-start.17 = (f32[18]{0:T(128)S(1)}, f32[18]{0:T(128)}, u32[]{:S(2)}) copy-start(f32[18]{0:T(128)} %constant.270) | copy-start | bytes 220
  25.1 10.7 %all-to-all-start.1 = ((f32[32,1,644]{2,1,0:T(1,128)}), f32[32,1,644]{2,1,0:T(1,128)S(1)}, u32[]{:S(2)}, u32[]{:S(2)}) async-start(f32[32,1,644]{2,1,0:T(1,128)} %all_to_all.19), calls=%async_computation.1 | async-start | bytes 196608 | tf_op jit(solution)/shard_map/all_to_all | solution.py:308
  36.0 0.6 copy-start.2
  36.9 2.0 %copy-start.5 = (f32[3,128,128]{2,1,0:T(8,128)S(1)}, f32[3,128,128]{2,1,0:T(8,128)}, u32[]{:S(2)}) copy-start(f32[3,128,128]{2,1,0:T(8,128)} %get-tuple-element.16) | copy-start | bytes 589828
  37.1 0.8 %slice-start = ((f32[8,4,644]{2,1,0:T(4,128)}), f32[8,4,260]{2,1,0:T(4,128)S(1)}, s32[]{:S(2)}) async-start(f32[8,4,644]{2,1,0:T(4,128)} %copy-done.2), calls=%async_computation.4 | async-start | bytes 98304 | tf_op jit(solution)/shard_map/slice | solution.py:309
  37.9 0.7 %copy-start.6 = (f32[18,130]{1,0:T(8,128)S(1)}, f32[18,130]{1,0:T(8,128)}, u32[]{:S(2)}) copy-start(f32[18,130]{1,0:T(8,128)} %constant.264.clone) | copy-start | bytes 28084
  38.9 0.7 copy-start.12
  40.2 0.9 %copy-start.7 = (f32[130,128]{1,0:T(8,128)S(1)}, f32[130,128]{1,0:T(8,128)}, u32[]{:S(2)}) copy-start(f32[130,128]{1,0:T(8,128)} %constant.259.clone) | copy-start | bytes 199684
  40.3 0.9 %copy-start.8 = (f32[130,128]{1,0:T(8,128)S(1)}, f32[130,128]{1,0:T(8,128)}, u32[]{:S(2)}) copy-start(f32[130,128]{1,0:T(8,128)} %constant.260.clone) | copy-start | bytes 199684
  40.3 0.9 %copy-start.9 = (f32[130,128]{1,0:T(8,128)S(1)}, f32[130,128]{1,0:T(8,128)}, u32[]{:S(2)}) copy-start(f32[130,128]{1,0:T(8,128)} %constant.261.clone) | copy-start | bytes 199684
  43.0 9.9 %all-to-all-start.2 = ((f32[32,2,128]{2,1,0:T(2,128)}), f32[32,2,128]{2,1,0:T(2,128)S(1)}, u32[]{:S(2)}, u32[]{:S(2)}) async-start(f32[32,2,128]{2,1,0:T(2,128)} %copy.69), calls=%async_computation.2 | async-start | bytes 65536 | tf_op jit(solution)/shard_map/all_to_all | solution.py:260
  54.5 4.6 %copy-start.10 = (f32[2,3,8,128]{3,2,1,0:T(8,128)S(1)}, f32[2,3,8,128]{3,2,1,0:T(8,128)}, u32[]{:S(2)}) copy-start(f32[2,3,8,128]{3,2,1,0:T(8,128)} %get-tuple-element.19) | copy-start | bytes 73732
  54.5 12.7 %all-to-all-start.3 = ((f32[32,1,644]{2,1,0:T(1,128)}), f32[32,1,644]{2,1,0:T(1,128)S(1)}, u32[]{:S(2)}, u32[]{:S(2)}) async-start(f32[32,1,644]{2,1,0:T(1,128)} %all_to_all.22), calls=%async_computation.3 | async-start | bytes 196608 | tf_op jit(solution)/shard_map/all_to_all | solution.py:308
  59.2 10.3 %collective-permute-start.2 = (f32[3,8,1,128]{3,1,0,2:T(8,128)S(1)}, f32[3,8,1,128]{3,1,0,2:T(8,128)S(1)}, u32[]{:S(2)}, u32[]{:S(2)}) collective-permute-start(f32[3,8,1,128]{3,1,0,2:T(8,128)S(1)} %get-tuple-element.47), channel_id=1, source_target_pairs={{0,4},{4,8},{8,12},{12,16},{16,20},{20,24},{24,28},{28,0},{1,5},{5... | collective-permute-start | bytes 36872 | tf_op jit(solution)/shard_map/ppermute | solution.py:290
  59.5 10.5 %collective-permute-start.3 = (f32[3,8,1,128]{3,1,0,2:T(8,128)S(1)}, f32[3,8,1,128]{3,1,0,2:T(8,128)S(1)}, u32[]{:S(2)}, u32[]{:S(2)}) collective-permute-start(f32[3,8,1,128]{3,1,0,2:T(8,128)S(1)} %get-tuple-element.48), channel_id=1, source_target_pairs={{4,0},{8,4},{12,8},{16,12},{20,16},{24,20},{28,24},{0,28},{5,1},{9... | collective-permute-start | bytes 36872 | tf_op jit(solution)/shard_map/ppermute | solution.py:291
  67.5 0.6 copy-start.3
  68.1 0.8 %slice-start.1 = ((f32[8,4,644]{2,1,0:T(4,128)}), f32[8,4,260]{2,1,0:T(4,128)S(1)}, s32[]{:S(2)}) async-start(f32[8,4,644]{2,1,0:T(4,128)} %copy-done.3), calls=%async_computation.5 | async-start | bytes 98304 | tf_op jit(solution)/shard_map/slice | solution.py:309
  69.8 0.9 %copy-start.4 = (f32[3,128,128]{2,1,0:T(8,128)S(1)}, f32[3,128,128]{2,1,0:T(8,128)}, u32[]{:S(2)}) copy-start(f32[3,128,128]{2,1,0:T(8,128)} %get-tuple-element.20) | copy-start | bytes 589828
  71.3 0.9 %copy-start.22 = (f32[3,128,128]{2,1,0:T(8,128)S(1)}, f32[3,128,128]{2,1,0:T(8,128)}, u32[]{:S(2)}) copy-start(f32[3,128,128]{2,1,0:T(8,128)} %get-tuple-element.17) | copy-start | bytes 589828
  71.4 1.0 %copy-start.1 = (f32[3,8,16,128]{3,2,1,0:T(8,128)S(1)}, f32[3,8,16,128]{3,2,1,0:T(8,128)}, u32[]{:S(2)}) copy-start(f32[3,8,16,128]{3,2,1,0:T(8,128)} %param.19) | copy-start | bytes 589828

commit v13 on v9

--- a/solution.py
+++ b/solution.py
@@ -352,6 +352,7 @@
     edge_trail[nb_dev + 1, nb_dev - 1] = 1.0
     join_b = join_b + lead * edge_lead + trail * edge_trail
 
+
     def assemble_ext(padded):
         last = padded.ndim - 1
         along_a = assemble_dim(
@@ -375,7 +376,9 @@
             stacked, edge_rows, edge_cols = pl.pallas_call(volume_kernel, out_shape=shapes)(
                 *operands
             )
-            partial = jnp.dot(analysis, surface, precision=highest)
+            partial = jnp.einsum(
+                "kca,ab->kcb", analysis.reshape(-1, 2, na_dev), surface, precision=highest
+            )
         stacked = stacked.reshape(parts.shape)
         sent = owner_map(partial)
         if carried_halo:
@@ -388,7 +391,11 @@
         flux_term = flux_of(returned)
         outer = padded[0, radial_nodes - 1] + flux_term
         outer_rate = assemble_ext(outer) / assembled[radial_nodes - 1]
-        padded = padded.at[0, radial_nodes - 1].add(flux_term)
+        outer_plane = lax.slice_in_dim(padded[:1], radial_nodes - 1, radial_nodes, axis=1)
+        first = jnp.concatenate(
+            [padded[:1, : radial_nodes - 1], outer_plane + flux_term], axis=1
+        )
+        padded = jnp.concatenate([first, padded[1:]], axis=0)
         plane_r = jnp.zeros_like(lax.slice_in_dim(padded, 0, 1, axis=1))
         padded = assemble_dim(padded, 1, plane_r, plane_r)
         return assemble_ext(padded) / assembled[None], outer_rate

time: 78.2 us -> 75.1 us (0.960)
  waiting for transfers between devices: 13 us -> 20.4 us
  matrix products: 7.76 us -> 3.89 us
  starting transfers between devices: 25.7 us -> 22.6 us
  local copies, waits for them, and re-layouts: 16.3 us -> 13.6 us
  other arithmetic: 4.39 us -> 3.6 us
    all_to_all x2, waiting for transfers between devices: 1.31 us -> 8.77 us  [owner_map(): gathered = lax.all_to_all(partial, both, 0, 0, tiled=True)]
    dot_general x2, matrix products: 4.31 us -> 0.45 us  [flux_of(): flux = -jnp.dot(synth, returned.reshape(-1, nb_dev + 2), precision=highest)]
    all_to_all x2, starting transfers between devices: 8.57 us -> 5.4 us  [joint_exchange(): lax.all_to_all(message, both, 0, 0, tiled=True).reshape(tiles, groups, -1)]
    unnamed x56 -> x55, local copies, waits for them, and re-layouts: 7.33 us -> 5.97 us
  transfers between devices with their start and end apart: 8 -> 8, of which waited for: 3 -> 4; matrix products, arithmetic and copies ran while one was open for 11% -> 7% of each run, Pallas kernels for 4% -> 0%
where the time goes in v13:
time: 75.1 us; the launch traced here: 74.4 us
  starting transfers between devices  22.6 us (30%)
  waiting for transfers between devices  20.4 us (27%)
  local copies, waits for them, and re-layouts  13.6 us (18%)
  Pallas kernels  9.46 us (13%)
  matrix products  3.89 us (5%)
  other arithmetic  3.6 us (5%)
    all_to_all x2, waiting for transfers between devices, joint_exchange(): lax.all_to_all(message, both, 0, 0, tiled=True).reshape(tiles, groups, -1)  11.6 us
    all_to_all x2, starting transfers between devices, owner_map(): gathered = lax.all_to_all(partial, both, 0, 0, tiled=True)  9.97 us
    all_to_all x2, waiting for transfers between devices, owner_map(): gathered = lax.all_to_all(partial, both, 0, 0, tiled=True)  8.77 us
    ppermute x2, starting transfers between devices, joint_exchange(): from_down = lax.ppermute(a_lo, 'tile', down)  6.8 us
    unnamed x55, local copies, waits for them, and re-layouts  5.97 us
    all_to_all x2, starting transfers between devices, joint_exchange(): lax.all_to_all(message, both, 0, 0, tiled=True).reshape(tiles, groups, -1)  5.4 us
    pallas_call x1, Pallas kernels, tendency(): pl.pallas_call(volume_kernel, out_shape=shapes)(*operands)  3.47 us
    pallas_call x1, Pallas kernels, tendency(): pl.pallas_call(first_volume_kernel, out_shape=shapes)(*operands, analysis)  3.42 us
  transfers between devices with their start and end apart: 8, of which 4 were waited for; matrix products, arithmetic and copies ran while one was open for 7% of the time, Pallas kernels for 0%

profile of v13, /device:TPU:0, one launch (start us, length us, event | category | flops | bytes accessed | tf_op | source)
XLA Modules:
  0.0 74.4 jit_solution(13673373613959588443)
XLA Ops:
  0.0 0.7 copy-done.16
  0.7 0.6 copy-done.19
  1.4 0.1 fusion.79
  1.5 0.1 copy.53
  1.6 2.6 %shard_map.175.grad_ref = f32[9,128,128]{2,1,0:T(8,128)} custom-call(f32[3,128,128]{2,1,0:T(8,128)} %bitcast.114, f32[6,128,128]{2,1,0:T(8,128)} %constant.254.clone.mats_ref), custom_call_target="tpu_custom_call" | custom-call | tf_op jit(solution)/shard_map/pallas_call | solution.py:243
  4.2 0.7 copy-done.17
  4.8 0.6 broadcast_multiply_fusion.1.table_ref
  5.4 3.4 %shard_map.176 = (f32[3,128,128]{2,1,0:T(8,128)}, f32[2,3,8,128]{3,2,1,0:T(8,128)}, f32[2,3,128]{2,1,0:T(4,128)}, f32[64,128]{1,0:T(8,128)}) custom-call(f32[3,128,128]{2,1,0:T(8,128)} %bitcast.123, f32[3,128,128]{2,1,0:T(8,128)} %bitcast.115, f32[9,128,128]{2,1,0:T(8,128)} %shard_map.175.grad_ref, f32[6,128,128]{2,1,0:T(8,128)} %constant.254.clone.mats_ref, ...), custom_call_target="tpu_custom_call" | custom-call | tf_op jit(solution)/shard_map/pallas_call | solution.py:372
  8.9 7.3 %all-to-all-start = ((f32[32,2,128]{2,1,0:T(2,128)}), f32[32,2,128]{2,1,0:T(2,128)S(1)}, u32[]{:S(2)}, u32[]{:S(2)}) async-start(f32[32,2,128]{2,1,0:T(2,128)} %bitcast.128), calls=%async_computation | async-start | bytes 65536 | tf_op jit(solution)/shard_map/all_to_all | solution.py:254
  16.2 0.3 collective-permute-start
  16.5 3.3 %collective-permute-start.1 = (f32[3,8,1,128]{3,1,0,2:T(8,128)S(1)}, f32[3,8,1,128]{3,1,0,2:T(8,128)S(1)}, u32[]{:S(2)}, u32[]{:S(2)}) collective-permute-start(f32[3,8,1,128]{3,1,0,2:T(8,128)S(1)} %get-tuple-element.49), channel_id=1, source_target_pairs={{4,0},{8,4},{12,8},{16,12},{20,16},{24,20},{28,24},{0,28},{5,1},{9... | collective-permute-start | bytes 36872 | tf_op jit(solution)/shard_map/ppermute | solution.py:285
  19.8 0.7 copy-done.14
  20.9 0.6 copy-done.20
  21.6 1.8 %all-to-all-done = f32[32,2,128]{2,1,0:T(2,128)S(1)} async-done(((f32[32,2,128]{2,1,0:T(2,128)}), f32[32,2,128]{2,1,0:T(2,128)S(1)}, u32[]{:S(2)}, u32[]{:S(2)}) %all-to-all-start) | async-done | bytes 32800 | tf_op jit(solution)/shard_map/all_to_all | solution.py:254
  23.5 0.2 fusion.45
  23.8 0.1 pad_maximum_fusion.14
  23.9 0.1 stack.52
  24.0 0.1 stack.51
  24.0 0.1 stack.50
  24.1 0.1 stack.49
  24.4 0.7 all_to_all.19
  25.1 2.7 %all-to-all-start.1 = ((f32[32,1,644]{2,1,0:T(1,128)}), f32[32,1,644]{2,1,0:T(1,128)S(1)}, u32[]{:S(2)}, u32[]{:S(2)}) async-start(f32[32,1,644]{2,1,0:T(1,128)} %all_to_all.19), calls=%async_computation.1 | async-start | bytes 196608 | tf_op jit(solution)/shard_map/all_to_all | solution.py:302
  27.8 0.6 fusion.105
  28.5 7.3 %all-to-all-done.1 = f32[32,1,644]{2,1,0:T(1,128)S(1)} async-done(((f32[32,1,644]{2,1,0:T(1,128)}), f32[32,1,644]{2,1,0:T(1,128)S(1)}, u32[]{:S(2)}, u32[]{:S(2)}) %all-to-all-start.1) | async-done | bytes 82464 | tf_op jit(solution)/shard_map/all_to_all | solution.py:302
  35.7 0.2 reduce
  36.0 0.1 fusion.89
  36.6 0.2 reshape.827
  36.9 0.2 reshape.828
  37.2 0.7 slice-done.1
  37.9 0.1 reshape_reshape.6
  38.0 0.6 copy-done.7
  38.7 0.2 bitcast_add_fusion
  38.9 0.3 fusion.18
  39.9 0.6 copy-done.10
  40.4 0.1 copy-done.5
  40.7 1.2 %fusion.3 = f32[3,8,16,128]{3,2,1,0:T(8,128)} fusion(f32[3,8,16,128]{3,2,1,0:T(8,128)S(1)} %copy-done.5, f32[3,8,2,1,130]{4,3,2,1,0:T(1,128)S(1)} %copy.67, f32[3,8,2,6,130]{4,3,2,1,0:T(8,128)S(1)} %slice.284, f32[3,8,2,1,130]{4,3,2,1,0:T(1,128)S(1)} %copy.66, f32[8,16,128]{2,1,0:T(8,128)S(1)} %broadcast_multiply_fusion, f32[130,128]{1,0:T(8,128)S(1)} %copy-done.8, ...), kind=kOutput, calls=%fused_computation.5 | convolution fusion | flops 76990976 | bytes 858120 | tf_op jit(solution)/shard_map/dot_general | solution.py:361
  41.9 3.5 %shard_map.177 = (f32[3,128,128]{2,1,0:T(8,128)}, f32[2,3,8,128]{3,2,1,0:T(8,128)}, f32[2,3,128]{2,1,0:T(4,128)}) custom-call(f32[3,128,128]{2,1,0:T(8,128)} %bitcast.124, f32[3,128,128]{2,1,0:T(8,128)} %bitcast.116, f32[9,128,128]{2,1,0:T(8,128)} %shard_map.175.grad_ref, f32[6,128,128]{2,1,0:T(8,128)} %constant.254.clone.mats_ref, ...), custom_call_target="tpu_custom_call" | custom-call | tf_op jit(solution)/shard_map/pallas_call | solution.py:376
  45.4 0.2 fusion.11
  45.6 0.3 fusion.71
  45.9 0.6 copy.68
  46.6 2.7 %all-to-all-start.2 = ((f32[32,2,128]{2,1,0:T(2,128)}), f32[32,2,128]{2,1,0:T(2,128)S(1)}, u32[]{:S(2)}, u32[]{:S(2)}) async-start(f32[32,2,128]{2,1,0:T(2,128)} %copy.68), calls=%async_computation.2 | async-start | bytes 65536 | tf_op jit(solution)/shard_map/all_to_all | solution.py:254
  49.6 6.9 %all-to-all-done.2 = f32[32,2,128]{2,1,0:T(2,128)S(1)} async-done(((f32[32,2,128]{2,1,0:T(2,128)}), f32[32,2,128]{2,1,0:T(2,128)S(1)}, u32[]{:S(2)}, u32[]{:S(2)}) %all-to-all-start.2) | async-done | bytes 32800 | tf_op jit(solution)/shard_map/all_to_all | solution.py:254
  56.6 0.2 fusion.43
  56.9 0.1 pad_maximum_fusion.12
  57.0 0.1 stack.58
  57.1 0.1 stack.57
  57.2 0.1 stack.56
  57.2 0.1 stack.55
  57.5 0.7 all_to_all.22
  58.2 2.7 %all-to-all-start.3 = ((f32[32,1,644]{2,1,0:T(1,128)}), f32[32,1,644]{2,1,0:T(1,128)S(1)}, u32[]{:S(2)}, u32[]{:S(2)}) async-start(f32[32,1,644]{2,1,0:T(1,128)} %all_to_all.22), calls=%async_computation.3 | async-start | bytes 196608 | tf_op jit(solution)/shard_map/all_to_all | solution.py:302
  60.9 0.2 collective-permute-start.2
  61.1 3.5 %collective-permute-start.3 = (f32[3,8,1,128]{3,1,0,2:T(8,128)S(1)}, f32[3,8,1,128]{3,1,0,2:T(8,128)S(1)}, u32[]{:S(2)}, u32[]{:S(2)}) collective-permute-start(f32[3,8,1,128]{3,1,0,2:T(8,128)S(1)} %get-tuple-element.45), channel_id=1, source_target_pairs={{4,0},{8,4},{12,8},{16,12},{20,16},{24,20},{28,24},{0,28},{5,1},{9... | collective-permute-start | bytes 36872 | tf_op jit(solution)/shard_map/ppermute | solution.py:285
  64.6 4.4 %all-to-all-done.3 = f32[32,1,644]{2,1,0:T(1,128)S(1)} async-done(((f32[32,1,644]{2,1,0:T(1,128)}), f32[32,1,644]{2,1,0:T(1,128)S(1)}, u32[]{:S(2)}, u32[]{:S(2)}) %all-to-all-start.3) | async-done | bytes 82464 | tf_op jit(solution)/shard_map/all_to_all | solution.py:302
  69.0 0.2 reduce.7
  69.3 0.1 fusion.95
  69.8 0.1 reshape.818
  70.0 0.2 reshape.829
  70.2 0.2 reshape.830
  70.6 0.7 slice-done
  71.3 0.1 reshape_reshape.7
  71.4 0.2 fusion.8
  71.6 0.3 fusion.31
  72.4 0.7 copy-done.6
  73.2 1.2 %fusion.4 = f32[3,8,16,128]{3,2,1,0:T(8,128)} fusion(f32[3,8,2,1,130]{4,3,2,1,0:T(1,128)S(1)} %copy.83, f32[3,8,2,6,130]{4,3,2,1,0:T(8,128)S(1)} %slice.310, f32[3,8,2,1,130]{4,3,2,1,0:T(1,128)S(1)} %copy.82, f32[3,8,16,128]{3,2,1,0:T(8,128)S(1)} %copy-done.5, f32[3,8,16,128]{3,2,1,0:T(8,128)S(1)} %copy-done.6, ...), kind=kOutput, calls=%fused_computation.6 | convolution fusion | flops 77089280 | bytes 1054728 | tf_op jit(solution)/shard_map/dot_general | solution.py:361
  (134 shorter events, 3.8 us)
Async XLA Ops:
  0.0 23.5 %copy-start = (bf16[1,512,512]{2,1,0:T(8,128)(2,1)S(1)}, bf16[1,512,512]{2,1,0:T(8,128)(2,1)}, u32[]{:S(2)}) copy-start(bf16[1,512,512]{2,1,0:T(8,128)(2,1)} %param.20) | copy-start | bytes 1572868
  0.0 0.7 copy-start.16
  0.7 0.7 copy-start.19
  4.2 0.7 copy-start.17
  8.9 7.3 %copy-start.12 = (f32[2,3,8,128]{3,2,1,0:T(8,128)S(1)}, f32[2,3,8,128]{3,2,1,0:T(8,128)}, u32[]{:S(2)}) copy-start(f32[2,3,8,128]{3,2,1,0:T(8,128)} %get-tuple-element.14) | copy-start | bytes 73732
  8.9 14.6 %all-to-all-start = ((f32[32,2,128]{2,1,0:T(2,128)}), f32[32,2,128]{2,1,0:T(2,128)S(1)}, u32[]{:S(2)}, u32[]{:S(2)}) async-start(f32[32,2,128]{2,1,0:T(2,128)} %bitcast.128), calls=%async_computation | async-start | bytes 65536 | tf_op jit(solution)/shard_map/all_to_all | solution.py:254
  16.2 20.3 %collective-permute-start = (f32[3,8,1,128]{3,1,0,2:T(8,128)S(1)}, f32[3,8,1,128]{3,1,0,2:T(8,128)S(1)}, u32[]{:S(2)}, u32[]{:S(2)}) collective-permute-start(f32[3,8,1,128]{3,1,0,2:T(8,128)S(1)} %get-tuple-element.50), channel_id=1, source_target_pairs={{0,4},{4,8},{8,12},{12,16},{16,20},{20,24},{24,28},{28,0},{1,5},{5... | collective-permute-start | bytes 36872 | tf_op jit(solution)/shard_map/ppermute | solution.py:284
  16.5 20.6 %collective-permute-start.1 = (f32[3,8,1,128]{3,1,0,2:T(8,128)S(1)}, f32[3,8,1,128]{3,1,0,2:T(8,128)S(1)}, u32[]{:S(2)}, u32[]{:S(2)}) collective-permute-start(f32[3,8,1,128]{3,1,0,2:T(8,128)S(1)} %get-tuple-element.49), channel_id=1, source_target_pairs={{4,0},{8,4},{12,8},{16,12},{20,16},{24,20},{28,24},{0,28},{5,1},{9... | collective-permute-start | bytes 36872 | tf_op jit(solution)/shard_map/ppermute | solution.py:285
  19.8 0.7 copy-start.14
  20.8 0.7 copy-start.13
  20.8 0.7 copy-start.20
  20.8 0.7 copy-start.21
  20.8 0.7 copy-start.22
  25.1 2.7 %copy-start.18 = (f32[18]{0:T(128)S(1)}, f32[18]{0:T(128)}, u32[]{:S(2)}) copy-start(f32[18]{0:T(128)} %constant.266) | copy-start | bytes 220
  25.1 10.7 %all-to-all-start.1 = ((f32[32,1,644]{2,1,0:T(1,128)}), f32[32,1,644]{2,1,0:T(1,128)S(1)}, u32[]{:S(2)}, u32[]{:S(2)}) async-start(f32[32,1,644]{2,1,0:T(1,128)} %all_to_all.19), calls=%async_computation.1 | async-start | bytes 196608 | tf_op jit(solution)/shard_map/all_to_all | solution.py:302
  36.0 0.6 copy-start.4
  36.8 1.2 %copy-start.1 = (f32[3,128,128]{2,1,0:T(8,128)S(1)}, f32[3,128,128]{2,1,0:T(8,128)}, u32[]{:S(2)}) copy-start(f32[3,128,128]{2,1,0:T(8,128)} %get-tuple-element.15) | copy-start | bytes 589828
  37.1 0.8 %slice-start.1 = ((f32[8,4,644]{2,1,0:T(4,128)}), f32[8,4,260]{2,1,0:T(4,128)S(1)}, s32[]{:S(2)}) async-start(f32[8,4,644]{2,1,0:T(4,128)} %copy-done.4), calls=%async_computation.5 | async-start | bytes 98304 | tf_op jit(solution)/shard_map/slice | solution.py:303
  37.9 0.7 copy-start.7
  39.5 0.9 %copy-start.10 = (f32[130,128]{1,0:T(8,128)S(1)}, f32[130,128]{1,0:T(8,128)}, u32[]{:S(2)}) copy-start(f32[130,128]{1,0:T(8,128)} %constant.257.clone) | copy-start | bytes 199684
  39.6 0.9 %copy-start.5 = (f32[3,8,16,128]{3,2,1,0:T(8,128)S(1)}, f32[3,8,16,128]{3,2,1,0:T(8,128)}, u32[]{:S(2)}) copy-start(f32[3,8,16,128]{3,2,1,0:T(8,128)} %param.18) | copy-start | bytes 589828
  39.7 0.9 %copy-start.9 = (f32[130,128]{1,0:T(8,128)S(1)}, f32[130,128]{1,0:T(8,128)}, u32[]{:S(2)}) copy-start(f32[130,128]{1,0:T(8,128)} %constant.259.clone) | copy-start | bytes 199684
  39.8 0.9 %copy-start.8 = (f32[130,128]{1,0:T(8,128)S(1)}, f32[130,128]{1,0:T(8,128)}, u32[]{:S(2)}) copy-start(f32[130,128]{1,0:T(8,128)} %constant.258.clone) | copy-start | bytes 199684
  46.6 2.7 %copy-start.15 = (f32[2,3,128]{2,1,0:T(4,128)S(1)}, f32[2,3,128]{2,1,0:T(4,128)}, u32[]{:S(2)}) copy-start(f32[2,3,128]{2,1,0:T(4,128)} %get-tuple-element.16) | copy-start | bytes 9220
  46.6 10.0 %all-to-all-start.2 = ((f32[32,2,128]{2,1,0:T(2,128)}), f32[32,2,128]{2,1,0:T(2,128)S(1)}, u32[]{:S(2)}, u32[]{:S(2)}) async-start(f32[32,2,128]{2,1,0:T(2,128)} %copy.68), calls=%async_computation.2 | async-start | bytes 65536 | tf_op jit(solution)/shard_map/all_to_all | solution.py:254
  58.2 2.7 %copy-start.11 = (f32[2,3,8,128]{3,2,1,0:T(8,128)S(1)}, f32[2,3,8,128]{3,2,1,0:T(8,128)}, u32[]{:S(2)}) copy-start(f32[2,3,8,128]{3,2,1,0:T(8,128)} %get-tuple-element.17) | copy-start | bytes 73732
  58.2 10.8 %all-to-all-start.3 = ((f32[32,1,644]{2,1,0:T(1,128)}), f32[32,1,644]{2,1,0:T(1,128)S(1)}, u32[]{:S(2)}, u32[]{:S(2)}) async-start(f32[32,1,644]{2,1,0:T(1,128)} %all_to_all.22), calls=%async_computation.3 | async-start | bytes 196608 | tf_op jit(solution)/shard_map/all_to_all | solution.py:302
  60.9 8.9 %collective-permute-start.2 = (f32[3,8,1,128]{3,1,0,2:T(8,128)S(1)}, f32[3,8,1,128]{3,1,0,2:T(8,128)S(1)}, u32[]{:S(2)}, u32[]{:S(2)}) collective-permute-start(f32[3,8,1,128]{3,1,0,2:T(8,128)S(1)} %get-tuple-element.46), channel_id=1, source_target_pairs={{0,4},{4,8},{8,12},{12,16},{16,20},{20,24},{24,28},{28,0},{1,5},{5... | collective-permute-start | bytes 36872 | tf_op jit(solution)/shard_map/ppermute | solution.py:284
  61.1 9.4 %collective-permute-start.3 = (f32[3,8,1,128]{3,1,0,2:T(8,128)S(1)}, f32[3,8,1,128]{3,1,0,2:T(8,128)S(1)}, u32[]{:S(2)}, u32[]{:S(2)}) collective-permute-start(f32[3,8,1,128]{3,1,0,2:T(8,128)S(1)} %get-tuple-element.45), channel_id=1, source_target_pairs={{4,0},{8,4},{12,8},{16,12},{20,16},{24,20},{28,24},{0,28},{5,1},{9... | collective-permute-start | bytes 36872 | tf_op jit(solution)/shard_map/ppermute | solution.py:285
  69.3 0.7 copy-start.3
  70.2 1.2 %copy-start.2 = (f32[3,128,128]{2,1,0:T(8,128)S(1)}, f32[3,128,128]{2,1,0:T(8,128)}, u32[]{:S(2)}) copy-start(f32[3,128,128]{2,1,0:T(8,128)} %get-tuple-element.18) | copy-start | bytes 589828
  70.4 0.8 %slice-start = ((f32[8,4,644]{2,1,0:T(4,128)}), f32[8,4,260]{2,1,0:T(4,128)S(1)}, s32[]{:S(2)}) async-start(f32[8,4,644]{2,1,0:T(4,128)} %copy-done.3), calls=%async_computation.4 | async-start | bytes 98304 | tf_op jit(solution)/shard_map/slice | solution.py:303
  72.2 0.9 %copy-start.6 = (f32[3,8,16,128]{3,2,1,0:T(8,128)S(1)}, f32[3,8,16,128]{3,2,1,0:T(8,128)}, u32[]{:S(2)}) copy-start(f32[3,8,16,128]{3,2,1,0:T(8,128)} %fusion.3) | copy-start | bytes 589828

commit v14 on v11

--- a/solution.py
+++ b/solution.py
@@ -45,7 +45,9 @@
     volume_body(parts_ref, flow_ref, grad_ref, mats_ref, mass_ref, *outs)
 
 
-def first_volume_kernel(parts_ref, flow_ref, grad_ref, mats_ref, mass_ref, table_ref, *outs):
+def first_volume_kernel(parts_ref, flow_ref, mats_ref, mass_ref, table_ref, *outs):
+    grad_ref = outs[4]
+    gradient_kernel(flow_ref, mats_ref, grad_ref)
     volume_body(parts_ref, flow_ref, grad_ref, mats_ref, mass_ref, *outs[:3])
     depth = outs[0].shape[1] // outs[1].shape[2]
     surface = parts_ref[0, pl.ds(outs[0].shape[1] - depth, depth), :]
@@ -240,9 +242,6 @@
     mats = derivative_tables(radial_nodes, na_dev, nb_dev)
     flat_mass = mass3.reshape(rows, nb_dev)
     flat_flow = flow.reshape(3, rows, nb_dev)
-    grads = pl.pallas_call(
-        gradient_kernel, out_shape=jax.ShapeDtypeStruct((9, rows, nb_dev), jnp.float32)
-    )(flat_flow, mats)
 
     angle = phases(wave_of_slot, tile_index * elems_a, elems_a, span, points)
     analysis = (
@@ -362,21 +361,27 @@
         )
         return jnp.dot(along_a, join_b, precision=highest)
 
+    shapes = (
+        jax.ShapeDtypeStruct((3, rows, nb_dev), jnp.float32),
+        jax.ShapeDtypeStruct((2, 3, radial_nodes, nb_dev), jnp.float32),
+        jax.ShapeDtypeStruct((2, 3, rows), jnp.float32),
+    )
+    first_outs = pl.pallas_call(
+        first_volume_kernel,
+        out_shape=shapes
+        + (
+            jax.ShapeDtypeStruct(analysis.shape[:1] + (nb_dev,), jnp.float32),
+            jax.ShapeDtypeStruct((9, rows, nb_dev), jnp.float32),
+        ),
+    )(field.reshape(3, rows, nb_dev), flat_flow, mats, flat_mass, analysis)
+    grads = first_outs[4]
+
     def tendency(parts, surface):
-        shapes = (
-            jax.ShapeDtypeStruct((3, rows, nb_dev), jnp.float32),
-            jax.ShapeDtypeStruct((2, 3, radial_nodes, nb_dev), jnp.float32),
-            jax.ShapeDtypeStruct((2, 3, rows), jnp.float32),
-        )
-        operands = (parts.reshape(3, rows, nb_dev), flat_flow, grads, mats, flat_mass)
         if surface is None:
-            shapes = shapes + (jax.ShapeDtypeStruct(analysis.shape[:1] + (nb_dev,), jnp.float32),)
-            stacked, edge_rows, edge_cols, partial = pl.pallas_call(
-                first_volume_kernel, out_shape=shapes
-            )(*operands, analysis)
+            stacked, edge_rows, edge_cols, partial = first_outs[:4]
         else:
             stacked, edge_rows, edge_cols = pl.pallas_call(volume_kernel, out_shape=shapes)(
-                *operands
+                parts.reshape(3, rows, nb_dev), flat_flow, grads, mats, flat_mass
             )
             partial = jnp.dot(analysis, surface, precision=highest)
         stacked = stacked.reshape(parts.shape)

time: 73.7 us -> 71.7 us (0.973)
  Pallas kernels: 9.44 us -> 7.45 us
    pallas_call x3 -> x2, Pallas kernels: 9.44 us -> 7.45 us  [the longest x1 3.98 us: local(): pl.pallas_call(first_volume_kernel, out_shape=shapes + (jax.ShapeDtypeStr...]
where the time goes in v14:
time: 71.7 us; the launch traced here: 70.9 us
  starting transfers between devices  24.3 us (34%)
  local copies, waits for them, and re-layouts  16 us (22%)
  waiting for transfers between devices  14.8 us (21%)
  Pallas kernels  7.45 us (10%)
  matrix products  3.89 us (5%)
  other arithmetic  3.74 us (5%)
  between operations  0.72 us (1%)
    all_to_all x2, waiting for transfers between devices, joint_exchange(): lax.all_to_all(message, both, 0, 0, tiled=True).reshape(tiles, groups, -1)  11.6 us
    all_to_all x2, starting transfers between devices, owner_map(): gathered = lax.all_to_all(partial, both, 0, 0, tiled=True)  9.84 us
    unnamed x55, local copies, waits for them, and re-layouts  7.83 us
    all_to_all x2, starting transfers between devices, joint_exchange(): lax.all_to_all(message, both, 0, 0, tiled=True).reshape(tiles, groups, -1)  7.24 us
    ppermute x2, starting transfers between devices, joint_exchange(): from_down = lax.ppermute(a_lo, 'tile', down)  6.66 us
    pallas_call x1, Pallas kernels, local(): pl.pallas_call(first_volume_kernel, out_shape=shapes + (jax.ShapeDtypeStr...  3.98 us
    pallas_call x1, Pallas kernels, tendency(): pl.pallas_call(volume_kernel, out_shape=shapes)  3.47 us
    all_to_all x2, waiting for transfers between devices, owner_map(): gathered = lax.all_to_all(partial, both, 0, 0, tiled=True)  3.13 us
  transfers between devices with their start and end apart: 8, of which 4 were waited for; matrix products, arithmetic and copies ran while one was open for 10% of the time, Pallas kernels for 5%

profile of v14, /device:TPU:0, one launch (start us, length us, event | category | flops | bytes accessed | tf_op | source)
XLA Modules:
  0.0 70.9 jit_solution(15838739838236258236)
XLA Ops:
  0.0 0.7 copy-done.16
  0.7 0.7 copy-done.19
  1.4 0.1 fusion.47
  1.5 0.1 copy.54
  1.6 0.7 copy-done.17
  2.3 0.6 broadcast_multiply_fusion.1.table_ref
  2.9 4.0 %shard_map.184 = (f32[3,128,128]{2,1,0:T(8,128)}, f32[2,3,8,128]{3,2,1,0:T(8,128)}, f32[2,3,128]{2,1,0:T(4,128)}, f32[64,128]{1,0:T(8,128)}, f32[9,128,128]{2,1,0:T(8,128)}) custom-call(f32[3,128,128]{2,1,0:T(8,128)} %bitcast.114, f32[3,128,128]{2,1,0:T(8,128)} %bitcast.110, f32[6,128,128]{2,1,0:T(8,128)} %constant.256.clone.mats_ref, ...), custom_call_target="tpu_custom_call" | custom-call | tf_op jit(solution)/shard_map/pallas_call | solution.py:369
  6.8 7.3 %all-to-all-start = ((f32[32,2,128]{2,1,0:T(2,128)}), f32[32,2,128]{2,1,0:T(2,128)S(1)}, u32[]{:S(2)}, u32[]{:S(2)}) async-start(f32[32,2,128]{2,1,0:T(2,128)} %bitcast.121), calls=%async_computation | async-start | bytes 65536 | tf_op jit(solution)/shard_map/all_to_all | solution.py:253
  14.2 0.3 collective-permute-start
  14.5 3.3 %collective-permute-start.1 = (f32[3,8,1,128]{3,1,0,2:T(8,128)S(1)}, f32[3,8,1,128]{3,1,0,2:T(8,128)S(1)}, u32[]{:S(2)}, u32[]{:S(2)}) collective-permute-start(f32[3,8,1,128]{3,1,0,2:T(8,128)S(1)} %get-tuple-element.52), channel_id=1, source_target_pairs={{4,0},{8,4},{12,8},{16,12},{20,16},{24,20},{28,24},{0,28},{5,1},{9... | collective-permute-start | bytes 36872 | tf_op jit(solution)/shard_map/ppermute | solution.py:284
  17.8 0.7 copy-done.15
  18.9 0.6 copy-done.20
  19.6 1.8 %all-to-all-done = f32[32,2,128]{2,1,0:T(2,128)S(1)} async-done(((f32[32,2,128]{2,1,0:T(2,128)}), f32[32,2,128]{2,1,0:T(2,128)S(1)}, u32[]{:S(2)}, u32[]{:S(2)}) %all-to-all-start) | async-done | bytes 32800 | tf_op jit(solution)/shard_map/all_to_all | solution.py:253
  21.5 0.2 fusion.12
  21.8 0.1 pad_maximum_fusion.14
  21.9 0.1 stack.49
  22.0 0.1 stack.50
  22.1 0.1 stack.51
  22.1 0.1 stack.52
  22.4 0.7 all_to_all.19
  23.1 2.7 %all-to-all-start.1 = ((f32[32,1,644]{2,1,0:T(1,128)}), f32[32,1,644]{2,1,0:T(1,128)S(1)}, u32[]{:S(2)}, u32[]{:S(2)}) async-start(f32[32,1,644]{2,1,0:T(1,128)} %all_to_all.19), calls=%async_computation.1 | async-start | bytes 196608 | tf_op jit(solution)/shard_map/all_to_all | solution.py:301
  25.8 0.6 fusion.73
  26.5 7.3 %all-to-all-done.1 = f32[32,1,644]{2,1,0:T(1,128)S(1)} async-done(((f32[32,1,644]{2,1,0:T(1,128)}), f32[32,1,644]{2,1,0:T(1,128)S(1)}, u32[]{:S(2)}, u32[]{:S(2)}) %all-to-all-start.1) | async-done | bytes 82464 | tf_op jit(solution)/shard_map/all_to_all | solution.py:301
  33.7 0.2 reduce
  34.0 0.1 fusion.53
  34.7 0.2 reshape.880
  34.9 0.2 reshape.881
  35.2 0.7 slice-done
  35.9 0.1 reshape_reshape.6
  36.0 0.7 copy-done.7
  36.7 0.2 fusion.6
  36.9 0.7 copy-done.13
  37.6 0.4 multiply_add_fusion
  38.4 0.8 %copy-done.3 = f32[3,8,16,128]{3,2,1,0:T(8,128)S(1)} copy-done((f32[3,8,16,128]{3,2,1,0:T(8,128)S(1)}, f32[3,8,16,128]{3,2,1,0:T(8,128)}, u32[]{:S(2)}) %copy-start.3) | copy-done | bytes 196632
  39.3 0.2 fusion.9
  39.5 0.3 fusion.39
  39.8 0.6 copy.69
  40.5 2.5 %all-to-all-start.2 = ((f32[32,2,128]{2,1,0:T(2,128)}), f32[32,2,128]{2,1,0:T(2,128)S(1)}, u32[]{:S(2)}, u32[]{:S(2)}) async-start(f32[32,2,128]{2,1,0:T(2,128)} %copy.69), calls=%async_computation.2 | async-start | bytes 65536 | tf_op jit(solution)/shard_map/all_to_all | solution.py:253
  43.3 1.2 %fusion.3 = f32[3,8,16,128]{3,2,1,0:T(8,128)} fusion(f32[3,8,16,128]{3,2,1,0:T(8,128)S(1)} %copy-done.3, f32[3,8,2,1,130]{4,3,2,1,0:T(1,128)S(1)} %copy.68, f32[3,8,2,6,130]{4,3,2,1,0:T(8,128)S(1)} %slice.259, f32[3,8,2,1,130]{4,3,2,1,0:T(1,128)S(1)} %copy.67, f32[8,16,128]{2,1,0:T(8,128)S(1)} %broadcast_multiply_fusion, f32[130,128]{1,0:T(8,128)S(1)} %copy-done.9, ...), kind=kOutput, calls=%fused_computation.5 | convolution fusion | flops 76990976 | bytes 858120 | tf_op jit(solution)/shard_map/dot_general | solution.py:362
  44.5 3.5 %shard_map.185 = (f32[3,128,128]{2,1,0:T(8,128)}, f32[2,3,8,128]{3,2,1,0:T(8,128)}, f32[2,3,128]{2,1,0:T(4,128)}) custom-call(f32[3,128,128]{2,1,0:T(8,128)} %bitcast.117, f32[3,128,128]{2,1,0:T(8,128)} %bitcast.111, f32[9,128,128]{2,1,0:T(8,128)} %get-tuple-element.17.grad_ref, f32[6,128,128]{2,1,0:T(8,128)} %constant.256.clone.mats_ref, ...), custom_call_target="tpu_custom_call" | custom-call | tf_op jit(solution)/shard_map/pallas_call | solution.py:383
  48.0 0.7 fusion.78
  49.0 1.3 %all-to-all-done.2 = f32[32,2,128]{2,1,0:T(2,128)S(1)} async-done(((f32[32,2,128]{2,1,0:T(2,128)}), f32[32,2,128]{2,1,0:T(2,128)S(1)}, u32[]{:S(2)}, u32[]{:S(2)}) %all-to-all-start.2) | async-done | bytes 32800 | tf_op jit(solution)/shard_map/all_to_all | solution.py:253
  50.3 0.2 fusion.10
  50.6 0.1 pad_maximum_fusion.12
  50.7 0.1 stack.55
  50.8 0.1 stack.56
  50.9 0.1 stack.57
  51.0 0.1 stack.58
  51.2 0.7 %all_to_all.22 = f32[32,1,644]{2,1,0:T(1,128)} reshape(f32[32,644]{1,0:T(8,128)S(1)} %pad_maximum_fusion.2) | data formatting | bytes 164864 | tf_op jit(solution)/shard_map/all_to_all | solution.py:301
  51.9 4.5 %all-to-all-start.3 = ((f32[32,1,644]{2,1,0:T(1,128)}), f32[32,1,644]{2,1,0:T(1,128)S(1)}, u32[]{:S(2)}, u32[]{:S(2)}) async-start(f32[32,1,644]{2,1,0:T(1,128)} %all_to_all.22), calls=%async_computation.3 | async-start | bytes 196608 | tf_op jit(solution)/shard_map/all_to_all | solution.py:301
  56.5 0.3 collective-permute-start.2
  56.8 3.4 %collective-permute-start.3 = (f32[3,8,1,128]{3,1,0,2:T(8,128)S(1)}, f32[3,8,1,128]{3,1,0,2:T(8,128)S(1)}, u32[]{:S(2)}, u32[]{:S(2)}) collective-permute-start(f32[3,8,1,128]{3,1,0,2:T(8,128)S(1)} %get-tuple-element.48), channel_id=1, source_target_pairs={{4,0},{8,4},{12,8},{16,12},{20,16},{24,20},{28,24},{0,28},{5,1},{9... | collective-permute-start | bytes 36872 | tf_op jit(solution)/shard_map/ppermute | solution.py:284
  60.2 4.4 %all-to-all-done.3 = f32[32,1,644]{2,1,0:T(1,128)S(1)} async-done(((f32[32,1,644]{2,1,0:T(1,128)}), f32[32,1,644]{2,1,0:T(1,128)S(1)}, u32[]{:S(2)}, u32[]{:S(2)}) %all-to-all-start.3) | async-done | bytes 82464 | tf_op jit(solution)/shard_map/all_to_all | solution.py:301
  64.6 0.2 reduce.7
  64.9 0.1 fusion.59
  65.0 0.5 copy-done.2
  65.8 0.5 slice-done.1
  66.4 0.2 fusion.5
  66.9 0.2 reshape.882
  67.1 0.2 reshape.883
  67.5 0.6 copy-done.4
  68.0 0.4 maximum_add_fusion
  68.9 0.7 %copy-done.6 = f32[3,8,16,128]{3,2,1,0:T(8,128)S(1)} copy-done((f32[3,8,16,128]{3,2,1,0:T(8,128)S(1)}, f32[3,8,16,128]{3,2,1,0:T(8,128)}, u32[]{:S(2)}) %copy-start.6) | copy-done | bytes 196632
  69.7 1.2 %fusion.4 = f32[3,8,16,128]{3,2,1,0:T(8,128)} fusion(f32[3,8,2,1,130]{4,3,2,1,0:T(1,128)S(1)} %copy.84, f32[3,8,2,6,130]{4,3,2,1,0:T(8,128)S(1)} %slice.286, f32[3,8,2,1,130]{4,3,2,1,0:T(1,128)S(1)} %copy.83, f32[3,8,16,128]{3,2,1,0:T(8,128)S(1)} %copy-done.3, f32[3,8,16,128]{3,2,1,0:T(8,128)S(1)} %copy-done.6, ...), kind=kOutput, calls=%fused_computation.6 | convolution fusion | flops 77089280 | bytes 1054728 | tf_op jit(solution)/shard_map/dot_general | solution.py:362
  (133 shorter events, 3.9 us)
Async XLA Ops:
  0.0 21.5 %copy-start = (bf16[1,512,512]{2,1,0:T(8,128)(2,1)S(1)}, bf16[1,512,512]{2,1,0:T(8,128)(2,1)}, u32[]{:S(2)}) copy-start(bf16[1,512,512]{2,1,0:T(8,128)(2,1)} %param.21) | copy-start | bytes 1572868
  0.0 0.7 %copy-start.16 = (s32[32]{0:T(128)S(1)}, s32[32]{0:T(128)}, u32[]{:S(2)}) copy-start(s32[32]{0:T(128)} %param.22) | copy-start | bytes 388
  0.7 0.7 copy-start.19
  1.6 0.7 copy-start.17
  6.8 7.3 %copy-start.12 = (f32[2,3,8,128]{3,2,1,0:T(8,128)S(1)}, f32[2,3,8,128]{3,2,1,0:T(8,128)}, u32[]{:S(2)}) copy-start(f32[2,3,8,128]{3,2,1,0:T(8,128)} %get-tuple-element.15) | copy-start | bytes 73732
  6.8 14.6 %all-to-all-start = ((f32[32,2,128]{2,1,0:T(2,128)}), f32[32,2,128]{2,1,0:T(2,128)S(1)}, u32[]{:S(2)}, u32[]{:S(2)}) async-start(f32[32,2,128]{2,1,0:T(2,128)} %bitcast.121), calls=%async_computation | async-start | bytes 65536 | tf_op jit(solution)/shard_map/all_to_all | solution.py:253
  14.2 20.3 %collective-permute-start = (f32[3,8,1,128]{3,1,0,2:T(8,128)S(1)}, f32[3,8,1,128]{3,1,0,2:T(8,128)S(1)}, u32[]{:S(2)}, u32[]{:S(2)}) collective-permute-start(f32[3,8,1,128]{3,1,0,2:T(8,128)S(1)} %get-tuple-element.51), channel_id=1, source_target_pairs={{0,4},{4,8},{8,12},{12,16},{16,20},{20,24},{24,28},{28,0},{1,5},{5... | collective-permute-start | bytes 36872 | tf_op jit(solution)/shard_map/ppermute | solution.py:283
  14.5 20.6 %collective-permute-start.1 = (f32[3,8,1,128]{3,1,0,2:T(8,128)S(1)}, f32[3,8,1,128]{3,1,0,2:T(8,128)S(1)}, u32[]{:S(2)}, u32[]{:S(2)}) collective-permute-start(f32[3,8,1,128]{3,1,0,2:T(8,128)S(1)} %get-tuple-element.52), channel_id=1, source_target_pairs={{4,0},{8,4},{12,8},{16,12},{20,16},{24,20},{28,24},{0,28},{5,1},{9... | collective-permute-start | bytes 36872 | tf_op jit(solution)/shard_map/ppermute | solution.py:284
  17.8 0.7 copy-start.15
  18.8 0.7 %copy-start.14 = (f32[8,16]{1,0:T(8,128)S(1)}, f32[8,16]{1,0:T(8,128)}, u32[]{:S(2)}) copy-start(f32[8,16]{1,0:T(8,128)} %constant.271) | copy-start | bytes 1540
  18.8 0.7 copy-start.20
  18.8 0.7 copy-start.21
  18.8 0.7 copy-start.22
  23.1 2.7 %copy-start.18 = (f32[18]{0:T(128)S(1)}, f32[18]{0:T(128)}, u32[]{:S(2)}) copy-start(f32[18]{0:T(128)} %constant.270) | copy-start | bytes 220
  23.1 10.7 %all-to-all-start.1 = ((f32[32,1,644]{2,1,0:T(1,128)}), f32[32,1,644]{2,1,0:T(1,128)S(1)}, u32[]{:S(2)}, u32[]{:S(2)}) async-start(f32[32,1,644]{2,1,0:T(1,128)} %all_to_all.19), calls=%async_computation.1 | async-start | bytes 196608 | tf_op jit(solution)/shard_map/all_to_all | solution.py:301
  34.0 0.6 copy-start.1
  34.9 2.0 %copy-start.5 = (f32[3,128,128]{2,1,0:T(8,128)S(1)}, f32[3,128,128]{2,1,0:T(8,128)}, u32[]{:S(2)}) copy-start(f32[3,128,128]{2,1,0:T(8,128)} %get-tuple-element.16) | copy-start | bytes 589828
  35.1 0.8 %slice-start = ((f32[8,4,644]{2,1,0:T(4,128)}), f32[8,4,260]{2,1,0:T(4,128)S(1)}, s32[]{:S(2)}) async-start(f32[8,4,644]{2,1,0:T(4,128)} %copy-done.1), calls=%async_computation.4 | async-start | bytes 98304 | tf_op jit(solution)/shard_map/slice | solution.py:302
  35.9 0.7 %copy-start.7 = (f32[18,130]{1,0:T(8,128)S(1)}, f32[18,130]{1,0:T(8,128)}, u32[]{:S(2)}) copy-start(f32[18,130]{1,0:T(8,128)} %constant.264.clone) | copy-start | bytes 28084
  36.9 0.7 copy-start.13
  38.2 0.9 %copy-start.3 = (f32[3,8,16,128]{3,2,1,0:T(8,128)S(1)}, f32[3,8,16,128]{3,2,1,0:T(8,128)}, u32[]{:S(2)}) copy-start(f32[3,8,16,128]{3,2,1,0:T(8,128)} %param.19) | copy-start | bytes 589828
  38.3 1.0 %copy-start.8 = (f32[130,128]{1,0:T(8,128)S(1)}, f32[130,128]{1,0:T(8,128)}, u32[]{:S(2)}) copy-start(f32[130,128]{1,0:T(8,128)} %constant.259.clone) | copy-start | bytes 199684
  38.3 1.0 %copy-start.9 = (f32[130,128]{1,0:T(8,128)S(1)}, f32[130,128]{1,0:T(8,128)}, u32[]{:S(2)}) copy-start(f32[130,128]{1,0:T(8,128)} %constant.260.clone) | copy-start | bytes 199684
  38.3 1.0 %copy-start.10 = (f32[130,128]{1,0:T(8,128)S(1)}, f32[130,128]{1,0:T(8,128)}, u32[]{:S(2)}) copy-start(f32[130,128]{1,0:T(8,128)} %constant.261.clone) | copy-start | bytes 199684
  40.5 9.8 %all-to-all-start.2 = ((f32[32,2,128]{2,1,0:T(2,128)}), f32[32,2,128]{2,1,0:T(2,128)S(1)}, u32[]{:S(2)}, u32[]{:S(2)}) async-start(f32[32,2,128]{2,1,0:T(2,128)} %copy.69), calls=%async_computation.2 | async-start | bytes 65536 | tf_op jit(solution)/shard_map/all_to_all | solution.py:253
  51.9 4.6 %copy-start.11 = (f32[2,3,8,128]{3,2,1,0:T(8,128)S(1)}, f32[2,3,8,128]{3,2,1,0:T(8,128)}, u32[]{:S(2)}) copy-start(f32[2,3,8,128]{3,2,1,0:T(8,128)} %get-tuple-element.19) | copy-start | bytes 73732
  51.9 12.6 %all-to-all-start.3 = ((f32[32,1,644]{2,1,0:T(1,128)}), f32[32,1,644]{2,1,0:T(1,128)S(1)}, u32[]{:S(2)}, u32[]{:S(2)}) async-start(f32[32,1,644]{2,1,0:T(1,128)} %all_to_all.22), calls=%async_computation.3 | async-start | bytes 196608 | tf_op jit(solution)/shard_map/all_to_all | solution.py:301
  56.5 10.3 %collective-permute-start.2 = (f32[3,8,1,128]{3,1,0,2:T(8,128)S(1)}, f32[3,8,1,128]{3,1,0,2:T(8,128)S(1)}, u32[]{:S(2)}, u32[]{:S(2)}) collective-permute-start(f32[3,8,1,128]{3,1,0,2:T(8,128)S(1)} %get-tuple-element.47), channel_id=1, source_target_pairs={{0,4},{4,8},{8,12},{12,16},{16,20},{20,24},{24,28},{28,0},{1,5},{5... | collective-permute-start | bytes 36872 | tf_op jit(solution)/shard_map/ppermute | solution.py:283
  56.8 10.5 %collective-permute-start.3 = (f32[3,8,1,128]{3,1,0,2:T(8,128)S(1)}, f32[3,8,1,128]{3,1,0,2:T(8,128)S(1)}, u32[]{:S(2)}, u32[]{:S(2)}) collective-permute-start(f32[3,8,1,128]{3,1,0,2:T(8,128)S(1)} %get-tuple-element.48), channel_id=1, source_target_pairs={{4,0},{8,4},{12,8},{16,12},{20,16},{24,20},{28,24},{0,28},{5,1},{9... | collective-permute-start | bytes 36872 | tf_op jit(solution)/shard_map/ppermute | solution.py:284
  64.8 0.6 copy-start.2
  65.5 0.8 %slice-start.1 = ((f32[8,4,644]{2,1,0:T(4,128)}), f32[8,4,260]{2,1,0:T(4,128)S(1)}, s32[]{:S(2)}) async-start(f32[8,4,644]{2,1,0:T(4,128)} %copy-done.2), calls=%async_computation.5 | async-start | bytes 98304 | tf_op jit(solution)/shard_map/slice | solution.py:302
  67.1 0.9 %copy-start.4 = (f32[3,128,128]{2,1,0:T(8,128)S(1)}, f32[3,128,128]{2,1,0:T(8,128)}, u32[]{:S(2)}) copy-start(f32[3,128,128]{2,1,0:T(8,128)} %get-tuple-element.20) | copy-start | bytes 589828
  68.7 0.9 %copy-start.6 = (f32[3,8,16,128]{3,2,1,0:T(8,128)S(1)}, f32[3,8,16,128]{3,2,1,0:T(8,128)}, u32[]{:S(2)}) copy-start(f32[3,8,16,128]{3,2,1,0:T(8,128)} %fusion.3) | copy-start | bytes 589828

commit v15 on v14

--- a/solution.py
+++ b/solution.py
@@ -292,21 +292,17 @@
             ((-1, 1), b_hi),
             ((-1, -1), b_lo),
         ]
-        slots = jnp.zeros((tiles, groups, slot_len), jnp.float32)
+        slots = jnp.zeros((tiles * groups, 1, slot_len), jnp.float32)
         for (dt, dg), flat in out_pieces:
-            slots = lax.dynamic_update_slice(
-                slots, flat, ((tile_index + dt) % tiles, (group_index + dg) % groups, 0)
-            )
-        message = jnp.concatenate([sent, slots], axis=2).reshape(tiles * groups, -1)
-        received = lax.all_to_all(message, both, 0, 0, tiled=True).reshape(tiles, groups, -1)
-        returned = received[:, :, :mapped_len].reshape(tiles * groups, 2, nb_dev + 2)
+            target = ((tile_index + dt) % tiles) * groups + (group_index + dg) % groups
+            slots = lax.dynamic_update_slice(slots, flat, (target, 0, 0))
+        message = jnp.concatenate([sent.reshape(tiles * groups, 1, -1), slots], axis=2)
+        received = lax.all_to_all(message, both, 0, 0, tiled=True)
+        returned = received[:, 0, :mapped_len].reshape(tiles * groups, 2, nb_dev + 2)
 
         def take(dt, dg):
-            row = lax.dynamic_slice(
-                received,
-                ((tile_index - dt) % tiles, (group_index - dg) % groups, mapped_len),
-                (1, 1, slot_len),
-            )
+            source = ((tile_index - dt) % tiles) * groups + (group_index - dg) % groups
+            row = lax.dynamic_slice(received, (source, 0, mapped_len), (1, 1, slot_len))
             return row.reshape(3, radial_nodes, na_dev, 1)
 
         from_left = take(0, 1)

time: 71.7 us -> 69 us (0.962)
  local copies, waits for them, and re-layouts: 16 us -> 12.2 us
  other arithmetic: 3.74 us -> 4.79 us
    all_to_all x2 -> x0, local copies, waits for them, and re-layouts: 1.43 us -> none  [joint_exchange(): lax.all_to_all(message, both, 0, 0, tiled=True).reshape(tiles, groups, -1)]
    concatenate x4 -> x2, other arithmetic: 0.34 us -> 1.68 us  [joint_exchange(): jnp.concatenate([sent.reshape(tiles * groups, 1, -1), slots], axis=2)]
    slice x4 -> x2, local copies, waits for them, and re-layouts: 1.19 us -> 0.27 us  [joint_exchange(): received[:, 0, :mapped_len].reshape(tiles * groups, 2, nb_dev + 2)]
    unnamed x55 -> x51, local copies, waits for them, and re-layouts: 7.83 us -> 7.29 us
where the time goes in v15:
time: 69 us; the launch traced here: 68.4 us
  starting transfers between devices  24.1 us (35%)
  waiting for transfers between devices  15.2 us (22%)
  local copies, waits for them, and re-layouts  12.2 us (18%)
  Pallas kernels  7.46 us (11%)
  other arithmetic  4.79 us (7%)
  matrix products  3.89 us (6%)
  between operations  0.73 us (1%)
    all_to_all x2, waiting for transfers between devices, joint_exchange(): received = lax.all_to_all(message, both, 0, 0, tiled=True)  11.7 us
    all_to_all x2, starting transfers between devices, owner_map(): gathered = lax.all_to_all(partial, both, 0, 0, tiled=True)  9.84 us
    unnamed x51, local copies, waits for them, and re-layouts  7.29 us
    all_to_all x2, starting transfers between devices, joint_exchange(): received = lax.all_to_all(message, both, 0, 0, tiled=True)  7.07 us
    ppermute x2, starting transfers between devices, joint_exchange(): from_down = lax.ppermute(a_lo, 'tile', down)  6.59 us
    pallas_call x1, Pallas kernels, local(): pl.pallas_call(first_volume_kernel, out_shape=shapes + (jax.ShapeDtypeStr...  3.99 us
    pallas_call x1, Pallas kernels, tendency(): pl.pallas_call(volume_kernel, out_shape=shapes)  3.48 us
    all_to_all x2, waiting for transfers between devices, owner_map(): gathered = lax.all_to_all(partial, both, 0, 0, tiled=True)  3.46 us
  transfers between devices with their start and end apart: 8, of which 4 were waited for; matrix products, arithmetic and copies ran while one was open for 10% of the time, Pallas kernels for 5%

profile of v15, /device:TPU:0, one launch (start us, length us, event | category | flops | bytes accessed | tf_op | source)
XLA Modules:
  0.0 68.4 jit_solution(3067777237339580895)
XLA Ops:
  0.0 0.7 %copy-done.14 = s32[32]{0:T(128)S(1)} copy-done((s32[32]{0:T(128)S(1)}, s32[32]{0:T(128)}, u32[]{:S(2)}) %copy-start.14) | copy-done | bytes 152
  0.7 0.7 copy-done.17
  1.4 0.1 fusion.47
  1.5 0.1 copy.54
  1.6 0.7 copy-done.15
  2.3 0.6 broadcast_multiply_fusion.1.table_ref
  2.9 4.0 %shard_map.184 = (f32[3,128,128]{2,1,0:T(8,128)}, f32[2,3,8,128]{3,2,1,0:T(8,128)}, f32[2,3,128]{2,1,0:T(4,128)}, f32[64,128]{1,0:T(8,128)}, f32[9,128,128]{2,1,0:T(8,128)}) custom-call(f32[3,128,128]{2,1,0:T(8,128)} %bitcast.130, f32[3,128,128]{2,1,0:T(8,128)} %bitcast.126, f32[6,128,128]{2,1,0:T(8,128)} %constant.256.clone.mats_ref, ...), custom_call_target="tpu_custom_call" | custom-call | tf_op jit(solution)/shard_map/pallas_call | solution.py:365
  6.8 7.3 %all-to-all-start = ((f32[32,2,128]{2,1,0:T(2,128)}), f32[32,2,128]{2,1,0:T(2,128)S(1)}, u32[]{:S(2)}, u32[]{:S(2)}) async-start(f32[32,2,128]{2,1,0:T(2,128)} %bitcast.137), calls=%async_computation | async-start | bytes 65536 | tf_op jit(solution)/shard_map/all_to_all | solution.py:253
  14.2 0.3 collective-permute-start
  14.5 3.3 %collective-permute-start.1 = (f32[3,8,1,128]{3,1,0,2:T(8,128)S(1)}, f32[3,8,1,128]{3,1,0,2:T(8,128)S(1)}, u32[]{:S(2)}, u32[]{:S(2)}) collective-permute-start(f32[3,8,1,128]{3,1,0,2:T(8,128)S(1)} %get-tuple-element.52), channel_id=1, source_target_pairs={{4,0},{8,4},{12,8},{16,12},{20,16},{24,20},{28,24},{0,28},{5,1},{9... | collective-permute-start | bytes 36872 | tf_op jit(solution)/shard_map/ppermute | solution.py:284
  17.8 0.7 copy-done.13
  18.7 0.6 copy-done.18
  19.3 0.1 broadcast_multiply_fusion
  19.4 2.0 %all-to-all-done = f32[32,2,128]{2,1,0:T(2,128)S(1)} async-done(((f32[32,2,128]{2,1,0:T(2,128)}), f32[32,2,128]{2,1,0:T(2,128)S(1)}, u32[]{:S(2)}, u32[]{:S(2)}) %all-to-all-start) | async-done | bytes 32800 | tf_op jit(solution)/shard_map/all_to_all | solution.py:253
  21.5 0.2 fusion.12
  21.8 0.1 fusion.54
  21.9 0.1 reshape_reshape.6
  22.1 0.8 %pad_maximum_fusion.1 = f32[32,1,644]{2,1,0:T(1,128)} fusion(f32[32,1,384]{2,1,0:T(1,128)S(1)} %constant_dynamic-update-slice_fusion.6, f32[32,1,260]{2,1,0:T(1,128)S(1)} %reshape_reshape.6), kind=kLoop, calls=%fused_computation.34 | loop fusion | flops 20608 | bytes 164864 | tf_op jit(solution)/shard_map/concatenate | solution.py:299
  22.9 2.7 %all-to-all-start.1 = ((f32[32,1,644]{2,1,0:T(1,128)}), f32[32,1,644]{2,1,0:T(1,128)S(1)}, u32[]{:S(2)}, u32[]{:S(2)}) async-start(f32[32,1,644]{2,1,0:T(1,128)} %pad_maximum_fusion.1), calls=%async_computation.1 | async-start | bytes 196608 | tf_op jit(solution)/shard_map/all_to_all | solution.py:300
  25.6 0.6 fusion.77
  26.3 7.3 %all-to-all-done.1 = f32[32,1,644]{2,1,0:T(1,128)S(1)} async-done(((f32[32,1,644]{2,1,0:T(1,128)}), f32[32,1,644]{2,1,0:T(1,128)S(1)}, u32[]{:S(2)}, u32[]{:S(2)}) %all-to-all-start.1) | async-done | bytes 82464 | tf_op jit(solution)/shard_map/all_to_all | solution.py:300
  33.5 0.1 fusion.57
  33.7 0.1 reshape.806
  33.7 0.1 reshape.807
  33.8 0.1 reshape.811
  34.1 0.1 pad_maximum_fusion.4
  34.2 0.2 reshape.838
  34.4 0.2 reshape.839
  34.6 0.1 pad_maximum_fusion.5
  34.7 0.1 slice_reduce_fusion.1
  35.0 0.7 copy-done.5
  35.6 0.2 fusion.6
  35.9 0.7 copy-done.11
  36.5 0.4 multiply_add_fusion
  37.3 0.8 %copy-done.1 = f32[3,8,16,128]{3,2,1,0:T(8,128)S(1)} copy-done((f32[3,8,16,128]{3,2,1,0:T(8,128)S(1)}, f32[3,8,16,128]{3,2,1,0:T(8,128)}, u32[]{:S(2)}) %copy-start.1) | copy-done | bytes 196632
  38.2 0.2 fusion.9
  38.4 0.3 fusion.39
  38.8 0.6 copy.69
  39.4 2.5 %all-to-all-start.2 = ((f32[32,2,128]{2,1,0:T(2,128)}), f32[32,2,128]{2,1,0:T(2,128)S(1)}, u32[]{:S(2)}, u32[]{:S(2)}) async-start(f32[32,2,128]{2,1,0:T(2,128)} %copy.69), calls=%async_computation.2 | async-start | bytes 65536 | tf_op jit(solution)/shard_map/all_to_all | solution.py:253
  42.2 1.2 %fusion.3 = f32[3,8,16,128]{3,2,1,0:T(8,128)} fusion(f32[3,8,16,128]{3,2,1,0:T(8,128)S(1)} %copy-done.1, f32[3,8,2,1,130]{4,3,2,1,0:T(1,128)S(1)} %copy.68, f32[3,8,2,6,130]{4,3,2,1,0:T(8,128)S(1)} %slice.259, f32[3,8,2,1,130]{4,3,2,1,0:T(1,128)S(1)} %copy.67, f32[8,16,128]{2,1,0:T(8,128)S(1)} %broadcast_multiply_fusion, f32[130,128]{1,0:T(8,128)S(1)} %copy-done.7, ...), kind=kOutput, calls=%fused_computation.5 | convolution fusion | flops 76990976 | bytes 858120 | tf_op jit(solution)/shard_map/dot_general | solution.py:358
  43.5 3.5 %shard_map.185 = (f32[3,128,128]{2,1,0:T(8,128)}, f32[2,3,8,128]{3,2,1,0:T(8,128)}, f32[2,3,128]{2,1,0:T(4,128)}) custom-call(f32[3,128,128]{2,1,0:T(8,128)} %bitcast.133, f32[3,128,128]{2,1,0:T(8,128)} %bitcast.127, f32[9,128,128]{2,1,0:T(8,128)} %get-tuple-element.17.grad_ref, f32[6,128,128]{2,1,0:T(8,128)} %constant.256.clone.mats_ref, ...), custom_call_target="tpu_custom_call" | custom-call | tf_op jit(solution)/shard_map/pallas_call | solution.py:379
  46.9 0.7 fusion.82
  47.8 1.5 %all-to-all-done.2 = f32[32,2,128]{2,1,0:T(2,128)S(1)} async-done(((f32[32,2,128]{2,1,0:T(2,128)}), f32[32,2,128]{2,1,0:T(2,128)S(1)}, u32[]{:S(2)}, u32[]{:S(2)}) %all-to-all-start.2) | async-done | bytes 32800 | tf_op jit(solution)/shard_map/all_to_all | solution.py:253
  49.3 0.2 fusion.10
  49.6 0.1 fusion.52
  49.7 0.1 reshape_reshape.7
  49.9 0.8 %pad_maximum_fusion.2 = f32[32,1,644]{2,1,0:T(1,128)} fusion(f32[32,1,384]{2,1,0:T(1,128)S(1)} %constant_dynamic-update-slice_fusion, f32[32,1,260]{2,1,0:T(1,128)S(1)} %reshape_reshape.7), kind=kLoop, calls=%fused_computation.35 | loop fusion | flops 20608 | bytes 164864 | tf_op jit(solution)/shard_map/concatenate | solution.py:299
  50.7 4.4 %all-to-all-start.3 = ((f32[32,1,644]{2,1,0:T(1,128)}), f32[32,1,644]{2,1,0:T(1,128)S(1)}, u32[]{:S(2)}, u32[]{:S(2)}) async-start(f32[32,1,644]{2,1,0:T(1,128)} %pad_maximum_fusion.2), calls=%async_computation.3 | async-start | bytes 196608 | tf_op jit(solution)/shard_map/all_to_all | solution.py:300
  55.1 0.3 collective-permute-start.2
  55.4 3.3 %collective-permute-start.3 = (f32[3,8,1,128]{3,1,0,2:T(8,128)S(1)}, f32[3,8,1,128]{3,1,0,2:T(8,128)S(1)}, u32[]{:S(2)}, u32[]{:S(2)}) collective-permute-start(f32[3,8,1,128]{3,1,0,2:T(8,128)S(1)} %get-tuple-element.48), channel_id=1, source_target_pairs={{4,0},{8,4},{12,8},{16,12},{20,16},{24,20},{28,24},{0,28},{5,1},{9... | collective-permute-start | bytes 36872 | tf_op jit(solution)/shard_map/ppermute | solution.py:284
  58.7 4.5 %all-to-all-done.3 = f32[32,1,644]{2,1,0:T(1,128)S(1)} async-done(((f32[32,1,644]{2,1,0:T(1,128)}), f32[32,1,644]{2,1,0:T(1,128)S(1)}, u32[]{:S(2)}, u32[]{:S(2)}) %all-to-all-start.3) | async-done | bytes 82464 | tf_op jit(solution)/shard_map/all_to_all | solution.py:300
  63.2 0.1 fusion.63
  63.3 0.1 reshape.825
  63.6 0.1 slice_reduce_fusion
  63.8 0.2 fusion.5
  64.0 0.1 reshape.830
  64.2 0.1 pad_maximum_fusion.6
  64.3 0.2 reshape.840
  64.6 0.2 reshape.841
  64.8 0.1 pad_maximum_fusion.7
  64.9 0.6 copy-done.2
  65.5 0.4 maximum_add_fusion
  66.4 0.7 %copy-done.4 = f32[3,8,16,128]{3,2,1,0:T(8,128)S(1)} copy-done((f32[3,8,16,128]{3,2,1,0:T(8,128)S(1)}, f32[3,8,16,128]{3,2,1,0:T(8,128)}, u32[]{:S(2)}) %copy-start.4) | copy-done | bytes 196632
  67.1 1.2 %fusion.4 = f32[3,8,16,128]{3,2,1,0:T(8,128)} fusion(f32[3,8,2,1,130]{4,3,2,1,0:T(1,128)S(1)} %copy.84, f32[3,8,2,6,130]{4,3,2,1,0:T(8,128)S(1)} %slice.286, f32[3,8,2,1,130]{4,3,2,1,0:T(1,128)S(1)} %copy.83, f32[3,8,16,128]{3,2,1,0:T(8,128)S(1)} %copy-done.1, f32[3,8,16,128]{3,2,1,0:T(8,128)S(1)} %copy-done.4, ...), kind=kOutput, calls=%fused_computation.6 | convolution fusion | flops 77089280 | bytes 1054728 | tf_op jit(solution)/shard_map/dot_general | solution.py:358
  (111 shorter events, 2.6 us)
Async XLA Ops:
  0.0 21.5 %copy-start = (bf16[1,512,512]{2,1,0:T(8,128)(2,1)S(1)}, bf16[1,512,512]{2,1,0:T(8,128)(2,1)}, u32[]{:S(2)}) copy-start(bf16[1,512,512]{2,1,0:T(8,128)(2,1)} %param.21) | copy-start | bytes 1572868
  0.0 0.7 %copy-start.14 = (s32[32]{0:T(128)S(1)}, s32[32]{0:T(128)}, u32[]{:S(2)}) copy-start(s32[32]{0:T(128)} %param.22) | copy-start | bytes 388
  0.7 0.7 copy-start.17
  1.6 0.7 copy-start.15
  6.8 7.3 %copy-start.10 = (f32[2,3,8,128]{3,2,1,0:T(8,128)S(1)}, f32[2,3,8,128]{3,2,1,0:T(8,128)}, u32[]{:S(2)}) copy-start(f32[2,3,8,128]{3,2,1,0:T(8,128)} %get-tuple-element.15) | copy-start | bytes 73732
  6.8 14.6 %all-to-all-start = ((f32[32,2,128]{2,1,0:T(2,128)}), f32[32,2,128]{2,1,0:T(2,128)S(1)}, u32[]{:S(2)}, u32[]{:S(2)}) async-start(f32[32,2,128]{2,1,0:T(2,128)} %bitcast.137), calls=%async_computation | async-start | bytes 65536 | tf_op jit(solution)/shard_map/all_to_all | solution.py:253
  14.2 19.9 %collective-permute-start = (f32[3,8,1,128]{3,1,0,2:T(8,128)S(1)}, f32[3,8,1,128]{3,1,0,2:T(8,128)S(1)}, u32[]{:S(2)}, u32[]{:S(2)}) collective-permute-start(f32[3,8,1,128]{3,1,0,2:T(8,128)S(1)} %get-tuple-element.51), channel_id=1, source_target_pairs={{0,4},{4,8},{8,12},{12,16},{16,20},{20,24},{24,28},{28,0},{1,5},{5... | collective-permute-start | bytes 36872 | tf_op jit(solution)/shard_map/ppermute | solution.py:283
  14.5 20.1 %collective-permute-start.1 = (f32[3,8,1,128]{3,1,0,2:T(8,128)S(1)}, f32[3,8,1,128]{3,1,0,2:T(8,128)S(1)}, u32[]{:S(2)}, u32[]{:S(2)}) collective-permute-start(f32[3,8,1,128]{3,1,0,2:T(8,128)S(1)} %get-tuple-element.52), channel_id=1, source_target_pairs={{4,0},{8,4},{12,8},{16,12},{20,16},{24,20},{28,24},{0,28},{5,1},{9... | collective-permute-start | bytes 36872 | tf_op jit(solution)/shard_map/ppermute | solution.py:284
  17.8 0.7 copy-start.13
  18.6 0.7 %copy-start.12 = (f32[8,16]{1,0:T(8,128)S(1)}, f32[8,16]{1,0:T(8,128)}, u32[]{:S(2)}) copy-start(f32[8,16]{1,0:T(8,128)} %constant.271) | copy-start | bytes 1540
  18.6 0.7 copy-start.18
  18.7 0.7 copy-start.19
  18.7 0.7 copy-start.20
  22.9 2.7 %copy-start.16 = (f32[18]{0:T(128)S(1)}, f32[18]{0:T(128)}, u32[]{:S(2)}) copy-start(f32[18]{0:T(128)} %constant.270) | copy-start | bytes 220
  22.9 10.6 %all-to-all-start.1 = ((f32[32,1,644]{2,1,0:T(1,128)}), f32[32,1,644]{2,1,0:T(1,128)S(1)}, u32[]{:S(2)}, u32[]{:S(2)}) async-start(f32[32,1,644]{2,1,0:T(1,128)} %pad_maximum_fusion.1), calls=%async_computation.1 | async-start | bytes 196608 | tf_op jit(solution)/shard_map/all_to_all | solution.py:300
  34.7 1.2 %copy-start.3 = (f32[3,128,128]{2,1,0:T(8,128)S(1)}, f32[3,128,128]{2,1,0:T(8,128)}, u32[]{:S(2)}) copy-start(f32[3,128,128]{2,1,0:T(8,128)} %get-tuple-element.16) | copy-start | bytes 589828
  34.9 0.7 %copy-start.5 = (f32[18,130]{1,0:T(8,128)S(1)}, f32[18,130]{1,0:T(8,128)}, u32[]{:S(2)}) copy-start(f32[18,130]{1,0:T(8,128)} %constant.264.clone) | copy-start | bytes 28084
  35.8 0.7 %copy-start.11 = (f32[3,8]{1,0:T(4,128)S(1)}, f32[3,8]{1,0:T(4,128)}, u32[]{:S(2)}) copy-start(f32[3,8]{1,0:T(4,128)} %constant.269) | copy-start | bytes 292
  37.2 0.9 %copy-start.1 = (f32[3,8,16,128]{3,2,1,0:T(8,128)S(1)}, f32[3,8,16,128]{3,2,1,0:T(8,128)}, u32[]{:S(2)}) copy-start(f32[3,8,16,128]{3,2,1,0:T(8,128)} %param.19) | copy-start | bytes 589828
  37.2 1.0 %copy-start.6 = (f32[130,128]{1,0:T(8,128)S(1)}, f32[130,128]{1,0:T(8,128)}, u32[]{:S(2)}) copy-start(f32[130,128]{1,0:T(8,128)} %constant.259.clone) | copy-start | bytes 199684
  37.2 1.0 %copy-start.7 = (f32[130,128]{1,0:T(8,128)S(1)}, f32[130,128]{1,0:T(8,128)}, u32[]{:S(2)}) copy-start(f32[130,128]{1,0:T(8,128)} %constant.260.clone) | copy-start | bytes 199684
  37.2 1.0 %copy-start.8 = (f32[130,128]{1,0:T(8,128)S(1)}, f32[130,128]{1,0:T(8,128)}, u32[]{:S(2)}) copy-start(f32[130,128]{1,0:T(8,128)} %constant.261.clone) | copy-start | bytes 199684
  39.4 9.9 %all-to-all-start.2 = ((f32[32,2,128]{2,1,0:T(2,128)}), f32[32,2,128]{2,1,0:T(2,128)S(1)}, u32[]{:S(2)}, u32[]{:S(2)}) async-start(f32[32,2,128]{2,1,0:T(2,128)} %copy.69), calls=%async_computation.2 | async-start | bytes 65536 | tf_op jit(solution)/shard_map/all_to_all | solution.py:253
  50.7 4.4 %copy-start.9 = (f32[2,3,8,128]{3,2,1,0:T(8,128)S(1)}, f32[2,3,8,128]{3,2,1,0:T(8,128)}, u32[]{:S(2)}) copy-start(f32[2,3,8,128]{3,2,1,0:T(8,128)} %get-tuple-element.19) | copy-start | bytes 73732
  50.7 12.5 %all-to-all-start.3 = ((f32[32,1,644]{2,1,0:T(1,128)}), f32[32,1,644]{2,1,0:T(1,128)S(1)}, u32[]{:S(2)}, u32[]{:S(2)}) async-start(f32[32,1,644]{2,1,0:T(1,128)} %pad_maximum_fusion.2), calls=%async_computation.3 | async-start | bytes 196608 | tf_op jit(solution)/shard_map/all_to_all | solution.py:300
  55.1 9.1 %collective-permute-start.2 = (f32[3,8,1,128]{3,1,0,2:T(8,128)S(1)}, f32[3,8,1,128]{3,1,0,2:T(8,128)S(1)}, u32[]{:S(2)}, u32[]{:S(2)}) collective-permute-start(f32[3,8,1,128]{3,1,0,2:T(8,128)S(1)} %get-tuple-element.47), channel_id=1, source_target_pairs={{0,4},{4,8},{8,12},{12,16},{16,20},{20,24},{24,28},{28,0},{1,5},{5... | collective-permute-start | bytes 36872 | tf_op jit(solution)/shard_map/ppermute | solution.py:283
  55.4 9.4 %collective-permute-start.3 = (f32[3,8,1,128]{3,1,0,2:T(8,128)S(1)}, f32[3,8,1,128]{3,1,0,2:T(8,128)S(1)}, u32[]{:S(2)}, u32[]{:S(2)}) collective-permute-start(f32[3,8,1,128]{3,1,0,2:T(8,128)S(1)} %get-tuple-element.48), channel_id=1, source_target_pairs={{4,0},{8,4},{12,8},{16,12},{20,16},{24,20},{28,24},{0,28},{5,1},{9... | collective-permute-start | bytes 36872 | tf_op jit(solution)/shard_map/ppermute | solution.py:284
  64.6 0.9 %copy-start.2 = (f32[3,128,128]{2,1,0:T(8,128)S(1)}, f32[3,128,128]{2,1,0:T(8,128)}, u32[]{:S(2)}) copy-start(f32[3,128,128]{2,1,0:T(8,128)} %get-tuple-element.20) | copy-start | bytes 589828
  66.2 0.9 %copy-start.4 = (f32[3,8,16,128]{3,2,1,0:T(8,128)S(1)}, f32[3,8,16,128]{3,2,1,0:T(8,128)}, u32[]{:S(2)}) copy-start(f32[3,8,16,128]{3,2,1,0:T(8,128)} %fusion.3) | copy-start | bytes 589828

commit v16 on v15

--- a/solution.py
+++ b/solution.py
@@ -236,7 +236,16 @@
     rows_ext = (tile_index * na_dev - 1 + jnp.arange(na_dev + 2, dtype=jnp.int32)) % (na_dev * tiles)
     row_points = (np.arange(na_dev + 2) - 1) % P_SIZE
     col_points = (np.arange(nb_dev + 2) - 1) % P_SIZE
-    surface_ext = diffusivity * weights[row_points][:, None] * weights[col_points][None, :]
+    cols_ext = group_index * nb_dev - 1 + jnp.arange(nb_dev + 2, dtype=jnp.int32)
+
+    def weight_at(index):
+        point = index % P_SIZE
+        total = jnp.zeros(index.shape, jnp.float32)
+        for p in range(P_SIZE):
+            total = total + jnp.where(point == p, float(weights[p]), 0.0)
+        return total
+
+    surface_ext = diffusivity * weight_at(rows_ext)[:, None] * weight_at(cols_ext)[None, :]
 
     rows = radial_nodes * na_dev
     mats = derivative_tables(radial_nodes, na_dev, nb_dev)
@@ -347,8 +356,14 @@
     edge_trail[nb_dev + 1, nb_dev - 1] = 1.0
     join_b = join_b + lead * edge_lead + trail * edge_trail
 
-    plane_mask = np.zeros((3, radial_nodes, 1, 1), np.float32)
-    plane_mask[0, radial_nodes - 1] = 1.0
+    mask_shape = (3, radial_nodes, 1, 1)
+    outer_index = radial_nodes - 1 + jnp.minimum(tile_index, 0)
+    plane_mask = jnp.where(
+        (lax.broadcasted_iota(jnp.int32, mask_shape, 0) == 0)
+        & (lax.broadcasted_iota(jnp.int32, mask_shape, 1) == outer_index),
+        1.0,
+        0.0,
+    )
 
     def assemble_ext(padded):
         last = padded.ndim - 1

time: 69 us -> 68.8 us (level)
  starting transfers between devices: 24.1 us -> 24.8 us
  waiting for transfers between devices: 15.2 us -> 14.5 us
    all_to_all x2, waiting for transfers between devices: 3.46 us -> 2.12 us  [owner_map(): gathered = lax.all_to_all(partial, both, 0, 0, tiled=True)]
    all_to_all x2, starting transfers between devices: 7.07 us -> 7.77 us  [joint_exchange(): received = lax.all_to_all(message, both, 0, 0, tiled=True)]
    unnamed x51 -> x47, local copies, waits for them, and re-layouts: 7.29 us -> 6.96 us
  transfers between devices with their start and end apart: 8 -> 8, of which waited for: 4 -> 4; matrix products, arithmetic and copies ran while one was open for 10% -> 11% of each run, Pallas kernels for 5% -> 5%
where the time goes in v16:
time: 68.8 us; the launch traced here: 68.1 us
  starting transfers between devices  24.8 us (36%)
  waiting for transfers between devices  14.5 us (21%)
  local copies, waits for them, and re-layouts  11.9 us (17%)
  Pallas kernels  7.46 us (11%)
  other arithmetic  4.91 us (7%)
  matrix products  3.9 us (6%)
  between operations  0.71 us (1%)
    all_to_all x2, waiting for transfers between devices, joint_exchange(): received = lax.all_to_all(message, both, 0, 0, tiled=True)  12.3 us
    all_to_all x2, starting transfers between devices, owner_map(): gathered = lax.all_to_all(partial, both, 0, 0, tiled=True)  9.84 us
    all_to_all x2, starting transfers between devices, joint_exchange(): received = lax.all_to_all(message, both, 0, 0, tiled=True)  7.77 us
    unnamed x47, local copies, waits for them, and re-layouts  6.96 us
    ppermute x2, starting transfers between devices, joint_exchange(): from_down = lax.ppermute(a_lo, 'tile', down)  6.59 us
    pallas_call x1, Pallas kernels, local(): pl.pallas_call(first_volume_kernel, out_shape=shapes + (jax.ShapeDtypeStr...  3.99 us
    pallas_call x1, Pallas kernels, tendency(): pl.pallas_call(volume_kernel, out_shape=shapes)  3.48 us
    dot_general x3, matrix products, assemble_ext(): return jnp.dot(along_a, join_b, precision=highest)  2.66 us
  transfers between devices with their start and end apart: 8, of which 4 were waited for; matrix products, arithmetic and copies ran while one was open for 11% of the time, Pallas kernels for 5%

profile of v16, /device:TPU:0, one launch (start us, length us, event | category | flops | bytes accessed | tf_op | source)
XLA Modules:
  0.0 68.1 jit_solution(15017126989090018719)
XLA Ops:
  0.0 0.7 %copy-done.12 = s32[32]{0:T(128)S(1)} copy-done((s32[32]{0:T(128)S(1)}, s32[32]{0:T(128)}, u32[]{:S(2)}) %copy-start.12) | copy-done | bytes 152
  0.7 0.7 copy-done.15
  1.4 0.1 fusion.47
  1.5 0.1 copy.52
  1.6 0.7 copy-done.13
  2.3 0.6 broadcast_multiply_fusion.1.table_ref
  2.9 4.0 %shard_map.166 = (f32[3,128,128]{2,1,0:T(8,128)}, f32[2,3,8,128]{3,2,1,0:T(8,128)}, f32[2,3,128]{2,1,0:T(4,128)}, f32[64,128]{1,0:T(8,128)}, f32[9,128,128]{2,1,0:T(8,128)}) custom-call(f32[3,128,128]{2,1,0:T(8,128)} %bitcast.130, f32[3,128,128]{2,1,0:T(8,128)} %bitcast.126, f32[6,128,128]{2,1,0:T(8,128)} %constant.298.clone.mats_ref, ...), custom_call_target="tpu_custom_call" | custom-call | tf_op jit(solution)/shard_map/pallas_call | solution.py:380
  6.8 7.3 %all-to-all-start = ((f32[32,2,128]{2,1,0:T(2,128)}), f32[32,2,128]{2,1,0:T(2,128)S(1)}, u32[]{:S(2)}, u32[]{:S(2)}) async-start(f32[32,2,128]{2,1,0:T(2,128)} %bitcast.137), calls=%async_computation | async-start | bytes 65536 | tf_op jit(solution)/shard_map/all_to_all | solution.py:262
  14.2 0.3 collective-permute-start
  14.5 3.3 %collective-permute-start.1 = (f32[3,8,1,128]{3,1,0,2:T(8,128)S(1)}, f32[3,8,1,128]{3,1,0,2:T(8,128)S(1)}, u32[]{:S(2)}, u32[]{:S(2)}) collective-permute-start(f32[3,8,1,128]{3,1,0,2:T(8,128)S(1)} %get-tuple-element.52), channel_id=1, source_target_pairs={{4,0},{8,4},{12,8},{16,12},{20,16},{24,20},{28,24},{0,28},{5,1},{9... | collective-permute-start | bytes 36872 | tf_op jit(solution)/shard_map/ppermute | solution.py:293
  17.8 0.7 copy-done.11
  18.7 0.6 copy-done.14
  19.3 0.6 fusion.93
  20.1 0.6 copy-done.10
  20.7 0.1 broadcast_multiply_fusion
  20.8 0.7 %all-to-all-done = f32[32,2,128]{2,1,0:T(2,128)S(1)} async-done(((f32[32,2,128]{2,1,0:T(2,128)}), f32[32,2,128]{2,1,0:T(2,128)S(1)}, u32[]{:S(2)}, u32[]{:S(2)}) %all-to-all-start) | async-done | bytes 32800 | tf_op jit(solution)/shard_map/all_to_all | solution.py:262
  21.5 0.2 fusion.12
  21.8 0.1 fusion.54
  21.9 0.1 reshape_reshape.6
  22.1 0.8 %pad_maximum_fusion.1 = f32[32,1,644]{2,1,0:T(1,128)} fusion(f32[32,1,384]{2,1,0:T(1,128)S(1)} %constant_dynamic-update-slice_fusion.6, f32[32,1,260]{2,1,0:T(1,128)S(1)} %reshape_reshape.6), kind=kLoop, calls=%fused_computation.34 | loop fusion | flops 20608 | bytes 164864 | tf_op jit(solution)/shard_map/concatenate | solution.py:308
  22.9 3.4 %all-to-all-start.1 = ((f32[32,1,644]{2,1,0:T(1,128)}), f32[32,1,644]{2,1,0:T(1,128)S(1)}, u32[]{:S(2)}, u32[]{:S(2)}) async-start(f32[32,1,644]{2,1,0:T(1,128)} %pad_maximum_fusion.1), calls=%async_computation.1 | async-start | bytes 196608 | tf_op jit(solution)/shard_map/all_to_all | solution.py:309
  26.3 7.9 %all-to-all-done.1 = f32[32,1,644]{2,1,0:T(1,128)S(1)} async-done(((f32[32,1,644]{2,1,0:T(1,128)}), f32[32,1,644]{2,1,0:T(1,128)S(1)}, u32[]{:S(2)}, u32[]{:S(2)}) %all-to-all-start.1) | async-done | bytes 82464 | tf_op jit(solution)/shard_map/all_to_all | solution.py:309
  34.2 0.1 fusion.57
  34.3 0.1 reshape.921
  34.4 0.1 reshape.922
  34.5 0.1 reshape.926
  34.7 0.1 pad_maximum_fusion.4
  34.8 0.2 reshape.953
  35.1 0.2 reshape.954
  35.3 0.1 pad_maximum_fusion.5
  35.4 0.1 slice_reduce_fusion.1
  35.6 0.2 fusion.6
  35.8 0.4 copy-done.3
  36.3 0.4 multiply_add_fusion
  37.1 0.8 %copy-done.1 = f32[3,8,16,128]{3,2,1,0:T(8,128)S(1)} copy-done((f32[3,8,16,128]{3,2,1,0:T(8,128)S(1)}, f32[3,8,16,128]{3,2,1,0:T(8,128)}, u32[]{:S(2)}) %copy-start.1) | copy-done | bytes 196632
  38.0 0.2 fusion.9
  38.2 0.3 fusion.39
  38.5 0.6 copy.67
  39.1 2.5 %all-to-all-start.2 = ((f32[32,2,128]{2,1,0:T(2,128)}), f32[32,2,128]{2,1,0:T(2,128)S(1)}, u32[]{:S(2)}, u32[]{:S(2)}) async-start(f32[32,2,128]{2,1,0:T(2,128)} %copy.67), calls=%async_computation.2 | async-start | bytes 65536 | tf_op jit(solution)/shard_map/all_to_all | solution.py:262
  42.0 1.2 %fusion.3 = f32[3,8,16,128]{3,2,1,0:T(8,128)} fusion(f32[3,8,16,128]{3,2,1,0:T(8,128)S(1)} %copy-done.1, f32[3,8,2,1,130]{4,3,2,1,0:T(1,128)S(1)} %copy.66, f32[3,8,2,6,130]{4,3,2,1,0:T(8,128)S(1)} %slice.259, f32[3,8,2,1,130]{4,3,2,1,0:T(1,128)S(1)} %copy.65, f32[8,16,128]{2,1,0:T(8,128)S(1)} %broadcast_multiply_fusion, f32[130,128]{1,0:T(8,128)S(1)} %copy-done.6, ...), kind=kOutput, calls=%fused_computation.5 | convolution fusion | flops 76990976 | bytes 858120 | tf_op jit(solution)/shard_map/dot_general | solution.py:373
  43.2 3.5 %shard_map.167 = (f32[3,128,128]{2,1,0:T(8,128)}, f32[2,3,8,128]{3,2,1,0:T(8,128)}, f32[2,3,128]{2,1,0:T(4,128)}) custom-call(f32[3,128,128]{2,1,0:T(8,128)} %bitcast.133, f32[3,128,128]{2,1,0:T(8,128)} %bitcast.127, f32[9,128,128]{2,1,0:T(8,128)} %get-tuple-element.17.grad_ref, f32[6,128,128]{2,1,0:T(8,128)} %constant.298.clone.mats_ref, ...), custom_call_target="tpu_custom_call" | custom-call | tf_op jit(solution)/shard_map/pallas_call | solution.py:394
  46.7 0.7 %fusion.98 = (f32[1,3,128]{2,1,0:T(4,128)S(1)}, f32[1,3,128]{2,1,0:T(4,128)S(1)}) fusion(f32[2,3,128]{2,1,0:T(4,128)} %get-tuple-element.18), kind=kLoop, calls=%fused_computation.234 | loop fusion | bytes 6144 | tf_op jit(solution)/shard_map/slice | solution.py:294
  47.5 1.4 %all-to-all-done.2 = f32[32,2,128]{2,1,0:T(2,128)S(1)} async-done(((f32[32,2,128]{2,1,0:T(2,128)}), f32[32,2,128]{2,1,0:T(2,128)S(1)}, u32[]{:S(2)}, u32[]{:S(2)}) %all-to-all-start.2) | async-done | bytes 32800 | tf_op jit(solution)/shard_map/all_to_all | solution.py:262
  49.0 0.2 fusion.10
  49.3 0.1 fusion.52
  49.5 0.1 reshape_reshape.7
  49.6 0.8 %pad_maximum_fusion.2 = f32[32,1,644]{2,1,0:T(1,128)} fusion(f32[32,1,384]{2,1,0:T(1,128)S(1)} %constant_dynamic-update-slice_fusion, f32[32,1,260]{2,1,0:T(1,128)S(1)} %reshape_reshape.7), kind=kLoop, calls=%fused_computation.35 | loop fusion | flops 20608 | bytes 164864 | tf_op jit(solution)/shard_map/concatenate | solution.py:308
  50.4 4.4 %all-to-all-start.3 = ((f32[32,1,644]{2,1,0:T(1,128)}), f32[32,1,644]{2,1,0:T(1,128)S(1)}, u32[]{:S(2)}, u32[]{:S(2)}) async-start(f32[32,1,644]{2,1,0:T(1,128)} %pad_maximum_fusion.2), calls=%async_computation.3 | async-start | bytes 196608 | tf_op jit(solution)/shard_map/all_to_all | solution.py:309
  54.9 0.3 collective-permute-start.2
  55.2 3.3 %collective-permute-start.3 = (f32[3,8,1,128]{3,1,0,2:T(8,128)S(1)}, f32[3,8,1,128]{3,1,0,2:T(8,128)S(1)}, u32[]{:S(2)}, u32[]{:S(2)}) collective-permute-start(f32[3,8,1,128]{3,1,0,2:T(8,128)S(1)} %get-tuple-element.48), channel_id=1, source_target_pairs={{4,0},{8,4},{12,8},{16,12},{20,16},{24,20},{28,24},{0,28},{5,1},{9... | collective-permute-start | bytes 36872 | tf_op jit(solution)/shard_map/ppermute | solution.py:293
  58.5 4.5 %all-to-all-done.3 = f32[32,1,644]{2,1,0:T(1,128)S(1)} async-done(((f32[32,1,644]{2,1,0:T(1,128)}), f32[32,1,644]{2,1,0:T(1,128)S(1)}, u32[]{:S(2)}, u32[]{:S(2)}) %all-to-all-start.3) | async-done | bytes 82464 | tf_op jit(solution)/shard_map/all_to_all | solution.py:309
  62.9 0.1 fusion.63
  63.0 0.1 reshape.940
  63.4 0.1 slice_reduce_fusion
  63.6 0.2 fusion.5
  63.8 0.1 reshape.945
  64.0 0.1 pad_maximum_fusion.6
  64.1 0.2 reshape.955
  64.3 0.2 reshape.956
  64.6 0.1 pad_maximum_fusion.7
  64.7 0.6 copy-done.2
  65.2 0.4 maximum_add_fusion
  66.2 0.7 %copy-done.4 = f32[3,8,16,128]{3,2,1,0:T(8,128)S(1)} copy-done((f32[3,8,16,128]{3,2,1,0:T(8,128)S(1)}, f32[3,8,16,128]{3,2,1,0:T(8,128)}, u32[]{:S(2)}) %copy-start.4) | copy-done | bytes 196632
  66.9 1.2 %fusion.4 = f32[3,8,16,128]{3,2,1,0:T(8,128)} fusion(f32[3,8,2,1,130]{4,3,2,1,0:T(1,128)S(1)} %copy.82, f32[3,8,2,6,130]{4,3,2,1,0:T(8,128)S(1)} %slice.286, f32[3,8,2,1,130]{4,3,2,1,0:T(1,128)S(1)} %copy.81, f32[3,8,16,128]{3,2,1,0:T(8,128)S(1)} %copy-done.1, f32[3,8,16,128]{3,2,1,0:T(8,128)S(1)} %copy-done.4, ...), kind=kOutput, calls=%fused_computation.6 | convolution fusion | flops 77089280 | bytes 1054728 | tf_op jit(solution)/shard_map/dot_general | solution.py:373
  (112 shorter events, 2.7 us)
Async XLA Ops:
  0.0 21.5 %copy-start = (bf16[1,512,512]{2,1,0:T(8,128)(2,1)S(1)}, bf16[1,512,512]{2,1,0:T(8,128)(2,1)}, u32[]{:S(2)}) copy-start(bf16[1,512,512]{2,1,0:T(8,128)(2,1)} %param.19) | copy-start | bytes 1572868
  0.0 0.7 %copy-start.12 = (s32[32]{0:T(128)S(1)}, s32[32]{0:T(128)}, u32[]{:S(2)}) copy-start(s32[32]{0:T(128)} %param.20) | copy-start | bytes 388
  0.7 0.7 copy-start.15
  1.6 0.7 copy-start.13
  6.8 7.3 %copy-start.9 = (f32[2,3,8,128]{3,2,1,0:T(8,128)S(1)}, f32[2,3,8,128]{3,2,1,0:T(8,128)}, u32[]{:S(2)}) copy-start(f32[2,3,8,128]{3,2,1,0:T(8,128)} %get-tuple-element.15) | copy-start | bytes 73732
  6.8 14.6 %all-to-all-start = ((f32[32,2,128]{2,1,0:T(2,128)}), f32[32,2,128]{2,1,0:T(2,128)S(1)}, u32[]{:S(2)}, u32[]{:S(2)}) async-start(f32[32,2,128]{2,1,0:T(2,128)} %bitcast.137), calls=%async_computation | async-start | bytes 65536 | tf_op jit(solution)/shard_map/all_to_all | solution.py:262
  14.2 20.5 %collective-permute-start = (f32[3,8,1,128]{3,1,0,2:T(8,128)S(1)}, f32[3,8,1,128]{3,1,0,2:T(8,128)S(1)}, u32[]{:S(2)}, u32[]{:S(2)}) collective-permute-start(f32[3,8,1,128]{3,1,0,2:T(8,128)S(1)} %get-tuple-element.51), channel_id=1, source_target_pairs={{0,4},{4,8},{8,12},{12,16},{16,20},{20,24},{24,28},{28,0},{1,5},{5... | collective-permute-start | bytes 36872 | tf_op jit(solution)/shard_map/ppermute | solution.py:292
  14.5 20.8 %collective-permute-start.1 = (f32[3,8,1,128]{3,1,0,2:T(8,128)S(1)}, f32[3,8,1,128]{3,1,0,2:T(8,128)S(1)}, u32[]{:S(2)}, u32[]{:S(2)}) collective-permute-start(f32[3,8,1,128]{3,1,0,2:T(8,128)S(1)} %get-tuple-element.52), channel_id=1, source_target_pairs={{4,0},{8,4},{12,8},{16,12},{20,16},{24,20},{28,24},{0,28},{5,1},{9... | collective-permute-start | bytes 36872 | tf_op jit(solution)/shard_map/ppermute | solution.py:293
  17.8 0.7 copy-start.11
  18.7 0.7 copy-start.14
  19.3 0.7 %copy-start.16 = (f32[128]{0:T(128)S(1)}, f32[128]{0:T(128)}, u32[]{:S(2)}) copy-start(f32[128]{0:T(128)} %constant.294.clone) | copy-start | bytes 1540
  19.3 0.7 %copy-start.17 = (f32[128]{0:T(128)S(1)}, f32[128]{0:T(128)}, u32[]{:S(2)}) copy-start(f32[128]{0:T(128)} %constant.295.clone) | copy-start | bytes 1540
  19.3 0.7 %copy-start.18 = (f32[128]{0:T(128)S(1)}, f32[128]{0:T(128)}, u32[]{:S(2)}) copy-start(f32[128]{0:T(128)} %constant.296.clone) | copy-start | bytes 1540
  20.0 0.7 %copy-start.10 = (f32[8,16]{1,0:T(8,128)S(1)}, f32[8,16]{1,0:T(8,128)}, u32[]{:S(2)}) copy-start(f32[8,16]{1,0:T(8,128)} %constant.310) | copy-start | bytes 1540
  22.9 11.3 %all-to-all-start.1 = ((f32[32,1,644]{2,1,0:T(1,128)}), f32[32,1,644]{2,1,0:T(1,128)S(1)}, u32[]{:S(2)}, u32[]{:S(2)}) async-start(f32[32,1,644]{2,1,0:T(1,128)} %pad_maximum_fusion.1), calls=%async_computation.1 | async-start | bytes 196608 | tf_op jit(solution)/shard_map/all_to_all | solution.py:309
  35.4 0.9 %copy-start.3 = (f32[3,128,128]{2,1,0:T(8,128)S(1)}, f32[3,128,128]{2,1,0:T(8,128)}, u32[]{:S(2)}) copy-start(f32[3,128,128]{2,1,0:T(8,128)} %get-tuple-element.16) | copy-start | bytes 589828
  36.9 0.9 %copy-start.1 = (f32[3,8,16,128]{3,2,1,0:T(8,128)S(1)}, f32[3,8,16,128]{3,2,1,0:T(8,128)}, u32[]{:S(2)}) copy-start(f32[3,8,16,128]{3,2,1,0:T(8,128)} %param.17) | copy-start | bytes 589828
  37.0 1.0 %copy-start.5 = (f32[130,128]{1,0:T(8,128)S(1)}, f32[130,128]{1,0:T(8,128)}, u32[]{:S(2)}) copy-start(f32[130,128]{1,0:T(8,128)} %constant.301.clone) | copy-start | bytes 199684
  37.0 1.0 %copy-start.6 = (f32[130,128]{1,0:T(8,128)S(1)}, f32[130,128]{1,0:T(8,128)}, u32[]{:S(2)}) copy-start(f32[130,128]{1,0:T(8,128)} %constant.302.clone) | copy-start | bytes 199684
  37.0 1.0 %copy-start.7 = (f32[130,128]{1,0:T(8,128)S(1)}, f32[130,128]{1,0:T(8,128)}, u32[]{:S(2)}) copy-start(f32[130,128]{1,0:T(8,128)} %constant.303.clone) | copy-start | bytes 199684
  39.1 9.8 %all-to-all-start.2 = ((f32[32,2,128]{2,1,0:T(2,128)}), f32[32,2,128]{2,1,0:T(2,128)S(1)}, u32[]{:S(2)}, u32[]{:S(2)}) async-start(f32[32,2,128]{2,1,0:T(2,128)} %copy.67), calls=%async_computation.2 | async-start | bytes 65536 | tf_op jit(solution)/shard_map/all_to_all | solution.py:262
  50.4 4.4 %copy-start.8 = (f32[2,3,8,128]{3,2,1,0:T(8,128)S(1)}, f32[2,3,8,128]{3,2,1,0:T(8,128)}, u32[]{:S(2)}) copy-start(f32[2,3,8,128]{3,2,1,0:T(8,128)} %get-tuple-element.19) | copy-start | bytes 73732
  50.4 12.5 %all-to-all-start.3 = ((f32[32,1,644]{2,1,0:T(1,128)}), f32[32,1,644]{2,1,0:T(1,128)S(1)}, u32[]{:S(2)}, u32[]{:S(2)}) async-start(f32[32,1,644]{2,1,0:T(1,128)} %pad_maximum_fusion.2), calls=%async_computation.3 | async-start | bytes 196608 | tf_op jit(solution)/shard_map/all_to_all | solution.py:309
  54.9 9.1 %collective-permute-start.2 = (f32[3,8,1,128]{3,1,0,2:T(8,128)S(1)}, f32[3,8,1,128]{3,1,0,2:T(8,128)S(1)}, u32[]{:S(2)}, u32[]{:S(2)}) collective-permute-start(f32[3,8,1,128]{3,1,0,2:T(8,128)S(1)} %get-tuple-element.47), channel_id=1, source_target_pairs={{0,4},{4,8},{8,12},{12,16},{16,20},{20,24},{24,28},{28,0},{1,5},{5... | collective-permute-start | bytes 36872 | tf_op jit(solution)/shard_map/ppermute | solution.py:292
  55.2 9.4 %collective-permute-start.3 = (f32[3,8,1,128]{3,1,0,2:T(8,128)S(1)}, f32[3,8,1,128]{3,1,0,2:T(8,128)S(1)}, u32[]{:S(2)}, u32[]{:S(2)}) collective-permute-start(f32[3,8,1,128]{3,1,0,2:T(8,128)S(1)} %get-tuple-element.48), channel_id=1, source_target_pairs={{4,0},{8,4},{12,8},{16,12},{20,16},{24,20},{28,24},{0,28},{5,1},{9... | collective-permute-start | bytes 36872 | tf_op jit(solution)/shard_map/ppermute | solution.py:293
  64.3 0.9 %copy-start.2 = (f32[3,128,128]{2,1,0:T(8,128)S(1)}, f32[3,128,128]{2,1,0:T(8,128)}, u32[]{:S(2)}) copy-start(f32[3,128,128]{2,1,0:T(8,128)} %get-tuple-element.20) | copy-start | bytes 589828
  65.9 0.9 %copy-start.4 = (f32[3,8,16,128]{3,2,1,0:T(8,128)S(1)}, f32[3,8,16,128]{3,2,1,0:T(8,128)}, u32[]{:S(2)}) copy-start(f32[3,8,16,128]{3,2,1,0:T(8,128)} %fusion.3) | copy-start | bytes 589828

commit v17 on v16

--- a/solution.py
+++ b/solution.py
@@ -175,10 +175,19 @@
     return (np.tile(weights, count) + starts + ends * weights[0]).astype(np.float32)
 
 
+def table_at(values, index):
+    point = index % P_SIZE
+    total = jnp.zeros(index.shape, jnp.float32)
+    for p in range(P_SIZE):
+        total = total + jnp.where(point == p, float(values[p]), 0.0)
+    return total
+
+
 def phases(waves, elem_start, elem_count, span, points):
-    element = elem_start + jnp.arange(elem_count * P_SIZE, dtype=jnp.int32) // P_SIZE
+    position = elem_start * P_SIZE + jnp.arange(elem_count * P_SIZE, dtype=jnp.int32)
+    element = position // P_SIZE
     whole = waves[:, None] * (2 * element + 1)[None, :] % span
-    fraction = waves.astype(jnp.float32)[:, None] * np.tile(points, elem_count)[None, :]
+    fraction = waves.astype(jnp.float32)[:, None] * table_at(points, position)[None, :]
     return 2.0 * math.pi / span * (whole.astype(jnp.float32) + fraction)
 
 
@@ -239,11 +248,7 @@
     cols_ext = group_index * nb_dev - 1 + jnp.arange(nb_dev + 2, dtype=jnp.int32)
 
     def weight_at(index):
-        point = index % P_SIZE
-        total = jnp.zeros(index.shape, jnp.float32)
-        for p in range(P_SIZE):
-            total = total + jnp.where(point == p, float(weights[p]), 0.0)
-        return total
+        return table_at(weights, index)
 
     surface_ext = diffusivity * weight_at(rows_ext)[:, None] * weight_at(cols_ext)[None, :]
 
@@ -254,7 +259,10 @@
 
     angle = phases(wave_of_slot, tile_index * elems_a, elems_a, span, points)
     analysis = (
-        jnp.stack([jnp.cos(angle), jnp.sin(angle)], axis=1) * (w_a * scale)[None, None, :]
+        jnp.stack([jnp.cos(angle), jnp.sin(angle)], axis=1)
+        * (scale * weight_at(tile_index * na_dev + jnp.arange(na_dev, dtype=jnp.int32)))[
+            None, None, :
+        ]
     ).reshape(-1, na_dev)
 
     def owner_map(partial):
@@ -275,7 +283,7 @@
         )
 
     def flux_of(returned):
-        angle = phases_at(wave_of_slot, rows_ext // P_SIZE, points[row_points], span)
+        angle = phases_at(wave_of_slot, rows_ext // P_SIZE, table_at(points, rows_ext), span)
         synth = jnp.stack([jnp.cos(angle).T, jnp.sin(angle).T], axis=2).reshape(na_dev + 2, -1)
         flux = -jnp.dot(synth, returned.reshape(-1, nb_dev + 2), precision=highest)
         return surface_ext * flux

time: 68.8 us -> 66.9 us (0.972)
  local copies, waits for them, and re-layouts: 11.9 us -> 9.97 us
    unnamed x47 -> x43, local copies, waits for them, and re-layouts: 6.96 us -> 5.08 us
where the time goes in v17:
time: 66.9 us; the launch traced here: 66.3 us
  starting transfers between devices  24.2 us (36%)
  waiting for transfers between devices  15.1 us (23%)
  local copies, waits for them, and re-layouts  9.97 us (15%)
  Pallas kernels  7.45 us (11%)
  other arithmetic  4.98 us (7%)
  matrix products  3.9 us (6%)
  between operations  0.73 us (1%)
    all_to_all x2, waiting for transfers between devices, joint_exchange(): received = lax.all_to_all(message, both, 0, 0, tiled=True)  12.3 us
    all_to_all x2, starting transfers between devices, owner_map(): gathered = lax.all_to_all(partial, both, 0, 0, tiled=True)  9.85 us
    all_to_all x2, starting transfers between devices, joint_exchange(): received = lax.all_to_all(message, both, 0, 0, tiled=True)  7.14 us
    ppermute x2, starting transfers between devices, joint_exchange(): from_down = lax.ppermute(a_lo, 'tile', down)  6.59 us
    unnamed x43, local copies, waits for them, and re-layouts  5.08 us
    pallas_call x1, Pallas kernels, local(): pl.pallas_call(first_volume_kernel, out_shape=shapes + (jax.ShapeDtypeStr...  3.98 us
    pallas_call x1, Pallas kernels, tendency(): pl.pallas_call(volume_kernel, out_shape=shapes)  3.47 us
    all_to_all x2, waiting for transfers between devices, owner_map(): gathered = lax.all_to_all(partial, both, 0, 0, tiled=True)  2.75 us
  transfers between devices with their start and end apart: 8, of which 4 were waited for; matrix products, arithmetic and copies ran while one was open for 11% of the time, Pallas kernels for 5%

profile of v17, /device:TPU:0, one launch (start us, length us, event | category | flops | bytes accessed | tf_op | source)
XLA Modules:
  0.0 66.3 jit_solution(5328571981349691783)
XLA Ops:
  0.1 0.7 %copy-done.12 = s32[32]{0:T(128)S(1)} copy-done((s32[32]{0:T(128)S(1)}, s32[32]{0:T(128)}, u32[]{:S(2)}) %copy-start.12) | copy-done | bytes 152
  0.7 0.1 fusion.47
  0.9 0.1 copy.48
  1.0 0.6 broadcast_multiply_fusion.1.table_ref
  1.6 4.0 %shard_map.127 = (f32[3,128,128]{2,1,0:T(8,128)}, f32[2,3,8,128]{3,2,1,0:T(8,128)}, f32[2,3,128]{2,1,0:T(4,128)}, f32[64,128]{1,0:T(8,128)}, f32[9,128,128]{2,1,0:T(8,128)}) custom-call(f32[3,128,128]{2,1,0:T(8,128)} %bitcast.130, f32[3,128,128]{2,1,0:T(8,128)} %bitcast.126, f32[6,128,128]{2,1,0:T(8,128)} %constant.334.clone.mats_ref, ...), custom_call_target="tpu_custom_call" | custom-call | tf_op jit(solution)/shard_map/pallas_call | solution.py:388
  5.6 7.3 %all-to-all-start = ((f32[32,2,128]{2,1,0:T(2,128)}), f32[32,2,128]{2,1,0:T(2,128)S(1)}, u32[]{:S(2)}, u32[]{:S(2)}) async-start(f32[32,2,128]{2,1,0:T(2,128)} %bitcast.137), calls=%async_computation | async-start | bytes 65536 | tf_op jit(solution)/shard_map/all_to_all | solution.py:270
  12.9 0.3 collective-permute-start
  13.2 3.3 %collective-permute-start.1 = (f32[3,8,1,128]{3,1,0,2:T(8,128)S(1)}, f32[3,8,1,128]{3,1,0,2:T(8,128)S(1)}, u32[]{:S(2)}, u32[]{:S(2)}) collective-permute-start(f32[3,8,1,128]{3,1,0,2:T(8,128)S(1)} %get-tuple-element.52), channel_id=1, source_target_pairs={{4,0},{8,4},{12,8},{16,12},{20,16},{24,20},{28,24},{0,28},{5,1},{9... | collective-permute-start | bytes 36872 | tf_op jit(solution)/shard_map/ppermute | solution.py:301
  16.6 0.6 copy-done.11
  17.5 0.6 fusion.112
  18.2 0.6 copy-done.10
  18.8 0.1 broadcast_multiply_fusion
  18.9 1.3 %all-to-all-done = f32[32,2,128]{2,1,0:T(2,128)S(1)} async-done(((f32[32,2,128]{2,1,0:T(2,128)}), f32[32,2,128]{2,1,0:T(2,128)S(1)}, u32[]{:S(2)}, u32[]{:S(2)}) %all-to-all-start) | async-done | bytes 32800 | tf_op jit(solution)/shard_map/all_to_all | solution.py:270
  20.2 0.2 fusion.12
  20.5 0.1 fusion.54
  20.7 0.1 reshape_reshape.6
  20.8 0.8 %pad_maximum_fusion.1 = f32[32,1,644]{2,1,0:T(1,128)} fusion(f32[32,1,384]{2,1,0:T(1,128)S(1)} %constant_dynamic-update-slice_fusion.6, f32[32,1,260]{2,1,0:T(1,128)S(1)} %reshape_reshape.6), kind=kLoop, calls=%fused_computation.34 | loop fusion | flops 20608 | bytes 164864 | tf_op jit(solution)/shard_map/concatenate | solution.py:316
  21.6 2.8 %all-to-all-start.1 = ((f32[32,1,644]{2,1,0:T(1,128)}), f32[32,1,644]{2,1,0:T(1,128)S(1)}, u32[]{:S(2)}, u32[]{:S(2)}) async-start(f32[32,1,644]{2,1,0:T(1,128)} %pad_maximum_fusion.1), calls=%async_computation.1 | async-start | bytes 196608 | tf_op jit(solution)/shard_map/all_to_all | solution.py:317
  24.5 7.9 %all-to-all-done.1 = f32[32,1,644]{2,1,0:T(1,128)S(1)} async-done(((f32[32,1,644]{2,1,0:T(1,128)}), f32[32,1,644]{2,1,0:T(1,128)S(1)}, u32[]{:S(2)}, u32[]{:S(2)}) %all-to-all-start.1) | async-done | bytes 82464 | tf_op jit(solution)/shard_map/all_to_all | solution.py:317
  32.3 0.1 fusion.57
  32.4 0.1 reshape.849
  32.6 0.1 reshape.848
  32.8 0.1 reshape.854
  32.8 0.1 reshape.853
  32.9 0.1 pad_maximum_fusion.4
  33.1 0.2 reshape.879
  33.3 0.2 reshape.880
  33.5 0.1 pad_maximum_fusion.5
  33.6 0.1 slice_reduce_fusion.1
  33.8 0.2 fusion.6
  34.1 0.4 copy-done.3
  34.5 0.4 multiply_add_fusion
  35.3 0.8 %copy-done.1 = f32[3,8,16,128]{3,2,1,0:T(8,128)S(1)} copy-done((f32[3,8,16,128]{3,2,1,0:T(8,128)S(1)}, f32[3,8,16,128]{3,2,1,0:T(8,128)}, u32[]{:S(2)}) %copy-start.1) | copy-done | bytes 196632
  36.2 0.2 fusion.9
  36.4 0.3 fusion.39
  36.7 0.6 copy.63
  37.4 2.5 %all-to-all-start.2 = ((f32[32,2,128]{2,1,0:T(2,128)}), f32[32,2,128]{2,1,0:T(2,128)S(1)}, u32[]{:S(2)}, u32[]{:S(2)}) async-start(f32[32,2,128]{2,1,0:T(2,128)} %copy.63), calls=%async_computation.2 | async-start | bytes 65536 | tf_op jit(solution)/shard_map/all_to_all | solution.py:270
  40.2 1.2 %fusion.3 = f32[3,8,16,128]{3,2,1,0:T(8,128)} fusion(f32[3,8,16,128]{3,2,1,0:T(8,128)S(1)} %copy-done.1, f32[3,8,2,1,130]{4,3,2,1,0:T(1,128)S(1)} %copy.62, f32[3,8,2,6,130]{4,3,2,1,0:T(8,128)S(1)} %slice.259, f32[3,8,2,1,130]{4,3,2,1,0:T(1,128)S(1)} %copy.61, f32[8,16,128]{2,1,0:T(8,128)S(1)} %broadcast_multiply_fusion, f32[130,128]{1,0:T(8,128)S(1)} %copy-done.6, ...), kind=kOutput, calls=%fused_computation.5 | convolution fusion | flops 76990976 | bytes 858120 | tf_op jit(solution)/shard_map/dot_general | solution.py:381
  41.4 3.5 %shard_map.128 = (f32[3,128,128]{2,1,0:T(8,128)}, f32[2,3,8,128]{3,2,1,0:T(8,128)}, f32[2,3,128]{2,1,0:T(4,128)}) custom-call(f32[3,128,128]{2,1,0:T(8,128)} %bitcast.133, f32[3,128,128]{2,1,0:T(8,128)} %bitcast.127, f32[9,128,128]{2,1,0:T(8,128)} %get-tuple-element.17.grad_ref, f32[6,128,128]{2,1,0:T(8,128)} %constant.334.clone.mats_ref, ...), custom_call_target="tpu_custom_call" | custom-call | tf_op jit(solution)/shard_map/pallas_call | solution.py:402
  44.9 0.7 %fusion.117 = (f32[1,3,128]{2,1,0:T(4,128)S(1)}, f32[1,3,128]{2,1,0:T(4,128)S(1)}) fusion(f32[2,3,128]{2,1,0:T(4,128)} %get-tuple-element.18), kind=kLoop, calls=%fused_computation.280 | loop fusion | bytes 6144 | tf_op jit(solution)/shard_map/slice | solution.py:302
  45.8 1.5 %all-to-all-done.2 = f32[32,2,128]{2,1,0:T(2,128)S(1)} async-done(((f32[32,2,128]{2,1,0:T(2,128)}), f32[32,2,128]{2,1,0:T(2,128)S(1)}, u32[]{:S(2)}, u32[]{:S(2)}) %all-to-all-start.2) | async-done | bytes 32800 | tf_op jit(solution)/shard_map/all_to_all | solution.py:270
  47.3 0.2 fusion.10
  47.6 0.1 fusion.52
  47.7 0.1 reshape_reshape.7
  47.8 0.8 %pad_maximum_fusion.2 = f32[32,1,644]{2,1,0:T(1,128)} fusion(f32[32,1,384]{2,1,0:T(1,128)S(1)} %constant_dynamic-update-slice_fusion, f32[32,1,260]{2,1,0:T(1,128)S(1)} %reshape_reshape.7), kind=kLoop, calls=%fused_computation.35 | loop fusion | flops 20608 | bytes 164864 | tf_op jit(solution)/shard_map/concatenate | solution.py:316
  48.7 4.4 %all-to-all-start.3 = ((f32[32,1,644]{2,1,0:T(1,128)}), f32[32,1,644]{2,1,0:T(1,128)S(1)}, u32[]{:S(2)}, u32[]{:S(2)}) async-start(f32[32,1,644]{2,1,0:T(1,128)} %pad_maximum_fusion.2), calls=%async_computation.3 | async-start | bytes 196608 | tf_op jit(solution)/shard_map/all_to_all | solution.py:317
  53.1 0.3 collective-permute-start.2
  53.4 3.3 %collective-permute-start.3 = (f32[3,8,1,128]{3,1,0,2:T(8,128)S(1)}, f32[3,8,1,128]{3,1,0,2:T(8,128)S(1)}, u32[]{:S(2)}, u32[]{:S(2)}) collective-permute-start(f32[3,8,1,128]{3,1,0,2:T(8,128)S(1)} %get-tuple-element.48), channel_id=1, source_target_pairs={{4,0},{8,4},{12,8},{16,12},{20,16},{24,20},{28,24},{0,28},{5,1},{9... | collective-permute-start | bytes 36872 | tf_op jit(solution)/shard_map/ppermute | solution.py:301
  56.7 4.5 %all-to-all-done.3 = f32[32,1,644]{2,1,0:T(1,128)S(1)} async-done(((f32[32,1,644]{2,1,0:T(1,128)}), f32[32,1,644]{2,1,0:T(1,128)S(1)}, u32[]{:S(2)}, u32[]{:S(2)}) %all-to-all-start.3) | async-done | bytes 82464 | tf_op jit(solution)/shard_map/all_to_all | solution.py:317
  61.1 0.1 fusion.63
  61.2 0.1 reshape.867
  61.4 0.1 reshape.866
  61.6 0.1 slice_reduce_fusion
  61.8 0.2 fusion.5
  62.0 0.1 reshape.872
  62.1 0.1 reshape.871
  62.2 0.1 pad_maximum_fusion.6
  62.3 0.2 reshape.881
  62.5 0.2 reshape.882
  62.8 0.1 pad_maximum_fusion.7
  62.9 0.6 copy-done.2
  63.4 0.4 maximum_add_fusion
  64.4 0.7 %copy-done.4 = f32[3,8,16,128]{3,2,1,0:T(8,128)S(1)} copy-done((f32[3,8,16,128]{3,2,1,0:T(8,128)S(1)}, f32[3,8,16,128]{3,2,1,0:T(8,128)}, u32[]{:S(2)}) %copy-start.4) | copy-done | bytes 196632
  65.1 1.2 %fusion.4 = f32[3,8,16,128]{3,2,1,0:T(8,128)} fusion(f32[3,8,2,1,130]{4,3,2,1,0:T(1,128)S(1)} %copy.78, f32[3,8,2,6,130]{4,3,2,1,0:T(8,128)S(1)} %slice.286, f32[3,8,2,1,130]{4,3,2,1,0:T(1,128)S(1)} %copy.77, f32[3,8,16,128]{3,2,1,0:T(8,128)S(1)} %copy-done.1, f32[3,8,16,128]{3,2,1,0:T(8,128)S(1)} %copy-done.4, ...), kind=kOutput, calls=%fused_computation.6 | convolution fusion | flops 77089280 | bytes 1054728 | tf_op jit(solution)/shard_map/dot_general | solution.py:381
  (110 shorter events, 2.6 us)
Async XLA Ops:
  0.0 20.2 %copy-start = (bf16[1,512,512]{2,1,0:T(8,128)(2,1)S(1)}, bf16[1,512,512]{2,1,0:T(8,128)(2,1)}, u32[]{:S(2)}) copy-start(bf16[1,512,512]{2,1,0:T(8,128)(2,1)} %param.15) | copy-start | bytes 1572868
  0.0 0.7 %copy-start.12 = (s32[32]{0:T(128)S(1)}, s32[32]{0:T(128)}, u32[]{:S(2)}) copy-start(s32[32]{0:T(128)} %param.16) | copy-start | bytes 388
  5.6 7.3 %copy-start.9 = (f32[2,3,8,128]{3,2,1,0:T(8,128)S(1)}, f32[2,3,8,128]{3,2,1,0:T(8,128)}, u32[]{:S(2)}) copy-start(f32[2,3,8,128]{3,2,1,0:T(8,128)} %get-tuple-element.15) | copy-start | bytes 73732
  5.6 14.6 %all-to-all-start = ((f32[32,2,128]{2,1,0:T(2,128)}), f32[32,2,128]{2,1,0:T(2,128)S(1)}, u32[]{:S(2)}, u32[]{:S(2)}) async-start(f32[32,2,128]{2,1,0:T(2,128)} %bitcast.137), calls=%async_computation | async-start | bytes 65536 | tf_op jit(solution)/shard_map/all_to_all | solution.py:270
  12.9 20.0 %collective-permute-start = (f32[3,8,1,128]{3,1,0,2:T(8,128)S(1)}, f32[3,8,1,128]{3,1,0,2:T(8,128)S(1)}, u32[]{:S(2)}, u32[]{:S(2)}) collective-permute-start(f32[3,8,1,128]{3,1,0,2:T(8,128)S(1)} %get-tuple-element.51), channel_id=1, source_target_pairs={{0,4},{4,8},{8,12},{12,16},{16,20},{20,24},{24,28},{28,0},{1,5},{5... | collective-permute-start | bytes 36872 | tf_op jit(solution)/shard_map/ppermute | solution.py:300
  13.2 20.3 %collective-permute-start.1 = (f32[3,8,1,128]{3,1,0,2:T(8,128)S(1)}, f32[3,8,1,128]{3,1,0,2:T(8,128)S(1)}, u32[]{:S(2)}, u32[]{:S(2)}) collective-permute-start(f32[3,8,1,128]{3,1,0,2:T(8,128)S(1)} %get-tuple-element.52), channel_id=1, source_target_pairs={{4,0},{8,4},{12,8},{16,12},{20,16},{24,20},{28,24},{0,28},{5,1},{9... | collective-permute-start | bytes 36872 | tf_op jit(solution)/shard_map/ppermute | solution.py:301
  16.5 0.7 %copy-start.11 = (f32[2,3,128]{2,1,0:T(4,128)S(1)}, f32[2,3,128]{2,1,0:T(4,128)}, u32[]{:S(2)}) copy-start(f32[2,3,128]{2,1,0:T(4,128)} %get-tuple-element.14) | copy-start | bytes 9220
  17.4 0.8 %copy-start.13 = (f32[128]{0:T(128)S(1)}, f32[128]{0:T(128)}, u32[]{:S(2)}) copy-start(f32[128]{0:T(128)} %constant.330.clone) | copy-start | bytes 1540
  17.4 0.7 %copy-start.14 = (f32[128]{0:T(128)S(1)}, f32[128]{0:T(128)}, u32[]{:S(2)}) copy-start(f32[128]{0:T(128)} %constant.331.clone) | copy-start | bytes 1540
  17.5 0.7 %copy-start.15 = (f32[128]{0:T(128)S(1)}, f32[128]{0:T(128)}, u32[]{:S(2)}) copy-start(f32[128]{0:T(128)} %constant.332.clone) | copy-start | bytes 1540
  18.1 0.7 %copy-start.10 = (f32[8,16]{1,0:T(8,128)S(1)}, f32[8,16]{1,0:T(8,128)}, u32[]{:S(2)}) copy-start(f32[8,16]{1,0:T(8,128)} %constant.340) | copy-start | bytes 1540
  21.6 10.7 %all-to-all-start.1 = ((f32[32,1,644]{2,1,0:T(1,128)}), f32[32,1,644]{2,1,0:T(1,128)S(1)}, u32[]{:S(2)}, u32[]{:S(2)}) async-start(f32[32,1,644]{2,1,0:T(1,128)} %pad_maximum_fusion.1), calls=%async_computation.1 | async-start | bytes 196608 | tf_op jit(solution)/shard_map/all_to_all | solution.py:317
  33.6 0.9 %copy-start.3 = (f32[3,128,128]{2,1,0:T(8,128)S(1)}, f32[3,128,128]{2,1,0:T(8,128)}, u32[]{:S(2)}) copy-start(f32[3,128,128]{2,1,0:T(8,128)} %get-tuple-element.16) | copy-start | bytes 589828
  35.2 0.9 %copy-start.1 = (f32[3,8,16,128]{3,2,1,0:T(8,128)S(1)}, f32[3,8,16,128]{3,2,1,0:T(8,128)}, u32[]{:S(2)}) copy-start(f32[3,8,16,128]{3,2,1,0:T(8,128)} %param.13) | copy-start | bytes 589828
  35.2 1.0 %copy-start.5 = (f32[130,128]{1,0:T(8,128)S(1)}, f32[130,128]{1,0:T(8,128)}, u32[]{:S(2)}) copy-start(f32[130,128]{1,0:T(8,128)} %constant.335.clone) | copy-start | bytes 199684
  35.2 1.0 %copy-start.6 = (f32[130,128]{1,0:T(8,128)S(1)}, f32[130,128]{1,0:T(8,128)}, u32[]{:S(2)}) copy-start(f32[130,128]{1,0:T(8,128)} %constant.336.clone) | copy-start | bytes 199684
  35.2 1.0 %copy-start.7 = (f32[130,128]{1,0:T(8,128)S(1)}, f32[130,128]{1,0:T(8,128)}, u32[]{:S(2)}) copy-start(f32[130,128]{1,0:T(8,128)} %constant.337.clone) | copy-start | bytes 199684
  37.4 9.9 %all-to-all-start.2 = ((f32[32,2,128]{2,1,0:T(2,128)}), f32[32,2,128]{2,1,0:T(2,128)S(1)}, u32[]{:S(2)}, u32[]{:S(2)}) async-start(f32[32,2,128]{2,1,0:T(2,128)} %copy.63), calls=%async_computation.2 | async-start | bytes 65536 | tf_op jit(solution)/shard_map/all_to_all | solution.py:270
  48.7 4.4 %copy-start.8 = (f32[2,3,8,128]{3,2,1,0:T(8,128)S(1)}, f32[2,3,8,128]{3,2,1,0:T(8,128)}, u32[]{:S(2)}) copy-start(f32[2,3,8,128]{3,2,1,0:T(8,128)} %get-tuple-element.19) | copy-start | bytes 73732
  48.7 12.5 %all-to-all-start.3 = ((f32[32,1,644]{2,1,0:T(1,128)}), f32[32,1,644]{2,1,0:T(1,128)S(1)}, u32[]{:S(2)}, u32[]{:S(2)}) async-start(f32[32,1,644]{2,1,0:T(1,128)} %pad_maximum_fusion.2), calls=%async_computation.3 | async-start | bytes 196608 | tf_op jit(solution)/shard_map/all_to_all | solution.py:317
  53.1 9.1 %collective-permute-start.2 = (f32[3,8,1,128]{3,1,0,2:T(8,128)S(1)}, f32[3,8,1,128]{3,1,0,2:T(8,128)S(1)}, u32[]{:S(2)}, u32[]{:S(2)}) collective-permute-start(f32[3,8,1,128]{3,1,0,2:T(8,128)S(1)} %get-tuple-element.47), channel_id=1, source_target_pairs={{0,4},{4,8},{8,12},{12,16},{16,20},{20,24},{24,28},{28,0},{1,5},{5... | collective-permute-start | bytes 36872 | tf_op jit(solution)/shard_map/ppermute | solution.py:300
  53.4 9.4 %collective-permute-start.3 = (f32[3,8,1,128]{3,1,0,2:T(8,128)S(1)}, f32[3,8,1,128]{3,1,0,2:T(8,128)S(1)}, u32[]{:S(2)}, u32[]{:S(2)}) collective-permute-start(f32[3,8,1,128]{3,1,0,2:T(8,128)S(1)} %get-tuple-element.48), channel_id=1, source_target_pairs={{4,0},{8,4},{12,8},{16,12},{20,16},{24,20},{28,24},{0,28},{5,1},{9... | collective-permute-start | bytes 36872 | tf_op jit(solution)/shard_map/ppermute | solution.py:301
  62.5 0.9 %copy-start.2 = (f32[3,128,128]{2,1,0:T(8,128)S(1)}, f32[3,128,128]{2,1,0:T(8,128)}, u32[]{:S(2)}) copy-start(f32[3,128,128]{2,1,0:T(8,128)} %get-tuple-element.20) | copy-start | bytes 589828
  64.1 0.9 %copy-start.4 = (f32[3,8,16,128]{3,2,1,0:T(8,128)S(1)}, f32[3,8,16,128]{3,2,1,0:T(8,128)}, u32[]{:S(2)}) copy-start(f32[3,8,16,128]{3,2,1,0:T(8,128)} %fusion.3) | copy-start | bytes 589828

commit v18 on v17

--- a/solution.py
+++ b/solution.py
@@ -230,17 +230,27 @@
     w_a = np.tile(weights, elems_a)
     w_b = np.tile(weights, elems_b)
     mass3 = w_r[:, None, None] * w_a[None, :, None] * w_b[None, None, :]
-    b_first = np.zeros((nb_dev,), np.float32)
-    b_first[0] = weights[P_SIZE - 1]
-    b_last = np.zeros((nb_dev,), np.float32)
-    b_last[nb_dev - 1] = weights[0]
-    assembled_b = static_assembled(weights, elems_b, 0.0, 0.0) + lead * b_first + trail * b_last
+    origin = jnp.minimum(tile_index, 0)
+
+    def assembled_at(length, lead_value, trail_value):
+        position = origin + jnp.arange(length, dtype=jnp.int32)
+        local_point = position % P_SIZE
+        element = position // P_SIZE
+        count = length // P_SIZE
+        starts = jnp.where(
+            local_point == 0, jnp.where(element > 0, 1.0, lead_value), 0.0
+        ) * float(weights[P_SIZE - 1])
+        ends = jnp.where(
+            local_point == P_SIZE - 1, jnp.where(element < count - 1, 1.0, trail_value), 0.0
+        ) * float(weights[0])
+        return table_at(weights, position) + starts + ends
+
     assembled = (
         (
-            static_assembled(weights, radial_nodes // P_SIZE, 0.0, 0.0)[:, None]
-            * static_assembled(weights, elems_a, 1.0, 1.0)[None, :]
+            assembled_at(radial_nodes, 0.0, 0.0)[:, None]
+            * assembled_at(na_dev, 1.0, 1.0)[None, :]
         )[:, :, None]
-        * assembled_b[None, None, :]
+        * assembled_at(nb_dev, lead, trail)[None, None, :]
     )
     rows_ext = (tile_index * na_dev - 1 + jnp.arange(na_dev + 2, dtype=jnp.int32)) % (na_dev * tiles)
     row_points = (np.arange(na_dev + 2) - 1) % P_SIZE

time: 66.9 us -> 66.7 us (level)
    unnamed x43 -> x35, local copies, waits for them, and re-layouts: 5.08 us -> 4.45 us
where the time goes in v18:
time: 66.7 us; the launch traced here: 66.1 us
  starting transfers between devices  24 us (36%)
  waiting for transfers between devices  15.6 us (23%)
  local copies, waits for them, and re-layouts  9.35 us (14%)
  Pallas kernels  7.45 us (11%)
  other arithmetic  5.11 us (8%)
  matrix products  3.9 us (6%)
  between operations  0.69 us (1%)
    all_to_all x2, waiting for transfers between devices, joint_exchange(): received = lax.all_to_all(message, both, 0, 0, tiled=True)  12.3 us
    all_to_all x2, starting transfers between devices, owner_map(): gathered = lax.all_to_all(partial, both, 0, 0, tiled=True)  9.84 us
    all_to_all x2, starting transfers between devices, joint_exchange(): received = lax.all_to_all(message, both, 0, 0, tiled=True)  6.94 us
    ppermute x2, starting transfers between devices, joint_exchange(): from_down = lax.ppermute(a_lo, 'tile', down)  6.59 us
    unnamed x35, local copies, waits for them, and re-layouts  4.45 us
    pallas_call x1, Pallas kernels, local(): pl.pallas_call(first_volume_kernel, out_shape=shapes + (jax.ShapeDtypeStr...  3.98 us
    pallas_call x1, Pallas kernels, tendency(): pl.pallas_call(volume_kernel, out_shape=shapes)  3.47 us
    all_to_all x2, waiting for transfers between devices, owner_map(): gathered = lax.all_to_all(partial, both, 0, 0, tiled=True)  3.28 us
  transfers between devices with their start and end apart: 8, of which 4 were waited for; matrix products, arithmetic and copies ran while one was open for 11% of the time, Pallas kernels for 5%

profile of v18, /device:TPU:0, one launch (start us, length us, event | category | flops | bytes accessed | tf_op | source)
XLA Modules:
  0.0 66.1 jit_solution(16951518058801808065)
XLA Ops:
  0.1 0.7 %copy-done.11 = s32[32]{0:T(128)S(1)} copy-done((s32[32]{0:T(128)S(1)}, s32[32]{0:T(128)}, u32[]{:S(2)}) %copy-start.11) | copy-done | bytes 152
  0.7 0.1 fusion.47
  0.9 0.1 copy.44
  1.0 0.6 broadcast_multiply_fusion.1.table_ref
  1.6 4.0 %shard_map.91 = (f32[3,128,128]{2,1,0:T(8,128)}, f32[2,3,8,128]{3,2,1,0:T(8,128)}, f32[2,3,128]{2,1,0:T(4,128)}, f32[64,128]{1,0:T(8,128)}, f32[9,128,128]{2,1,0:T(8,128)}) custom-call(f32[3,128,128]{2,1,0:T(8,128)} %bitcast.130, f32[3,128,128]{2,1,0:T(8,128)} %bitcast.126, f32[6,128,128]{2,1,0:T(8,128)} %constant.397.clone.mats_ref, ...), custom_call_target="tpu_custom_call" | custom-call | tf_op jit(solution)/shard_map/pallas_call | solution.py:398
  5.6 7.3 %all-to-all-start = ((f32[32,2,128]{2,1,0:T(2,128)}), f32[32,2,128]{2,1,0:T(2,128)S(1)}, u32[]{:S(2)}, u32[]{:S(2)}) async-start(f32[32,2,128]{2,1,0:T(2,128)} %bitcast.137), calls=%async_computation | async-start | bytes 65536 | tf_op jit(solution)/shard_map/all_to_all | solution.py:280
  12.9 0.3 collective-permute-start
  13.2 3.3 %collective-permute-start.1 = (f32[3,8,1,128]{3,1,0,2:T(8,128)S(1)}, f32[3,8,1,128]{3,1,0,2:T(8,128)S(1)}, u32[]{:S(2)}, u32[]{:S(2)}) collective-permute-start(f32[3,8,1,128]{3,1,0,2:T(8,128)S(1)} %get-tuple-element.52), channel_id=1, source_target_pairs={{4,0},{8,4},{12,8},{16,12},{20,16},{24,20},{28,24},{0,28},{5,1},{9... | collective-permute-start | bytes 36872 | tf_op jit(solution)/shard_map/ppermute | solution.py:311
  16.6 0.6 copy-done.10
  17.4 0.6 fusion.146
  18.2 0.1 broadcast_multiply_fusion
  18.4 1.8 %all-to-all-done = f32[32,2,128]{2,1,0:T(2,128)S(1)} async-done(((f32[32,2,128]{2,1,0:T(2,128)}), f32[32,2,128]{2,1,0:T(2,128)S(1)}, u32[]{:S(2)}, u32[]{:S(2)}) %all-to-all-start) | async-done | bytes 32800 | tf_op jit(solution)/shard_map/all_to_all | solution.py:280
  20.2 0.2 fusion.12
  20.5 0.1 fusion.54
  20.6 0.1 reshape_reshape.6
  20.8 0.8 %pad_maximum_fusion.1 = f32[32,1,644]{2,1,0:T(1,128)} fusion(f32[32,1,384]{2,1,0:T(1,128)S(1)} %constant_dynamic-update-slice_fusion.6, f32[32,1,260]{2,1,0:T(1,128)S(1)} %reshape_reshape.6), kind=kLoop, calls=%fused_computation.34 | loop fusion | flops 20608 | bytes 164864 | tf_op jit(solution)/shard_map/concatenate | solution.py:326
  21.6 2.6 %all-to-all-start.1 = ((f32[32,1,644]{2,1,0:T(1,128)}), f32[32,1,644]{2,1,0:T(1,128)S(1)}, u32[]{:S(2)}, u32[]{:S(2)}) async-start(f32[32,1,644]{2,1,0:T(1,128)} %pad_maximum_fusion.1), calls=%async_computation.1 | async-start | bytes 196608 | tf_op jit(solution)/shard_map/all_to_all | solution.py:327
  24.2 7.9 %all-to-all-done.1 = f32[32,1,644]{2,1,0:T(1,128)S(1)} async-done(((f32[32,1,644]{2,1,0:T(1,128)}), f32[32,1,644]{2,1,0:T(1,128)S(1)}, u32[]{:S(2)}, u32[]{:S(2)}) %all-to-all-start.1) | async-done | bytes 82464 | tf_op jit(solution)/shard_map/all_to_all | solution.py:327
  32.1 0.1 fusion.57
  32.2 0.1 reshape.1045
  32.4 0.1 reshape.1044
  32.5 0.1 reshape.1050
  32.6 0.1 reshape.1049
  32.7 0.1 pad_maximum_fusion.4
  32.8 0.2 reshape.1075
  33.1 0.2 reshape.1076
  33.3 0.1 pad_maximum_fusion.5
  33.4 0.1 slice_reduce_fusion.1
  33.6 0.2 fusion.6
  33.8 0.4 copy-done.3
  34.3 0.4 multiply_add_fusion
  35.1 0.8 %copy-done.1 = f32[3,8,16,128]{3,2,1,0:T(8,128)S(1)} copy-done((f32[3,8,16,128]{3,2,1,0:T(8,128)S(1)}, f32[3,8,16,128]{3,2,1,0:T(8,128)}, u32[]{:S(2)}) %copy-start.1) | copy-done | bytes 196632
  36.0 0.2 fusion.9
  36.2 0.3 fusion.39
  36.5 0.6 copy.59
  37.2 2.5 %all-to-all-start.2 = ((f32[32,2,128]{2,1,0:T(2,128)}), f32[32,2,128]{2,1,0:T(2,128)S(1)}, u32[]{:S(2)}, u32[]{:S(2)}) async-start(f32[32,2,128]{2,1,0:T(2,128)} %copy.59), calls=%async_computation.2 | async-start | bytes 65536 | tf_op jit(solution)/shard_map/all_to_all | solution.py:280
  40.0 1.2 %fusion.3 = f32[3,8,16,128]{3,2,1,0:T(8,128)} fusion(f32[3,8,16,128]{3,2,1,0:T(8,128)S(1)} %copy-done.1, f32[3,8,2,1,130]{4,3,2,1,0:T(1,128)S(1)} %copy.58, f32[3,8,2,6,130]{4,3,2,1,0:T(8,128)S(1)} %slice.259, f32[3,8,2,1,130]{4,3,2,1,0:T(1,128)S(1)} %copy.57, f32[8,16,128]{2,1,0:T(8,128)S(1)} %broadcast_multiply_fusion, f32[130,128]{1,0:T(8,128)S(1)} %copy-done.6, ...), kind=kOutput, calls=%fused_computation.5 | convolution fusion | flops 76990976 | bytes 858120 | tf_op jit(solution)/shard_map/dot_general | solution.py:391
  41.2 3.5 %shard_map.92 = (f32[3,128,128]{2,1,0:T(8,128)}, f32[2,3,8,128]{3,2,1,0:T(8,128)}, f32[2,3,128]{2,1,0:T(4,128)}) custom-call(f32[3,128,128]{2,1,0:T(8,128)} %bitcast.133, f32[3,128,128]{2,1,0:T(8,128)} %bitcast.127, f32[9,128,128]{2,1,0:T(8,128)} %get-tuple-element.17.grad_ref, f32[6,128,128]{2,1,0:T(8,128)} %constant.397.clone.mats_ref, ...), custom_call_target="tpu_custom_call" | custom-call | tf_op jit(solution)/shard_map/pallas_call | solution.py:412
  44.7 0.7 %fusion.151 = (f32[1,3,128]{2,1,0:T(4,128)S(1)}, f32[1,3,128]{2,1,0:T(4,128)S(1)}) fusion(f32[2,3,128]{2,1,0:T(4,128)} %get-tuple-element.18), kind=kLoop, calls=%fused_computation.361 | loop fusion | bytes 6144 | tf_op jit(solution)/shard_map/slice | solution.py:312
  45.5 1.5 %all-to-all-done.2 = f32[32,2,128]{2,1,0:T(2,128)S(1)} async-done(((f32[32,2,128]{2,1,0:T(2,128)}), f32[32,2,128]{2,1,0:T(2,128)S(1)}, u32[]{:S(2)}, u32[]{:S(2)}) %all-to-all-start.2) | async-done | bytes 32800 | tf_op jit(solution)/shard_map/all_to_all | solution.py:280
  47.0 0.2 fusion.10
  47.3 0.1 fusion.52
  47.5 0.1 reshape_reshape.7
  47.6 0.8 %pad_maximum_fusion.2 = f32[32,1,644]{2,1,0:T(1,128)} fusion(f32[32,1,384]{2,1,0:T(1,128)S(1)} %constant_dynamic-update-slice_fusion, f32[32,1,260]{2,1,0:T(1,128)S(1)} %reshape_reshape.7), kind=kLoop, calls=%fused_computation.35 | loop fusion | flops 20608 | bytes 164864 | tf_op jit(solution)/shard_map/concatenate | solution.py:326
  48.4 4.4 %all-to-all-start.3 = ((f32[32,1,644]{2,1,0:T(1,128)}), f32[32,1,644]{2,1,0:T(1,128)S(1)}, u32[]{:S(2)}, u32[]{:S(2)}) async-start(f32[32,1,644]{2,1,0:T(1,128)} %pad_maximum_fusion.2), calls=%async_computation.3 | async-start | bytes 196608 | tf_op jit(solution)/shard_map/all_to_all | solution.py:327
  52.9 0.3 collective-permute-start.2
  53.2 3.3 %collective-permute-start.3 = (f32[3,8,1,128]{3,1,0,2:T(8,128)S(1)}, f32[3,8,1,128]{3,1,0,2:T(8,128)S(1)}, u32[]{:S(2)}, u32[]{:S(2)}) collective-permute-start(f32[3,8,1,128]{3,1,0,2:T(8,128)S(1)} %get-tuple-element.48), channel_id=1, source_target_pairs={{4,0},{8,4},{12,8},{16,12},{20,16},{24,20},{28,24},{0,28},{5,1},{9... | collective-permute-start | bytes 36872 | tf_op jit(solution)/shard_map/ppermute | solution.py:311
  56.5 4.5 %all-to-all-done.3 = f32[32,1,644]{2,1,0:T(1,128)S(1)} async-done(((f32[32,1,644]{2,1,0:T(1,128)}), f32[32,1,644]{2,1,0:T(1,128)S(1)}, u32[]{:S(2)}, u32[]{:S(2)}) %all-to-all-start.3) | async-done | bytes 82464 | tf_op jit(solution)/shard_map/all_to_all | solution.py:327
  60.9 0.1 fusion.63
  61.0 0.1 reshape.1063
  61.2 0.1 reshape.1062
  61.3 0.1 slice_reduce_fusion
  61.5 0.1 reshape_reshape_squeeze.7
  61.6 0.2 fusion.5
  61.8 0.1 reshape.1068
  61.9 0.1 reshape.1067
  62.0 0.1 pad_maximum_fusion.6
  62.1 0.2 reshape.1077
  62.3 0.2 reshape.1078
  62.5 0.1 pad_maximum_fusion.7
  62.6 0.6 copy-done.2
  63.2 0.4 maximum_add_fusion
  64.1 0.7 %copy-done.4 = f32[3,8,16,128]{3,2,1,0:T(8,128)S(1)} copy-done((f32[3,8,16,128]{3,2,1,0:T(8,128)S(1)}, f32[3,8,16,128]{3,2,1,0:T(8,128)}, u32[]{:S(2)}) %copy-start.4) | copy-done | bytes 196632
  64.8 1.2 %fusion.4 = f32[3,8,16,128]{3,2,1,0:T(8,128)} fusion(f32[3,8,2,1,130]{4,3,2,1,0:T(1,128)S(1)} %copy.74, f32[3,8,2,6,130]{4,3,2,1,0:T(8,128)S(1)} %slice.286, f32[3,8,2,1,130]{4,3,2,1,0:T(1,128)S(1)} %copy.73, f32[3,8,16,128]{3,2,1,0:T(8,128)S(1)} %copy-done.1, f32[3,8,16,128]{3,2,1,0:T(8,128)S(1)} %copy-done.4, ...), kind=kOutput, calls=%fused_computation.6 | convolution fusion | flops 77089280 | bytes 1054728 | tf_op jit(solution)/shard_map/dot_general | solution.py:391
  (105 shorter events, 2.6 us)
Async XLA Ops:
  0.0 20.2 %copy-start = (bf16[1,512,512]{2,1,0:T(8,128)(2,1)S(1)}, bf16[1,512,512]{2,1,0:T(8,128)(2,1)}, u32[]{:S(2)}) copy-start(bf16[1,512,512]{2,1,0:T(8,128)(2,1)} %param.11) | copy-start | bytes 1572868
  0.0 0.7 %copy-start.11 = (s32[32]{0:T(128)S(1)}, s32[32]{0:T(128)}, u32[]{:S(2)}) copy-start(s32[32]{0:T(128)} %param.12) | copy-start | bytes 388
  5.6 7.3 %copy-start.9 = (f32[2,3,8,128]{3,2,1,0:T(8,128)S(1)}, f32[2,3,8,128]{3,2,1,0:T(8,128)}, u32[]{:S(2)}) copy-start(f32[2,3,8,128]{3,2,1,0:T(8,128)} %get-tuple-element.15) | copy-start | bytes 73732
  5.6 14.6 %all-to-all-start = ((f32[32,2,128]{2,1,0:T(2,128)}), f32[32,2,128]{2,1,0:T(2,128)S(1)}, u32[]{:S(2)}, u32[]{:S(2)}) async-start(f32[32,2,128]{2,1,0:T(2,128)} %bitcast.137), calls=%async_computation | async-start | bytes 65536 | tf_op jit(solution)/shard_map/all_to_all | solution.py:280
  12.9 19.8 %collective-permute-start = (f32[3,8,1,128]{3,1,0,2:T(8,128)S(1)}, f32[3,8,1,128]{3,1,0,2:T(8,128)S(1)}, u32[]{:S(2)}, u32[]{:S(2)}) collective-permute-start(f32[3,8,1,128]{3,1,0,2:T(8,128)S(1)} %get-tuple-element.51), channel_id=1, source_target_pairs={{0,4},{4,8},{8,12},{12,16},{16,20},{20,24},{24,28},{28,0},{1,5},{5... | collective-permute-start | bytes 36872 | tf_op jit(solution)/shard_map/ppermute | solution.py:310
  13.2 20.1 %collective-permute-start.1 = (f32[3,8,1,128]{3,1,0,2:T(8,128)S(1)}, f32[3,8,1,128]{3,1,0,2:T(8,128)S(1)}, u32[]{:S(2)}, u32[]{:S(2)}) collective-permute-start(f32[3,8,1,128]{3,1,0,2:T(8,128)S(1)} %get-tuple-element.52), channel_id=1, source_target_pairs={{4,0},{8,4},{12,8},{16,12},{20,16},{24,20},{28,24},{0,28},{5,1},{9... | collective-permute-start | bytes 36872 | tf_op jit(solution)/shard_map/ppermute | solution.py:311
  16.6 0.7 %copy-start.10 = (f32[2,3,128]{2,1,0:T(4,128)S(1)}, f32[2,3,128]{2,1,0:T(4,128)}, u32[]{:S(2)}) copy-start(f32[2,3,128]{2,1,0:T(4,128)} %get-tuple-element.14) | copy-start | bytes 9220
  21.6 10.5 %all-to-all-start.1 = ((f32[32,1,644]{2,1,0:T(1,128)}), f32[32,1,644]{2,1,0:T(1,128)S(1)}, u32[]{:S(2)}, u32[]{:S(2)}) async-start(f32[32,1,644]{2,1,0:T(1,128)} %pad_maximum_fusion.1), calls=%async_computation.1 | async-start | bytes 196608 | tf_op jit(solution)/shard_map/all_to_all | solution.py:327
  33.4 0.9 %copy-start.3 = (f32[3,128,128]{2,1,0:T(8,128)S(1)}, f32[3,128,128]{2,1,0:T(8,128)}, u32[]{:S(2)}) copy-start(f32[3,128,128]{2,1,0:T(8,128)} %get-tuple-element.16) | copy-start | bytes 589828
  35.0 0.9 %copy-start.1 = (f32[3,8,16,128]{3,2,1,0:T(8,128)S(1)}, f32[3,8,16,128]{3,2,1,0:T(8,128)}, u32[]{:S(2)}) copy-start(f32[3,8,16,128]{3,2,1,0:T(8,128)} %param.9) | copy-start | bytes 589828
  35.0 1.0 %copy-start.5 = (f32[130,128]{1,0:T(8,128)S(1)}, f32[130,128]{1,0:T(8,128)}, u32[]{:S(2)}) copy-start(f32[130,128]{1,0:T(8,128)} %constant.398.clone) | copy-start | bytes 199684
  35.0 1.0 %copy-start.6 = (f32[130,128]{1,0:T(8,128)S(1)}, f32[130,128]{1,0:T(8,128)}, u32[]{:S(2)}) copy-start(f32[130,128]{1,0:T(8,128)} %constant.399.clone) | copy-start | bytes 199684
  35.0 1.0 %copy-start.7 = (f32[130,128]{1,0:T(8,128)S(1)}, f32[130,128]{1,0:T(8,128)}, u32[]{:S(2)}) copy-start(f32[130,128]{1,0:T(8,128)} %constant.400.clone) | copy-start | bytes 199684
  37.2 9.8 %all-to-all-start.2 = ((f32[32,2,128]{2,1,0:T(2,128)}), f32[32,2,128]{2,1,0:T(2,128)S(1)}, u32[]{:S(2)}, u32[]{:S(2)}) async-start(f32[32,2,128]{2,1,0:T(2,128)} %copy.59), calls=%async_computation.2 | async-start | bytes 65536 | tf_op jit(solution)/shard_map/all_to_all | solution.py:280
  48.4 4.4 %copy-start.8 = (f32[2,3,8,128]{3,2,1,0:T(8,128)S(1)}, f32[2,3,8,128]{3,2,1,0:T(8,128)}, u32[]{:S(2)}) copy-start(f32[2,3,8,128]{3,2,1,0:T(8,128)} %get-tuple-element.19) | copy-start | bytes 73732
  48.4 12.5 %all-to-all-start.3 = ((f32[32,1,644]{2,1,0:T(1,128)}), f32[32,1,644]{2,1,0:T(1,128)S(1)}, u32[]{:S(2)}, u32[]{:S(2)}) async-start(f32[32,1,644]{2,1,0:T(1,128)} %pad_maximum_fusion.2), calls=%async_computation.3 | async-start | bytes 196608 | tf_op jit(solution)/shard_map/all_to_all | solution.py:327
  52.9 9.1 %collective-permute-start.2 = (f32[3,8,1,128]{3,1,0,2:T(8,128)S(1)}, f32[3,8,1,128]{3,1,0,2:T(8,128)S(1)}, u32[]{:S(2)}, u32[]{:S(2)}) collective-permute-start(f32[3,8,1,128]{3,1,0,2:T(8,128)S(1)} %get-tuple-element.47), channel_id=1, source_target_pairs={{0,4},{4,8},{8,12},{12,16},{16,20},{20,24},{24,28},{28,0},{1,5},{5... | collective-permute-start | bytes 36872 | tf_op jit(solution)/shard_map/ppermute | solution.py:310
  53.2 9.4 %collective-permute-start.3 = (f32[3,8,1,128]{3,1,0,2:T(8,128)S(1)}, f32[3,8,1,128]{3,1,0,2:T(8,128)S(1)}, u32[]{:S(2)}, u32[]{:S(2)}) collective-permute-start(f32[3,8,1,128]{3,1,0,2:T(8,128)S(1)} %get-tuple-element.48), channel_id=1, source_target_pairs={{4,0},{8,4},{12,8},{16,12},{20,16},{24,20},{28,24},{0,28},{5,1},{9... | collective-permute-start | bytes 36872 | tf_op jit(solution)/shard_map/ppermute | solution.py:311
  62.3 0.9 %copy-start.2 = (f32[3,128,128]{2,1,0:T(8,128)S(1)}, f32[3,128,128]{2,1,0:T(8,128)}, u32[]{:S(2)}) copy-start(f32[3,128,128]{2,1,0:T(8,128)} %get-tuple-element.20) | copy-start | bytes 589828
  63.9 0.9 %copy-start.4 = (f32[3,8,16,128]{3,2,1,0:T(8,128)S(1)}, f32[3,8,16,128]{3,2,1,0:T(8,128)}, u32[]{:S(2)}) copy-start(f32[3,8,16,128]{3,2,1,0:T(8,128)} %fusion.3) | copy-start | bytes 589828

commit v19 on v18

--- a/solution.py
+++ b/solution.py
@@ -75,8 +75,9 @@
         result = mass * (stretch - carried) - diffusivity * spread
         out_ref[c] = result
         turned = result.T
-        cols_ref[0, c : c + 1, :] = turned[0:1, :]
-        cols_ref[1, c : c + 1, :] = turned[width - 1 : width, :]
+        span_of = out_ref.shape[1]
+        cols_ref[0, :, c * span_of : (c + 1) * span_of] = turned[0:1, :]
+        cols_ref[1, :, c * span_of : (c + 1) * span_of] = turned[width - 1 : width, :]
     for c in range(3):
         rows_ref[0, c] = out_ref[c, pl.ds(0, rows_ref.shape[2], stride=planes), :]
         rows_ref[1, c] = out_ref[c, pl.ds(planes - 1, rows_ref.shape[2], stride=planes), :]
@@ -309,8 +310,8 @@
         down = [(j, i) for i, j in up]
         from_up = lax.ppermute(a_hi, "tile", up)
         from_down = lax.ppermute(a_lo, "tile", down)
-        b_lo = edge_cols[0].reshape(1, 1, -1)
-        b_hi = edge_cols[1].reshape(1, 1, -1)
+        b_lo = edge_cols[0:1]
+        b_hi = edge_cols[1:2]
         out_pieces = [
             ((0, 1), b_hi),
             ((0, -1), b_lo),
@@ -393,7 +394,7 @@
     shapes = (
         jax.ShapeDtypeStruct((3, rows, nb_dev), jnp.float32),
         jax.ShapeDtypeStruct((2, 3, radial_nodes, nb_dev), jnp.float32),
-        jax.ShapeDtypeStruct((2, 3, rows), jnp.float32),
+        jax.ShapeDtypeStruct((2, 1, 3 * rows), jnp.float32),
     )
     first_outs = pl.pallas_call(
         first_volume_kernel,

time: 66.7 us -> 66.7 us (level)
    slice x2 -> x0, local copies, waits for them, and re-layouts: 0.69 us -> none  [joint_exchange(): b_lo = edge_cols[0].reshape(1, 1, -1)]
    unnamed x35 -> x37, local copies, waits for them, and re-layouts: 4.45 us -> 5.11 us
  transfers between devices with their start and end apart: 8 -> 8, of which waited for: 4 -> 4; matrix products, arithmetic and copies ran while one was open for 11% -> 10% of each run, Pallas kernels for 5% -> 5%
where the time goes in v19:
time: 66.7 us; the launch traced here: 66.1 us
  starting transfers between devices  23.9 us (36%)
  waiting for transfers between devices  15.8 us (24%)
  local copies, waits for them, and re-layouts  9.22 us (14%)
  Pallas kernels  7.48 us (11%)
  other arithmetic  5.13 us (8%)
  matrix products  3.9 us (6%)
  between operations  0.67 us (1%)
    all_to_all x2, waiting for transfers between devices, joint_exchange(): received = lax.all_to_all(message, both, 0, 0, tiled=True)  12.3 us
    all_to_all x2, starting transfers between devices, owner_map(): gathered = lax.all_to_all(partial, both, 0, 0, tiled=True)  9.85 us
    all_to_all x2, starting transfers between devices, joint_exchange(): received = lax.all_to_all(message, both, 0, 0, tiled=True)  6.86 us
    ppermute x2, starting transfers between devices, joint_exchange(): from_down = lax.ppermute(a_lo, 'tile', down)  6.59 us
    unnamed x37, local copies, waits for them, and re-layouts  5.11 us
    pallas_call x1, Pallas kernels, local(): pl.pallas_call(first_volume_kernel, out_shape=shapes + (jax.ShapeDtypeStr...  3.98 us
    pallas_call x1, Pallas kernels, tendency(): pl.pallas_call(volume_kernel, out_shape=shapes)  3.49 us
    all_to_all x2, waiting for transfers between devices, owner_map(): gathered = lax.all_to_all(partial, both, 0, 0, tiled=True)  3.41 us
  transfers between devices with their start and end apart: 8, of which 4 were waited for; matrix products, arithmetic and copies ran while one was open for 10% of the time, Pallas kernels for 5%

profile of v19, /device:TPU:0, one launch (start us, length us, event | category | flops | bytes accessed | tf_op | source)
XLA Modules:
  0.0 66.1 jit_solution(5265211599023245190)
XLA Ops:
  0.1 0.7 %copy-done.12 = s32[32]{0:T(128)S(1)} copy-done((s32[32]{0:T(128)S(1)}, s32[32]{0:T(128)}, u32[]{:S(2)}) %copy-start.12) | copy-done | bytes 152
  0.7 0.1 fusion.47
  0.9 0.1 copy.45
  1.0 0.6 broadcast_multiply_fusion.1.table_ref
  1.6 4.0 %shard_map.91 = (f32[3,128,128]{2,1,0:T(8,128)}, f32[2,3,8,128]{3,2,1,0:T(8,128)}, f32[2,1,384]{2,1,0:T(1,128)}, f32[64,128]{1,0:T(8,128)}, f32[9,128,128]{2,1,0:T(8,128)}) custom-call(f32[3,128,128]{2,1,0:T(8,128)} %bitcast.130, f32[3,128,128]{2,1,0:T(8,128)} %bitcast.126, f32[6,128,128]{2,1,0:T(8,128)} %constant.397.clone.mats_ref, ...), custom_call_target="tpu_custom_call" | custom-call | tf_op jit(solution)/shard_map/pallas_call | solution.py:399
  5.6 7.3 %all-to-all-start = ((f32[32,2,128]{2,1,0:T(2,128)}), f32[32,2,128]{2,1,0:T(2,128)S(1)}, u32[]{:S(2)}, u32[]{:S(2)}) async-start(f32[32,2,128]{2,1,0:T(2,128)} %bitcast.137), calls=%async_computation | async-start | bytes 65536 | tf_op jit(solution)/shard_map/all_to_all | solution.py:281
  12.9 0.3 collective-permute-start
  13.2 3.3 %collective-permute-start.1 = (f32[3,8,1,128]{3,1,0,2:T(8,128)S(1)}, f32[3,8,1,128]{3,1,0,2:T(8,128)S(1)}, u32[]{:S(2)}, u32[]{:S(2)}) collective-permute-start(f32[3,8,1,128]{3,1,0,2:T(8,128)S(1)} %get-tuple-element.52), channel_id=1, source_target_pairs={{4,0},{8,4},{12,8},{16,12},{20,16},{24,20},{28,24},{0,28},{5,1},{9... | collective-permute-start | bytes 36872 | tf_op jit(solution)/shard_map/ppermute | solution.py:312
  16.7 0.6 copy-done.8
  17.4 0.6 fusion.146
  18.2 0.1 broadcast_multiply_fusion
  18.3 1.9 %all-to-all-done = f32[32,2,128]{2,1,0:T(2,128)S(1)} async-done(((f32[32,2,128]{2,1,0:T(2,128)}), f32[32,2,128]{2,1,0:T(2,128)S(1)}, u32[]{:S(2)}, u32[]{:S(2)}) %all-to-all-start) | async-done | bytes 32800 | tf_op jit(solution)/shard_map/all_to_all | solution.py:281
  20.2 0.2 fusion.12
  20.5 0.1 fusion.54
  20.7 0.1 reshape_reshape.6
  20.8 0.8 %pad_maximum_fusion.1 = f32[32,1,644]{2,1,0:T(1,128)} fusion(f32[32,1,384]{2,1,0:T(1,128)S(1)} %constant_dynamic-update-slice_fusion.6, f32[32,1,260]{2,1,0:T(1,128)S(1)} %reshape_reshape.6), kind=kLoop, calls=%fused_computation.34 | loop fusion | flops 20608 | bytes 164864 | tf_op jit(solution)/shard_map/concatenate | solution.py:327
  21.6 2.6 %all-to-all-start.1 = ((f32[32,1,644]{2,1,0:T(1,128)}), f32[32,1,644]{2,1,0:T(1,128)S(1)}, u32[]{:S(2)}, u32[]{:S(2)}) async-start(f32[32,1,644]{2,1,0:T(1,128)} %pad_maximum_fusion.1), calls=%async_computation.1 | async-start | bytes 196608 | tf_op jit(solution)/shard_map/all_to_all | solution.py:328
  24.3 7.9 %all-to-all-done.1 = f32[32,1,644]{2,1,0:T(1,128)S(1)} async-done(((f32[32,1,644]{2,1,0:T(1,128)}), f32[32,1,644]{2,1,0:T(1,128)S(1)}, u32[]{:S(2)}, u32[]{:S(2)}) %all-to-all-start.1) | async-done | bytes 82464 | tf_op jit(solution)/shard_map/all_to_all | solution.py:328
  32.1 0.1 fusion.57
  32.3 0.1 reshape.1045
  32.4 0.1 reshape.1044
  32.6 0.1 reshape.1050
  32.6 0.1 reshape.1049
  32.8 0.1 pad_maximum_fusion.4
  32.9 0.2 reshape.1075
  33.1 0.2 reshape.1076
  33.3 0.1 pad_maximum_fusion.5
  33.4 0.1 slice_reduce_fusion.1
  33.6 0.1 reshape_reshape_squeeze.6
  33.6 0.2 fusion.6
  33.9 0.4 copy-done.3
  34.3 0.4 multiply_add_fusion
  35.1 0.8 %copy-done.1 = f32[3,8,16,128]{3,2,1,0:T(8,128)S(1)} copy-done((f32[3,8,16,128]{3,2,1,0:T(8,128)S(1)}, f32[3,8,16,128]{3,2,1,0:T(8,128)}, u32[]{:S(2)}) %copy-start.1) | copy-done | bytes 196632
  36.0 0.2 fusion.9
  36.2 0.3 fusion.39
  36.6 0.6 copy.60
  37.2 2.5 %all-to-all-start.2 = ((f32[32,2,128]{2,1,0:T(2,128)}), f32[32,2,128]{2,1,0:T(2,128)S(1)}, u32[]{:S(2)}, u32[]{:S(2)}) async-start(f32[32,2,128]{2,1,0:T(2,128)} %copy.60), calls=%async_computation.2 | async-start | bytes 65536 | tf_op jit(solution)/shard_map/all_to_all | solution.py:281
  40.0 1.2 %fusion.3 = f32[3,8,16,128]{3,2,1,0:T(8,128)} fusion(f32[3,8,16,128]{3,2,1,0:T(8,128)S(1)} %copy-done.1, f32[3,8,2,1,130]{4,3,2,1,0:T(1,128)S(1)} %copy.59, f32[3,8,2,6,130]{4,3,2,1,0:T(8,128)S(1)} %slice.259, f32[3,8,2,1,130]{4,3,2,1,0:T(1,128)S(1)} %copy.58, f32[8,16,128]{2,1,0:T(8,128)S(1)} %broadcast_multiply_fusion, f32[130,128]{1,0:T(8,128)S(1)} %copy-done.6, ...), kind=kOutput, calls=%fused_computation.5 | convolution fusion | flops 76990976 | bytes 858120 | tf_op jit(solution)/shard_map/dot_general | solution.py:392
  41.3 3.5 %shard_map.92 = (f32[3,128,128]{2,1,0:T(8,128)}, f32[2,3,8,128]{3,2,1,0:T(8,128)}, f32[2,1,384]{2,1,0:T(1,128)}) custom-call(f32[3,128,128]{2,1,0:T(8,128)} %bitcast.133, f32[3,128,128]{2,1,0:T(8,128)} %bitcast.127, f32[9,128,128]{2,1,0:T(8,128)} %get-tuple-element.17.grad_ref, f32[6,128,128]{2,1,0:T(8,128)} %constant.397.clone.mats_ref, ...), custom_call_target="tpu_custom_call" | custom-call | tf_op jit(solution)/shard_map/pallas_call | solution.py:413
  44.8 0.7 copy-done.9
  45.5 1.5 %all-to-all-done.2 = f32[32,2,128]{2,1,0:T(2,128)S(1)} async-done(((f32[32,2,128]{2,1,0:T(2,128)}), f32[32,2,128]{2,1,0:T(2,128)S(1)}, u32[]{:S(2)}, u32[]{:S(2)}) %all-to-all-start.2) | async-done | bytes 32800 | tf_op jit(solution)/shard_map/all_to_all | solution.py:281
  47.1 0.2 fusion.10
  47.4 0.1 fusion.52
  47.5 0.1 reshape_reshape.7
  47.7 0.8 %pad_maximum_fusion.2 = f32[32,1,644]{2,1,0:T(1,128)} fusion(f32[32,1,384]{2,1,0:T(1,128)S(1)} %constant_dynamic-update-slice_fusion, f32[32,1,260]{2,1,0:T(1,128)S(1)} %reshape_reshape.7), kind=kLoop, calls=%fused_computation.35 | loop fusion | flops 20608 | bytes 164864 | tf_op jit(solution)/shard_map/concatenate | solution.py:327
  48.5 4.3 %all-to-all-start.3 = ((f32[32,1,644]{2,1,0:T(1,128)}), f32[32,1,644]{2,1,0:T(1,128)S(1)}, u32[]{:S(2)}, u32[]{:S(2)}) async-start(f32[32,1,644]{2,1,0:T(1,128)} %pad_maximum_fusion.2), calls=%async_computation.3 | async-start | bytes 196608 | tf_op jit(solution)/shard_map/all_to_all | solution.py:328
  52.8 0.3 collective-permute-start.2
  53.1 3.3 %collective-permute-start.3 = (f32[3,8,1,128]{3,1,0,2:T(8,128)S(1)}, f32[3,8,1,128]{3,1,0,2:T(8,128)S(1)}, u32[]{:S(2)}, u32[]{:S(2)}) collective-permute-start(f32[3,8,1,128]{3,1,0,2:T(8,128)S(1)} %get-tuple-element.48), channel_id=1, source_target_pairs={{4,0},{8,4},{12,8},{16,12},{20,16},{24,20},{28,24},{0,28},{5,1},{9... | collective-permute-start | bytes 36872 | tf_op jit(solution)/shard_map/ppermute | solution.py:312
  56.4 4.5 %all-to-all-done.3 = f32[32,1,644]{2,1,0:T(1,128)S(1)} async-done(((f32[32,1,644]{2,1,0:T(1,128)}), f32[32,1,644]{2,1,0:T(1,128)S(1)}, u32[]{:S(2)}, u32[]{:S(2)}) %all-to-all-start.3) | async-done | bytes 82464 | tf_op jit(solution)/shard_map/all_to_all | solution.py:328
  60.9 0.1 fusion.63
  61.0 0.1 reshape.1063
  61.2 0.1 reshape.1062
  61.3 0.1 slice_reduce_fusion
  61.5 0.2 fusion.5
  61.8 0.1 reshape.1068
  61.8 0.1 reshape.1067
  61.9 0.1 pad_maximum_fusion.6
  62.1 0.2 reshape.1077
  62.3 0.2 reshape.1078
  62.5 0.1 pad_maximum_fusion.7
  62.6 0.6 copy-done.2
  63.2 0.4 maximum_add_fusion
  64.1 0.7 %copy-done.4 = f32[3,8,16,128]{3,2,1,0:T(8,128)S(1)} copy-done((f32[3,8,16,128]{3,2,1,0:T(8,128)S(1)}, f32[3,8,16,128]{3,2,1,0:T(8,128)}, u32[]{:S(2)}) %copy-start.4) | copy-done | bytes 196632
  64.8 1.2 %fusion.4 = f32[3,8,16,128]{3,2,1,0:T(8,128)} fusion(f32[3,8,2,1,130]{4,3,2,1,0:T(1,128)S(1)} %copy.75, f32[3,8,2,6,130]{4,3,2,1,0:T(8,128)S(1)} %slice.286, f32[3,8,2,1,130]{4,3,2,1,0:T(1,128)S(1)} %copy.74, f32[3,8,16,128]{3,2,1,0:T(8,128)S(1)} %copy-done.1, f32[3,8,16,128]{3,2,1,0:T(8,128)S(1)} %copy-done.4, ...), kind=kOutput, calls=%fused_computation.6 | convolution fusion | flops 77089280 | bytes 1054728 | tf_op jit(solution)/shard_map/dot_general | solution.py:392
  (101 shorter events, 2.5 us)
Async XLA Ops:
  0.0 20.2 %copy-start = (bf16[1,512,512]{2,1,0:T(8,128)(2,1)S(1)}, bf16[1,512,512]{2,1,0:T(8,128)(2,1)}, u32[]{:S(2)}) copy-start(bf16[1,512,512]{2,1,0:T(8,128)(2,1)} %param.11) | copy-start | bytes 1572868
  0.0 0.7 %copy-start.12 = (s32[32]{0:T(128)S(1)}, s32[32]{0:T(128)}, u32[]{:S(2)}) copy-start(s32[32]{0:T(128)} %param.12) | copy-start | bytes 388
  5.6 7.3 %copy-start.11 = (f32[2,3,8,128]{3,2,1,0:T(8,128)S(1)}, f32[2,3,8,128]{3,2,1,0:T(8,128)}, u32[]{:S(2)}) copy-start(f32[2,3,8,128]{3,2,1,0:T(8,128)} %get-tuple-element.15) | copy-start | bytes 73732
  5.6 14.6 %all-to-all-start = ((f32[32,2,128]{2,1,0:T(2,128)}), f32[32,2,128]{2,1,0:T(2,128)S(1)}, u32[]{:S(2)}, u32[]{:S(2)}) async-start(f32[32,2,128]{2,1,0:T(2,128)} %bitcast.137), calls=%async_computation | async-start | bytes 65536 | tf_op jit(solution)/shard_map/all_to_all | solution.py:281
  12.9 19.8 %collective-permute-start = (f32[3,8,1,128]{3,1,0,2:T(8,128)S(1)}, f32[3,8,1,128]{3,1,0,2:T(8,128)S(1)}, u32[]{:S(2)}, u32[]{:S(2)}) collective-permute-start(f32[3,8,1,128]{3,1,0,2:T(8,128)S(1)} %get-tuple-element.51), channel_id=1, source_target_pairs={{0,4},{4,8},{8,12},{12,16},{16,20},{20,24},{24,28},{28,0},{1,5},{5... | collective-permute-start | bytes 36872 | tf_op jit(solution)/shard_map/ppermute | solution.py:311
  13.2 20.1 %collective-permute-start.1 = (f32[3,8,1,128]{3,1,0,2:T(8,128)S(1)}, f32[3,8,1,128]{3,1,0,2:T(8,128)S(1)}, u32[]{:S(2)}, u32[]{:S(2)}) collective-permute-start(f32[3,8,1,128]{3,1,0,2:T(8,128)S(1)} %get-tuple-element.52), channel_id=1, source_target_pairs={{4,0},{8,4},{12,8},{16,12},{20,16},{24,20},{28,24},{0,28},{5,1},{9... | collective-permute-start | bytes 36872 | tf_op jit(solution)/shard_map/ppermute | solution.py:312
  16.7 0.7 %copy-start.8 = (f32[2,1,384]{2,1,0:T(1,128)S(1)}, f32[2,1,384]{2,1,0:T(1,128)}, u32[]{:S(2)}) copy-start(f32[2,1,384]{2,1,0:T(1,128)} %get-tuple-element.14) | copy-start | bytes 9220
  21.6 10.5 %all-to-all-start.1 = ((f32[32,1,644]{2,1,0:T(1,128)}), f32[32,1,644]{2,1,0:T(1,128)S(1)}, u32[]{:S(2)}, u32[]{:S(2)}) async-start(f32[32,1,644]{2,1,0:T(1,128)} %pad_maximum_fusion.1), calls=%async_computation.1 | async-start | bytes 196608 | tf_op jit(solution)/shard_map/all_to_all | solution.py:328
  33.4 0.9 %copy-start.3 = (f32[3,128,128]{2,1,0:T(8,128)S(1)}, f32[3,128,128]{2,1,0:T(8,128)}, u32[]{:S(2)}) copy-start(f32[3,128,128]{2,1,0:T(8,128)} %get-tuple-element.16) | copy-start | bytes 589828
  35.0 0.9 %copy-start.1 = (f32[3,8,16,128]{3,2,1,0:T(8,128)S(1)}, f32[3,8,16,128]{3,2,1,0:T(8,128)}, u32[]{:S(2)}) copy-start(f32[3,8,16,128]{3,2,1,0:T(8,128)} %param.9) | copy-start | bytes 589828
  35.0 1.0 %copy-start.5 = (f32[130,128]{1,0:T(8,128)S(1)}, f32[130,128]{1,0:T(8,128)}, u32[]{:S(2)}) copy-start(f32[130,128]{1,0:T(8,128)} %constant.398.clone) | copy-start | bytes 199684
  35.0 1.0 %copy-start.6 = (f32[130,128]{1,0:T(8,128)S(1)}, f32[130,128]{1,0:T(8,128)}, u32[]{:S(2)}) copy-start(f32[130,128]{1,0:T(8,128)} %constant.399.clone) | copy-start | bytes 199684
  35.0 1.0 %copy-start.7 = (f32[130,128]{1,0:T(8,128)S(1)}, f32[130,128]{1,0:T(8,128)}, u32[]{:S(2)}) copy-start(f32[130,128]{1,0:T(8,128)} %constant.400.clone) | copy-start | bytes 199684
  37.2 9.9 %all-to-all-start.2 = ((f32[32,2,128]{2,1,0:T(2,128)}), f32[32,2,128]{2,1,0:T(2,128)S(1)}, u32[]{:S(2)}, u32[]{:S(2)}) async-start(f32[32,2,128]{2,1,0:T(2,128)} %copy.60), calls=%async_computation.2 | async-start | bytes 65536 | tf_op jit(solution)/shard_map/all_to_all | solution.py:281
  44.8 0.7 %copy-start.9 = (f32[2,1,384]{2,1,0:T(1,128)S(1)}, f32[2,1,384]{2,1,0:T(1,128)}, u32[]{:S(2)}) copy-start(f32[2,1,384]{2,1,0:T(1,128)} %get-tuple-element.18) | copy-start | bytes 9220
  48.5 4.3 %copy-start.10 = (f32[2,3,8,128]{3,2,1,0:T(8,128)S(1)}, f32[2,3,8,128]{3,2,1,0:T(8,128)}, u32[]{:S(2)}) copy-start(f32[2,3,8,128]{3,2,1,0:T(8,128)} %get-tuple-element.19) | copy-start | bytes 73732
  48.5 12.4 %all-to-all-start.3 = ((f32[32,1,644]{2,1,0:T(1,128)}), f32[32,1,644]{2,1,0:T(1,128)S(1)}, u32[]{:S(2)}, u32[]{:S(2)}) async-start(f32[32,1,644]{2,1,0:T(1,128)} %pad_maximum_fusion.2), calls=%async_computation.3 | async-start | bytes 196608 | tf_op jit(solution)/shard_map/all_to_all | solution.py:328
  52.8 9.1 %collective-permute-start.2 = (f32[3,8,1,128]{3,1,0,2:T(8,128)S(1)}, f32[3,8,1,128]{3,1,0,2:T(8,128)S(1)}, u32[]{:S(2)}, u32[]{:S(2)}) collective-permute-start(f32[3,8,1,128]{3,1,0,2:T(8,128)S(1)} %get-tuple-element.47), channel_id=1, source_target_pairs={{0,4},{4,8},{8,12},{12,16},{16,20},{20,24},{24,28},{28,0},{1,5},{5... | collective-permute-start | bytes 36872 | tf_op jit(solution)/shard_map/ppermute | solution.py:311
  53.1 9.4 %collective-permute-start.3 = (f32[3,8,1,128]{3,1,0,2:T(8,128)S(1)}, f32[3,8,1,128]{3,1,0,2:T(8,128)S(1)}, u32[]{:S(2)}, u32[]{:S(2)}) collective-permute-start(f32[3,8,1,128]{3,1,0,2:T(8,128)S(1)} %get-tuple-element.48), channel_id=1, source_target_pairs={{4,0},{8,4},{12,8},{16,12},{20,16},{24,20},{28,24},{0,28},{5,1},{9... | collective-permute-start | bytes 36872 | tf_op jit(solution)/shard_map/ppermute | solution.py:312
  62.3 0.9 %copy-start.2 = (f32[3,128,128]{2,1,0:T(8,128)S(1)}, f32[3,128,128]{2,1,0:T(8,128)}, u32[]{:S(2)}) copy-start(f32[3,128,128]{2,1,0:T(8,128)} %get-tuple-element.20) | copy-start | bytes 589828
  63.9 0.9 %copy-start.4 = (f32[3,8,16,128]{3,2,1,0:T(8,128)S(1)}, f32[3,8,16,128]{3,2,1,0:T(8,128)}, u32[]{:S(2)}) copy-start(f32[3,8,16,128]{3,2,1,0:T(8,128)} %fusion.3) | copy-start | bytes 589828

commit v20 on v19

--- a/solution.py
+++ b/solution.py
@@ -30,7 +30,7 @@
 
 
 def product(a, b):
-    return jnp.dot(a, b, precision=highest, preferred_element_type=jnp.float32)
+    return jnp.dot(a, b, precision=lax.Precision.HIGH, preferred_element_type=jnp.float32)
 
 
 def gradient_kernel(flow_ref, mats_ref, out_ref):

time: 66.7 us -> 65.3 us (0.979)
  Pallas kernels: 7.48 us -> 6.08 us
    pallas_call x1, Pallas kernels: 3.98 us -> 3.19 us  [local(): pl.pallas_call(first_volume_kernel, out_shape=shapes + (jax.ShapeDtypeStr...]
  transfers between devices with their start and end apart: 8 -> 8, of which waited for: 4 -> 4; matrix products, arithmetic and copies ran while one was open for 10% -> 10% of each run, Pallas kernels for 5% -> 4%
where the time goes in v20:
time: 65.3 us; the launch traced here: 64.7 us
  starting transfers between devices  23.3 us (36%)
  waiting for transfers between devices  16.4 us (25%)
  local copies, waits for them, and re-layouts  9.22 us (14%)
  Pallas kernels  6.08 us (9%)
  other arithmetic  5.13 us (8%)
  matrix products  3.9 us (6%)
  between operations  0.67 us (1%)
    all_to_all x2, waiting for transfers between devices, joint_exchange(): received = lax.all_to_all(message, both, 0, 0, tiled=True)  12.3 us
    all_to_all x2, starting transfers between devices, owner_map(): gathered = lax.all_to_all(partial, both, 0, 0, tiled=True)  9.85 us
    ppermute x2, starting transfers between devices, joint_exchange(): from_down = lax.ppermute(a_lo, 'tile', down)  6.59 us
    all_to_all x2, starting transfers between devices, joint_exchange(): received = lax.all_to_all(message, both, 0, 0, tiled=True)  6.27 us
    unnamed x37, local copies, waits for them, and re-layouts  5.11 us
    all_to_all x2, waiting for transfers between devices, owner_map(): gathered = lax.all_to_all(partial, both, 0, 0, tiled=True)  4.01 us
    pallas_call x1, Pallas kernels, local(): pl.pallas_call(first_volume_kernel, out_shape=shapes + (jax.ShapeDtypeStr...  3.19 us
    pallas_call x1, Pallas kernels, tendency(): pl.pallas_call(volume_kernel, out_shape=shapes)  2.9 us
  transfers between devices with their start and end apart: 8, of which 4 were waited for; matrix products, arithmetic and copies ran while one was open for 10% of the time, Pallas kernels for 4%

profile of v20, /device:TPU:0, one launch (start us, length us, event | category | flops | bytes accessed | tf_op | source)
XLA Modules:
  0.0 64.7 jit_solution(6487018991060126587)
XLA Ops:
  0.1 0.7 %copy-done.12 = s32[32]{0:T(128)S(1)} copy-done((s32[32]{0:T(128)S(1)}, s32[32]{0:T(128)}, u32[]{:S(2)}) %copy-start.12) | copy-done | bytes 152
  0.7 0.1 fusion.47
  0.9 0.1 copy.45
  1.0 0.6 broadcast_multiply_fusion.1.table_ref
  1.6 3.2 %shard_map.91 = (f32[3,128,128]{2,1,0:T(8,128)}, f32[2,3,8,128]{3,2,1,0:T(8,128)}, f32[2,1,384]{2,1,0:T(1,128)}, f32[64,128]{1,0:T(8,128)}, f32[9,128,128]{2,1,0:T(8,128)}) custom-call(f32[3,128,128]{2,1,0:T(8,128)} %bitcast.130, f32[3,128,128]{2,1,0:T(8,128)} %bitcast.126, f32[6,128,128]{2,1,0:T(8,128)} %constant.397.clone.mats_ref, ...), custom_call_target="tpu_custom_call" | custom-call | tf_op jit(solution)/shard_map/pallas_call | solution.py:399
  4.8 7.3 %all-to-all-start = ((f32[32,2,128]{2,1,0:T(2,128)}), f32[32,2,128]{2,1,0:T(2,128)S(1)}, u32[]{:S(2)}, u32[]{:S(2)}) async-start(f32[32,2,128]{2,1,0:T(2,128)} %bitcast.137), calls=%async_computation | async-start | bytes 65536 | tf_op jit(solution)/shard_map/all_to_all | solution.py:281
  12.1 0.3 collective-permute-start
  12.4 3.3 %collective-permute-start.1 = (f32[3,8,1,128]{3,1,0,2:T(8,128)S(1)}, f32[3,8,1,128]{3,1,0,2:T(8,128)S(1)}, u32[]{:S(2)}, u32[]{:S(2)}) collective-permute-start(f32[3,8,1,128]{3,1,0,2:T(8,128)S(1)} %get-tuple-element.52), channel_id=1, source_target_pairs={{4,0},{8,4},{12,8},{16,12},{20,16},{24,20},{28,24},{0,28},{5,1},{9... | collective-permute-start | bytes 36872 | tf_op jit(solution)/shard_map/ppermute | solution.py:312
  15.9 0.6 copy-done.8
  16.6 0.6 fusion.146
  17.4 0.1 broadcast_multiply_fusion
  17.5 1.9 %all-to-all-done = f32[32,2,128]{2,1,0:T(2,128)S(1)} async-done(((f32[32,2,128]{2,1,0:T(2,128)}), f32[32,2,128]{2,1,0:T(2,128)S(1)}, u32[]{:S(2)}, u32[]{:S(2)}) %all-to-all-start) | async-done | bytes 32800 | tf_op jit(solution)/shard_map/all_to_all | solution.py:281
  19.4 0.2 fusion.12
  19.7 0.1 fusion.54
  19.9 0.1 reshape_reshape.6
  20.0 0.8 %pad_maximum_fusion.1 = f32[32,1,644]{2,1,0:T(1,128)} fusion(f32[32,1,384]{2,1,0:T(1,128)S(1)} %constant_dynamic-update-slice_fusion.6, f32[32,1,260]{2,1,0:T(1,128)S(1)} %reshape_reshape.6), kind=kLoop, calls=%fused_computation.34 | loop fusion | flops 20608 | bytes 164864 | tf_op jit(solution)/shard_map/concatenate | solution.py:327
  20.8 2.6 %all-to-all-start.1 = ((f32[32,1,644]{2,1,0:T(1,128)}), f32[32,1,644]{2,1,0:T(1,128)S(1)}, u32[]{:S(2)}, u32[]{:S(2)}) async-start(f32[32,1,644]{2,1,0:T(1,128)} %pad_maximum_fusion.1), calls=%async_computation.1 | async-start | bytes 196608 | tf_op jit(solution)/shard_map/all_to_all | solution.py:328
  23.5 7.9 %all-to-all-done.1 = f32[32,1,644]{2,1,0:T(1,128)S(1)} async-done(((f32[32,1,644]{2,1,0:T(1,128)}), f32[32,1,644]{2,1,0:T(1,128)S(1)}, u32[]{:S(2)}, u32[]{:S(2)}) %all-to-all-start.1) | async-done | bytes 82464 | tf_op jit(solution)/shard_map/all_to_all | solution.py:328
  31.3 0.1 fusion.57
  31.5 0.1 reshape.1045
  31.6 0.1 reshape.1044
  31.8 0.1 reshape.1050
  31.9 0.1 reshape.1049
  32.0 0.1 pad_maximum_fusion.4
  32.1 0.2 reshape.1075
  32.3 0.2 reshape.1076
  32.5 0.1 pad_maximum_fusion.5
  32.6 0.1 slice_reduce_fusion.1
  32.8 0.1 reshape_reshape_squeeze.6
  32.8 0.2 fusion.6
  33.1 0.4 copy-done.3
  33.5 0.4 multiply_add_fusion
  34.3 0.8 %copy-done.1 = f32[3,8,16,128]{3,2,1,0:T(8,128)S(1)} copy-done((f32[3,8,16,128]{3,2,1,0:T(8,128)S(1)}, f32[3,8,16,128]{3,2,1,0:T(8,128)}, u32[]{:S(2)}) %copy-start.1) | copy-done | bytes 196632
  35.2 0.2 fusion.9
  35.4 0.3 fusion.39
  35.8 0.6 copy.60
  36.4 2.5 %all-to-all-start.2 = ((f32[32,2,128]{2,1,0:T(2,128)}), f32[32,2,128]{2,1,0:T(2,128)S(1)}, u32[]{:S(2)}, u32[]{:S(2)}) async-start(f32[32,2,128]{2,1,0:T(2,128)} %copy.60), calls=%async_computation.2 | async-start | bytes 65536 | tf_op jit(solution)/shard_map/all_to_all | solution.py:281
  39.2 1.2 %fusion.3 = f32[3,8,16,128]{3,2,1,0:T(8,128)} fusion(f32[3,8,16,128]{3,2,1,0:T(8,128)S(1)} %copy-done.1, f32[3,8,2,1,130]{4,3,2,1,0:T(1,128)S(1)} %copy.59, f32[3,8,2,6,130]{4,3,2,1,0:T(8,128)S(1)} %slice.259, f32[3,8,2,1,130]{4,3,2,1,0:T(1,128)S(1)} %copy.58, f32[8,16,128]{2,1,0:T(8,128)S(1)} %broadcast_multiply_fusion, f32[130,128]{1,0:T(8,128)S(1)} %copy-done.6, ...), kind=kOutput, calls=%fused_computation.5 | convolution fusion | flops 76990976 | bytes 858120 | tf_op jit(solution)/shard_map/dot_general | solution.py:392
  40.5 2.9 %shard_map.92 = (f32[3,128,128]{2,1,0:T(8,128)}, f32[2,3,8,128]{3,2,1,0:T(8,128)}, f32[2,1,384]{2,1,0:T(1,128)}) custom-call(f32[3,128,128]{2,1,0:T(8,128)} %bitcast.133, f32[3,128,128]{2,1,0:T(8,128)} %bitcast.127, f32[9,128,128]{2,1,0:T(8,128)} %get-tuple-element.17.grad_ref, f32[6,128,128]{2,1,0:T(8,128)} %constant.397.clone.mats_ref, ...), custom_call_target="tpu_custom_call" | custom-call | tf_op jit(solution)/shard_map/pallas_call | solution.py:413
  43.4 0.7 %copy-done.9 = f32[2,1,384]{2,1,0:T(1,128)S(1)} copy-done((f32[2,1,384]{2,1,0:T(1,128)S(1)}, f32[2,1,384]{2,1,0:T(1,128)}, u32[]{:S(2)}) %copy-start.9) | copy-done | bytes 3096
  44.1 2.1 %all-to-all-done.2 = f32[32,2,128]{2,1,0:T(2,128)S(1)} async-done(((f32[32,2,128]{2,1,0:T(2,128)}), f32[32,2,128]{2,1,0:T(2,128)S(1)}, u32[]{:S(2)}, u32[]{:S(2)}) %all-to-all-start.2) | async-done | bytes 32800 | tf_op jit(solution)/shard_map/all_to_all | solution.py:281
  46.3 0.2 fusion.10
  46.6 0.1 fusion.52
  46.7 0.1 reshape_reshape.7
  46.9 0.8 %pad_maximum_fusion.2 = f32[32,1,644]{2,1,0:T(1,128)} fusion(f32[32,1,384]{2,1,0:T(1,128)S(1)} %constant_dynamic-update-slice_fusion, f32[32,1,260]{2,1,0:T(1,128)S(1)} %reshape_reshape.7), kind=kLoop, calls=%fused_computation.35 | loop fusion | flops 20608 | bytes 164864 | tf_op jit(solution)/shard_map/concatenate | solution.py:327
  47.7 3.7 %all-to-all-start.3 = ((f32[32,1,644]{2,1,0:T(1,128)}), f32[32,1,644]{2,1,0:T(1,128)S(1)}, u32[]{:S(2)}, u32[]{:S(2)}) async-start(f32[32,1,644]{2,1,0:T(1,128)} %pad_maximum_fusion.2), calls=%async_computation.3 | async-start | bytes 196608 | tf_op jit(solution)/shard_map/all_to_all | solution.py:328
  51.4 0.3 collective-permute-start.2
  51.7 3.3 %collective-permute-start.3 = (f32[3,8,1,128]{3,1,0,2:T(8,128)S(1)}, f32[3,8,1,128]{3,1,0,2:T(8,128)S(1)}, u32[]{:S(2)}, u32[]{:S(2)}) collective-permute-start(f32[3,8,1,128]{3,1,0,2:T(8,128)S(1)} %get-tuple-element.48), channel_id=1, source_target_pairs={{4,0},{8,4},{12,8},{16,12},{20,16},{24,20},{28,24},{0,28},{5,1},{9... | collective-permute-start | bytes 36872 | tf_op jit(solution)/shard_map/ppermute | solution.py:312
  55.0 4.5 %all-to-all-done.3 = f32[32,1,644]{2,1,0:T(1,128)S(1)} async-done(((f32[32,1,644]{2,1,0:T(1,128)}), f32[32,1,644]{2,1,0:T(1,128)S(1)}, u32[]{:S(2)}, u32[]{:S(2)}) %all-to-all-start.3) | async-done | bytes 82464 | tf_op jit(solution)/shard_map/all_to_all | solution.py:328
  59.5 0.1 fusion.63
  59.6 0.1 reshape.1063
  59.8 0.1 reshape.1062
  59.9 0.1 slice_reduce_fusion
  60.1 0.2 fusion.5
  60.4 0.1 reshape.1068
  60.5 0.1 reshape.1067
  60.5 0.1 pad_maximum_fusion.6
  60.7 0.2 reshape.1077
  60.9 0.2 reshape.1078
  61.1 0.1 pad_maximum_fusion.7
  61.2 0.6 copy-done.2
  61.8 0.4 maximum_add_fusion
  62.7 0.7 %copy-done.4 = f32[3,8,16,128]{3,2,1,0:T(8,128)S(1)} copy-done((f32[3,8,16,128]{3,2,1,0:T(8,128)S(1)}, f32[3,8,16,128]{3,2,1,0:T(8,128)}, u32[]{:S(2)}) %copy-start.4) | copy-done | bytes 196632
  63.4 1.2 %fusion.4 = f32[3,8,16,128]{3,2,1,0:T(8,128)} fusion(f32[3,8,2,1,130]{4,3,2,1,0:T(1,128)S(1)} %copy.75, f32[3,8,2,6,130]{4,3,2,1,0:T(8,128)S(1)} %slice.286, f32[3,8,2,1,130]{4,3,2,1,0:T(1,128)S(1)} %copy.74, f32[3,8,16,128]{3,2,1,0:T(8,128)S(1)} %copy-done.1, f32[3,8,16,128]{3,2,1,0:T(8,128)S(1)} %copy-done.4, ...), kind=kOutput, calls=%fused_computation.6 | convolution fusion | flops 77089280 | bytes 1054728 | tf_op jit(solution)/shard_map/dot_general | solution.py:392
  (101 shorter events, 2.5 us)
Async XLA Ops:
  0.0 19.4 %copy-start = (bf16[1,512,512]{2,1,0:T(8,128)(2,1)S(1)}, bf16[1,512,512]{2,1,0:T(8,128)(2,1)}, u32[]{:S(2)}) copy-start(bf16[1,512,512]{2,1,0:T(8,128)(2,1)} %param.11) | copy-start | bytes 1572868
  0.0 0.7 %copy-start.12 = (s32[32]{0:T(128)S(1)}, s32[32]{0:T(128)}, u32[]{:S(2)}) copy-start(s32[32]{0:T(128)} %param.12) | copy-start | bytes 388
  4.8 7.3 %copy-start.11 = (f32[2,3,8,128]{3,2,1,0:T(8,128)S(1)}, f32[2,3,8,128]{3,2,1,0:T(8,128)}, u32[]{:S(2)}) copy-start(f32[2,3,8,128]{3,2,1,0:T(8,128)} %get-tuple-element.15) | copy-start | bytes 73732
  4.8 14.6 %all-to-all-start = ((f32[32,2,128]{2,1,0:T(2,128)}), f32[32,2,128]{2,1,0:T(2,128)S(1)}, u32[]{:S(2)}, u32[]{:S(2)}) async-start(f32[32,2,128]{2,1,0:T(2,128)} %bitcast.137), calls=%async_computation | async-start | bytes 65536 | tf_op jit(solution)/shard_map/all_to_all | solution.py:281
  12.1 19.8 %collective-permute-start = (f32[3,8,1,128]{3,1,0,2:T(8,128)S(1)}, f32[3,8,1,128]{3,1,0,2:T(8,128)S(1)}, u32[]{:S(2)}, u32[]{:S(2)}) collective-permute-start(f32[3,8,1,128]{3,1,0,2:T(8,128)S(1)} %get-tuple-element.51), channel_id=1, source_target_pairs={{0,4},{4,8},{8,12},{12,16},{16,20},{20,24},{24,28},{28,0},{1,5},{5... | collective-permute-start | bytes 36872 | tf_op jit(solution)/shard_map/ppermute | solution.py:311
  12.4 20.1 %collective-permute-start.1 = (f32[3,8,1,128]{3,1,0,2:T(8,128)S(1)}, f32[3,8,1,128]{3,1,0,2:T(8,128)S(1)}, u32[]{:S(2)}, u32[]{:S(2)}) collective-permute-start(f32[3,8,1,128]{3,1,0,2:T(8,128)S(1)} %get-tuple-element.52), channel_id=1, source_target_pairs={{4,0},{8,4},{12,8},{16,12},{20,16},{24,20},{28,24},{0,28},{5,1},{9... | collective-permute-start | bytes 36872 | tf_op jit(solution)/shard_map/ppermute | solution.py:312
  15.9 0.7 %copy-start.8 = (f32[2,1,384]{2,1,0:T(1,128)S(1)}, f32[2,1,384]{2,1,0:T(1,128)}, u32[]{:S(2)}) copy-start(f32[2,1,384]{2,1,0:T(1,128)} %get-tuple-element.14) | copy-start | bytes 9220
  20.8 10.5 %all-to-all-start.1 = ((f32[32,1,644]{2,1,0:T(1,128)}), f32[32,1,644]{2,1,0:T(1,128)S(1)}, u32[]{:S(2)}, u32[]{:S(2)}) async-start(f32[32,1,644]{2,1,0:T(1,128)} %pad_maximum_fusion.1), calls=%async_computation.1 | async-start | bytes 196608 | tf_op jit(solution)/shard_map/all_to_all | solution.py:328
  32.6 0.9 %copy-start.3 = (f32[3,128,128]{2,1,0:T(8,128)S(1)}, f32[3,128,128]{2,1,0:T(8,128)}, u32[]{:S(2)}) copy-start(f32[3,128,128]{2,1,0:T(8,128)} %get-tuple-element.16) | copy-start | bytes 589828
  34.2 0.9 %copy-start.1 = (f32[3,8,16,128]{3,2,1,0:T(8,128)S(1)}, f32[3,8,16,128]{3,2,1,0:T(8,128)}, u32[]{:S(2)}) copy-start(f32[3,8,16,128]{3,2,1,0:T(8,128)} %param.9) | copy-start | bytes 589828
  34.2 1.0 %copy-start.5 = (f32[130,128]{1,0:T(8,128)S(1)}, f32[130,128]{1,0:T(8,128)}, u32[]{:S(2)}) copy-start(f32[130,128]{1,0:T(8,128)} %constant.398.clone) | copy-start | bytes 199684
  34.2 1.0 %copy-start.6 = (f32[130,128]{1,0:T(8,128)S(1)}, f32[130,128]{1,0:T(8,128)}, u32[]{:S(2)}) copy-start(f32[130,128]{1,0:T(8,128)} %constant.399.clone) | copy-start | bytes 199684
  34.2 1.0 %copy-start.7 = (f32[130,128]{1,0:T(8,128)S(1)}, f32[130,128]{1,0:T(8,128)}, u32[]{:S(2)}) copy-start(f32[130,128]{1,0:T(8,128)} %constant.400.clone) | copy-start | bytes 199684
  36.4 9.9 %all-to-all-start.2 = ((f32[32,2,128]{2,1,0:T(2,128)}), f32[32,2,128]{2,1,0:T(2,128)S(1)}, u32[]{:S(2)}, u32[]{:S(2)}) async-start(f32[32,2,128]{2,1,0:T(2,128)} %copy.60), calls=%async_computation.2 | async-start | bytes 65536 | tf_op jit(solution)/shard_map/all_to_all | solution.py:281
  43.4 0.7 %copy-start.9 = (f32[2,1,384]{2,1,0:T(1,128)S(1)}, f32[2,1,384]{2,1,0:T(1,128)}, u32[]{:S(2)}) copy-start(f32[2,1,384]{2,1,0:T(1,128)} %get-tuple-element.18) | copy-start | bytes 9220
  47.7 3.7 %copy-start.10 = (f32[2,3,8,128]{3,2,1,0:T(8,128)S(1)}, f32[2,3,8,128]{3,2,1,0:T(8,128)}, u32[]{:S(2)}) copy-start(f32[2,3,8,128]{3,2,1,0:T(8,128)} %get-tuple-element.19) | copy-start | bytes 73732
  47.7 11.8 %all-to-all-start.3 = ((f32[32,1,644]{2,1,0:T(1,128)}), f32[32,1,644]{2,1,0:T(1,128)S(1)}, u32[]{:S(2)}, u32[]{:S(2)}) async-start(f32[32,1,644]{2,1,0:T(1,128)} %pad_maximum_fusion.2), calls=%async_computation.3 | async-start | bytes 196608 | tf_op jit(solution)/shard_map/all_to_all | solution.py:328
  51.4 9.1 %collective-permute-start.2 = (f32[3,8,1,128]{3,1,0,2:T(8,128)S(1)}, f32[3,8,1,128]{3,1,0,2:T(8,128)S(1)}, u32[]{:S(2)}, u32[]{:S(2)}) collective-permute-start(f32[3,8,1,128]{3,1,0,2:T(8,128)S(1)} %get-tuple-element.47), channel_id=1, source_target_pairs={{0,4},{4,8},{8,12},{12,16},{16,20},{20,24},{24,28},{28,0},{1,5},{5... | collective-permute-start | bytes 36872 | tf_op jit(solution)/shard_map/ppermute | solution.py:311
  51.7 9.4 %collective-permute-start.3 = (f32[3,8,1,128]{3,1,0,2:T(8,128)S(1)}, f32[3,8,1,128]{3,1,0,2:T(8,128)S(1)}, u32[]{:S(2)}, u32[]{:S(2)}) collective-permute-start(f32[3,8,1,128]{3,1,0,2:T(8,128)S(1)} %get-tuple-element.48), channel_id=1, source_target_pairs={{4,0},{8,4},{12,8},{16,12},{20,16},{24,20},{28,24},{0,28},{5,1},{9... | collective-permute-start | bytes 36872 | tf_op jit(solution)/shard_map/ppermute | solution.py:312
  60.9 0.9 %copy-start.2 = (f32[3,128,128]{2,1,0:T(8,128)S(1)}, f32[3,128,128]{2,1,0:T(8,128)}, u32[]{:S(2)}) copy-start(f32[3,128,128]{2,1,0:T(8,128)} %get-tuple-element.20) | copy-start | bytes 589828
  62.5 0.9 %copy-start.4 = (f32[3,8,16,128]{3,2,1,0:T(8,128)S(1)}, f32[3,8,16,128]{3,2,1,0:T(8,128)}, u32[]{:S(2)}) copy-start(f32[3,8,16,128]{3,2,1,0:T(8,128)} %fusion.3) | copy-start | bytes 589828

commit v21 on v20

--- a/solution.py
+++ b/solution.py
@@ -296,7 +296,7 @@
     def flux_of(returned):
         angle = phases_at(wave_of_slot, rows_ext // P_SIZE, table_at(points, rows_ext), span)
         synth = jnp.stack([jnp.cos(angle).T, jnp.sin(angle).T], axis=2).reshape(na_dev + 2, -1)
-        flux = -jnp.dot(synth, returned.reshape(-1, nb_dev + 2), precision=highest)
+        flux = -jnp.dot(synth, returned.reshape(-1, nb_dev + 2), precision=lax.Precision.HIGH)
         return surface_ext * flux
 
     mapped_len = 2 * (nb_dev + 2)
@@ -389,7 +389,7 @@
         along_a = assemble_dim(
             padded[..., 1:-1, :], last - 1, padded[..., 0:1, :], padded[..., -1:, :]
         )
-        return jnp.dot(along_a, join_b, precision=highest)
+        return jnp.dot(along_a, join_b, precision=lax.Precision.HIGH)
 
     shapes = (
         jax.ShapeDtypeStruct((3, rows, nb_dev), jnp.float32),
@@ -413,7 +413,7 @@
             stacked, edge_rows, edge_cols = pl.pallas_call(volume_kernel, out_shape=shapes)(
                 parts.reshape(3, rows, nb_dev), flat_flow, grads, mats, flat_mass
             )
-            partial = jnp.dot(analysis, surface, precision=highest)
+            partial = jnp.dot(analysis, surface, precision=lax.Precision.HIGH)
         stacked = stacked.reshape(parts.shape)
         sent = owner_map(partial)
         if carried_halo:

time: 65.3 us -> 64.9 us (level)
  transfers between devices with their start and end apart: 8 -> 8, of which waited for: 4 -> 4; matrix products, arithmetic and copies ran while one was open for 10% -> 10% of each run, Pallas kernels for 4% -> 5%
where the time goes in v21:
time: 64.9 us; the launch traced here: 64.3 us
  starting transfers between devices  23.2 us (36%)
  waiting for transfers between devices  16.5 us (25%)
  local copies, waits for them, and re-layouts  9.24 us (14%)
  Pallas kernels  6.09 us (9%)
  other arithmetic  5.13 us (8%)
  matrix products  3.51 us (5%)
  between operations  0.67 us (1%)
    all_to_all x2, waiting for transfers between devices, joint_exchange(): received = lax.all_to_all(message, both, 0, 0, tiled=True)  12.3 us
    all_to_all x2, starting transfers between devices, owner_map(): gathered = lax.all_to_all(partial, both, 0, 0, tiled=True)  9.85 us
    ppermute x2, starting transfers between devices, joint_exchange(): from_down = lax.ppermute(a_lo, 'tile', down)  6.59 us
    all_to_all x2, starting transfers between devices, joint_exchange(): received = lax.all_to_all(message, both, 0, 0, tiled=True)  6.12 us
    unnamed x37, local copies, waits for them, and re-layouts  5.13 us
    all_to_all x2, waiting for transfers between devices, owner_map(): gathered = lax.all_to_all(partial, both, 0, 0, tiled=True)  4.16 us
    pallas_call x1, Pallas kernels, local(): pl.pallas_call(first_volume_kernel, out_shape=shapes + (jax.ShapeDtypeStr...  3.19 us
    pallas_call x1, Pallas kernels, tendency(): pl.pallas_call(volume_kernel, out_shape=shapes)  2.9 us
  transfers between devices with their start and end apart: 8, of which 4 were waited for; matrix products, arithmetic and copies ran while one was open for 10% of the time, Pallas kernels for 5%

profile of v21, /device:TPU:0, one launch (start us, length us, event | category | flops | bytes accessed | tf_op | source)
XLA Modules:
  0.0 64.3 jit_solution(1160913611696321083)
XLA Ops:
  0.1 0.7 %copy-done.12 = s32[32]{0:T(128)S(1)} copy-done((s32[32]{0:T(128)S(1)}, s32[32]{0:T(128)}, u32[]{:S(2)}) %copy-start.12) | copy-done | bytes 152
  0.7 0.1 fusion.47
  0.9 0.1 copy.45
  1.0 0.6 broadcast_multiply_fusion.1.table_ref
  1.6 3.2 %shard_map.91 = (f32[3,128,128]{2,1,0:T(8,128)}, f32[2,3,8,128]{3,2,1,0:T(8,128)}, f32[2,1,384]{2,1,0:T(1,128)}, f32[64,128]{1,0:T(8,128)}, f32[9,128,128]{2,1,0:T(8,128)}) custom-call(f32[3,128,128]{2,1,0:T(8,128)} %bitcast.130, f32[3,128,128]{2,1,0:T(8,128)} %bitcast.126, f32[6,128,128]{2,1,0:T(8,128)} %constant.397.clone.mats_ref, ...), custom_call_target="tpu_custom_call" | custom-call | tf_op jit(solution)/shard_map/pallas_call | solution.py:399
  4.8 7.3 %all-to-all-start = ((f32[32,2,128]{2,1,0:T(2,128)}), f32[32,2,128]{2,1,0:T(2,128)S(1)}, u32[]{:S(2)}, u32[]{:S(2)}) async-start(f32[32,2,128]{2,1,0:T(2,128)} %bitcast.137), calls=%async_computation | async-start | bytes 65536 | tf_op jit(solution)/shard_map/all_to_all | solution.py:281
  12.1 0.3 collective-permute-start
  12.4 3.3 %collective-permute-start.1 = (f32[3,8,1,128]{3,1,0,2:T(8,128)S(1)}, f32[3,8,1,128]{3,1,0,2:T(8,128)S(1)}, u32[]{:S(2)}, u32[]{:S(2)}) collective-permute-start(f32[3,8,1,128]{3,1,0,2:T(8,128)S(1)} %get-tuple-element.52), channel_id=1, source_target_pairs={{4,0},{8,4},{12,8},{16,12},{20,16},{24,20},{28,24},{0,28},{5,1},{9... | collective-permute-start | bytes 36872 | tf_op jit(solution)/shard_map/ppermute | solution.py:312
  15.9 0.6 copy-done.8
  16.6 0.6 fusion.146
  17.4 0.1 broadcast_multiply_fusion
  17.5 1.9 %all-to-all-done = f32[32,2,128]{2,1,0:T(2,128)S(1)} async-done(((f32[32,2,128]{2,1,0:T(2,128)}), f32[32,2,128]{2,1,0:T(2,128)S(1)}, u32[]{:S(2)}, u32[]{:S(2)}) %all-to-all-start) | async-done | bytes 32800 | tf_op jit(solution)/shard_map/all_to_all | solution.py:281
  19.4 0.2 fusion.12
  19.7 0.1 fusion.54
  19.9 0.1 reshape_reshape.6
  20.0 0.8 %pad_maximum_fusion.1 = f32[32,1,644]{2,1,0:T(1,128)} fusion(f32[32,1,384]{2,1,0:T(1,128)S(1)} %constant_dynamic-update-slice_fusion.6, f32[32,1,260]{2,1,0:T(1,128)S(1)} %reshape_reshape.6), kind=kLoop, calls=%fused_computation.34 | loop fusion | flops 20608 | bytes 164864 | tf_op jit(solution)/shard_map/concatenate | solution.py:327
  20.8 2.6 %all-to-all-start.1 = ((f32[32,1,644]{2,1,0:T(1,128)}), f32[32,1,644]{2,1,0:T(1,128)S(1)}, u32[]{:S(2)}, u32[]{:S(2)}) async-start(f32[32,1,644]{2,1,0:T(1,128)} %pad_maximum_fusion.1), calls=%async_computation.1 | async-start | bytes 196608 | tf_op jit(solution)/shard_map/all_to_all | solution.py:328
  23.5 7.9 %all-to-all-done.1 = f32[32,1,644]{2,1,0:T(1,128)S(1)} async-done(((f32[32,1,644]{2,1,0:T(1,128)}), f32[32,1,644]{2,1,0:T(1,128)S(1)}, u32[]{:S(2)}, u32[]{:S(2)}) %all-to-all-start.1) | async-done | bytes 82464 | tf_op jit(solution)/shard_map/all_to_all | solution.py:328
  31.3 0.1 fusion.57
  31.5 0.1 reshape.1045
  31.6 0.1 reshape.1044
  31.8 0.1 reshape.1050
  31.9 0.1 reshape.1049
  32.0 0.1 pad_maximum_fusion.4
  32.1 0.2 reshape.1075
  32.3 0.2 reshape.1076
  32.5 0.1 pad_maximum_fusion.5
  32.6 0.1 slice_reduce_fusion.1
  32.8 0.2 fusion.6
  33.1 0.5 copy-done.3
  33.5 0.4 multiply_add_fusion
  34.3 0.8 %copy-done.1 = f32[3,8,16,128]{3,2,1,0:T(8,128)S(1)} copy-done((f32[3,8,16,128]{3,2,1,0:T(8,128)S(1)}, f32[3,8,16,128]{3,2,1,0:T(8,128)}, u32[]{:S(2)}) %copy-start.1) | copy-done | bytes 196632
  35.2 0.1 fusion.9
  35.4 0.3 fusion.39
  35.7 0.6 copy.60
  36.3 2.5 %all-to-all-start.2 = ((f32[32,2,128]{2,1,0:T(2,128)}), f32[32,2,128]{2,1,0:T(2,128)S(1)}, u32[]{:S(2)}, u32[]{:S(2)}) async-start(f32[32,2,128]{2,1,0:T(2,128)} %copy.60), calls=%async_computation.2 | async-start | bytes 65536 | tf_op jit(solution)/shard_map/all_to_all | solution.py:281
  39.2 1.1 %fusion.3 = f32[3,8,16,128]{3,2,1,0:T(8,128)} fusion(f32[3,8,16,128]{3,2,1,0:T(8,128)S(1)} %copy-done.1, f32[3,8,2,1,130]{4,3,2,1,0:T(1,128)S(1)} %copy.59, f32[3,8,2,6,130]{4,3,2,1,0:T(8,128)S(1)} %slice.259, f32[3,8,2,1,130]{4,3,2,1,0:T(1,128)S(1)} %copy.58, f32[8,16,128]{2,1,0:T(8,128)S(1)} %broadcast_multiply_fusion, f32[130,128]{1,0:T(8,128)S(1)} %copy-done.6, ...), kind=kOutput, calls=%fused_computation.5 | convolution fusion | flops 38652416 | bytes 858120 | tf_op jit(solution)/shard_map/dot_general | solution.py:392
  40.3 2.9 %shard_map.92 = (f32[3,128,128]{2,1,0:T(8,128)}, f32[2,3,8,128]{3,2,1,0:T(8,128)}, f32[2,1,384]{2,1,0:T(1,128)}) custom-call(f32[3,128,128]{2,1,0:T(8,128)} %bitcast.133, f32[3,128,128]{2,1,0:T(8,128)} %bitcast.127, f32[9,128,128]{2,1,0:T(8,128)} %get-tuple-element.17.grad_ref, f32[6,128,128]{2,1,0:T(8,128)} %constant.397.clone.mats_ref, ...), custom_call_target="tpu_custom_call" | custom-call | tf_op jit(solution)/shard_map/pallas_call | solution.py:413
  43.2 0.7 %copy-done.9 = f32[2,1,384]{2,1,0:T(1,128)S(1)} copy-done((f32[2,1,384]{2,1,0:T(1,128)S(1)}, f32[2,1,384]{2,1,0:T(1,128)}, u32[]{:S(2)}) %copy-start.9) | copy-done | bytes 3096
  43.9 2.3 %all-to-all-done.2 = f32[32,2,128]{2,1,0:T(2,128)S(1)} async-done(((f32[32,2,128]{2,1,0:T(2,128)}), f32[32,2,128]{2,1,0:T(2,128)S(1)}, u32[]{:S(2)}, u32[]{:S(2)}) %all-to-all-start.2) | async-done | bytes 32800 | tf_op jit(solution)/shard_map/all_to_all | solution.py:281
  46.2 0.2 fusion.10
  46.5 0.1 fusion.52
  46.7 0.1 reshape_reshape.7
  46.8 0.8 %pad_maximum_fusion.2 = f32[32,1,644]{2,1,0:T(1,128)} fusion(f32[32,1,384]{2,1,0:T(1,128)S(1)} %constant_dynamic-update-slice_fusion, f32[32,1,260]{2,1,0:T(1,128)S(1)} %reshape_reshape.7), kind=kLoop, calls=%fused_computation.35 | loop fusion | flops 20608 | bytes 164864 | tf_op jit(solution)/shard_map/concatenate | solution.py:327
  47.7 3.6 %all-to-all-start.3 = ((f32[32,1,644]{2,1,0:T(1,128)}), f32[32,1,644]{2,1,0:T(1,128)S(1)}, u32[]{:S(2)}, u32[]{:S(2)}) async-start(f32[32,1,644]{2,1,0:T(1,128)} %pad_maximum_fusion.2), calls=%async_computation.3 | async-start | bytes 196608 | tf_op jit(solution)/shard_map/all_to_all | solution.py:328
  51.2 0.3 collective-permute-start.2
  51.5 3.3 %collective-permute-start.3 = (f32[3,8,1,128]{3,1,0,2:T(8,128)S(1)}, f32[3,8,1,128]{3,1,0,2:T(8,128)S(1)}, u32[]{:S(2)}, u32[]{:S(2)}) collective-permute-start(f32[3,8,1,128]{3,1,0,2:T(8,128)S(1)} %get-tuple-element.48), channel_id=1, source_target_pairs={{4,0},{8,4},{12,8},{16,12},{20,16},{24,20},{28,24},{0,28},{5,1},{9... | collective-permute-start | bytes 36872 | tf_op jit(solution)/shard_map/ppermute | solution.py:312
  54.8 4.5 %all-to-all-done.3 = f32[32,1,644]{2,1,0:T(1,128)S(1)} async-done(((f32[32,1,644]{2,1,0:T(1,128)}), f32[32,1,644]{2,1,0:T(1,128)S(1)}, u32[]{:S(2)}, u32[]{:S(2)}) %all-to-all-start.3) | async-done | bytes 82464 | tf_op jit(solution)/shard_map/all_to_all | solution.py:328
  59.3 0.1 fusion.63
  59.4 0.1 reshape.1063
  59.6 0.1 reshape.1062
  59.7 0.1 slice_reduce_fusion
  59.9 0.1 reshape_reshape_squeeze.7
  59.9 0.2 fusion.5
  60.2 0.1 reshape.1068
  60.2 0.1 reshape.1067
  60.3 0.1 pad_maximum_fusion.6
  60.4 0.2 reshape.1077
  60.7 0.2 reshape.1078
  60.9 0.1 pad_maximum_fusion.7
  61.0 0.6 copy-done.2
  61.6 0.4 maximum_add_fusion
  62.5 0.7 %copy-done.4 = f32[3,8,16,128]{3,2,1,0:T(8,128)S(1)} copy-done((f32[3,8,16,128]{3,2,1,0:T(8,128)S(1)}, f32[3,8,16,128]{3,2,1,0:T(8,128)}, u32[]{:S(2)}) %copy-start.4) | copy-done | bytes 196632
  63.2 1.1 %fusion.4 = f32[3,8,16,128]{3,2,1,0:T(8,128)} fusion(f32[3,8,2,1,130]{4,3,2,1,0:T(1,128)S(1)} %copy.75, f32[3,8,2,6,130]{4,3,2,1,0:T(8,128)S(1)} %slice.286, f32[3,8,2,1,130]{4,3,2,1,0:T(1,128)S(1)} %copy.74, f32[3,8,16,128]{3,2,1,0:T(8,128)S(1)} %copy-done.1, f32[3,8,16,128]{3,2,1,0:T(8,128)S(1)} %copy-done.4, ...), kind=kOutput, calls=%fused_computation.6 | convolution fusion | flops 38750720 | bytes 1054728 | tf_op jit(solution)/shard_map/dot_general | solution.py:392
  (101 shorter events, 2.5 us)
Async XLA Ops:
  0.0 19.4 %copy-start = (bf16[1,512,512]{2,1,0:T(8,128)(2,1)S(1)}, bf16[1,512,512]{2,1,0:T(8,128)(2,1)}, u32[]{:S(2)}) copy-start(bf16[1,512,512]{2,1,0:T(8,128)(2,1)} %param.11) | copy-start | bytes 1572868
  0.0 0.7 %copy-start.12 = (s32[32]{0:T(128)S(1)}, s32[32]{0:T(128)}, u32[]{:S(2)}) copy-start(s32[32]{0:T(128)} %param.12) | copy-start | bytes 388
  4.8 7.3 %copy-start.11 = (f32[2,3,8,128]{3,2,1,0:T(8,128)S(1)}, f32[2,3,8,128]{3,2,1,0:T(8,128)}, u32[]{:S(2)}) copy-start(f32[2,3,8,128]{3,2,1,0:T(8,128)} %get-tuple-element.15) | copy-start | bytes 73732
  4.8 14.6 %all-to-all-start = ((f32[32,2,128]{2,1,0:T(2,128)}), f32[32,2,128]{2,1,0:T(2,128)S(1)}, u32[]{:S(2)}, u32[]{:S(2)}) async-start(f32[32,2,128]{2,1,0:T(2,128)} %bitcast.137), calls=%async_computation | async-start | bytes 65536 | tf_op jit(solution)/shard_map/all_to_all | solution.py:281
  12.1 19.8 %collective-permute-start = (f32[3,8,1,128]{3,1,0,2:T(8,128)S(1)}, f32[3,8,1,128]{3,1,0,2:T(8,128)S(1)}, u32[]{:S(2)}, u32[]{:S(2)}) collective-permute-start(f32[3,8,1,128]{3,1,0,2:T(8,128)S(1)} %get-tuple-element.51), channel_id=1, source_target_pairs={{0,4},{4,8},{8,12},{12,16},{16,20},{20,24},{24,28},{28,0},{1,5},{5... | collective-permute-start | bytes 36872 | tf_op jit(solution)/shard_map/ppermute | solution.py:311
  12.4 20.1 %collective-permute-start.1 = (f32[3,8,1,128]{3,1,0,2:T(8,128)S(1)}, f32[3,8,1,128]{3,1,0,2:T(8,128)S(1)}, u32[]{:S(2)}, u32[]{:S(2)}) collective-permute-start(f32[3,8,1,128]{3,1,0,2:T(8,128)S(1)} %get-tuple-element.52), channel_id=1, source_target_pairs={{4,0},{8,4},{12,8},{16,12},{20,16},{24,20},{28,24},{0,28},{5,1},{9... | collective-permute-start | bytes 36872 | tf_op jit(solution)/shard_map/ppermute | solution.py:312
  15.9 0.7 %copy-start.8 = (f32[2,1,384]{2,1,0:T(1,128)S(1)}, f32[2,1,384]{2,1,0:T(1,128)}, u32[]{:S(2)}) copy-start(f32[2,1,384]{2,1,0:T(1,128)} %get-tuple-element.14) | copy-start | bytes 9220
  20.8 10.5 %all-to-all-start.1 = ((f32[32,1,644]{2,1,0:T(1,128)}), f32[32,1,644]{2,1,0:T(1,128)S(1)}, u32[]{:S(2)}, u32[]{:S(2)}) async-start(f32[32,1,644]{2,1,0:T(1,128)} %pad_maximum_fusion.1), calls=%async_computation.1 | async-start | bytes 196608 | tf_op jit(solution)/shard_map/all_to_all | solution.py:328
  32.6 0.9 %copy-start.3 = (f32[3,128,128]{2,1,0:T(8,128)S(1)}, f32[3,128,128]{2,1,0:T(8,128)}, u32[]{:S(2)}) copy-start(f32[3,128,128]{2,1,0:T(8,128)} %get-tuple-element.16) | copy-start | bytes 589828
  34.2 0.9 %copy-start.1 = (f32[3,8,16,128]{3,2,1,0:T(8,128)S(1)}, f32[3,8,16,128]{3,2,1,0:T(8,128)}, u32[]{:S(2)}) copy-start(f32[3,8,16,128]{3,2,1,0:T(8,128)} %param.9) | copy-start | bytes 589828
  34.2 1.0 %copy-start.5 = (f32[130,128]{1,0:T(8,128)S(1)}, f32[130,128]{1,0:T(8,128)}, u32[]{:S(2)}) copy-start(f32[130,128]{1,0:T(8,128)} %constant.398.clone) | copy-start | bytes 199684
  34.2 1.0 %copy-start.6 = (f32[130,128]{1,0:T(8,128)S(1)}, f32[130,128]{1,0:T(8,128)}, u32[]{:S(2)}) copy-start(f32[130,128]{1,0:T(8,128)} %constant.399.clone) | copy-start | bytes 199684
  34.2 1.0 %copy-start.7 = (f32[130,128]{1,0:T(8,128)S(1)}, f32[130,128]{1,0:T(8,128)}, u32[]{:S(2)}) copy-start(f32[130,128]{1,0:T(8,128)} %constant.400.clone) | copy-start | bytes 199684
  36.3 9.9 %all-to-all-start.2 = ((f32[32,2,128]{2,1,0:T(2,128)}), f32[32,2,128]{2,1,0:T(2,128)S(1)}, u32[]{:S(2)}, u32[]{:S(2)}) async-start(f32[32,2,128]{2,1,0:T(2,128)} %copy.60), calls=%async_computation.2 | async-start | bytes 65536 | tf_op jit(solution)/shard_map/all_to_all | solution.py:281
  43.2 0.7 %copy-start.9 = (f32[2,1,384]{2,1,0:T(1,128)S(1)}, f32[2,1,384]{2,1,0:T(1,128)}, u32[]{:S(2)}) copy-start(f32[2,1,384]{2,1,0:T(1,128)} %get-tuple-element.18) | copy-start | bytes 9220
  47.6 3.6 %copy-start.10 = (f32[2,3,8,128]{3,2,1,0:T(8,128)S(1)}, f32[2,3,8,128]{3,2,1,0:T(8,128)}, u32[]{:S(2)}) copy-start(f32[2,3,8,128]{3,2,1,0:T(8,128)} %get-tuple-element.19) | copy-start | bytes 73732
  47.7 11.6 %all-to-all-start.3 = ((f32[32,1,644]{2,1,0:T(1,128)}), f32[32,1,644]{2,1,0:T(1,128)S(1)}, u32[]{:S(2)}, u32[]{:S(2)}) async-start(f32[32,1,644]{2,1,0:T(1,128)} %pad_maximum_fusion.2), calls=%async_computation.3 | async-start | bytes 196608 | tf_op jit(solution)/shard_map/all_to_all | solution.py:328
  51.2 9.1 %collective-permute-start.2 = (f32[3,8,1,128]{3,1,0,2:T(8,128)S(1)}, f32[3,8,1,128]{3,1,0,2:T(8,128)S(1)}, u32[]{:S(2)}, u32[]{:S(2)}) collective-permute-start(f32[3,8,1,128]{3,1,0,2:T(8,128)S(1)} %get-tuple-element.47), channel_id=1, source_target_pairs={{0,4},{4,8},{8,12},{12,16},{16,20},{20,24},{24,28},{28,0},{1,5},{5... | collective-permute-start | bytes 36872 | tf_op jit(solution)/shard_map/ppermute | solution.py:311
  51.5 9.3 %collective-permute-start.3 = (f32[3,8,1,128]{3,1,0,2:T(8,128)S(1)}, f32[3,8,1,128]{3,1,0,2:T(8,128)S(1)}, u32[]{:S(2)}, u32[]{:S(2)}) collective-permute-start(f32[3,8,1,128]{3,1,0,2:T(8,128)S(1)} %get-tuple-element.48), channel_id=1, source_target_pairs={{4,0},{8,4},{12,8},{16,12},{20,16},{24,20},{28,24},{0,28},{5,1},{9... | collective-permute-start | bytes 36872 | tf_op jit(solution)/shard_map/ppermute | solution.py:312
  60.7 0.9 %copy-start.2 = (f32[3,128,128]{2,1,0:T(8,128)S(1)}, f32[3,128,128]{2,1,0:T(8,128)}, u32[]{:S(2)}) copy-start(f32[3,128,128]{2,1,0:T(8,128)} %get-tuple-element.20) | copy-start | bytes 589828
  62.3 0.9 %copy-start.4 = (f32[3,8,16,128]{3,2,1,0:T(8,128)S(1)}, f32[3,8,16,128]{3,2,1,0:T(8,128)}, u32[]{:S(2)}) copy-start(f32[3,8,16,128]{3,2,1,0:T(8,128)} %fusion.3) | copy-start | bytes 589828

commit v22 on v21

--- a/solution.py
+++ b/solution.py
@@ -52,6 +52,10 @@
     depth = outs[0].shape[1] // outs[1].shape[2]
     surface = parts_ref[0, pl.ds(outs[0].shape[1] - depth, depth), :]
     outs[3][...] = product(table_ref[...], surface)
+
+
+def partial_kernel(table_ref, surface_ref, out_ref):
+    out_ref[...] = product(table_ref[...], surface_ref[...])
 
 
 def volume_body(parts_ref, flow_ref, grad_ref, mats_ref, mass_ref, out_ref, rows_ref, cols_ref):
@@ -413,7 +417,10 @@
             stacked, edge_rows, edge_cols = pl.pallas_call(volume_kernel, out_shape=shapes)(
                 parts.reshape(3, rows, nb_dev), flat_flow, grads, mats, flat_mass
             )
-            partial = jnp.dot(analysis, surface, precision=lax.Precision.HIGH)
+            partial = pl.pallas_call(
+                partial_kernel,
+                out_shape=jax.ShapeDtypeStruct(analysis.shape[:1] + (nb_dev,), jnp.float32),
+            )(analysis, surface)
         stacked = stacked.reshape(parts.shape)
         sent = owner_map(partial)
         if carried_halo:

time: 64.9 us -> 66.1 us (1.018)
  Pallas kernels: 6.09 us -> 7.6 us
    pallas_call x0 -> x1, Pallas kernels: none -> 1.51 us  [tendency(): pl.pallas_call(partial_kernel, out_shape=jax.ShapeDtypeStruct(analysis.sh...]
    unnamed x37 -> x36, local copies, waits for them, and re-layouts: 5.13 us -> 5.13 us
  transfers between devices with their start and end apart: 8 -> 8, of which waited for: 4 -> 4; matrix products, arithmetic and copies ran while one was open for 10% -> 10% of each run, Pallas kernels for 5% -> 4%
where the time goes in v22:
time: 66.1 us; the launch traced here: 65.5 us
  starting transfers between devices  23.2 us (35%)
  waiting for transfers between devices  16.5 us (25%)
  local copies, waits for them, and re-layouts  8.61 us (13%)
  Pallas kernels  7.6 us (11%)
  other arithmetic  5.13 us (8%)
  matrix products  3.82 us (6%)
    all_to_all x2, waiting for transfers between devices, joint_exchange(): received = lax.all_to_all(message, both, 0, 0, tiled=True)  12.3 us
    all_to_all x2, starting transfers between devices, owner_map(): gathered = lax.all_to_all(partial, both, 0, 0, tiled=True)  9.84 us
    ppermute x2, starting transfers between devices, joint_exchange(): from_down = lax.ppermute(a_lo, 'tile', down)  6.59 us
    all_to_all x2, starting transfers between devices, joint_exchange(): received = lax.all_to_all(message, both, 0, 0, tiled=True)  6.12 us
    unnamed x36, local copies, waits for them, and re-layouts  5.13 us
    all_to_all x2, waiting for transfers between devices, owner_map(): gathered = lax.all_to_all(partial, both, 0, 0, tiled=True)  4.15 us
    pallas_call x1, Pallas kernels, local(): pl.pallas_call(first_volume_kernel, out_shape=shapes + (jax.ShapeDtypeStr...  3.2 us
    dot_general x3, matrix products, assemble_ext(): return jnp.dot(along_a, join_b, precision=lax.Precision.HIGH)  2.95 us
  transfers between devices with their start and end apart: 8, of which 4 were waited for; matrix products, arithmetic and copies ran while one was open for 10% of the time, Pallas kernels for 4%

profile of v22, /device:TPU:0, one launch (start us, length us, event | category | flops | bytes accessed | tf_op | source)
XLA Modules:
  0.0 65.5 jit_solution(8888876149781054904)
XLA Ops:
  0.1 0.7 %copy-done.12 = s32[32]{0:T(128)S(1)} copy-done((s32[32]{0:T(128)S(1)}, s32[32]{0:T(128)}, u32[]{:S(2)}) %copy-start.12) | copy-done | bytes 152
  0.7 0.1 fusion.43
  0.9 0.1 copy.43
  1.0 0.6 broadcast_multiply_fusion.1.table_ref
  1.6 3.2 %shard_map.91 = (f32[3,128,128]{2,1,0:T(8,128)}, f32[2,3,8,128]{3,2,1,0:T(8,128)}, f32[2,1,384]{2,1,0:T(1,128)}, f32[64,128]{1,0:T(8,128)}, f32[9,128,128]{2,1,0:T(8,128)}) custom-call(f32[3,128,128]{2,1,0:T(8,128)} %bitcast.126, f32[3,128,128]{2,1,0:T(8,128)} %bitcast.122, f32[6,128,128]{2,1,0:T(8,128)} %constant.397.clone.mats_ref, ...), custom_call_target="tpu_custom_call" | custom-call | tf_op jit(solution)/shard_map/pallas_call | solution.py:403
  4.8 7.3 %all-to-all-start = ((f32[32,2,128]{2,1,0:T(2,128)}), f32[32,2,128]{2,1,0:T(2,128)S(1)}, u32[]{:S(2)}, u32[]{:S(2)}) async-start(f32[32,2,128]{2,1,0:T(2,128)} %bitcast.134), calls=%async_computation | async-start | bytes 65536 | tf_op jit(solution)/shard_map/all_to_all | solution.py:285
  12.1 0.3 collective-permute-start
  12.4 3.3 %collective-permute-start.1 = (f32[3,8,1,128]{3,1,0,2:T(8,128)S(1)}, f32[3,8,1,128]{3,1,0,2:T(8,128)S(1)}, u32[]{:S(2)}, u32[]{:S(2)}) collective-permute-start(f32[3,8,1,128]{3,1,0,2:T(8,128)S(1)} %get-tuple-element.52), channel_id=1, source_target_pairs={{4,0},{8,4},{12,8},{16,12},{20,16},{24,20},{28,24},{0,28},{5,1},{9... | collective-permute-start | bytes 36872 | tf_op jit(solution)/shard_map/ppermute | solution.py:316
  15.9 0.6 copy-done.8
  16.6 0.6 fusion.141
  17.4 0.1 broadcast_multiply_fusion
  17.5 1.9 %all-to-all-done = f32[32,2,128]{2,1,0:T(2,128)S(1)} async-done(((f32[32,2,128]{2,1,0:T(2,128)}), f32[32,2,128]{2,1,0:T(2,128)S(1)}, u32[]{:S(2)}, u32[]{:S(2)}) %all-to-all-start) | async-done | bytes 32800 | tf_op jit(solution)/shard_map/all_to_all | solution.py:285
  19.4 0.2 fusion.11
  19.7 0.1 fusion.47
  19.9 0.1 reshape_reshape.6
  20.0 0.8 %pad_maximum_fusion.1 = f32[32,1,644]{2,1,0:T(1,128)} fusion(f32[32,1,384]{2,1,0:T(1,128)S(1)} %constant_dynamic-update-slice_fusion.6, f32[32,1,260]{2,1,0:T(1,128)S(1)} %reshape_reshape.6), kind=kLoop, calls=%fused_computation.33 | loop fusion | flops 20608 | bytes 164864 | tf_op jit(solution)/shard_map/concatenate | solution.py:331
  20.8 2.6 %all-to-all-start.1 = ((f32[32,1,644]{2,1,0:T(1,128)}), f32[32,1,644]{2,1,0:T(1,128)S(1)}, u32[]{:S(2)}, u32[]{:S(2)}) async-start(f32[32,1,644]{2,1,0:T(1,128)} %pad_maximum_fusion.1), calls=%async_computation.1 | async-start | bytes 196608 | tf_op jit(solution)/shard_map/all_to_all | solution.py:332
  23.5 7.9 %all-to-all-done.1 = f32[32,1,644]{2,1,0:T(1,128)S(1)} async-done(((f32[32,1,644]{2,1,0:T(1,128)}), f32[32,1,644]{2,1,0:T(1,128)S(1)}, u32[]{:S(2)}, u32[]{:S(2)}) %all-to-all-start.1) | async-done | bytes 82464 | tf_op jit(solution)/shard_map/all_to_all | solution.py:332
  31.3 0.1 fusion.52
  31.5 0.1 reshape.1041
  31.6 0.1 reshape.1040
  31.8 0.1 reshape.1046
  31.8 0.1 reshape.1045
  32.0 0.1 pad_maximum_fusion.4
  32.1 0.2 reshape.1071
  32.3 0.2 reshape.1072
  32.5 0.1 pad_maximum_fusion.5
  32.6 0.1 slice_reduce_fusion.1
  32.8 0.1 reshape_reshape_squeeze.6
  32.8 0.2 fusion.6
  33.0 0.5 copy-done.3
  33.5 0.4 multiply_add_fusion
  34.3 0.8 %copy-done.1 = f32[3,8,16,128]{3,2,1,0:T(8,128)S(1)} copy-done((f32[3,8,16,128]{3,2,1,0:T(8,128)S(1)}, f32[3,8,16,128]{3,2,1,0:T(8,128)}, u32[]{:S(2)}) %copy-start.1) | copy-done | bytes 196632
  35.2 0.8 %fusion.8.surface_ref = f32[16,128]{1,0:T(8,128)} fusion(f32[130,128]{1,0:T(8,128)S(1)} %copy-done.6, f32[130,128]{1,0:T(8,128)S(1)} %copy-done.7, f32[130,128]{1,0:T(8,128)S(1)} %copy-done.5, f32[]{:T(128)S(6)} %convert_element_type.67, f32[]{:T(128)S(6)} %convert_element_type.66, f32[2,1,130]{2,1,0:T(1,128)S(1)} %get-tuple-element.54, ...), kind=kOutput, calls=%fused_computation.13 | convolution fusion | flops 1674304 | bytes 232584 | tf_op jit(solution)/shard_map/dot_general | solution.py:396
  36.0 1.5 %shard_map.92 = f32[64,128]{1,0:T(8,128)} custom-call(f32[64,16]{1,0:T(8,128)} %broadcast_multiply_fusion.1.table_ref, f32[16,128]{1,0:T(8,128)} %fusion.8.surface_ref), custom_call_target="tpu_custom_call" | custom-call | tf_op jit(solution)/shard_map/pallas_call | solution.py:420
  37.5 2.5 %all-to-all-start.2 = ((f32[32,2,128]{2,1,0:T(2,128)}), f32[32,2,128]{2,1,0:T(2,128)S(1)}, u32[]{:S(2)}, u32[]{:S(2)}) async-start(f32[32,2,128]{2,1,0:T(2,128)} %bitcast.132), calls=%async_computation.2 | async-start | bytes 65536 | tf_op jit(solution)/shard_map/all_to_all | solution.py:285
  40.3 1.1 %fusion.3 = f32[3,8,16,128]{3,2,1,0:T(8,128)} fusion(f32[3,8,16,128]{3,2,1,0:T(8,128)S(1)} %copy-done.1, f32[3,8,2,1,130]{4,3,2,1,0:T(1,128)S(1)} %copy.57, f32[3,8,2,6,130]{4,3,2,1,0:T(8,128)S(1)} %slice.259, f32[3,8,2,1,130]{4,3,2,1,0:T(1,128)S(1)} %copy.56, f32[8,16,128]{2,1,0:T(8,128)S(1)} %broadcast_multiply_fusion, f32[130,128]{1,0:T(8,128)S(1)} %copy-done.6, ...), kind=kOutput, calls=%fused_computation.5 | convolution fusion | flops 38652416 | bytes 858120 | tf_op jit(solution)/shard_map/dot_general | solution.py:396
  41.4 2.9 %shard_map.93 = (f32[3,128,128]{2,1,0:T(8,128)}, f32[2,3,8,128]{3,2,1,0:T(8,128)}, f32[2,1,384]{2,1,0:T(1,128)}) custom-call(f32[3,128,128]{2,1,0:T(8,128)} %bitcast.129, f32[3,128,128]{2,1,0:T(8,128)} %bitcast.123, f32[9,128,128]{2,1,0:T(8,128)} %get-tuple-element.17.grad_ref, f32[6,128,128]{2,1,0:T(8,128)} %constant.397.clone.mats_ref, ...), custom_call_target="tpu_custom_call" | custom-call | tf_op jit(solution)/shard_map/pallas_call | solution.py:417
  44.4 0.7 copy-done.9
  45.1 2.3 %all-to-all-done.2 = f32[32,2,128]{2,1,0:T(2,128)S(1)} async-done(((f32[32,2,128]{2,1,0:T(2,128)}), f32[32,2,128]{2,1,0:T(2,128)S(1)}, u32[]{:S(2)}, u32[]{:S(2)}) %all-to-all-start.2) | async-done | bytes 32800 | tf_op jit(solution)/shard_map/all_to_all | solution.py:285
  47.4 0.2 fusion.9
  47.7 0.1 fusion.45
  47.8 0.1 reshape_reshape.7
  48.0 0.8 %pad_maximum_fusion.2 = f32[32,1,644]{2,1,0:T(1,128)} fusion(f32[32,1,384]{2,1,0:T(1,128)S(1)} %constant_dynamic-update-slice_fusion, f32[32,1,260]{2,1,0:T(1,128)S(1)} %reshape_reshape.7), kind=kLoop, calls=%fused_computation.34 | loop fusion | flops 20608 | bytes 164864 | tf_op jit(solution)/shard_map/concatenate | solution.py:331
  48.8 3.6 %all-to-all-start.3 = ((f32[32,1,644]{2,1,0:T(1,128)}), f32[32,1,644]{2,1,0:T(1,128)S(1)}, u32[]{:S(2)}, u32[]{:S(2)}) async-start(f32[32,1,644]{2,1,0:T(1,128)} %pad_maximum_fusion.2), calls=%async_computation.3 | async-start | bytes 196608 | tf_op jit(solution)/shard_map/all_to_all | solution.py:332
  52.4 0.3 collective-permute-start.2
  52.7 3.3 %collective-permute-start.3 = (f32[3,8,1,128]{3,1,0,2:T(8,128)S(1)}, f32[3,8,1,128]{3,1,0,2:T(8,128)S(1)}, u32[]{:S(2)}, u32[]{:S(2)}) collective-permute-start(f32[3,8,1,128]{3,1,0,2:T(8,128)S(1)} %get-tuple-element.48), channel_id=1, source_target_pairs={{4,0},{8,4},{12,8},{16,12},{20,16},{24,20},{28,24},{0,28},{5,1},{9... | collective-permute-start | bytes 36872 | tf_op jit(solution)/shard_map/ppermute | solution.py:316
  56.0 4.5 %all-to-all-done.3 = f32[32,1,644]{2,1,0:T(1,128)S(1)} async-done(((f32[32,1,644]{2,1,0:T(1,128)}), f32[32,1,644]{2,1,0:T(1,128)S(1)}, u32[]{:S(2)}, u32[]{:S(2)}) %all-to-all-start.3) | async-done | bytes 82464 | tf_op jit(solution)/shard_map/all_to_all | solution.py:332
  60.4 0.1 fusion.58
  60.6 0.1 reshape.1060
  60.7 0.1 reshape.1059
  60.9 0.1 slice_reduce_fusion
  61.0 0.1 reshape_reshape_squeeze.7
  61.1 0.2 fusion.5
  61.3 0.1 reshape.1065
  61.4 0.1 reshape.1064
  61.5 0.1 pad_maximum_fusion.6
  61.6 0.2 reshape.1073
  61.8 0.2 reshape.1074
  62.0 0.1 pad_maximum_fusion.7
  62.2 0.6 copy-done.2
  62.7 0.4 maximum_add_fusion
  63.6 0.7 %copy-done.4 = f32[3,8,16,128]{3,2,1,0:T(8,128)S(1)} copy-done((f32[3,8,16,128]{3,2,1,0:T(8,128)S(1)}, f32[3,8,16,128]{3,2,1,0:T(8,128)}, u32[]{:S(2)}) %copy-start.4) | copy-done | bytes 196632
  64.4 1.1 %fusion.4 = f32[3,8,16,128]{3,2,1,0:T(8,128)} fusion(f32[3,8,2,1,130]{4,3,2,1,0:T(1,128)S(1)} %copy.71, f32[3,8,2,6,130]{4,3,2,1,0:T(8,128)S(1)} %slice.286, f32[3,8,2,1,130]{4,3,2,1,0:T(1,128)S(1)} %copy.70, f32[3,8,16,128]{3,2,1,0:T(8,128)S(1)} %copy-done.1, f32[3,8,16,128]{3,2,1,0:T(8,128)S(1)} %copy-done.4, ...), kind=kOutput, calls=%fused_computation.6 | convolution fusion | flops 38750720 | bytes 1054728 | tf_op jit(solution)/shard_map/dot_general | solution.py:396
  (99 shorter events, 2.4 us)
Async XLA Ops:
  0.0 19.4 %copy-start = (bf16[1,512,512]{2,1,0:T(8,128)(2,1)S(1)}, bf16[1,512,512]{2,1,0:T(8,128)(2,1)}, u32[]{:S(2)}) copy-start(bf16[1,512,512]{2,1,0:T(8,128)(2,1)} %param.11) | copy-start | bytes 1572868
  0.0 0.7 %copy-start.12 = (s32[32]{0:T(128)S(1)}, s32[32]{0:T(128)}, u32[]{:S(2)}) copy-start(s32[32]{0:T(128)} %param.12) | copy-start | bytes 388
  4.8 7.3 %copy-start.11 = (f32[2,3,8,128]{3,2,1,0:T(8,128)S(1)}, f32[2,3,8,128]{3,2,1,0:T(8,128)}, u32[]{:S(2)}) copy-start(f32[2,3,8,128]{3,2,1,0:T(8,128)} %get-tuple-element.15) | copy-start | bytes 73732
  4.8 14.6 %all-to-all-start = ((f32[32,2,128]{2,1,0:T(2,128)}), f32[32,2,128]{2,1,0:T(2,128)S(1)}, u32[]{:S(2)}, u32[]{:S(2)}) async-start(f32[32,2,128]{2,1,0:T(2,128)} %bitcast.134), calls=%async_computation | async-start | bytes 65536 | tf_op jit(solution)/shard_map/all_to_all | solution.py:285
  12.1 19.8 %collective-permute-start = (f32[3,8,1,128]{3,1,0,2:T(8,128)S(1)}, f32[3,8,1,128]{3,1,0,2:T(8,128)S(1)}, u32[]{:S(2)}, u32[]{:S(2)}) collective-permute-start(f32[3,8,1,128]{3,1,0,2:T(8,128)S(1)} %get-tuple-element.51), channel_id=1, source_target_pairs={{0,4},{4,8},{8,12},{12,16},{16,20},{20,24},{24,28},{28,0},{1,5},{5... | collective-permute-start | bytes 36872 | tf_op jit(solution)/shard_map/ppermute | solution.py:315
  12.4 20.1 %collective-permute-start.1 = (f32[3,8,1,128]{3,1,0,2:T(8,128)S(1)}, f32[3,8,1,128]{3,1,0,2:T(8,128)S(1)}, u32[]{:S(2)}, u32[]{:S(2)}) collective-permute-start(f32[3,8,1,128]{3,1,0,2:T(8,128)S(1)} %get-tuple-element.52), channel_id=1, source_target_pairs={{4,0},{8,4},{12,8},{16,12},{20,16},{24,20},{28,24},{0,28},{5,1},{9... | collective-permute-start | bytes 36872 | tf_op jit(solution)/shard_map/ppermute | solution.py:316
  15.9 0.7 %copy-start.8 = (f32[2,1,384]{2,1,0:T(1,128)S(1)}, f32[2,1,384]{2,1,0:T(1,128)}, u32[]{:S(2)}) copy-start(f32[2,1,384]{2,1,0:T(1,128)} %get-tuple-element.14) | copy-start | bytes 9220
  20.8 10.5 %all-to-all-start.1 = ((f32[32,1,644]{2,1,0:T(1,128)}), f32[32,1,644]{2,1,0:T(1,128)S(1)}, u32[]{:S(2)}, u32[]{:S(2)}) async-start(f32[32,1,644]{2,1,0:T(1,128)} %pad_maximum_fusion.1), calls=%async_computation.1 | async-start | bytes 196608 | tf_op jit(solution)/shard_map/all_to_all | solution.py:332
  32.6 0.9 %copy-start.3 = (f32[3,128,128]{2,1,0:T(8,128)S(1)}, f32[3,128,128]{2,1,0:T(8,128)}, u32[]{:S(2)}) copy-start(f32[3,128,128]{2,1,0:T(8,128)} %get-tuple-element.16) | copy-start | bytes 589828
  34.2 0.9 %copy-start.1 = (f32[3,8,16,128]{3,2,1,0:T(8,128)S(1)}, f32[3,8,16,128]{3,2,1,0:T(8,128)}, u32[]{:S(2)}) copy-start(f32[3,8,16,128]{3,2,1,0:T(8,128)} %param.9) | copy-start | bytes 589828
  34.2 1.0 %copy-start.5 = (f32[130,128]{1,0:T(8,128)S(1)}, f32[130,128]{1,0:T(8,128)}, u32[]{:S(2)}) copy-start(f32[130,128]{1,0:T(8,128)} %constant.398.clone) | copy-start | bytes 199684
  34.2 1.0 %copy-start.6 = (f32[130,128]{1,0:T(8,128)S(1)}, f32[130,128]{1,0:T(8,128)}, u32[]{:S(2)}) copy-start(f32[130,128]{1,0:T(8,128)} %constant.399.clone) | copy-start | bytes 199684
  34.2 1.0 %copy-start.7 = (f32[130,128]{1,0:T(8,128)S(1)}, f32[130,128]{1,0:T(8,128)}, u32[]{:S(2)}) copy-start(f32[130,128]{1,0:T(8,128)} %constant.400.clone) | copy-start | bytes 199684
  37.5 9.9 %all-to-all-start.2 = ((f32[32,2,128]{2,1,0:T(2,128)}), f32[32,2,128]{2,1,0:T(2,128)S(1)}, u32[]{:S(2)}, u32[]{:S(2)}) async-start(f32[32,2,128]{2,1,0:T(2,128)} %bitcast.132), calls=%async_computation.2 | async-start | bytes 65536 | tf_op jit(solution)/shard_map/all_to_all | solution.py:285
  44.3 0.7 %copy-start.9 = (f32[2,1,384]{2,1,0:T(1,128)S(1)}, f32[2,1,384]{2,1,0:T(1,128)}, u32[]{:S(2)}) copy-start(f32[2,1,384]{2,1,0:T(1,128)} %get-tuple-element.18) | copy-start | bytes 9220
  48.8 3.6 %copy-start.10 = (f32[2,3,8,128]{3,2,1,0:T(8,128)S(1)}, f32[2,3,8,128]{3,2,1,0:T(8,128)}, u32[]{:S(2)}) copy-start(f32[2,3,8,128]{3,2,1,0:T(8,128)} %get-tuple-element.19) | copy-start | bytes 73732
  48.8 11.6 %all-to-all-start.3 = ((f32[32,1,644]{2,1,0:T(1,128)}), f32[32,1,644]{2,1,0:T(1,128)S(1)}, u32[]{:S(2)}, u32[]{:S(2)}) async-start(f32[32,1,644]{2,1,0:T(1,128)} %pad_maximum_fusion.2), calls=%async_computation.3 | async-start | bytes 196608 | tf_op jit(solution)/shard_map/all_to_all | solution.py:332
  52.4 9.1 %collective-permute-start.2 = (f32[3,8,1,128]{3,1,0,2:T(8,128)S(1)}, f32[3,8,1,128]{3,1,0,2:T(8,128)S(1)}, u32[]{:S(2)}, u32[]{:S(2)}) collective-permute-start(f32[3,8,1,128]{3,1,0,2:T(8,128)S(1)} %get-tuple-element.47), channel_id=1, source_target_pairs={{0,4},{4,8},{8,12},{12,16},{16,20},{20,24},{24,28},{28,0},{1,5},{5... | collective-permute-start | bytes 36872 | tf_op jit(solution)/shard_map/ppermute | solution.py:315
  52.7 9.3 %collective-permute-start.3 = (f32[3,8,1,128]{3,1,0,2:T(8,128)S(1)}, f32[3,8,1,128]{3,1,0,2:T(8,128)S(1)}, u32[]{:S(2)}, u32[]{:S(2)}) collective-permute-start(f32[3,8,1,128]{3,1,0,2:T(8,128)S(1)} %get-tuple-element.48), channel_id=1, source_target_pairs={{4,0},{8,4},{12,8},{16,12},{20,16},{24,20},{28,24},{0,28},{5,1},{9... | collective-permute-start | bytes 36872 | tf_op jit(solution)/shard_map/ppermute | solution.py:316
  61.8 0.9 %copy-start.2 = (f32[3,128,128]{2,1,0:T(8,128)S(1)}, f32[3,128,128]{2,1,0:T(8,128)}, u32[]{:S(2)}) copy-start(f32[3,128,128]{2,1,0:T(8,128)} %get-tuple-element.20) | copy-start | bytes 589828
  63.4 0.9 %copy-start.4 = (f32[3,8,16,128]{3,2,1,0:T(8,128)S(1)}, f32[3,8,16,128]{3,2,1,0:T(8,128)}, u32[]{:S(2)}) copy-start(f32[3,8,16,128]{3,2,1,0:T(8,128)} %fusion.3) | copy-start | bytes 589828

commit v23 on v21

--- a/solution.py
+++ b/solution.py
@@ -435,7 +435,8 @@
     section = field + time_step * first_rate
     section_outer = field[0, radial_nodes - 1] + time_step * first_outer
     second_rate, _ = tendency(section, section_outer)
-    return 0.5 * (field + section + time_step * second_rate)
+    settled = lax.optimization_barrier(0.5 * (field + section))
+    return settled + (0.5 * time_step) * second_rate
 
 
 def solution(mesh):

time: 64.9 us -> 64.1 us (0.988)
  local copies, waits for them, and re-layouts: 9.24 us -> 8.52 us
    unnamed x37 -> x35, local copies, waits for them, and re-layouts: 5.13 us -> 4.4 us
where the time goes in v23:
time: 64.1 us; the launch traced here: 63.6 us
  starting transfers between devices  23.2 us (36%)
  waiting for transfers between devices  16.5 us (26%)
  local copies, waits for them, and re-layouts  8.52 us (13%)
  Pallas kernels  6.08 us (9%)
  other arithmetic  5.14 us (8%)
  matrix products  3.51 us (5%)
  between operations  0.66 us (1%)
    all_to_all x2, waiting for transfers between devices, joint_exchange(): received = lax.all_to_all(message, both, 0, 0, tiled=True)  12.3 us
    all_to_all x2, starting transfers between devices, owner_map(): gathered = lax.all_to_all(partial, both, 0, 0, tiled=True)  9.85 us
    ppermute x2, starting transfers between devices, joint_exchange(): from_down = lax.ppermute(a_lo, 'tile', down)  6.59 us
    all_to_all x2, starting transfers between devices, joint_exchange(): received = lax.all_to_all(message, both, 0, 0, tiled=True)  6.12 us
    unnamed x35, local copies, waits for them, and re-layouts  4.4 us
    all_to_all x2, waiting for transfers between devices, owner_map(): gathered = lax.all_to_all(partial, both, 0, 0, tiled=True)  4.16 us
    pallas_call x1, Pallas kernels, local(): pl.pallas_call(first_volume_kernel, out_shape=shapes + (jax.ShapeDtypeStr...  3.19 us
    pallas_call x1, Pallas kernels, tendency(): pl.pallas_call(volume_kernel, out_shape=shapes)  2.9 us
  transfers between devices with their start and end apart: 8, of which 4 were waited for; matrix products, arithmetic and copies ran while one was open for 10% of the time, Pallas kernels for 5%

profile of v23, /device:TPU:0, one launch (start us, length us, event | category | flops | bytes accessed | tf_op | source)
XLA Modules:
  0.0 63.6 jit_solution(16800170180532232008)
XLA Ops:
  0.1 0.7 %copy-done.11 = s32[32]{0:T(128)S(1)} copy-done((s32[32]{0:T(128)S(1)}, s32[32]{0:T(128)}, u32[]{:S(2)}) %copy-start.11) | copy-done | bytes 152
  0.7 0.1 fusion.46
  0.9 0.1 copy.45
  1.0 0.6 broadcast_multiply_fusion.1.table_ref
  1.6 3.2 %shard_map.91 = (f32[3,128,128]{2,1,0:T(8,128)}, f32[2,3,8,128]{3,2,1,0:T(8,128)}, f32[2,1,384]{2,1,0:T(1,128)}, f32[64,128]{1,0:T(8,128)}, f32[9,128,128]{2,1,0:T(8,128)}) custom-call(f32[3,128,128]{2,1,0:T(8,128)} %bitcast.134, f32[3,128,128]{2,1,0:T(8,128)} %bitcast.130, f32[6,128,128]{2,1,0:T(8,128)} %constant.399.clone.mats_ref, ...), custom_call_target="tpu_custom_call" | custom-call | tf_op jit(solution)/shard_map/pallas_call | solution.py:399
  4.8 7.3 %all-to-all-start = ((f32[32,2,128]{2,1,0:T(2,128)}), f32[32,2,128]{2,1,0:T(2,128)S(1)}, u32[]{:S(2)}, u32[]{:S(2)}) async-start(f32[32,2,128]{2,1,0:T(2,128)} %bitcast.141), calls=%async_computation | async-start | bytes 65536 | tf_op jit(solution)/shard_map/all_to_all | solution.py:281
  12.1 0.3 collective-permute-start
  12.4 3.3 %collective-permute-start.1 = (f32[3,8,1,128]{3,1,0,2:T(8,128)S(1)}, f32[3,8,1,128]{3,1,0,2:T(8,128)S(1)}, u32[]{:S(2)}, u32[]{:S(2)}) collective-permute-start(f32[3,8,1,128]{3,1,0,2:T(8,128)S(1)} %get-tuple-element.52), channel_id=1, source_target_pairs={{4,0},{8,4},{12,8},{16,12},{20,16},{24,20},{28,24},{0,28},{5,1},{9... | collective-permute-start | bytes 36872 | tf_op jit(solution)/shard_map/ppermute | solution.py:312
  15.9 0.6 copy-done.7
  16.6 0.6 fusion.145
  17.4 0.1 broadcast_multiply_fusion
  17.5 1.9 %all-to-all-done = f32[32,2,128]{2,1,0:T(2,128)S(1)} async-done(((f32[32,2,128]{2,1,0:T(2,128)}), f32[32,2,128]{2,1,0:T(2,128)S(1)}, u32[]{:S(2)}, u32[]{:S(2)}) %all-to-all-start) | async-done | bytes 32800 | tf_op jit(solution)/shard_map/all_to_all | solution.py:281
  19.4 0.2 fusion.11
  19.7 0.1 fusion.53
  19.9 0.1 reshape_reshape.6
  20.0 0.8 %pad_maximum_fusion.1 = f32[32,1,644]{2,1,0:T(1,128)} fusion(f32[32,1,384]{2,1,0:T(1,128)S(1)} %constant_dynamic-update-slice_fusion.6, f32[32,1,260]{2,1,0:T(1,128)S(1)} %reshape_reshape.6), kind=kLoop, calls=%fused_computation.34 | loop fusion | flops 20608 | bytes 164864 | tf_op jit(solution)/shard_map/concatenate | solution.py:327
  20.8 2.6 %all-to-all-start.1 = ((f32[32,1,644]{2,1,0:T(1,128)}), f32[32,1,644]{2,1,0:T(1,128)S(1)}, u32[]{:S(2)}, u32[]{:S(2)}) async-start(f32[32,1,644]{2,1,0:T(1,128)} %pad_maximum_fusion.1), calls=%async_computation.1 | async-start | bytes 196608 | tf_op jit(solution)/shard_map/all_to_all | solution.py:328
  23.5 7.9 %all-to-all-done.1 = f32[32,1,644]{2,1,0:T(1,128)S(1)} async-done(((f32[32,1,644]{2,1,0:T(1,128)}), f32[32,1,644]{2,1,0:T(1,128)S(1)}, u32[]{:S(2)}, u32[]{:S(2)}) %all-to-all-start.1) | async-done | bytes 82464 | tf_op jit(solution)/shard_map/all_to_all | solution.py:328
  31.3 0.1 fusion.56
  31.5 0.1 reshape.1045
  31.6 0.1 reshape.1044
  31.8 0.1 reshape.1050
  31.9 0.1 reshape.1049
  32.0 0.1 pad_maximum_fusion.4
  32.1 0.2 reshape.1075
  32.3 0.2 reshape.1076
  32.5 0.1 pad_maximum_fusion.5
  32.6 0.1 slice_reduce_fusion.1
  32.8 0.1 reshape_reshape_squeeze.6
  32.8 0.2 fusion.5
  33.1 0.5 copy-done.3
  33.5 0.4 multiply_add_fusion
  34.3 0.8 %copy-done.1 = f32[3,8,16,128]{3,2,1,0:T(8,128)S(1)} copy-done((f32[3,8,16,128]{3,2,1,0:T(8,128)S(1)}, f32[3,8,16,128]{3,2,1,0:T(8,128)}, u32[]{:S(2)}) %copy-start.1) | copy-done | bytes 196632
  35.2 0.1 fusion.8
  35.4 0.3 fusion.38
  35.7 0.6 %copy.60 = f32[32,2,128]{2,1,0:T(2,128)} copy(f32[32,2,128]{2,0,1:T(8,128)S(1)} %fusion.38) | data formatting | bytes 65536 | tf_op jit(solution)/shard_map/dot_general | solution.py:416
  36.3 2.5 %all-to-all-start.2 = ((f32[32,2,128]{2,1,0:T(2,128)}), f32[32,2,128]{2,1,0:T(2,128)S(1)}, u32[]{:S(2)}, u32[]{:S(2)}) async-start(f32[32,2,128]{2,1,0:T(2,128)} %copy.60), calls=%async_computation.2 | async-start | bytes 65536 | tf_op jit(solution)/shard_map/all_to_all | solution.py:281
  39.2 1.1 %add_multiply_fusion = (f32[3,8,16,128]{3,2,1,0:T(8,128)S(1)}, f32[3,8,16,128]{3,2,1,0:T(8,128)}) fusion(f32[3,8,16,128]{3,2,1,0:T(8,128)S(1)} %copy-done.1, f32[8,16,128]{2,1,0:T(8,128)S(1)} %broadcast_multiply_fusion, f32[130,128]{1,0:T(8,128)S(1)} %copy-done.6, f32[130,128]{1,0:T(8,128)S(1)} %copy-done.5, f32[130,128]{1,0:T(8,128)S(1)} %copy-done.4, ...), kind=kOutput, calls=%fused_computation.33 | convolution fusion | flops 38750720 | bytes 1054728 | tf_op jit(solution)/shard_map/dot_general | solution.py:392
  40.3 2.9 %shard_map.92 = (f32[3,128,128]{2,1,0:T(8,128)}, f32[2,3,8,128]{3,2,1,0:T(8,128)}, f32[2,1,384]{2,1,0:T(1,128)}) custom-call(f32[3,128,128]{2,1,0:T(8,128)} %bitcast.137, f32[3,128,128]{2,1,0:T(8,128)} %bitcast.131, f32[9,128,128]{2,1,0:T(8,128)} %get-tuple-element.17.grad_ref, f32[6,128,128]{2,1,0:T(8,128)} %constant.399.clone.mats_ref, ...), custom_call_target="tpu_custom_call" | custom-call | tf_op jit(solution)/shard_map/pallas_call | solution.py:413
  43.2 0.7 %copy-done.8 = f32[2,1,384]{2,1,0:T(1,128)S(1)} copy-done((f32[2,1,384]{2,1,0:T(1,128)S(1)}, f32[2,1,384]{2,1,0:T(1,128)}, u32[]{:S(2)}) %copy-start.8) | copy-done | bytes 3096
  43.9 2.3 %all-to-all-done.2 = f32[32,2,128]{2,1,0:T(2,128)S(1)} async-done(((f32[32,2,128]{2,1,0:T(2,128)}), f32[32,2,128]{2,1,0:T(2,128)S(1)}, u32[]{:S(2)}, u32[]{:S(2)}) %all-to-all-start.2) | async-done | bytes 32800 | tf_op jit(solution)/shard_map/all_to_all | solution.py:281
  46.2 0.2 fusion.9
  46.5 0.1 fusion.51
  46.7 0.1 reshape_reshape.7
  46.8 0.8 %pad_maximum_fusion.2 = f32[32,1,644]{2,1,0:T(1,128)} fusion(f32[32,1,384]{2,1,0:T(1,128)S(1)} %constant_dynamic-update-slice_fusion, f32[32,1,260]{2,1,0:T(1,128)S(1)} %reshape_reshape.7), kind=kLoop, calls=%fused_computation.35 | loop fusion | flops 20608 | bytes 164864 | tf_op jit(solution)/shard_map/concatenate | solution.py:327
  47.7 3.6 %all-to-all-start.3 = ((f32[32,1,644]{2,1,0:T(1,128)}), f32[32,1,644]{2,1,0:T(1,128)S(1)}, u32[]{:S(2)}, u32[]{:S(2)}) async-start(f32[32,1,644]{2,1,0:T(1,128)} %pad_maximum_fusion.2), calls=%async_computation.3 | async-start | bytes 196608 | tf_op jit(solution)/shard_map/all_to_all | solution.py:328
  51.2 0.3 collective-permute-start.2
  51.6 3.3 %collective-permute-start.3 = (f32[3,8,1,128]{3,1,0,2:T(8,128)S(1)}, f32[3,8,1,128]{3,1,0,2:T(8,128)S(1)}, u32[]{:S(2)}, u32[]{:S(2)}) collective-permute-start(f32[3,8,1,128]{3,1,0,2:T(8,128)S(1)} %get-tuple-element.48), channel_id=1, source_target_pairs={{4,0},{8,4},{12,8},{16,12},{20,16},{24,20},{28,24},{0,28},{5,1},{9... | collective-permute-start | bytes 36872 | tf_op jit(solution)/shard_map/ppermute | solution.py:312
  54.8 4.5 %all-to-all-done.3 = f32[32,1,644]{2,1,0:T(1,128)S(1)} async-done(((f32[32,1,644]{2,1,0:T(1,128)}), f32[32,1,644]{2,1,0:T(1,128)S(1)}, u32[]{:S(2)}, u32[]{:S(2)}) %all-to-all-start.3) | async-done | bytes 82464 | tf_op jit(solution)/shard_map/all_to_all | solution.py:328
  59.3 0.1 fusion.62
  59.4 0.1 reshape.1063
  59.6 0.1 reshape.1062
  59.7 0.1 slice_reduce_fusion
  59.9 0.1 reshape_reshape_squeeze.7
  59.9 0.2 fusion.4
  60.2 0.1 reshape.1068
  60.2 0.1 reshape.1067
  60.3 0.1 pad_maximum_fusion.6
  60.4 0.2 reshape.1077
  60.7 0.2 reshape.1078
  60.9 0.1 pad_maximum_fusion.7
  61.0 0.6 copy-done.2
  61.6 0.4 maximum_add_fusion
  62.5 1.1 %fusion.1 = f32[3,8,16,128]{3,2,1,0:T(8,128)} fusion(f32[3,8,16,128]{3,2,1,0:T(8,128)S(1)} %get-tuple-element.73, f32[3,8,2,1,130]{4,3,2,1,0:T(1,128)S(1)} %copy.75, f32[3,8,2,6,130]{4,3,2,1,0:T(8,128)S(1)} %slice.286, f32[3,8,2,1,130]{4,3,2,1,0:T(1,128)S(1)} %copy.74, f32[8,16,128]{2,1,0:T(8,128)S(1)} %broadcast_multiply_fusion, ...), kind=kOutput, calls=%fused_computation.2 | convolution fusion | flops 38652416 | bytes 858120 | tf_op jit(solution)/shard_map/dot_general | solution.py:392
  (99 shorter events, 2.4 us)
Async XLA Ops:
  0.0 19.4 %copy-start = (bf16[1,512,512]{2,1,0:T(8,128)(2,1)S(1)}, bf16[1,512,512]{2,1,0:T(8,128)(2,1)}, u32[]{:S(2)}) copy-start(bf16[1,512,512]{2,1,0:T(8,128)(2,1)} %param.11) | copy-start | bytes 1572868
  0.0 0.7 %copy-start.11 = (s32[32]{0:T(128)S(1)}, s32[32]{0:T(128)}, u32[]{:S(2)}) copy-start(s32[32]{0:T(128)} %param.12) | copy-start | bytes 388
  4.8 7.3 %copy-start.10 = (f32[2,3,8,128]{3,2,1,0:T(8,128)S(1)}, f32[2,3,8,128]{3,2,1,0:T(8,128)}, u32[]{:S(2)}) copy-start(f32[2,3,8,128]{3,2,1,0:T(8,128)} %get-tuple-element.15) | copy-start | bytes 73732
  4.8 14.6 %all-to-all-start = ((f32[32,2,128]{2,1,0:T(2,128)}), f32[32,2,128]{2,1,0:T(2,128)S(1)}, u32[]{:S(2)}, u32[]{:S(2)}) async-start(f32[32,2,128]{2,1,0:T(2,128)} %bitcast.141), calls=%async_computation | async-start | bytes 65536 | tf_op jit(solution)/shard_map/all_to_all | solution.py:281
  12.1 19.8 %collective-permute-start = (f32[3,8,1,128]{3,1,0,2:T(8,128)S(1)}, f32[3,8,1,128]{3,1,0,2:T(8,128)S(1)}, u32[]{:S(2)}, u32[]{:S(2)}) collective-permute-start(f32[3,8,1,128]{3,1,0,2:T(8,128)S(1)} %get-tuple-element.51), channel_id=1, source_target_pairs={{0,4},{4,8},{8,12},{12,16},{16,20},{20,24},{24,28},{28,0},{1,5},{5... | collective-permute-start | bytes 36872 | tf_op jit(solution)/shard_map/ppermute | solution.py:311
  12.4 20.1 %collective-permute-start.1 = (f32[3,8,1,128]{3,1,0,2:T(8,128)S(1)}, f32[3,8,1,128]{3,1,0,2:T(8,128)S(1)}, u32[]{:S(2)}, u32[]{:S(2)}) collective-permute-start(f32[3,8,1,128]{3,1,0,2:T(8,128)S(1)} %get-tuple-element.52), channel_id=1, source_target_pairs={{4,0},{8,4},{12,8},{16,12},{20,16},{24,20},{28,24},{0,28},{5,1},{9... | collective-permute-start | bytes 36872 | tf_op jit(solution)/shard_map/ppermute | solution.py:312
  15.9 0.7 %copy-start.7 = (f32[2,1,384]{2,1,0:T(1,128)S(1)}, f32[2,1,384]{2,1,0:T(1,128)}, u32[]{:S(2)}) copy-start(f32[2,1,384]{2,1,0:T(1,128)} %get-tuple-element.14) | copy-start | bytes 9220
  20.8 10.5 %all-to-all-start.1 = ((f32[32,1,644]{2,1,0:T(1,128)}), f32[32,1,644]{2,1,0:T(1,128)S(1)}, u32[]{:S(2)}, u32[]{:S(2)}) async-start(f32[32,1,644]{2,1,0:T(1,128)} %pad_maximum_fusion.1), calls=%async_computation.1 | async-start | bytes 196608 | tf_op jit(solution)/shard_map/all_to_all | solution.py:328
  32.6 0.9 %copy-start.3 = (f32[3,128,128]{2,1,0:T(8,128)S(1)}, f32[3,128,128]{2,1,0:T(8,128)}, u32[]{:S(2)}) copy-start(f32[3,128,128]{2,1,0:T(8,128)} %get-tuple-element.16) | copy-start | bytes 589828
  34.2 0.9 %copy-start.1 = (f32[3,8,16,128]{3,2,1,0:T(8,128)S(1)}, f32[3,8,16,128]{3,2,1,0:T(8,128)}, u32[]{:S(2)}) copy-start(f32[3,8,16,128]{3,2,1,0:T(8,128)} %param.9) | copy-start | bytes 589828
  34.2 1.0 %copy-start.4 = (f32[130,128]{1,0:T(8,128)S(1)}, f32[130,128]{1,0:T(8,128)}, u32[]{:S(2)}) copy-start(f32[130,128]{1,0:T(8,128)} %constant.400.clone) | copy-start | bytes 199684
  34.2 1.0 %copy-start.5 = (f32[130,128]{1,0:T(8,128)S(1)}, f32[130,128]{1,0:T(8,128)}, u32[]{:S(2)}) copy-start(f32[130,128]{1,0:T(8,128)} %constant.401.clone) | copy-start | bytes 199684
  34.2 1.0 %copy-start.6 = (f32[130,128]{1,0:T(8,128)S(1)}, f32[130,128]{1,0:T(8,128)}, u32[]{:S(2)}) copy-start(f32[130,128]{1,0:T(8,128)} %constant.402.clone) | copy-start | bytes 199684
  36.3 9.9 %all-to-all-start.2 = ((f32[32,2,128]{2,1,0:T(2,128)}), f32[32,2,128]{2,1,0:T(2,128)S(1)}, u32[]{:S(2)}, u32[]{:S(2)}) async-start(f32[32,2,128]{2,1,0:T(2,128)} %copy.60), calls=%async_computation.2 | async-start | bytes 65536 | tf_op jit(solution)/shard_map/all_to_all | solution.py:281
  43.2 0.7 %copy-start.8 = (f32[2,1,384]{2,1,0:T(1,128)S(1)}, f32[2,1,384]{2,1,0:T(1,128)}, u32[]{:S(2)}) copy-start(f32[2,1,384]{2,1,0:T(1,128)} %get-tuple-element.18) | copy-start | bytes 9220
  47.7 3.6 %copy-start.9 = (f32[2,3,8,128]{3,2,1,0:T(8,128)S(1)}, f32[2,3,8,128]{3,2,1,0:T(8,128)}, u32[]{:S(2)}) copy-start(f32[2,3,8,128]{3,2,1,0:T(8,128)} %get-tuple-element.19) | copy-start | bytes 73732
  47.7 11.6 %all-to-all-start.3 = ((f32[32,1,644]{2,1,0:T(1,128)}), f32[32,1,644]{2,1,0:T(1,128)S(1)}, u32[]{:S(2)}, u32[]{:S(2)}) async-start(f32[32,1,644]{2,1,0:T(1,128)} %pad_maximum_fusion.2), calls=%async_computation.3 | async-start | bytes 196608 | tf_op jit(solution)/shard_map/all_to_all | solution.py:328
  51.2 9.1 %collective-permute-start.2 = (f32[3,8,1,128]{3,1,0,2:T(8,128)S(1)}, f32[3,8,1,128]{3,1,0,2:T(8,128)S(1)}, u32[]{:S(2)}, u32[]{:S(2)}) collective-permute-start(f32[3,8,1,128]{3,1,0,2:T(8,128)S(1)} %get-tuple-element.47), channel_id=1, source_target_pairs={{0,4},{4,8},{8,12},{12,16},{16,20},{20,24},{24,28},{28,0},{1,5},{5... | collective-permute-start | bytes 36872 | tf_op jit(solution)/shard_map/ppermute | solution.py:311
  51.6 9.3 %collective-permute-start.3 = (f32[3,8,1,128]{3,1,0,2:T(8,128)S(1)}, f32[3,8,1,128]{3,1,0,2:T(8,128)S(1)}, u32[]{:S(2)}, u32[]{:S(2)}) collective-permute-start(f32[3,8,1,128]{3,1,0,2:T(8,128)S(1)} %get-tuple-element.48), channel_id=1, source_target_pairs={{4,0},{8,4},{12,8},{16,12},{20,16},{24,20},{28,24},{0,28},{5,1},{9... | collective-permute-start | bytes 36872 | tf_op jit(solution)/shard_map/ppermute | solution.py:312
  60.7 0.9 %copy-start.2 = (f32[3,128,128]{2,1,0:T(8,128)S(1)}, f32[3,128,128]{2,1,0:T(8,128)}, u32[]{:S(2)}) copy-start(f32[3,128,128]{2,1,0:T(8,128)} %get-tuple-element.20) | copy-start | bytes 589828

commit v24 on v23

--- a/solution.py
+++ b/solution.py
@@ -433,7 +433,8 @@
 
     first_rate, first_outer = tendency(field, None)
     section = field + time_step * first_rate
-    section_outer = field[0, radial_nodes - 1] + time_step * first_outer
+    field_outer = lax.optimization_barrier(field[0, radial_nodes - 1])
+    section_outer = field_outer + time_step * first_outer
     second_rate, _ = tendency(section, section_outer)
     settled = lax.optimization_barrier(0.5 * (field + section))
     return settled + (0.5 * time_step) * second_rate

time: 64.1 us -> 64.3 us (level)
    another operation x2, local copies, waits for them, and re-layouts: 0.01 us -> 0.73 us  [joint_exchange(): a_hi = edge_rows[1].reshape(3, radial_nodes, 1, nb_dev)]
    unnamed x35 -> x33, local copies, waits for them, and re-layouts: 4.4 us -> 4.29 us
  transfers between devices with their start and end apart: 8 -> 8, of which waited for: 4 -> 4; matrix products, arithmetic and copies ran while one was open for 10% -> 12% of each run, Pallas kernels for 5% -> 5%
where the time goes in v24:
time: 64.3 us; the launch traced here: 63.7 us
  starting transfers between devices  23.4 us (36%)
  waiting for transfers between devices  15.9 us (25%)
  local copies, waits for them, and re-layouts  9.11 us (14%)
  Pallas kernels  6.06 us (9%)
  other arithmetic  5.12 us (8%)
  matrix products  3.51 us (5%)
  between operations  0.66 us (1%)
    all_to_all x2, waiting for transfers between devices, joint_exchange(): received = lax.all_to_all(message, both, 0, 0, tiled=True)  12.3 us
    all_to_all x2, starting transfers between devices, owner_map(): gathered = lax.all_to_all(partial, both, 0, 0, tiled=True)  9.85 us
    ppermute x2, starting transfers between devices, joint_exchange(): from_down = lax.ppermute(a_lo, 'tile', down)  6.59 us
    all_to_all x2, starting transfers between devices, joint_exchange(): received = lax.all_to_all(message, both, 0, 0, tiled=True)  6.38 us
    unnamed x33, local copies, waits for them, and re-layouts  4.29 us
    all_to_all x2, waiting for transfers between devices, owner_map(): gathered = lax.all_to_all(partial, both, 0, 0, tiled=True)  3.52 us
    pallas_call x1, Pallas kernels, local(): pl.pallas_call(first_volume_kernel, out_shape=shapes + (jax.ShapeDtypeStr...  3.18 us
    pallas_call x1, Pallas kernels, tendency(): pl.pallas_call(volume_kernel, out_shape=shapes)  2.88 us
  transfers between devices with their start and end apart: 8, of which 4 were waited for; matrix products, arithmetic and copies ran while one was open for 12% of the time, Pallas kernels for 5%

profile of v24, /device:TPU:0, one launch (start us, length us, event | category | flops | bytes accessed | tf_op | source)
XLA Modules:
  0.0 63.7 jit_solution(4490851400443994188)
XLA Ops:
  0.1 0.7 %copy-done.10 = s32[32]{0:T(128)S(1)} copy-done((s32[32]{0:T(128)S(1)}, s32[32]{0:T(128)}, u32[]{:S(2)}) %copy-start.10) | copy-done | bytes 152
  0.7 0.1 fusion.46
  0.9 0.1 copy.45
  1.0 0.6 broadcast_multiply_fusion.1.table_ref
  1.6 3.2 %shard_map.91 = (f32[3,128,128]{2,1,0:T(8,128)}, f32[2,3,8,128]{3,2,1,0:T(8,128)}, f32[2,1,384]{2,1,0:T(1,128)}, f32[64,128]{1,0:T(8,128)}, f32[9,128,128]{2,1,0:T(8,128)}) custom-call(f32[3,128,128]{2,1,0:T(8,128)} %bitcast.134, f32[3,128,128]{2,1,0:T(8,128)} %bitcast.130, f32[6,128,128]{2,1,0:T(8,128)} %constant.399.clone.mats_ref, ...), custom_call_target="tpu_custom_call" | custom-call | tf_op jit(solution)/shard_map/pallas_call | solution.py:399
  4.8 7.3 %all-to-all-start = ((f32[32,2,128]{2,1,0:T(2,128)}), f32[32,2,128]{2,1,0:T(2,128)S(1)}, u32[]{:S(2)}, u32[]{:S(2)}) async-start(f32[32,2,128]{2,1,0:T(2,128)} %bitcast.141), calls=%async_computation | async-start | bytes 65536 | tf_op jit(solution)/shard_map/all_to_all | solution.py:281
  12.1 0.7 %slice_bitcast_fusion.23 = (f32[3,8,1,128]{3,1,0,2:T(8,128)S(1)}, f32[3,8,1,128]{3,1,0,2:T(8,128)S(1)}) fusion(f32[2,3,8,128]{3,2,1,0:T(8,128)} %get-tuple-element.15), kind=kLoop, calls=%fused_computation.98 | loop fusion | bytes 49152 | tf_op jit(solution)/shard_map/reshape;squeeze | solution.py:308
  12.8 0.3 collective-permute-start
  13.0 3.3 %collective-permute-start.1 = (f32[3,8,1,128]{3,1,0,2:T(8,128)S(1)}, f32[3,8,1,128]{3,1,0,2:T(8,128)S(1)}, u32[]{:S(2)}, u32[]{:S(2)}) collective-permute-start(f32[3,8,1,128]{3,1,0,2:T(8,128)S(1)} %get-tuple-element.52), channel_id=1, source_target_pairs={{4,0},{8,4},{12,8},{16,12},{20,16},{24,20},{28,24},{0,28},{5,1},{9... | collective-permute-start | bytes 36872 | tf_op jit(solution)/shard_map/ppermute | solution.py:312
  16.6 0.6 copy-done.7
  17.2 0.6 fusion.145
  18.0 0.1 broadcast_multiply_fusion
  18.2 1.2 %all-to-all-done = f32[32,2,128]{2,1,0:T(2,128)S(1)} async-done(((f32[32,2,128]{2,1,0:T(2,128)}), f32[32,2,128]{2,1,0:T(2,128)S(1)}, u32[]{:S(2)}, u32[]{:S(2)}) %all-to-all-start) | async-done | bytes 32800 | tf_op jit(solution)/shard_map/all_to_all | solution.py:281
  19.4 0.2 fusion.11
  19.7 0.1 fusion.53
  19.8 0.1 reshape_reshape.6
  20.0 0.8 %pad_maximum_fusion.1 = f32[32,1,644]{2,1,0:T(1,128)} fusion(f32[32,1,384]{2,1,0:T(1,128)S(1)} %constant_dynamic-update-slice_fusion.6, f32[32,1,260]{2,1,0:T(1,128)S(1)} %reshape_reshape.6), kind=kLoop, calls=%fused_computation.34 | loop fusion | flops 20608 | bytes 164864 | tf_op jit(solution)/shard_map/concatenate | solution.py:327
  20.8 2.8 %all-to-all-start.1 = ((f32[32,1,644]{2,1,0:T(1,128)}), f32[32,1,644]{2,1,0:T(1,128)S(1)}, u32[]{:S(2)}, u32[]{:S(2)}) async-start(f32[32,1,644]{2,1,0:T(1,128)} %pad_maximum_fusion.1), calls=%async_computation.1 | async-start | bytes 196608 | tf_op jit(solution)/shard_map/all_to_all | solution.py:328
  23.7 7.9 %all-to-all-done.1 = f32[32,1,644]{2,1,0:T(1,128)S(1)} async-done(((f32[32,1,644]{2,1,0:T(1,128)}), f32[32,1,644]{2,1,0:T(1,128)S(1)}, u32[]{:S(2)}, u32[]{:S(2)}) %all-to-all-start.1) | async-done | bytes 82464 | tf_op jit(solution)/shard_map/all_to_all | solution.py:328
  31.6 0.1 fusion.56
  31.7 0.1 reshape.1045
  31.9 0.1 reshape.1044
  32.0 0.1 reshape.1050
  32.1 0.1 reshape.1049
  32.2 0.1 pad_maximum_fusion.4
  32.3 0.2 reshape.1075
  32.6 0.2 reshape.1076
  32.8 0.1 pad_maximum_fusion.5
  32.9 0.1 slice_reduce_fusion.1
  33.1 0.2 fusion.5
  33.3 0.5 copy-done.3
  33.8 0.4 multiply_add_fusion
  34.5 0.8 %copy-done.4 = f32[130,128]{1,0:T(8,128)S(1)} copy-done((f32[130,128]{1,0:T(8,128)S(1)}, f32[130,128]{1,0:T(8,128)}, u32[]{:S(2)}) %copy-start.4) | copy-done | bytes 66584
  35.4 0.1 fusion.8
  35.5 0.3 fusion.38
  35.9 0.6 copy.60
  36.5 2.6 %all-to-all-start.2 = ((f32[32,2,128]{2,1,0:T(2,128)}), f32[32,2,128]{2,1,0:T(2,128)S(1)}, u32[]{:S(2)}, u32[]{:S(2)}) async-start(f32[32,2,128]{2,1,0:T(2,128)} %copy.60), calls=%async_computation.2 | async-start | bytes 65536 | tf_op jit(solution)/shard_map/all_to_all | solution.py:281
  39.3 1.1 %add_multiply_fusion = (f32[3,8,16,128]{3,2,1,0:T(8,128)S(1)}, f32[3,8,16,128]{3,2,1,0:T(8,128)}) fusion(f32[3,8,16,128]{3,2,1,0:T(8,128)S(1)} %copy-done.1, f32[8,16,128]{2,1,0:T(8,128)S(1)} %broadcast_multiply_fusion, f32[130,128]{1,0:T(8,128)S(1)} %copy-done.6, f32[130,128]{1,0:T(8,128)S(1)} %copy-done.5, f32[130,128]{1,0:T(8,128)S(1)} %copy-done.4, ...), kind=kOutput, calls=%fused_computation.33 | convolution fusion | flops 38750720 | bytes 1054728 | tf_op jit(solution)/shard_map/dot_general | solution.py:392
  40.4 2.9 %shard_map.92 = (f32[3,128,128]{2,1,0:T(8,128)}, f32[2,3,8,128]{3,2,1,0:T(8,128)}, f32[2,1,384]{2,1,0:T(1,128)}) custom-call(f32[3,128,128]{2,1,0:T(8,128)} %bitcast.137, f32[3,128,128]{2,1,0:T(8,128)} %bitcast.131, f32[9,128,128]{2,1,0:T(8,128)} %get-tuple-element.17.grad_ref, f32[6,128,128]{2,1,0:T(8,128)} %constant.399.clone.mats_ref, ...), custom_call_target="tpu_custom_call" | custom-call | tf_op jit(solution)/shard_map/pallas_call | solution.py:413
  43.3 0.6 %copy-done.8 = f32[2,1,384]{2,1,0:T(1,128)S(1)} copy-done((f32[2,1,384]{2,1,0:T(1,128)S(1)}, f32[2,1,384]{2,1,0:T(1,128)}, u32[]{:S(2)}) %copy-start.8) | copy-done | bytes 3096
  44.0 2.3 %all-to-all-done.2 = f32[32,2,128]{2,1,0:T(2,128)S(1)} async-done(((f32[32,2,128]{2,1,0:T(2,128)}), f32[32,2,128]{2,1,0:T(2,128)S(1)}, u32[]{:S(2)}, u32[]{:S(2)}) %all-to-all-start.2) | async-done | bytes 32800 | tf_op jit(solution)/shard_map/all_to_all | solution.py:281
  46.4 0.2 fusion.9
  46.7 0.1 fusion.51
  46.8 0.1 reshape_reshape.7
  47.0 0.8 %pad_maximum_fusion.2 = f32[32,1,644]{2,1,0:T(1,128)} fusion(f32[32,1,384]{2,1,0:T(1,128)S(1)} %constant_dynamic-update-slice_fusion, f32[32,1,260]{2,1,0:T(1,128)S(1)} %reshape_reshape.7), kind=kLoop, calls=%fused_computation.35 | loop fusion | flops 20608 | bytes 164864 | tf_op jit(solution)/shard_map/concatenate | solution.py:327
  47.8 3.5 %all-to-all-start.3 = ((f32[32,1,644]{2,1,0:T(1,128)}), f32[32,1,644]{2,1,0:T(1,128)S(1)}, u32[]{:S(2)}, u32[]{:S(2)}) async-start(f32[32,1,644]{2,1,0:T(1,128)} %pad_maximum_fusion.2), calls=%async_computation.3 | async-start | bytes 196608 | tf_op jit(solution)/shard_map/all_to_all | solution.py:328
  51.4 0.3 collective-permute-start.2
  51.7 3.3 %collective-permute-start.3 = (f32[3,8,1,128]{3,1,0,2:T(8,128)S(1)}, f32[3,8,1,128]{3,1,0,2:T(8,128)S(1)}, u32[]{:S(2)}, u32[]{:S(2)}) collective-permute-start(f32[3,8,1,128]{3,1,0,2:T(8,128)S(1)} %get-tuple-element.48), channel_id=1, source_target_pairs={{4,0},{8,4},{12,8},{16,12},{20,16},{24,20},{28,24},{0,28},{5,1},{9... | collective-permute-start | bytes 36872 | tf_op jit(solution)/shard_map/ppermute | solution.py:312
  55.0 4.5 %all-to-all-done.3 = f32[32,1,644]{2,1,0:T(1,128)S(1)} async-done(((f32[32,1,644]{2,1,0:T(1,128)}), f32[32,1,644]{2,1,0:T(1,128)S(1)}, u32[]{:S(2)}, u32[]{:S(2)}) %all-to-all-start.3) | async-done | bytes 82464 | tf_op jit(solution)/shard_map/all_to_all | solution.py:328
  59.4 0.1 fusion.62
  59.5 0.1 reshape.1063
  59.7 0.1 reshape.1062
  59.8 0.1 slice_reduce_fusion
  60.0 0.1 reshape_reshape_squeeze.7
  60.1 0.2 fusion.4
  60.3 0.1 reshape.1068
  60.4 0.1 reshape.1067
  60.5 0.1 pad_maximum_fusion.6
  60.6 0.2 reshape.1077
  60.8 0.2 reshape.1078
  61.0 0.1 pad_maximum_fusion.7
  61.1 0.6 copy-done.2
  61.7 0.4 maximum_add_fusion
  62.6 1.1 %fusion.1 = f32[3,8,16,128]{3,2,1,0:T(8,128)} fusion(f32[3,8,16,128]{3,2,1,0:T(8,128)S(1)} %get-tuple-element.73, f32[3,8,2,1,130]{4,3,2,1,0:T(1,128)S(1)} %copy.75, f32[3,8,2,6,130]{4,3,2,1,0:T(8,128)S(1)} %slice.286, f32[3,8,2,1,130]{4,3,2,1,0:T(1,128)S(1)} %copy.74, f32[8,16,128]{2,1,0:T(8,128)S(1)} %broadcast_multiply_fusion, ...), kind=kOutput, calls=%fused_computation.2 | convolution fusion | flops 38652416 | bytes 858120 | tf_op jit(solution)/shard_map/dot_general | solution.py:392
  (98 shorter events, 2.4 us)
Async XLA Ops:
  0.0 19.4 %copy-start = (bf16[1,512,512]{2,1,0:T(8,128)(2,1)S(1)}, bf16[1,512,512]{2,1,0:T(8,128)(2,1)}, u32[]{:S(2)}) copy-start(bf16[1,512,512]{2,1,0:T(8,128)(2,1)} %param.11) | copy-start | bytes 1572868
  0.0 0.7 %copy-start.10 = (s32[32]{0:T(128)S(1)}, s32[32]{0:T(128)}, u32[]{:S(2)}) copy-start(s32[32]{0:T(128)} %param.12) | copy-start | bytes 388
  4.8 11.7 %copy-start.1 = (f32[3,8,16,128]{3,2,1,0:T(8,128)S(1)}, f32[3,8,16,128]{3,2,1,0:T(8,128)}, u32[]{:S(2)}) copy-start(f32[3,8,16,128]{3,2,1,0:T(8,128)} %param.9) | copy-start | bytes 589828
  4.8 14.6 %all-to-all-start = ((f32[32,2,128]{2,1,0:T(2,128)}), f32[32,2,128]{2,1,0:T(2,128)S(1)}, u32[]{:S(2)}, u32[]{:S(2)}) async-start(f32[32,2,128]{2,1,0:T(2,128)} %bitcast.141), calls=%async_computation | async-start | bytes 65536 | tf_op jit(solution)/shard_map/all_to_all | solution.py:281
  12.8 19.4 %collective-permute-start = (f32[3,8,1,128]{3,1,0,2:T(8,128)S(1)}, f32[3,8,1,128]{3,1,0,2:T(8,128)S(1)}, u32[]{:S(2)}, u32[]{:S(2)}) collective-permute-start(f32[3,8,1,128]{3,1,0,2:T(8,128)S(1)} %get-tuple-element.51), channel_id=1, source_target_pairs={{0,4},{4,8},{8,12},{12,16},{16,20},{20,24},{24,28},{28,0},{1,5},{5... | collective-permute-start | bytes 36872 | tf_op jit(solution)/shard_map/ppermute | solution.py:311
  13.0 19.7 %collective-permute-start.1 = (f32[3,8,1,128]{3,1,0,2:T(8,128)S(1)}, f32[3,8,1,128]{3,1,0,2:T(8,128)S(1)}, u32[]{:S(2)}, u32[]{:S(2)}) collective-permute-start(f32[3,8,1,128]{3,1,0,2:T(8,128)S(1)} %get-tuple-element.52), channel_id=1, source_target_pairs={{4,0},{8,4},{12,8},{16,12},{20,16},{24,20},{28,24},{0,28},{5,1},{9... | collective-permute-start | bytes 36872 | tf_op jit(solution)/shard_map/ppermute | solution.py:312
  16.5 0.7 %copy-start.7 = (f32[2,1,384]{2,1,0:T(1,128)S(1)}, f32[2,1,384]{2,1,0:T(1,128)}, u32[]{:S(2)}) copy-start(f32[2,1,384]{2,1,0:T(1,128)} %get-tuple-element.14) | copy-start | bytes 9220
  20.8 10.8 %all-to-all-start.1 = ((f32[32,1,644]{2,1,0:T(1,128)}), f32[32,1,644]{2,1,0:T(1,128)S(1)}, u32[]{:S(2)}, u32[]{:S(2)}) async-start(f32[32,1,644]{2,1,0:T(1,128)} %pad_maximum_fusion.1), calls=%async_computation.1 | async-start | bytes 196608 | tf_op jit(solution)/shard_map/all_to_all | solution.py:328
  32.9 0.9 %copy-start.3 = (f32[3,128,128]{2,1,0:T(8,128)S(1)}, f32[3,128,128]{2,1,0:T(8,128)}, u32[]{:S(2)}) copy-start(f32[3,128,128]{2,1,0:T(8,128)} %get-tuple-element.16) | copy-start | bytes 589828
  34.4 0.9 %copy-start.4 = (f32[130,128]{1,0:T(8,128)S(1)}, f32[130,128]{1,0:T(8,128)}, u32[]{:S(2)}) copy-start(f32[130,128]{1,0:T(8,128)} %constant.400.clone) | copy-start | bytes 199684
  34.5 0.9 %copy-start.5 = (f32[130,128]{1,0:T(8,128)S(1)}, f32[130,128]{1,0:T(8,128)}, u32[]{:S(2)}) copy-start(f32[130,128]{1,0:T(8,128)} %constant.401.clone) | copy-start | bytes 199684
  34.5 0.9 %copy-start.6 = (f32[130,128]{1,0:T(8,128)S(1)}, f32[130,128]{1,0:T(8,128)}, u32[]{:S(2)}) copy-start(f32[130,128]{1,0:T(8,128)} %constant.402.clone) | copy-start | bytes 199684
  36.5 9.9 %all-to-all-start.2 = ((f32[32,2,128]{2,1,0:T(2,128)}), f32[32,2,128]{2,1,0:T(2,128)S(1)}, u32[]{:S(2)}, u32[]{:S(2)}) async-start(f32[32,2,128]{2,1,0:T(2,128)} %copy.60), calls=%async_computation.2 | async-start | bytes 65536 | tf_op jit(solution)/shard_map/all_to_all | solution.py:281
  43.3 0.7 %copy-start.8 = (f32[2,1,384]{2,1,0:T(1,128)S(1)}, f32[2,1,384]{2,1,0:T(1,128)}, u32[]{:S(2)}) copy-start(f32[2,1,384]{2,1,0:T(1,128)} %get-tuple-element.18) | copy-start | bytes 9220
  47.8 3.5 %copy-start.9 = (f32[2,3,8,128]{3,2,1,0:T(8,128)S(1)}, f32[2,3,8,128]{3,2,1,0:T(8,128)}, u32[]{:S(2)}) copy-start(f32[2,3,8,128]{3,2,1,0:T(8,128)} %get-tuple-element.19) | copy-start | bytes 73732
  47.8 11.6 %all-to-all-start.3 = ((f32[32,1,644]{2,1,0:T(1,128)}), f32[32,1,644]{2,1,0:T(1,128)S(1)}, u32[]{:S(2)}, u32[]{:S(2)}) async-start(f32[32,1,644]{2,1,0:T(1,128)} %pad_maximum_fusion.2), calls=%async_computation.3 | async-start | bytes 196608 | tf_op jit(solution)/shard_map/all_to_all | solution.py:328
  51.4 9.1 %collective-permute-start.2 = (f32[3,8,1,128]{3,1,0,2:T(8,128)S(1)}, f32[3,8,1,128]{3,1,0,2:T(8,128)S(1)}, u32[]{:S(2)}, u32[]{:S(2)}) collective-permute-start(f32[3,8,1,128]{3,1,0,2:T(8,128)S(1)} %get-tuple-element.47), channel_id=1, source_target_pairs={{0,4},{4,8},{8,12},{12,16},{16,20},{20,24},{24,28},{28,0},{1,5},{5... | collective-permute-start | bytes 36872 | tf_op jit(solution)/shard_map/ppermute | solution.py:311
  51.7 9.3 %collective-permute-start.3 = (f32[3,8,1,128]{3,1,0,2:T(8,128)S(1)}, f32[3,8,1,128]{3,1,0,2:T(8,128)S(1)}, u32[]{:S(2)}, u32[]{:S(2)}) collective-permute-start(f32[3,8,1,128]{3,1,0,2:T(8,128)S(1)} %get-tuple-element.48), channel_id=1, source_target_pairs={{4,0},{8,4},{12,8},{16,12},{20,16},{24,20},{28,24},{0,28},{5,1},{9... | collective-permute-start | bytes 36872 | tf_op jit(solution)/shard_map/ppermute | solution.py:312
  60.8 0.9 %copy-start.2 = (f32[3,128,128]{2,1,0:T(8,128)S(1)}, f32[3,128,128]{2,1,0:T(8,128)}, u32[]{:S(2)}) copy-start(f32[3,128,128]{2,1,0:T(8,128)} %get-tuple-element.20) | copy-start | bytes 589828
